TPU v7x, 256 devices: a whole 4x4x8 slice. The times are simulated.
256 devices in a mesh: ctx: 32 (over x, z_lo, core), tp: 8 (over z_hi, y).
Axes of the slice: x: 4, y: 4, z: 8 (z_hi: 2, z_lo: 4; z = z_hi * 4 + z_lo), core: 2. Of those that a mesh axis runs over, the one named last changes fastest.
Arguments:
- queries: bfloat16 [8192, 8192], P('ctx', 'tp'), may hold values from -8 to 8
- key_rows: bfloat16 [8192, 1024], P('ctx', 'tp'), may hold values from -8 to 8
- value_head_rows: bfloat16 [8192, 1024], P('ctx', 'tp'), may hold values from -6 to 6
- ssm_input: bfloat16 [8192, 8192], P('ctx', 'tp'), may hold values from -6 to 6
- gate_input: bfloat16 [8192, 8192], P('ctx', 'tp'), may hold values from -6 to 6
- b_matrix: bfloat16 [8192, 1024], P('ctx', 'tp'), may hold values from -6 to 6
- c_matrix: bfloat16 [8192, 1024], P('ctx', 'tp'), may hold values from -0.5 to 0.5
- step_size: float32 [128, 8192], P('tp', 'ctx'), may hold values from 0.02 to 0.2
- log_decay: float32 [128, 8192], P('tp', 'ctx'), may hold values from -1.5 to 0
- skip_gain: float32 [128], P('tp'), may hold values from 0.5 to 1.5
- norm_gain: bfloat16 [8192], P('tp'), may hold values from 0.099609375 to 1.8984375
Outputs:
- attention_out: bfloat16 [8192, 8192], P('ctx', 'tp')
- mixer_out: bfloat16 [8192, 8192], P('ctx', 'tp')
All inputs are finite; a program needn't handle non-finite values.
Results may differ from a plain program's by a relative error of at most 0.022.
Values may be sent and summed in bfloat16 or wider, within the bound.
No kernel may reach another device: no remote copies, remote signals or barrier semaphores. Data moves between devices by JAX's collectives and lax.ppermute only.
A program may use at most 128 MiB of HBM per device.

v0:
```python
import math

import jax
import jax.numpy as jnp
from jax import lax
from jax.sharding import PartitionSpec as P

HEAD_WIDTH = 128
STATE_HEADS = 128
P_SIZE = 64
N = 128


causal_score = -1e30


def passed_along(block, axis, distance):
    devices = range(lax.axis_size(axis))
    route = [(i - distance, i) for i in devices if i - distance in devices]
    return lax.ppermute(block, axis, route)


def attend_rows(running_in, key_block, value_block, key_start, query_head_rows, query_pos):
    row_count = key_block.shape[0]
    sub_width = math.gcd(row_count, 512)
    kv_heads = query_head_rows.shape[1]
    score_factor = query_head_rows.shape[3] ** (-0.5)

    def sub_step(sub_id, running):
        run_max, run_sum, summed_so_far = running
        offset = sub_id * sub_width
        key_portion = key_block.reshape(sub_width, kv_heads, -1)
        value_portion = value_block.reshape(sub_width, kv_heads, -1)
        key_pos = key_start + offset + jnp.arange(sub_width, dtype=jnp.int32)
        is_valid = key_pos[None, :] <= query_pos[:, None]
        score_matrix = (
            jnp.einsum(
                "faqo,bao->aqfb", query_head_rows, key_portion, preferred_element_type=jnp.float32
            )
            * score_factor
        )
        score_matrix = jnp.where(is_valid, score_matrix, causal_score)
        new_max = jnp.maximum(run_max, jnp.max(score_matrix, axis=-1))
        weights = jnp.where(is_valid, jnp.exp(score_matrix - new_max[..., None]), 0.0)
        correction_factor = jnp.exp(run_max - new_max)
        run_sum = run_sum * correction_factor + jnp.sum(weights, axis=-1)
        summed_so_far = summed_so_far * correction_factor[..., None] + jnp.einsum(
            "wlhc,cwm->wlhm",
            weights.astype(jnp.bfloat16),
            value_portion,
            preferred_element_type=jnp.float32,
        )
        return (new_max, run_sum, summed_so_far)

    return lax.fori_loop(0, row_count // sub_width, sub_step, running_in)


def local(
    queries,
    key_rows,
    value_head_rows,
    ssm_input,
    gate_input,
    b_matrix,
    c_matrix,
    step_size,
    log_decay,
    skip_gain,
    norm_gain,
):
    tok_rows = queries.shape[0]
    kv_heads = key_rows.shape[1] // HEAD_WIDTH
    query_per_key_heads = queries.shape[1] // HEAD_WIDTH // kv_heads
    query_head_rows = queries.reshape(tok_rows, kv_heads, query_per_key_heads, HEAD_WIDTH)
    ctx_count = lax.axis_size("ctx")
    position = lax.axis_index("ctx")
    query_pos = position * tok_rows + jnp.arange(tok_rows, dtype=jnp.int32)
    starting_state = (
        jnp.full((kv_heads, query_per_key_heads, tok_rows), causal_score, jnp.float32),
        jnp.zeros((kv_heads, query_per_key_heads, tok_rows), jnp.float32),
        jnp.zeros((kv_heads, query_per_key_heads, tok_rows, HEAD_WIDTH), jnp.float32),
    )
    first_pass = attend_rows(
        starting_state, key_rows, value_head_rows, position * tok_rows, query_head_rows, query_pos
    )

    def cycle_step(step_id, state):
        stacked, running = state
        stacked = passed_along(stacked, "ctx", 1)
        sender_index = position - step_id
        key_start = jnp.where(sender_index >= 0, sender_index * tok_rows, ctx_count * tok_rows)
        return (
            stacked,
            attend_rows(running, stacked[0], stacked[1], key_start, query_head_rows, query_pos),
        )

    _, (run_max, run_sum, summed_so_far) = lax.fori_loop(
        1, ctx_count, cycle_step, (jnp.stack((key_rows, value_head_rows)), first_pass)
    )
    attention_out = (
        (summed_so_far / run_sum[..., None])
        .transpose(2, 0, 1, 3)
        .reshape(tok_rows, -1)
        .astype(jnp.bfloat16)
    )
    heads_local = step_size.shape[0]
    groups_local = b_matrix.shape[1] // N
    heads_group = heads_local // groups_local
    mixer_in = ssm_input.reshape(tok_rows, groups_local, heads_group, P_SIZE)
    in_maps = b_matrix.reshape(tok_rows, groups_local, N)
    out_maps = c_matrix.reshape(tok_rows, groups_local, N)
    steps_here = step_size.reshape(groups_local, heads_group, tok_rows)
    cumul = jnp.cumsum(log_decay.reshape(groups_local, heads_group, tok_rows), axis=-1)
    causal = jnp.tril(jnp.ones((tok_rows, tok_rows), dtype=bool))
    gram = jnp.einsum("tgn,sgn->gts", out_maps, in_maps, preferred_element_type=jnp.float32)
    spread = jnp.where(causal, cumul[..., :, None] - cumul[..., None, :], 0.0)
    mixing = jnp.where(
        causal, gram[:, None] * jnp.exp(spread) * steps_here[..., None, :], 0.0
    ).astype(jnp.bfloat16)
    inner = jnp.einsum("ghts,sghp->tghp", mixing, mixer_in, preferred_element_type=jnp.float32)
    weight_end = jnp.exp(cumul[..., -1:] - cumul) * steps_here
    weighted = (mixer_in * weight_end.transpose(2, 0, 1)[..., None]).astype(jnp.bfloat16)
    local_state = jnp.einsum(
        "sghp,sgn->ghpn", weighted, in_maps, preferred_element_type=jnp.float32
    )
    block_decay = jnp.exp(cumul[..., -1])

    def relay_step(step_id, pair):
        received, outgoing = pair
        received = passed_along(outgoing.astype(jnp.bfloat16), "ctx", 1).astype(outgoing.dtype)
        return (received, block_decay[..., None, None] * received + local_state)

    incoming, _ = lax.fori_loop(
        1, ctx_count, relay_step, (jnp.zeros_like(local_state), local_state)
    )
    carried_out = jnp.einsum(
        "ghpn,tgn->tghp", incoming, out_maps.astype(jnp.float32), precision=lax.Precision.HIGHEST
    )
    carried_out = carried_out * jnp.exp(cumul).transpose(2, 0, 1)[..., None]
    direct = skip_gain.reshape(groups_local, heads_group)[None, :, :, None] * mixer_in.astype(
        jnp.float32
    )
    outputs = (inner + carried_out + direct).reshape(tok_rows, -1)
    gated = outputs * jax.nn.silu(gate_input.astype(jnp.float32))
    square_total = lax.psum(jnp.sum(gated * gated, axis=-1), "tp")
    scaling = lax.rsqrt(square_total / (STATE_HEADS * P_SIZE) + 1e-05)
    mixer_out = (gated * scaling[:, None] * norm_gain.astype(jnp.float32)).astype(jnp.bfloat16)
    return (attention_out, mixer_out)


def solution(mesh):
    placed = (
        P("ctx", "tp"),
        P("ctx", "tp"),
        P("ctx", "tp"),
        P("ctx", "tp"),
        P("ctx", "tp"),
        P("ctx", "tp"),
        P("ctx", "tp"),
        P("tp", "ctx"),
        P("tp", "ctx"),
        P("tp"),
        P("tp"),
    )
    return jax.shard_map(
        local,
        mesh=mesh,
        in_specs=placed,
        out_specs=(P("ctx", "tp"), P("ctx", "tp")),
        check_vma=False,
    )
```

profile of v0, /device:TPU:2, one launch (start us, length us, event | category | flops | bytes accessed | tf_op | source)
XLA Modules:
  0.0 740.2 jit_solution(10609625799831482986)
XLA Ops:
  5.4 343.8 %while.55 = (s32[]{:T(128)}, bf16[2,256,128]{2,1,0:T(8,128)(2,1)S(1)}, f32[1,8,256]{2,1,0:T(8,128)S(1)}, f32[1,8,256]{2,1,0:T(8,128)S(1)}, f32[1,8,256,128]{3,2,...) while((s32[]{:T(128)}, ...), condition=%wide.region_5.6_spmd.clone, body=%wide.region_2.5_spmd.clone.sunk | while | flops 275847680 | bytes 10227923 | solution.py:97
  7.5 6.9 collective-permute-done.1
  18.6 6.9 collective-permute-done.1
  29.6 6.9 collective-permute-done.1
  40.7 6.9 collective-permute-done.1
  51.8 6.9 collective-permute-done.1
  62.9 6.9 collective-permute-done.1
  74.0 6.9 collective-permute-done.1
  85.1 6.9 collective-permute-done.1
  96.2 6.9 collective-permute-done.1
  107.3 6.9 collective-permute-done.1
  118.4 6.9 collective-permute-done.1
  129.5 6.9 collective-permute-done.1
  140.6 6.9 collective-permute-done.1
  151.6 6.9 collective-permute-done.1
  162.7 6.9 collective-permute-done.1
  173.8 6.9 collective-permute-done.1
  184.9 6.9 collective-permute-done.1
  196.0 6.9 collective-permute-done.1
  207.1 6.9 collective-permute-done.1
  218.2 6.9 collective-permute-done.1
  229.3 6.9 collective-permute-done.1
  240.4 6.9 collective-permute-done.1
  251.5 6.9 collective-permute-done.1
  262.5 6.9 collective-permute-done.1
  284.7 6.9 collective-permute-done.1
  295.8 6.9 collective-permute-done.1
  306.9 6.9 collective-permute-done.1
  318.0 6.9 collective-permute-done.1
  329.1 6.9 collective-permute-done.1
  340.2 6.9 collective-permute-done.1
  353.0 347.9 %while.54 = (s32[]{:T(128)}, f32[1,16,64,128]{3,2,1,0:T(8,128)}, bf16[1,16,64,128]{3,2,1,0:T(8,128)(2,1)S(1)}, f32[1,16]{1,0:T(1,128)S(1)}, f32[1,16,64,128]{3,2,1,0:T(8,128)S(1)}, /*index=5*/s32[]{:T(128)}) while((s32[]{:T(128)}, f32[1,16,64,128]{3,2,1,0:T(8,128)}, bf16[1,16,64,128]{3,2,1,0:T(8,128)(2,1)S(1)}, f32[1,16]{1,0:T(1,128)S(1)}, ...), condition=%wide.region_9.10_spmd, body=%wide.region_8.9_spmd.sunk | while | flops 524290 | bytes 2621613 | solution.py:133
  354.9 8.5 %collective-permute-done = bf16[1,16,64,128]{3,2,1,0:T(8,128)(2,1)S(1)} collective-permute-done((bf16[1,16,64,128]{3,2,1,0:T(8,128)(2,1)S(1)}, bf16[1,16,64,128]{3,2,1,0:T(8,128)(2,1)S(1)}, u32[]{:S(2)}, u32[]{:S(2)}) %collective-permute-start) | collective-permute-done | bytes 262176 | tf_op jit(solution)/shard_map/while/body/eval_jaxpr/ppermute | solution.py:20
  366.1 8.5 %collective-permute-done = bf16[1,16,64,128]{3,2,1,0:T(8,128)(2,1)S(1)} collective-permute-done((bf16[1,16,64,128]{3,2,1,0:T(8,128)(2,1)S(1)}, bf16[1,16,64,128]{3,2,1,0:T(8,128)(2,1)S(1)}, u32[]{:S(2)}, u32[]{:S(2)}) %collective-permute-start) | collective-permute-done | bytes 262176 | tf_op jit(solution)/shard_map/while/body/eval_jaxpr/ppermute | solution.py:20
  377.4 8.5 %collective-permute-done = bf16[1,16,64,128]{3,2,1,0:T(8,128)(2,1)S(1)} collective-permute-done((bf16[1,16,64,128]{3,2,1,0:T(8,128)(2,1)S(1)}, bf16[1,16,64,128]{3,2,1,0:T(8,128)(2,1)S(1)}, u32[]{:S(2)}, u32[]{:S(2)}) %collective-permute-start) | collective-permute-done | bytes 262176 | tf_op jit(solution)/shard_map/while/body/eval_jaxpr/ppermute | solution.py:20
  388.6 8.5 %collective-permute-done = bf16[1,16,64,128]{3,2,1,0:T(8,128)(2,1)S(1)} collective-permute-done((bf16[1,16,64,128]{3,2,1,0:T(8,128)(2,1)S(1)}, bf16[1,16,64,128]{3,2,1,0:T(8,128)(2,1)S(1)}, u32[]{:S(2)}, u32[]{:S(2)}) %collective-permute-start) | collective-permute-done | bytes 262176 | tf_op jit(solution)/shard_map/while/body/eval_jaxpr/ppermute | solution.py:20
  399.8 8.5 %collective-permute-done = bf16[1,16,64,128]{3,2,1,0:T(8,128)(2,1)S(1)} collective-permute-done((bf16[1,16,64,128]{3,2,1,0:T(8,128)(2,1)S(1)}, bf16[1,16,64,128]{3,2,1,0:T(8,128)(2,1)S(1)}, u32[]{:S(2)}, u32[]{:S(2)}) %collective-permute-start) | collective-permute-done | bytes 262176 | tf_op jit(solution)/shard_map/while/body/eval_jaxpr/ppermute | solution.py:20
  411.0 8.5 %collective-permute-done = bf16[1,16,64,128]{3,2,1,0:T(8,128)(2,1)S(1)} collective-permute-done((bf16[1,16,64,128]{3,2,1,0:T(8,128)(2,1)S(1)}, bf16[1,16,64,128]{3,2,1,0:T(8,128)(2,1)S(1)}, u32[]{:S(2)}, u32[]{:S(2)}) %collective-permute-start) | collective-permute-done | bytes 262176 | tf_op jit(solution)/shard_map/while/body/eval_jaxpr/ppermute | solution.py:20
  422.2 8.5 %collective-permute-done = bf16[1,16,64,128]{3,2,1,0:T(8,128)(2,1)S(1)} collective-permute-done((bf16[1,16,64,128]{3,2,1,0:T(8,128)(2,1)S(1)}, bf16[1,16,64,128]{3,2,1,0:T(8,128)(2,1)S(1)}, u32[]{:S(2)}, u32[]{:S(2)}) %collective-permute-start) | collective-permute-done | bytes 262176 | tf_op jit(solution)/shard_map/while/body/eval_jaxpr/ppermute | solution.py:20
  433.4 8.5 %collective-permute-done = bf16[1,16,64,128]{3,2,1,0:T(8,128)(2,1)S(1)} collective-permute-done((bf16[1,16,64,128]{3,2,1,0:T(8,128)(2,1)S(1)}, bf16[1,16,64,128]{3,2,1,0:T(8,128)(2,1)S(1)}, u32[]{:S(2)}, u32[]{:S(2)}) %collective-permute-start) | collective-permute-done | bytes 262176 | tf_op jit(solution)/shard_map/while/body/eval_jaxpr/ppermute | solution.py:20
  444.7 8.5 %collective-permute-done = bf16[1,16,64,128]{3,2,1,0:T(8,128)(2,1)S(1)} collective-permute-done((bf16[1,16,64,128]{3,2,1,0:T(8,128)(2,1)S(1)}, bf16[1,16,64,128]{3,2,1,0:T(8,128)(2,1)S(1)}, u32[]{:S(2)}, u32[]{:S(2)}) %collective-permute-start) | collective-permute-done | bytes 262176 | tf_op jit(solution)/shard_map/while/body/eval_jaxpr/ppermute | solution.py:20
  455.9 8.5 %collective-permute-done = bf16[1,16,64,128]{3,2,1,0:T(8,128)(2,1)S(1)} collective-permute-done((bf16[1,16,64,128]{3,2,1,0:T(8,128)(2,1)S(1)}, bf16[1,16,64,128]{3,2,1,0:T(8,128)(2,1)S(1)}, u32[]{:S(2)}, u32[]{:S(2)}) %collective-permute-start) | collective-permute-done | bytes 262176 | tf_op jit(solution)/shard_map/while/body/eval_jaxpr/ppermute | solution.py:20
  467.1 8.5 %collective-permute-done = bf16[1,16,64,128]{3,2,1,0:T(8,128)(2,1)S(1)} collective-permute-done((bf16[1,16,64,128]{3,2,1,0:T(8,128)(2,1)S(1)}, bf16[1,16,64,128]{3,2,1,0:T(8,128)(2,1)S(1)}, u32[]{:S(2)}, u32[]{:S(2)}) %collective-permute-start) | collective-permute-done | bytes 262176 | tf_op jit(solution)/shard_map/while/body/eval_jaxpr/ppermute | solution.py:20
  478.3 8.5 %collective-permute-done = bf16[1,16,64,128]{3,2,1,0:T(8,128)(2,1)S(1)} collective-permute-done((bf16[1,16,64,128]{3,2,1,0:T(8,128)(2,1)S(1)}, bf16[1,16,64,128]{3,2,1,0:T(8,128)(2,1)S(1)}, u32[]{:S(2)}, u32[]{:S(2)}) %collective-permute-start) | collective-permute-done | bytes 262176 | tf_op jit(solution)/shard_map/while/body/eval_jaxpr/ppermute | solution.py:20
  489.5 8.5 %collective-permute-done = bf16[1,16,64,128]{3,2,1,0:T(8,128)(2,1)S(1)} collective-permute-done((bf16[1,16,64,128]{3,2,1,0:T(8,128)(2,1)S(1)}, bf16[1,16,64,128]{3,2,1,0:T(8,128)(2,1)S(1)}, u32[]{:S(2)}, u32[]{:S(2)}) %collective-permute-start) | collective-permute-done | bytes 262176 | tf_op jit(solution)/shard_map/while/body/eval_jaxpr/ppermute | solution.py:20
  500.8 8.5 %collective-permute-done = bf16[1,16,64,128]{3,2,1,0:T(8,128)(2,1)S(1)} collective-permute-done((bf16[1,16,64,128]{3,2,1,0:T(8,128)(2,1)S(1)}, bf16[1,16,64,128]{3,2,1,0:T(8,128)(2,1)S(1)}, u32[]{:S(2)}, u32[]{:S(2)}) %collective-permute-start) | collective-permute-done | bytes 262176 | tf_op jit(solution)/shard_map/while/body/eval_jaxpr/ppermute | solution.py:20
  512.0 8.5 %collective-permute-done = bf16[1,16,64,128]{3,2,1,0:T(8,128)(2,1)S(1)} collective-permute-done((bf16[1,16,64,128]{3,2,1,0:T(8,128)(2,1)S(1)}, bf16[1,16,64,128]{3,2,1,0:T(8,128)(2,1)S(1)}, u32[]{:S(2)}, u32[]{:S(2)}) %collective-permute-start) | collective-permute-done | bytes 262176 | tf_op jit(solution)/shard_map/while/body/eval_jaxpr/ppermute | solution.py:20
  523.2 8.5 %collective-permute-done = bf16[1,16,64,128]{3,2,1,0:T(8,128)(2,1)S(1)} collective-permute-done((bf16[1,16,64,128]{3,2,1,0:T(8,128)(2,1)S(1)}, bf16[1,16,64,128]{3,2,1,0:T(8,128)(2,1)S(1)}, u32[]{:S(2)}, u32[]{:S(2)}) %collective-permute-start) | collective-permute-done | bytes 262176 | tf_op jit(solution)/shard_map/while/body/eval_jaxpr/ppermute | solution.py:20
  534.4 8.5 %collective-permute-done = bf16[1,16,64,128]{3,2,1,0:T(8,128)(2,1)S(1)} collective-permute-done((bf16[1,16,64,128]{3,2,1,0:T(8,128)(2,1)S(1)}, bf16[1,16,64,128]{3,2,1,0:T(8,128)(2,1)S(1)}, u32[]{:S(2)}, u32[]{:S(2)}) %collective-permute-start) | collective-permute-done | bytes 262176 | tf_op jit(solution)/shard_map/while/body/eval_jaxpr/ppermute | solution.py:20
  545.6 8.5 %collective-permute-done = bf16[1,16,64,128]{3,2,1,0:T(8,128)(2,1)S(1)} collective-permute-done((bf16[1,16,64,128]{3,2,1,0:T(8,128)(2,1)S(1)}, bf16[1,16,64,128]{3,2,1,0:T(8,128)(2,1)S(1)}, u32[]{:S(2)}, u32[]{:S(2)}) %collective-permute-start) | collective-permute-done | bytes 262176 | tf_op jit(solution)/shard_map/while/body/eval_jaxpr/ppermute | solution.py:20
  556.9 8.5 %collective-permute-done = bf16[1,16,64,128]{3,2,1,0:T(8,128)(2,1)S(1)} collective-permute-done((bf16[1,16,64,128]{3,2,1,0:T(8,128)(2,1)S(1)}, bf16[1,16,64,128]{3,2,1,0:T(8,128)(2,1)S(1)}, u32[]{:S(2)}, u32[]{:S(2)}) %collective-permute-start) | collective-permute-done | bytes 262176 | tf_op jit(solution)/shard_map/while/body/eval_jaxpr/ppermute | solution.py:20
  568.1 8.5 %collective-permute-done = bf16[1,16,64,128]{3,2,1,0:T(8,128)(2,1)S(1)} collective-permute-done((bf16[1,16,64,128]{3,2,1,0:T(8,128)(2,1)S(1)}, bf16[1,16,64,128]{3,2,1,0:T(8,128)(2,1)S(1)}, u32[]{:S(2)}, u32[]{:S(2)}) %collective-permute-start) | collective-permute-done | bytes 262176 | tf_op jit(solution)/shard_map/while/body/eval_jaxpr/ppermute | solution.py:20
  579.3 8.5 %collective-permute-done = bf16[1,16,64,128]{3,2,1,0:T(8,128)(2,1)S(1)} collective-permute-done((bf16[1,16,64,128]{3,2,1,0:T(8,128)(2,1)S(1)}, bf16[1,16,64,128]{3,2,1,0:T(8,128)(2,1)S(1)}, u32[]{:S(2)}, u32[]{:S(2)}) %collective-permute-start) | collective-permute-done | bytes 262176 | tf_op jit(solution)/shard_map/while/body/eval_jaxpr/ppermute | solution.py:20
  590.5 8.5 %collective-permute-done = bf16[1,16,64,128]{3,2,1,0:T(8,128)(2,1)S(1)} collective-permute-done((bf16[1,16,64,128]{3,2,1,0:T(8,128)(2,1)S(1)}, bf16[1,16,64,128]{3,2,1,0:T(8,128)(2,1)S(1)}, u32[]{:S(2)}, u32[]{:S(2)}) %collective-permute-start) | collective-permute-done | bytes 262176 | tf_op jit(solution)/shard_map/while/body/eval_jaxpr/ppermute | solution.py:20
  601.7 8.5 %collective-permute-done = bf16[1,16,64,128]{3,2,1,0:T(8,128)(2,1)S(1)} collective-permute-done((bf16[1,16,64,128]{3,2,1,0:T(8,128)(2,1)S(1)}, bf16[1,16,64,128]{3,2,1,0:T(8,128)(2,1)S(1)}, u32[]{:S(2)}, u32[]{:S(2)}) %collective-permute-start) | collective-permute-done | bytes 262176 | tf_op jit(solution)/shard_map/while/body/eval_jaxpr/ppermute | solution.py:20
  613.0 8.5 %collective-permute-done = bf16[1,16,64,128]{3,2,1,0:T(8,128)(2,1)S(1)} collective-permute-done((bf16[1,16,64,128]{3,2,1,0:T(8,128)(2,1)S(1)}, bf16[1,16,64,128]{3,2,1,0:T(8,128)(2,1)S(1)}, u32[]{:S(2)}, u32[]{:S(2)}) %collective-permute-start) | collective-permute-done | bytes 262176 | tf_op jit(solution)/shard_map/while/body/eval_jaxpr/ppermute | solution.py:20
  624.2 8.5 %collective-permute-done = bf16[1,16,64,128]{3,2,1,0:T(8,128)(2,1)S(1)} collective-permute-done((bf16[1,16,64,128]{3,2,1,0:T(8,128)(2,1)S(1)}, bf16[1,16,64,128]{3,2,1,0:T(8,128)(2,1)S(1)}, u32[]{:S(2)}, u32[]{:S(2)}) %collective-permute-start) | collective-permute-done | bytes 262176 | tf_op jit(solution)/shard_map/while/body/eval_jaxpr/ppermute | solution.py:20
  635.4 8.5 %collective-permute-done = bf16[1,16,64,128]{3,2,1,0:T(8,128)(2,1)S(1)} collective-permute-done((bf16[1,16,64,128]{3,2,1,0:T(8,128)(2,1)S(1)}, bf16[1,16,64,128]{3,2,1,0:T(8,128)(2,1)S(1)}, u32[]{:S(2)}, u32[]{:S(2)}) %collective-permute-start) | collective-permute-done | bytes 262176 | tf_op jit(solution)/shard_map/while/body/eval_jaxpr/ppermute | solution.py:20
  646.6 8.5 %collective-permute-done = bf16[1,16,64,128]{3,2,1,0:T(8,128)(2,1)S(1)} collective-permute-done((bf16[1,16,64,128]{3,2,1,0:T(8,128)(2,1)S(1)}, bf16[1,16,64,128]{3,2,1,0:T(8,128)(2,1)S(1)}, u32[]{:S(2)}, u32[]{:S(2)}) %collective-permute-start) | collective-permute-done | bytes 262176 | tf_op jit(solution)/shard_map/while/body/eval_jaxpr/ppermute | solution.py:20
  657.8 8.5 %collective-permute-done = bf16[1,16,64,128]{3,2,1,0:T(8,128)(2,1)S(1)} collective-permute-done((bf16[1,16,64,128]{3,2,1,0:T(8,128)(2,1)S(1)}, bf16[1,16,64,128]{3,2,1,0:T(8,128)(2,1)S(1)}, u32[]{:S(2)}, u32[]{:S(2)}) %collective-permute-start) | collective-permute-done | bytes 262176 | tf_op jit(solution)/shard_map/while/body/eval_jaxpr/ppermute | solution.py:20
  669.1 8.5 %collective-permute-done = bf16[1,16,64,128]{3,2,1,0:T(8,128)(2,1)S(1)} collective-permute-done((bf16[1,16,64,128]{3,2,1,0:T(8,128)(2,1)S(1)}, bf16[1,16,64,128]{3,2,1,0:T(8,128)(2,1)S(1)}, u32[]{:S(2)}, u32[]{:S(2)}) %collective-permute-start) | collective-permute-done | bytes 262176 | tf_op jit(solution)/shard_map/while/body/eval_jaxpr/ppermute | solution.py:20
  680.3 8.5 %collective-permute-done = bf16[1,16,64,128]{3,2,1,0:T(8,128)(2,1)S(1)} collective-permute-done((bf16[1,16,64,128]{3,2,1,0:T(8,128)(2,1)S(1)}, bf16[1,16,64,128]{3,2,1,0:T(8,128)(2,1)S(1)}, u32[]{:S(2)}, u32[]{:S(2)}) %collective-permute-start) | collective-permute-done | bytes 262176 | tf_op jit(solution)/shard_map/while/body/eval_jaxpr/ppermute | solution.py:20
  691.5 8.5 %collective-permute-done = bf16[1,16,64,128]{3,2,1,0:T(8,128)(2,1)S(1)} collective-permute-done((bf16[1,16,64,128]{3,2,1,0:T(8,128)(2,1)S(1)}, bf16[1,16,64,128]{3,2,1,0:T(8,128)(2,1)S(1)}, u32[]{:S(2)}, u32[]{:S(2)}) %collective-permute-start) | collective-permute-done | bytes 262176 | tf_op jit(solution)/shard_map/while/body/eval_jaxpr/ppermute | solution.py:20
  705.6 33.4 %psum.7 = f32[256]{0:T(256)S(1)} all-reduce(f32[256]{0:T(256)S(1)} %multiply_reduce_fusion), channel_id=1, replica_groups=mesh['ctx'=32,'tp'=8] {'tp'}, use_global_device_ids=true, to_apply=%region_11.12 | all-reduce | flops 256 | bytes 2048 | tf_op jit(solution)/shard_map/psum | solution.py:145
  (433 shorter events, 232.6 us)
Async XLA Ops:
  0.6 352.0 %copy-start = (bf16[256,128]{1,0:T(8,128)(2,1)S(1)}, bf16[256,128]{1,0:T(8,128)(2,1)}, u32[]{:S(2)}) copy-start(bf16[256,128]{1,0:T(8,128)(2,1)} %param.20) | copy-start | bytes 196612
  5.4 9.0 %collective-permute-start.1 = (bf16[2,256,128]{2,1,0:T(8,128)(2,1)S(1)}, bf16[2,256,128]{2,1,0:T(8,128)(2,1)S(1)}, u32[]{:S(2)}, u32[]{:S(2)}) collective-permute-start(bf16[2,256,128]{2,1,0:T(8,128)(2,1)S(1)} %get-tuple-element.440), channel_id=1, source_target_pairs={{0,8},{8,16},{16,24},{24,32},{32,40},{40,48},{48,56},{56,64},{64,7... | collective-permute-start | bytes 393224 | tf_op jit(solution)/shard_map/while/body/eval_jaxpr/ppermute | solution.py:20
  16.5 9.0 %collective-permute-start.1 = (bf16[2,256,128]{2,1,0:T(8,128)(2,1)S(1)}, bf16[2,256,128]{2,1,0:T(8,128)(2,1)S(1)}, u32[]{:S(2)}, u32[]{:S(2)}) collective-permute-start(bf16[2,256,128]{2,1,0:T(8,128)(2,1)S(1)} %get-tuple-element.440), channel_id=1, source_target_pairs={{0,8},{8,16},{16,24},{24,32},{32,40},{40,48},{48,56},{56,64},{64,7... | collective-permute-start | bytes 393224 | tf_op jit(solution)/shard_map/while/body/eval_jaxpr/ppermute | solution.py:20
  27.6 9.0 %collective-permute-start.1 = (bf16[2,256,128]{2,1,0:T(8,128)(2,1)S(1)}, bf16[2,256,128]{2,1,0:T(8,128)(2,1)S(1)}, u32[]{:S(2)}, u32[]{:S(2)}) collective-permute-start(bf16[2,256,128]{2,1,0:T(8,128)(2,1)S(1)} %get-tuple-element.440), channel_id=1, source_target_pairs={{0,8},{8,16},{16,24},{24,32},{32,40},{40,48},{48,56},{56,64},{64,7... | collective-permute-start | bytes 393224 | tf_op jit(solution)/shard_map/while/body/eval_jaxpr/ppermute | solution.py:20
  38.7 9.0 %collective-permute-start.1 = (bf16[2,256,128]{2,1,0:T(8,128)(2,1)S(1)}, bf16[2,256,128]{2,1,0:T(8,128)(2,1)S(1)}, u32[]{:S(2)}, u32[]{:S(2)}) collective-permute-start(bf16[2,256,128]{2,1,0:T(8,128)(2,1)S(1)} %get-tuple-element.440), channel_id=1, source_target_pairs={{0,8},{8,16},{16,24},{24,32},{32,40},{40,48},{48,56},{56,64},{64,7... | collective-permute-start | bytes 393224 | tf_op jit(solution)/shard_map/while/body/eval_jaxpr/ppermute | solution.py:20
  49.8 9.0 %collective-permute-start.1 = (bf16[2,256,128]{2,1,0:T(8,128)(2,1)S(1)}, bf16[2,256,128]{2,1,0:T(8,128)(2,1)S(1)}, u32[]{:S(2)}, u32[]{:S(2)}) collective-permute-start(bf16[2,256,128]{2,1,0:T(8,128)(2,1)S(1)} %get-tuple-element.440), channel_id=1, source_target_pairs={{0,8},{8,16},{16,24},{24,32},{32,40},{40,48},{48,56},{56,64},{64,7... | collective-permute-start | bytes 393224 | tf_op jit(solution)/shard_map/while/body/eval_jaxpr/ppermute | solution.py:20
  60.9 9.0 %collective-permute-start.1 = (bf16[2,256,128]{2,1,0:T(8,128)(2,1)S(1)}, bf16[2,256,128]{2,1,0:T(8,128)(2,1)S(1)}, u32[]{:S(2)}, u32[]{:S(2)}) collective-permute-start(bf16[2,256,128]{2,1,0:T(8,128)(2,1)S(1)} %get-tuple-element.440), channel_id=1, source_target_pairs={{0,8},{8,16},{16,24},{24,32},{32,40},{40,48},{48,56},{56,64},{64,7... | collective-permute-start | bytes 393224 | tf_op jit(solution)/shard_map/while/body/eval_jaxpr/ppermute | solution.py:20
  71.9 9.0 %collective-permute-start.1 = (bf16[2,256,128]{2,1,0:T(8,128)(2,1)S(1)}, bf16[2,256,128]{2,1,0:T(8,128)(2,1)S(1)}, u32[]{:S(2)}, u32[]{:S(2)}) collective-permute-start(bf16[2,256,128]{2,1,0:T(8,128)(2,1)S(1)} %get-tuple-element.440), channel_id=1, source_target_pairs={{0,8},{8,16},{16,24},{24,32},{32,40},{40,48},{48,56},{56,64},{64,7... | collective-permute-start | bytes 393224 | tf_op jit(solution)/shard_map/while/body/eval_jaxpr/ppermute | solution.py:20
  83.0 9.0 %collective-permute-start.1 = (bf16[2,256,128]{2,1,0:T(8,128)(2,1)S(1)}, bf16[2,256,128]{2,1,0:T(8,128)(2,1)S(1)}, u32[]{:S(2)}, u32[]{:S(2)}) collective-permute-start(bf16[2,256,128]{2,1,0:T(8,128)(2,1)S(1)} %get-tuple-element.440), channel_id=1, source_target_pairs={{0,8},{8,16},{16,24},{24,32},{32,40},{40,48},{48,56},{56,64},{64,7... | collective-permute-start | bytes 393224 | tf_op jit(solution)/shard_map/while/body/eval_jaxpr/ppermute | solution.py:20
  94.1 9.0 %collective-permute-start.1 = (bf16[2,256,128]{2,1,0:T(8,128)(2,1)S(1)}, bf16[2,256,128]{2,1,0:T(8,128)(2,1)S(1)}, u32[]{:S(2)}, u32[]{:S(2)}) collective-permute-start(bf16[2,256,128]{2,1,0:T(8,128)(2,1)S(1)} %get-tuple-element.440), channel_id=1, source_target_pairs={{0,8},{8,16},{16,24},{24,32},{32,40},{40,48},{48,56},{56,64},{64,7... | collective-permute-start | bytes 393224 | tf_op jit(solution)/shard_map/while/body/eval_jaxpr/ppermute | solution.py:20
  105.2 9.0 %collective-permute-start.1 = (bf16[2,256,128]{2,1,0:T(8,128)(2,1)S(1)}, bf16[2,256,128]{2,1,0:T(8,128)(2,1)S(1)}, u32[]{:S(2)}, u32[]{:S(2)}) collective-permute-start(bf16[2,256,128]{2,1,0:T(8,128)(2,1)S(1)} %get-tuple-element.440), channel_id=1, source_target_pairs={{0,8},{8,16},{16,24},{24,32},{32,40},{40,48},{48,56},{56,64},{64,7... | collective-permute-start | bytes 393224 | tf_op jit(solution)/shard_map/while/body/eval_jaxpr/ppermute | solution.py:20
  116.3 9.0 %collective-permute-start.1 = (bf16[2,256,128]{2,1,0:T(8,128)(2,1)S(1)}, bf16[2,256,128]{2,1,0:T(8,128)(2,1)S(1)}, u32[]{:S(2)}, u32[]{:S(2)}) collective-permute-start(bf16[2,256,128]{2,1,0:T(8,128)(2,1)S(1)} %get-tuple-element.440), channel_id=1, source_target_pairs={{0,8},{8,16},{16,24},{24,32},{32,40},{40,48},{48,56},{56,64},{64,7... | collective-permute-start | bytes 393224 | tf_op jit(solution)/shard_map/while/body/eval_jaxpr/ppermute | solution.py:20
  127.4 9.0 %collective-permute-start.1 = (bf16[2,256,128]{2,1,0:T(8,128)(2,1)S(1)}, bf16[2,256,128]{2,1,0:T(8,128)(2,1)S(1)}, u32[]{:S(2)}, u32[]{:S(2)}) collective-permute-start(bf16[2,256,128]{2,1,0:T(8,128)(2,1)S(1)} %get-tuple-element.440), channel_id=1, source_target_pairs={{0,8},{8,16},{16,24},{24,32},{32,40},{40,48},{48,56},{56,64},{64,7... | collective-permute-start | bytes 393224 | tf_op jit(solution)/shard_map/while/body/eval_jaxpr/ppermute | solution.py:20
  138.5 9.0 %collective-permute-start.1 = (bf16[2,256,128]{2,1,0:T(8,128)(2,1)S(1)}, bf16[2,256,128]{2,1,0:T(8,128)(2,1)S(1)}, u32[]{:S(2)}, u32[]{:S(2)}) collective-permute-start(bf16[2,256,128]{2,1,0:T(8,128)(2,1)S(1)} %get-tuple-element.440), channel_id=1, source_target_pairs={{0,8},{8,16},{16,24},{24,32},{32,40},{40,48},{48,56},{56,64},{64,7... | collective-permute-start | bytes 393224 | tf_op jit(solution)/shard_map/while/body/eval_jaxpr/ppermute | solution.py:20
  149.6 9.0 %collective-permute-start.1 = (bf16[2,256,128]{2,1,0:T(8,128)(2,1)S(1)}, bf16[2,256,128]{2,1,0:T(8,128)(2,1)S(1)}, u32[]{:S(2)}, u32[]{:S(2)}) collective-permute-start(bf16[2,256,128]{2,1,0:T(8,128)(2,1)S(1)} %get-tuple-element.440), channel_id=1, source_target_pairs={{0,8},{8,16},{16,24},{24,32},{32,40},{40,48},{48,56},{56,64},{64,7... | collective-permute-start | bytes 393224 | tf_op jit(solution)/shard_map/while/body/eval_jaxpr/ppermute | solution.py:20
  160.7 9.0 %collective-permute-start.1 = (bf16[2,256,128]{2,1,0:T(8,128)(2,1)S(1)}, bf16[2,256,128]{2,1,0:T(8,128)(2,1)S(1)}, u32[]{:S(2)}, u32[]{:S(2)}) collective-permute-start(bf16[2,256,128]{2,1,0:T(8,128)(2,1)S(1)} %get-tuple-element.440), channel_id=1, source_target_pairs={{0,8},{8,16},{16,24},{24,32},{32,40},{40,48},{48,56},{56,64},{64,7... | collective-permute-start | bytes 393224 | tf_op jit(solution)/shard_map/while/body/eval_jaxpr/ppermute | solution.py:20
  171.8 9.0 %collective-permute-start.1 = (bf16[2,256,128]{2,1,0:T(8,128)(2,1)S(1)}, bf16[2,256,128]{2,1,0:T(8,128)(2,1)S(1)}, u32[]{:S(2)}, u32[]{:S(2)}) collective-permute-start(bf16[2,256,128]{2,1,0:T(8,128)(2,1)S(1)} %get-tuple-element.440), channel_id=1, source_target_pairs={{0,8},{8,16},{16,24},{24,32},{32,40},{40,48},{48,56},{56,64},{64,7... | collective-permute-start | bytes 393224 | tf_op jit(solution)/shard_map/while/body/eval_jaxpr/ppermute | solution.py:20
  182.9 9.0 %collective-permute-start.1 = (bf16[2,256,128]{2,1,0:T(8,128)(2,1)S(1)}, bf16[2,256,128]{2,1,0:T(8,128)(2,1)S(1)}, u32[]{:S(2)}, u32[]{:S(2)}) collective-permute-start(bf16[2,256,128]{2,1,0:T(8,128)(2,1)S(1)} %get-tuple-element.440), channel_id=1, source_target_pairs={{0,8},{8,16},{16,24},{24,32},{32,40},{40,48},{48,56},{56,64},{64,7... | collective-permute-start | bytes 393224 | tf_op jit(solution)/shard_map/while/body/eval_jaxpr/ppermute | solution.py:20
  193.9 9.0 %collective-permute-start.1 = (bf16[2,256,128]{2,1,0:T(8,128)(2,1)S(1)}, bf16[2,256,128]{2,1,0:T(8,128)(2,1)S(1)}, u32[]{:S(2)}, u32[]{:S(2)}) collective-permute-start(bf16[2,256,128]{2,1,0:T(8,128)(2,1)S(1)} %get-tuple-element.440), channel_id=1, source_target_pairs={{0,8},{8,16},{16,24},{24,32},{32,40},{40,48},{48,56},{56,64},{64,7... | collective-permute-start | bytes 393224 | tf_op jit(solution)/shard_map/while/body/eval_jaxpr/ppermute | solution.py:20
  205.0 9.0 %collective-permute-start.1 = (bf16[2,256,128]{2,1,0:T(8,128)(2,1)S(1)}, bf16[2,256,128]{2,1,0:T(8,128)(2,1)S(1)}, u32[]{:S(2)}, u32[]{:S(2)}) collective-permute-start(bf16[2,256,128]{2,1,0:T(8,128)(2,1)S(1)} %get-tuple-element.440), channel_id=1, source_target_pairs={{0,8},{8,16},{16,24},{24,32},{32,40},{40,48},{48,56},{56,64},{64,7... | collective-permute-start | bytes 393224 | tf_op jit(solution)/shard_map/while/body/eval_jaxpr/ppermute | solution.py:20
  216.1 9.0 %collective-permute-start.1 = (bf16[2,256,128]{2,1,0:T(8,128)(2,1)S(1)}, bf16[2,256,128]{2,1,0:T(8,128)(2,1)S(1)}, u32[]{:S(2)}, u32[]{:S(2)}) collective-permute-start(bf16[2,256,128]{2,1,0:T(8,128)(2,1)S(1)} %get-tuple-element.440), channel_id=1, source_target_pairs={{0,8},{8,16},{16,24},{24,32},{32,40},{40,48},{48,56},{56,64},{64,7... | collective-permute-start | bytes 393224 | tf_op jit(solution)/shard_map/while/body/eval_jaxpr/ppermute | solution.py:20
  227.2 9.0 %collective-permute-start.1 = (bf16[2,256,128]{2,1,0:T(8,128)(2,1)S(1)}, bf16[2,256,128]{2,1,0:T(8,128)(2,1)S(1)}, u32[]{:S(2)}, u32[]{:S(2)}) collective-permute-start(bf16[2,256,128]{2,1,0:T(8,128)(2,1)S(1)} %get-tuple-element.440), channel_id=1, source_target_pairs={{0,8},{8,16},{16,24},{24,32},{32,40},{40,48},{48,56},{56,64},{64,7... | collective-permute-start | bytes 393224 | tf_op jit(solution)/shard_map/while/body/eval_jaxpr/ppermute | solution.py:20
  238.3 9.0 %collective-permute-start.1 = (bf16[2,256,128]{2,1,0:T(8,128)(2,1)S(1)}, bf16[2,256,128]{2,1,0:T(8,128)(2,1)S(1)}, u32[]{:S(2)}, u32[]{:S(2)}) collective-permute-start(bf16[2,256,128]{2,1,0:T(8,128)(2,1)S(1)} %get-tuple-element.440), channel_id=1, source_target_pairs={{0,8},{8,16},{16,24},{24,32},{32,40},{40,48},{48,56},{56,64},{64,7... | collective-permute-start | bytes 393224 | tf_op jit(solution)/shard_map/while/body/eval_jaxpr/ppermute | solution.py:20
  249.4 9.0 %collective-permute-start.1 = (bf16[2,256,128]{2,1,0:T(8,128)(2,1)S(1)}, bf16[2,256,128]{2,1,0:T(8,128)(2,1)S(1)}, u32[]{:S(2)}, u32[]{:S(2)}) collective-permute-start(bf16[2,256,128]{2,1,0:T(8,128)(2,1)S(1)} %get-tuple-element.440), channel_id=1, source_target_pairs={{0,8},{8,16},{16,24},{24,32},{32,40},{40,48},{48,56},{56,64},{64,7... | collective-permute-start | bytes 393224 | tf_op jit(solution)/shard_map/while/body/eval_jaxpr/ppermute | solution.py:20
  260.5 9.0 %collective-permute-start.1 = (bf16[2,256,128]{2,1,0:T(8,128)(2,1)S(1)}, bf16[2,256,128]{2,1,0:T(8,128)(2,1)S(1)}, u32[]{:S(2)}, u32[]{:S(2)}) collective-permute-start(bf16[2,256,128]{2,1,0:T(8,128)(2,1)S(1)} %get-tuple-element.440), channel_id=1, source_target_pairs={{0,8},{8,16},{16,24},{24,32},{32,40},{40,48},{48,56},{56,64},{64,7... | collective-permute-start | bytes 393224 | tf_op jit(solution)/shard_map/while/body/eval_jaxpr/ppermute | solution.py:20
  271.6 9.0 %collective-permute-start.1 = (bf16[2,256,128]{2,1,0:T(8,128)(2,1)S(1)}, bf16[2,256,128]{2,1,0:T(8,128)(2,1)S(1)}, u32[]{:S(2)}, u32[]{:S(2)}) collective-permute-start(bf16[2,256,128]{2,1,0:T(8,128)(2,1)S(1)} %get-tuple-element.440), channel_id=1, source_target_pairs={{0,8},{8,16},{16,24},{24,32},{32,40},{40,48},{48,56},{56,64},{64,7... | collective-permute-start | bytes 393224 | tf_op jit(solution)/shard_map/while/body/eval_jaxpr/ppermute | solution.py:20
  282.7 9.0 %collective-permute-start.1 = (bf16[2,256,128]{2,1,0:T(8,128)(2,1)S(1)}, bf16[2,256,128]{2,1,0:T(8,128)(2,1)S(1)}, u32[]{:S(2)}, u32[]{:S(2)}) collective-permute-start(bf16[2,256,128]{2,1,0:T(8,128)(2,1)S(1)} %get-tuple-element.440), channel_id=1, source_target_pairs={{0,8},{8,16},{16,24},{24,32},{32,40},{40,48},{48,56},{56,64},{64,7... | collective-permute-start | bytes 393224 | tf_op jit(solution)/shard_map/while/body/eval_jaxpr/ppermute | solution.py:20
  293.8 9.0 %collective-permute-start.1 = (bf16[2,256,128]{2,1,0:T(8,128)(2,1)S(1)}, bf16[2,256,128]{2,1,0:T(8,128)(2,1)S(1)}, u32[]{:S(2)}, u32[]{:S(2)}) collective-permute-start(bf16[2,256,128]{2,1,0:T(8,128)(2,1)S(1)} %get-tuple-element.440), channel_id=1, source_target_pairs={{0,8},{8,16},{16,24},{24,32},{32,40},{40,48},{48,56},{56,64},{64,7... | collective-permute-start | bytes 393224 | tf_op jit(solution)/shard_map/while/body/eval_jaxpr/ppermute | solution.py:20
  304.8 9.0 %collective-permute-start.1 = (bf16[2,256,128]{2,1,0:T(8,128)(2,1)S(1)}, bf16[2,256,128]{2,1,0:T(8,128)(2,1)S(1)}, u32[]{:S(2)}, u32[]{:S(2)}) collective-permute-start(bf16[2,256,128]{2,1,0:T(8,128)(2,1)S(1)} %get-tuple-element.440), channel_id=1, source_target_pairs={{0,8},{8,16},{16,24},{24,32},{32,40},{40,48},{48,56},{56,64},{64,7... | collective-permute-start | bytes 393224 | tf_op jit(solution)/shard_map/while/body/eval_jaxpr/ppermute | solution.py:20
  315.9 9.0 %collective-permute-start.1 = (bf16[2,256,128]{2,1,0:T(8,128)(2,1)S(1)}, bf16[2,256,128]{2,1,0:T(8,128)(2,1)S(1)}, u32[]{:S(2)}, u32[]{:S(2)}) collective-permute-start(bf16[2,256,128]{2,1,0:T(8,128)(2,1)S(1)} %get-tuple-element.440), channel_id=1, source_target_pairs={{0,8},{8,16},{16,24},{24,32},{32,40},{40,48},{48,56},{56,64},{64,7... | collective-permute-start | bytes 393224 | tf_op jit(solution)/shard_map/while/body/eval_jaxpr/ppermute | solution.py:20
  327.0 9.0 %collective-permute-start.1 = (bf16[2,256,128]{2,1,0:T(8,128)(2,1)S(1)}, bf16[2,256,128]{2,1,0:T(8,128)(2,1)S(1)}, u32[]{:S(2)}, u32[]{:S(2)}) collective-permute-start(bf16[2,256,128]{2,1,0:T(8,128)(2,1)S(1)} %get-tuple-element.440), channel_id=1, source_target_pairs={{0,8},{8,16},{16,24},{24,32},{32,40},{40,48},{48,56},{56,64},{64,7... | collective-permute-start | bytes 393224 | tf_op jit(solution)/shard_map/while/body/eval_jaxpr/ppermute | solution.py:20
  338.1 9.0 %collective-permute-start.1 = (bf16[2,256,128]{2,1,0:T(8,128)(2,1)S(1)}, bf16[2,256,128]{2,1,0:T(8,128)(2,1)S(1)}, u32[]{:S(2)}, u32[]{:S(2)}) collective-permute-start(bf16[2,256,128]{2,1,0:T(8,128)(2,1)S(1)} %get-tuple-element.440), channel_id=1, source_target_pairs={{0,8},{8,16},{16,24},{24,32},{32,40},{40,48},{48,56},{56,64},{64,7... | collective-permute-start | bytes 393224 | tf_op jit(solution)/shard_map/while/body/eval_jaxpr/ppermute | solution.py:20
  353.0 347.9 %copy-start.4 = (bf16[256,128]{1,0:T(8,128)(2,1)S(1)}, bf16[256,128]{1,0:T(8,128)(2,1)}, u32[]{:S(2)}) copy-start(bf16[256,128]{1,0:T(8,128)(2,1)} %param.21) | copy-start | bytes 196612
  353.0 10.4 %collective-permute-start = (bf16[1,16,64,128]{3,2,1,0:T(8,128)(2,1)S(1)}, bf16[1,16,64,128]{3,2,1,0:T(8,128)(2,1)S(1)}, u32[]{:S(2)}, u32[]{:S(2)}) collective-permute-start(bf16[1,16,64,128]{3,2,1,0:T(8,128)(2,1)S(1)} %get-tuple-element.471), channel_id=1, source_target_pairs={{0,8},{8,16},{16,24},{24,32},{32,40},{40,48},{48,56},{56,64},{64,7... | collective-permute-start | bytes 786440 | tf_op jit(solution)/shard_map/while/body/eval_jaxpr/ppermute | solution.py:20
  364.2 10.4 %collective-permute-start = (bf16[1,16,64,128]{3,2,1,0:T(8,128)(2,1)S(1)}, bf16[1,16,64,128]{3,2,1,0:T(8,128)(2,1)S(1)}, u32[]{:S(2)}, u32[]{:S(2)}) collective-permute-start(bf16[1,16,64,128]{3,2,1,0:T(8,128)(2,1)S(1)} %get-tuple-element.471), channel_id=1, source_target_pairs={{0,8},{8,16},{16,24},{24,32},{32,40},{40,48},{48,56},{56,64},{64,7... | collective-permute-start | bytes 786440 | tf_op jit(solution)/shard_map/while/body/eval_jaxpr/ppermute | solution.py:20
  375.4 10.4 %collective-permute-start = (bf16[1,16,64,128]{3,2,1,0:T(8,128)(2,1)S(1)}, bf16[1,16,64,128]{3,2,1,0:T(8,128)(2,1)S(1)}, u32[]{:S(2)}, u32[]{:S(2)}) collective-permute-start(bf16[1,16,64,128]{3,2,1,0:T(8,128)(2,1)S(1)} %get-tuple-element.471), channel_id=1, source_target_pairs={{0,8},{8,16},{16,24},{24,32},{32,40},{40,48},{48,56},{56,64},{64,7... | collective-permute-start | bytes 786440 | tf_op jit(solution)/shard_map/while/body/eval_jaxpr/ppermute | solution.py:20
  386.7 10.4 %collective-permute-start = (bf16[1,16,64,128]{3,2,1,0:T(8,128)(2,1)S(1)}, bf16[1,16,64,128]{3,2,1,0:T(8,128)(2,1)S(1)}, u32[]{:S(2)}, u32[]{:S(2)}) collective-permute-start(bf16[1,16,64,128]{3,2,1,0:T(8,128)(2,1)S(1)} %get-tuple-element.471), channel_id=1, source_target_pairs={{0,8},{8,16},{16,24},{24,32},{32,40},{40,48},{48,56},{56,64},{64,7... | collective-permute-start | bytes 786440 | tf_op jit(solution)/shard_map/while/body/eval_jaxpr/ppermute | solution.py:20
  397.9 10.4 %collective-permute-start = (bf16[1,16,64,128]{3,2,1,0:T(8,128)(2,1)S(1)}, bf16[1,16,64,128]{3,2,1,0:T(8,128)(2,1)S(1)}, u32[]{:S(2)}, u32[]{:S(2)}) collective-permute-start(bf16[1,16,64,128]{3,2,1,0:T(8,128)(2,1)S(1)} %get-tuple-element.471), channel_id=1, source_target_pairs={{0,8},{8,16},{16,24},{24,32},{32,40},{40,48},{48,56},{56,64},{64,7... | collective-permute-start | bytes 786440 | tf_op jit(solution)/shard_map/while/body/eval_jaxpr/ppermute | solution.py:20
  409.1 10.4 %collective-permute-start = (bf16[1,16,64,128]{3,2,1,0:T(8,128)(2,1)S(1)}, bf16[1,16,64,128]{3,2,1,0:T(8,128)(2,1)S(1)}, u32[]{:S(2)}, u32[]{:S(2)}) collective-permute-start(bf16[1,16,64,128]{3,2,1,0:T(8,128)(2,1)S(1)} %get-tuple-element.471), channel_id=1, source_target_pairs={{0,8},{8,16},{16,24},{24,32},{32,40},{40,48},{48,56},{56,64},{64,7... | collective-permute-start | bytes 786440 | tf_op jit(solution)/shard_map/while/body/eval_jaxpr/ppermute | solution.py:20
  420.3 10.4 %collective-permute-start = (bf16[1,16,64,128]{3,2,1,0:T(8,128)(2,1)S(1)}, bf16[1,16,64,128]{3,2,1,0:T(8,128)(2,1)S(1)}, u32[]{:S(2)}, u32[]{:S(2)}) collective-permute-start(bf16[1,16,64,128]{3,2,1,0:T(8,128)(2,1)S(1)} %get-tuple-element.471), channel_id=1, source_target_pairs={{0,8},{8,16},{16,24},{24,32},{32,40},{40,48},{48,56},{56,64},{64,7... | collective-permute-start | bytes 786440 | tf_op jit(solution)/shard_map/while/body/eval_jaxpr/ppermute | solution.py:20
  431.5 10.4 %collective-permute-start = (bf16[1,16,64,128]{3,2,1,0:T(8,128)(2,1)S(1)}, bf16[1,16,64,128]{3,2,1,0:T(8,128)(2,1)S(1)}, u32[]{:S(2)}, u32[]{:S(2)}) collective-permute-start(bf16[1,16,64,128]{3,2,1,0:T(8,128)(2,1)S(1)} %get-tuple-element.471), channel_id=1, source_target_pairs={{0,8},{8,16},{16,24},{24,32},{32,40},{40,48},{48,56},{56,64},{64,7... | collective-permute-start | bytes 786440 | tf_op jit(solution)/shard_map/while/body/eval_jaxpr/ppermute | solution.py:20
  442.8 10.4 %collective-permute-start = (bf16[1,16,64,128]{3,2,1,0:T(8,128)(2,1)S(1)}, bf16[1,16,64,128]{3,2,1,0:T(8,128)(2,1)S(1)}, u32[]{:S(2)}, u32[]{:S(2)}) collective-permute-start(bf16[1,16,64,128]{3,2,1,0:T(8,128)(2,1)S(1)} %get-tuple-element.471), channel_id=1, source_target_pairs={{0,8},{8,16},{16,24},{24,32},{32,40},{40,48},{48,56},{56,64},{64,7... | collective-permute-start | bytes 786440 | tf_op jit(solution)/shard_map/while/body/eval_jaxpr/ppermute | solution.py:20
  454.0 10.4 %collective-permute-start = (bf16[1,16,64,128]{3,2,1,0:T(8,128)(2,1)S(1)}, bf16[1,16,64,128]{3,2,1,0:T(8,128)(2,1)S(1)}, u32[]{:S(2)}, u32[]{:S(2)}) collective-permute-start(bf16[1,16,64,128]{3,2,1,0:T(8,128)(2,1)S(1)} %get-tuple-element.471), channel_id=1, source_target_pairs={{0,8},{8,16},{16,24},{24,32},{32,40},{40,48},{48,56},{56,64},{64,7... | collective-permute-start | bytes 786440 | tf_op jit(solution)/shard_map/while/body/eval_jaxpr/ppermute | solution.py:20
  465.2 10.4 %collective-permute-start = (bf16[1,16,64,128]{3,2,1,0:T(8,128)(2,1)S(1)}, bf16[1,16,64,128]{3,2,1,0:T(8,128)(2,1)S(1)}, u32[]{:S(2)}, u32[]{:S(2)}) collective-permute-start(bf16[1,16,64,128]{3,2,1,0:T(8,128)(2,1)S(1)} %get-tuple-element.471), channel_id=1, source_target_pairs={{0,8},{8,16},{16,24},{24,32},{32,40},{40,48},{48,56},{56,64},{64,7... | collective-permute-start | bytes 786440 | tf_op jit(solution)/shard_map/while/body/eval_jaxpr/ppermute | solution.py:20
  476.4 10.4 %collective-permute-start = (bf16[1,16,64,128]{3,2,1,0:T(8,128)(2,1)S(1)}, bf16[1,16,64,128]{3,2,1,0:T(8,128)(2,1)S(1)}, u32[]{:S(2)}, u32[]{:S(2)}) collective-permute-start(bf16[1,16,64,128]{3,2,1,0:T(8,128)(2,1)S(1)} %get-tuple-element.471), channel_id=1, source_target_pairs={{0,8},{8,16},{16,24},{24,32},{32,40},{40,48},{48,56},{56,64},{64,7... | collective-permute-start | bytes 786440 | tf_op jit(solution)/shard_map/while/body/eval_jaxpr/ppermute | solution.py:20
  487.6 10.4 %collective-permute-start = (bf16[1,16,64,128]{3,2,1,0:T(8,128)(2,1)S(1)}, bf16[1,16,64,128]{3,2,1,0:T(8,128)(2,1)S(1)}, u32[]{:S(2)}, u32[]{:S(2)}) collective-permute-start(bf16[1,16,64,128]{3,2,1,0:T(8,128)(2,1)S(1)} %get-tuple-element.471), channel_id=1, source_target_pairs={{0,8},{8,16},{16,24},{24,32},{32,40},{40,48},{48,56},{56,64},{64,7... | collective-permute-start | bytes 786440 | tf_op jit(solution)/shard_map/while/body/eval_jaxpr/ppermute | solution.py:20
  498.8 10.4 %collective-permute-start = (bf16[1,16,64,128]{3,2,1,0:T(8,128)(2,1)S(1)}, bf16[1,16,64,128]{3,2,1,0:T(8,128)(2,1)S(1)}, u32[]{:S(2)}, u32[]{:S(2)}) collective-permute-start(bf16[1,16,64,128]{3,2,1,0:T(8,128)(2,1)S(1)} %get-tuple-element.471), channel_id=1, source_target_pairs={{0,8},{8,16},{16,24},{24,32},{32,40},{40,48},{48,56},{56,64},{64,7... | collective-permute-start | bytes 786440 | tf_op jit(solution)/shard_map/while/body/eval_jaxpr/ppermute | solution.py:20
  510.1 10.4 %collective-permute-start = (bf16[1,16,64,128]{3,2,1,0:T(8,128)(2,1)S(1)}, bf16[1,16,64,128]{3,2,1,0:T(8,128)(2,1)S(1)}, u32[]{:S(2)}, u32[]{:S(2)}) collective-permute-start(bf16[1,16,64,128]{3,2,1,0:T(8,128)(2,1)S(1)} %get-tuple-element.471), channel_id=1, source_target_pairs={{0,8},{8,16},{16,24},{24,32},{32,40},{40,48},{48,56},{56,64},{64,7... | collective-permute-start | bytes 786440 | tf_op jit(solution)/shard_map/while/body/eval_jaxpr/ppermute | solution.py:20
  521.3 10.4 %collective-permute-start = (bf16[1,16,64,128]{3,2,1,0:T(8,128)(2,1)S(1)}, bf16[1,16,64,128]{3,2,1,0:T(8,128)(2,1)S(1)}, u32[]{:S(2)}, u32[]{:S(2)}) collective-permute-start(bf16[1,16,64,128]{3,2,1,0:T(8,128)(2,1)S(1)} %get-tuple-element.471), channel_id=1, source_target_pairs={{0,8},{8,16},{16,24},{24,32},{32,40},{40,48},{48,56},{56,64},{64,7... | collective-permute-start | bytes 786440 | tf_op jit(solution)/shard_map/while/body/eval_jaxpr/ppermute | solution.py:20
  532.5 10.4 %collective-permute-start = (bf16[1,16,64,128]{3,2,1,0:T(8,128)(2,1)S(1)}, bf16[1,16,64,128]{3,2,1,0:T(8,128)(2,1)S(1)}, u32[]{:S(2)}, u32[]{:S(2)}) collective-permute-start(bf16[1,16,64,128]{3,2,1,0:T(8,128)(2,1)S(1)} %get-tuple-element.471), channel_id=1, source_target_pairs={{0,8},{8,16},{16,24},{24,32},{32,40},{40,48},{48,56},{56,64},{64,7... | collective-permute-start | bytes 786440 | tf_op jit(solution)/shard_map/while/body/eval_jaxpr/ppermute | solution.py:20
  543.7 10.4 %collective-permute-start = (bf16[1,16,64,128]{3,2,1,0:T(8,128)(2,1)S(1)}, bf16[1,16,64,128]{3,2,1,0:T(8,128)(2,1)S(1)}, u32[]{:S(2)}, u32[]{:S(2)}) collective-permute-start(bf16[1,16,64,128]{3,2,1,0:T(8,128)(2,1)S(1)} %get-tuple-element.471), channel_id=1, source_target_pairs={{0,8},{8,16},{16,24},{24,32},{32,40},{40,48},{48,56},{56,64},{64,7... | collective-permute-start | bytes 786440 | tf_op jit(solution)/shard_map/while/body/eval_jaxpr/ppermute | solution.py:20
  554.9 10.4 %collective-permute-start = (bf16[1,16,64,128]{3,2,1,0:T(8,128)(2,1)S(1)}, bf16[1,16,64,128]{3,2,1,0:T(8,128)(2,1)S(1)}, u32[]{:S(2)}, u32[]{:S(2)}) collective-permute-start(bf16[1,16,64,128]{3,2,1,0:T(8,128)(2,1)S(1)} %get-tuple-element.471), channel_id=1, source_target_pairs={{0,8},{8,16},{16,24},{24,32},{32,40},{40,48},{48,56},{56,64},{64,7... | collective-permute-start | bytes 786440 | tf_op jit(solution)/shard_map/while/body/eval_jaxpr/ppermute | solution.py:20
  566.2 10.4 %collective-permute-start = (bf16[1,16,64,128]{3,2,1,0:T(8,128)(2,1)S(1)}, bf16[1,16,64,128]{3,2,1,0:T(8,128)(2,1)S(1)}, u32[]{:S(2)}, u32[]{:S(2)}) collective-permute-start(bf16[1,16,64,128]{3,2,1,0:T(8,128)(2,1)S(1)} %get-tuple-element.471), channel_id=1, source_target_pairs={{0,8},{8,16},{16,24},{24,32},{32,40},{40,48},{48,56},{56,64},{64,7... | collective-permute-start | bytes 786440 | tf_op jit(solution)/shard_map/while/body/eval_jaxpr/ppermute | solution.py:20
  577.4 10.4 %collective-permute-start = (bf16[1,16,64,128]{3,2,1,0:T(8,128)(2,1)S(1)}, bf16[1,16,64,128]{3,2,1,0:T(8,128)(2,1)S(1)}, u32[]{:S(2)}, u32[]{:S(2)}) collective-permute-start(bf16[1,16,64,128]{3,2,1,0:T(8,128)(2,1)S(1)} %get-tuple-element.471), channel_id=1, source_target_pairs={{0,8},{8,16},{16,24},{24,32},{32,40},{40,48},{48,56},{56,64},{64,7... | collective-permute-start | bytes 786440 | tf_op jit(solution)/shard_map/while/body/eval_jaxpr/ppermute | solution.py:20
  588.6 10.4 %collective-permute-start = (bf16[1,16,64,128]{3,2,1,0:T(8,128)(2,1)S(1)}, bf16[1,16,64,128]{3,2,1,0:T(8,128)(2,1)S(1)}, u32[]{:S(2)}, u32[]{:S(2)}) collective-permute-start(bf16[1,16,64,128]{3,2,1,0:T(8,128)(2,1)S(1)} %get-tuple-element.471), channel_id=1, source_target_pairs={{0,8},{8,16},{16,24},{24,32},{32,40},{40,48},{48,56},{56,64},{64,7... | collective-permute-start | bytes 786440 | tf_op jit(solution)/shard_map/while/body/eval_jaxpr/ppermute | solution.py:20
  599.8 10.4 %collective-permute-start = (bf16[1,16,64,128]{3,2,1,0:T(8,128)(2,1)S(1)}, bf16[1,16,64,128]{3,2,1,0:T(8,128)(2,1)S(1)}, u32[]{:S(2)}, u32[]{:S(2)}) collective-permute-start(bf16[1,16,64,128]{3,2,1,0:T(8,128)(2,1)S(1)} %get-tuple-element.471), channel_id=1, source_target_pairs={{0,8},{8,16},{16,24},{24,32},{32,40},{40,48},{48,56},{56,64},{64,7... | collective-permute-start | bytes 786440 | tf_op jit(solution)/shard_map/while/body/eval_jaxpr/ppermute | solution.py:20
  611.0 10.4 %collective-permute-start = (bf16[1,16,64,128]{3,2,1,0:T(8,128)(2,1)S(1)}, bf16[1,16,64,128]{3,2,1,0:T(8,128)(2,1)S(1)}, u32[]{:S(2)}, u32[]{:S(2)}) collective-permute-start(bf16[1,16,64,128]{3,2,1,0:T(8,128)(2,1)S(1)} %get-tuple-element.471), channel_id=1, source_target_pairs={{0,8},{8,16},{16,24},{24,32},{32,40},{40,48},{48,56},{56,64},{64,7... | collective-permute-start | bytes 786440 | tf_op jit(solution)/shard_map/while/body/eval_jaxpr/ppermute | solution.py:20
  622.3 10.4 %collective-permute-start = (bf16[1,16,64,128]{3,2,1,0:T(8,128)(2,1)S(1)}, bf16[1,16,64,128]{3,2,1,0:T(8,128)(2,1)S(1)}, u32[]{:S(2)}, u32[]{:S(2)}) collective-permute-start(bf16[1,16,64,128]{3,2,1,0:T(8,128)(2,1)S(1)} %get-tuple-element.471), channel_id=1, source_target_pairs={{0,8},{8,16},{16,24},{24,32},{32,40},{40,48},{48,56},{56,64},{64,7... | collective-permute-start | bytes 786440 | tf_op jit(solution)/shard_map/while/body/eval_jaxpr/ppermute | solution.py:20
  633.5 10.4 %collective-permute-start = (bf16[1,16,64,128]{3,2,1,0:T(8,128)(2,1)S(1)}, bf16[1,16,64,128]{3,2,1,0:T(8,128)(2,1)S(1)}, u32[]{:S(2)}, u32[]{:S(2)}) collective-permute-start(bf16[1,16,64,128]{3,2,1,0:T(8,128)(2,1)S(1)} %get-tuple-element.471), channel_id=1, source_target_pairs={{0,8},{8,16},{16,24},{24,32},{32,40},{40,48},{48,56},{56,64},{64,7... | collective-permute-start | bytes 786440 | tf_op jit(solution)/shard_map/while/body/eval_jaxpr/ppermute | solution.py:20
  644.7 10.4 %collective-permute-start = (bf16[1,16,64,128]{3,2,1,0:T(8,128)(2,1)S(1)}, bf16[1,16,64,128]{3,2,1,0:T(8,128)(2,1)S(1)}, u32[]{:S(2)}, u32[]{:S(2)}) collective-permute-start(bf16[1,16,64,128]{3,2,1,0:T(8,128)(2,1)S(1)} %get-tuple-element.471), channel_id=1, source_target_pairs={{0,8},{8,16},{16,24},{24,32},{32,40},{40,48},{48,56},{56,64},{64,7... | collective-permute-start | bytes 786440 | tf_op jit(solution)/shard_map/while/body/eval_jaxpr/ppermute | solution.py:20
  655.9 10.4 %collective-permute-start = (bf16[1,16,64,128]{3,2,1,0:T(8,128)(2,1)S(1)}, bf16[1,16,64,128]{3,2,1,0:T(8,128)(2,1)S(1)}, u32[]{:S(2)}, u32[]{:S(2)}) collective-permute-start(bf16[1,16,64,128]{3,2,1,0:T(8,128)(2,1)S(1)} %get-tuple-element.471), channel_id=1, source_target_pairs={{0,8},{8,16},{16,24},{24,32},{32,40},{40,48},{48,56},{56,64},{64,7... | collective-permute-start | bytes 786440 | tf_op jit(solution)/shard_map/while/body/eval_jaxpr/ppermute | solution.py:20
  667.1 10.4 %collective-permute-start = (bf16[1,16,64,128]{3,2,1,0:T(8,128)(2,1)S(1)}, bf16[1,16,64,128]{3,2,1,0:T(8,128)(2,1)S(1)}, u32[]{:S(2)}, u32[]{:S(2)}) collective-permute-start(bf16[1,16,64,128]{3,2,1,0:T(8,128)(2,1)S(1)} %get-tuple-element.471), channel_id=1, source_target_pairs={{0,8},{8,16},{16,24},{24,32},{32,40},{40,48},{48,56},{56,64},{64,7... | collective-permute-start | bytes 786440 | tf_op jit(solution)/shard_map/while/body/eval_jaxpr/ppermute | solution.py:20
  678.4 10.4 %collective-permute-start = (bf16[1,16,64,128]{3,2,1,0:T(8,128)(2,1)S(1)}, bf16[1,16,64,128]{3,2,1,0:T(8,128)(2,1)S(1)}, u32[]{:S(2)}, u32[]{:S(2)}) collective-permute-start(bf16[1,16,64,128]{3,2,1,0:T(8,128)(2,1)S(1)} %get-tuple-element.471), channel_id=1, source_target_pairs={{0,8},{8,16},{16,24},{24,32},{32,40},{40,48},{48,56},{56,64},{64,7... | collective-permute-start | bytes 786440 | tf_op jit(solution)/shard_map/while/body/eval_jaxpr/ppermute | solution.py:20
  689.6 10.4 %collective-permute-start = (bf16[1,16,64,128]{3,2,1,0:T(8,128)(2,1)S(1)}, bf16[1,16,64,128]{3,2,1,0:T(8,128)(2,1)S(1)}, u32[]{:S(2)}, u32[]{:S(2)}) collective-permute-start(bf16[1,16,64,128]{3,2,1,0:T(8,128)(2,1)S(1)} %get-tuple-element.471), channel_id=1, source_target_pairs={{0,8},{8,16},{16,24},{24,32},{32,40},{40,48},{48,56},{56,64},{64,7... | collective-permute-start | bytes 786440 | tf_op jit(solution)/shard_map/while/body/eval_jaxpr/ppermute | solution.py:20
  (8 other events, 15.5 us)
where the time goes:
time: 743 us; the launch traced here: 740 us
  waiting for transfers between devices  477 us (64%)
  starting transfers between devices  119 us (16%)
  matrix products  52.5 us (7%)
  other arithmetic  50.4 us (7%)
  blocking collectives  33.4 us (4%)
    ppermute x62, waiting for transfers between devices, passed_along(): return lax.ppermute(block, axis, route)  477 us
    ppermute x62, starting transfers between devices, passed_along(): return lax.ppermute(block, axis, route)  119 us
    psum x1, blocking collectives, local(): square_total = lax.psum(jnp.sum(gated * gated, axis=-1), 'tp')  33.4 us
    dot_general x32, matrix products, sub_step(): jnp.einsum('wlhc,cwm->wlhm', weights.astype(jnp.bfloat16), value_portion,...  33 us
    add x31, other arithmetic, relay_step(): return (received, block_decay[..., None, None] * received + local_state)  26.1 us
    reduce_sum x32, other arithmetic, sub_step(): run_sum = run_sum * correction_factor + jnp.sum(weights, axis=-1)  16.5 us
    dot_general x32, matrix products, sub_step(): jnp.einsum('faqo,bao->aqfb', query_head_rows, key_portion, preferred_elem...  15.9 us
  transfers between devices with their start and end apart: 62, of which 62 were waited for; matrix products, arithmetic and copies ran while one was open for 0% of the time, Pallas kernels for 0%

commit v1 on v0

v1 whole, which is shorter than its diff:
```python
import functools

import jax
import jax.numpy as jnp
from jax import lax
from jax.experimental import pallas as pl
from jax.experimental.pallas import tpu as pltpu
from jax.sharding import PartitionSpec as P

HEAD_WIDTH = 128
STATE_HEADS = 128
P_SIZE = 64
N = 128


causal_score = -1e30


def attend_kernel(pos_ref, q_ref, kv_ref, o_ref, m_sc, l_sc, acc_sc, *, heads, width):
    key_block = pl.program_id(0)
    position = pos_ref[0]
    score_factor = width ** (-0.5)

    @pl.when(key_block == 0)
    def _init():
        m_sc[...] = jnp.full(m_sc.shape, causal_score, jnp.float32)
        l_sc[...] = jnp.zeros(l_sc.shape, jnp.float32)
        acc_sc[...] = jnp.zeros(acc_sc.shape, jnp.float32)

    def run_block(masked):
        key_portion = kv_ref[0]
        value_portion = kv_ref[1]
        rows = q_ref.shape[0]
        if masked:
            query_idx = lax.broadcasted_iota(jnp.int32, (rows, key_portion.shape[0]), 0)
            key_idx = lax.broadcasted_iota(jnp.int32, (rows, key_portion.shape[0]), 1)
            is_valid = key_idx <= query_idx
        for h in range(heads):
            query_rows = q_ref[:, h * width:(h + 1) * width]
            score_matrix = (
                lax.dot_general(
                    query_rows,
                    key_portion,
                    (((1,), (1,)), ((), ())),
                    preferred_element_type=jnp.float32,
                )
                * score_factor
            )
            if masked:
                score_matrix = jnp.where(is_valid, score_matrix, causal_score)
            run_max = m_sc[h]
            new_max = jnp.maximum(run_max, jnp.max(score_matrix, axis=-1, keepdims=True))
            weights = jnp.exp(score_matrix - new_max)
            if masked:
                weights = jnp.where(is_valid, weights, 0.0)
            correction_factor = jnp.exp(run_max - new_max)
            l_sc[h] = l_sc[h] * correction_factor + jnp.sum(weights, axis=-1, keepdims=True)
            acc_sc[h] = acc_sc[h] * correction_factor + jnp.dot(
                weights.astype(jnp.bfloat16), value_portion, preferred_element_type=jnp.float32
            )
            m_sc[h] = new_max

    @pl.when(key_block < position)
    def _full():
        run_block(False)

    @pl.when(key_block == position)
    def _diagonal():
        run_block(True)
        for h in range(heads):
            o_ref[:, h * width:(h + 1) * width] = (acc_sc[h] / l_sc[h]).astype(o_ref.dtype)


def causal_attention(position, queries, gathered_kv):
    blocks, _, tok_rows, width = gathered_kv.shape
    heads = queries.shape[1] // width
    kernel = functools.partial(attend_kernel, heads=heads, width=width)
    grid_spec = pltpu.PrefetchScalarGridSpec(
        num_scalar_prefetch=1,
        grid=(blocks,),
        in_specs=[
            pl.BlockSpec(queries.shape, lambda kb, pos: (0, 0)),
            pl.BlockSpec(
                (None, 2, tok_rows, width),
                lambda kb, pos: (jnp.minimum(kb, pos[0]), 0, 0, 0),
            ),
        ],
        out_specs=pl.BlockSpec(queries.shape, lambda kb, pos: (0, 0)),
        scratch_shapes=[
            pltpu.VMEM((heads, tok_rows, 1), jnp.float32),
            pltpu.VMEM((heads, tok_rows, 1), jnp.float32),
            pltpu.VMEM((heads, tok_rows, width), jnp.float32),
        ],
    )
    flops = 4 * queries.shape[0] * queries.shape[1] * tok_rows * blocks
    return pl.pallas_call(
        kernel,
        grid_spec=grid_spec,
        out_shape=jax.ShapeDtypeStruct(queries.shape, queries.dtype),
        compiler_params=pltpu.CompilerParams(dimension_semantics=("arbitrary",)),
        cost_estimate=pl.CostEstimate(
            flops=flops,
            transcendentals=heads * queries.shape[0] * tok_rows * blocks,
            bytes_accessed=2 * queries.size * 2 + gathered_kv.size * 2,
        ),
    )(position.reshape(1), queries, gathered_kv)


def local(
    queries,
    key_rows,
    value_head_rows,
    ssm_input,
    gate_input,
    b_matrix,
    c_matrix,
    step_size,
    log_decay,
    skip_gain,
    norm_gain,
):
    tok_rows = queries.shape[0]
    ctx_count = lax.axis_size("ctx")
    position = lax.axis_index("ctx")

    gathered_kv = lax.all_gather(jnp.stack((key_rows, value_head_rows)), "ctx")

    heads_local = step_size.shape[0]
    groups_local = b_matrix.shape[1] // N
    heads_group = heads_local // groups_local
    mixer_in = ssm_input.reshape(tok_rows, groups_local, heads_group, P_SIZE)
    in_maps = b_matrix.reshape(tok_rows, groups_local, N)
    out_maps = c_matrix.reshape(tok_rows, groups_local, N)
    steps_here = step_size.reshape(groups_local, heads_group, tok_rows)
    cumul = jnp.cumsum(log_decay.reshape(groups_local, heads_group, tok_rows), axis=-1)
    causal = jnp.tril(jnp.ones((tok_rows, tok_rows), dtype=bool))
    gram = jnp.einsum("tgn,sgn->gts", out_maps, in_maps, preferred_element_type=jnp.float32)
    spread = jnp.where(causal, cumul[..., :, None] - cumul[..., None, :], 0.0)
    mixing = jnp.where(
        causal, gram[:, None] * jnp.exp(spread) * steps_here[..., None, :], 0.0
    ).astype(jnp.bfloat16)
    inner = jnp.einsum("ghts,sghp->tghp", mixing, mixer_in, preferred_element_type=jnp.float32)
    weight_end = jnp.exp(cumul[..., -1:] - cumul) * steps_here
    weighted = (mixer_in * weight_end.transpose(2, 0, 1)[..., None]).astype(jnp.bfloat16)
    local_state = jnp.einsum(
        "sghp,sgn->ghpn", weighted, in_maps, preferred_element_type=jnp.float32
    )
    block_log_decay = cumul[..., -1]

    states = lax.all_gather(local_state.astype(jnp.bfloat16), "ctx")
    log_decays = lax.all_gather(block_log_decay, "ctx")
    source = jnp.arange(ctx_count, dtype=jnp.int32)
    between = (source[None, :] > source[:, None]) & (source[None, :] < position)
    span_decay = jnp.sum(
        jnp.where(between[:, :, None, None], log_decays[None, :], 0.0), axis=1
    )
    state_weight = jnp.where(
        (source < position)[:, None, None], jnp.exp(span_decay), 0.0
    )
    incoming = jnp.sum(
        state_weight[..., None, None] * states.astype(jnp.float32), axis=0
    )

    attention_out = causal_attention(position, queries, gathered_kv)

    carried_out = jnp.einsum(
        "ghpn,tgn->tghp", incoming, out_maps.astype(jnp.float32), precision=lax.Precision.HIGHEST
    )
    carried_out = carried_out * jnp.exp(cumul).transpose(2, 0, 1)[..., None]
    direct = skip_gain.reshape(groups_local, heads_group)[None, :, :, None] * mixer_in.astype(
        jnp.float32
    )
    outputs = (inner + carried_out + direct).reshape(tok_rows, -1)
    gated = outputs * jax.nn.silu(gate_input.astype(jnp.float32))
    square_parts = lax.all_gather(jnp.sum(gated * gated, axis=-1), "tp")
    square_total = jnp.sum(square_parts, axis=0)
    scaling = lax.rsqrt(square_total / (STATE_HEADS * P_SIZE) + 1e-05)
    mixer_out = (gated * scaling[:, None] * norm_gain.astype(jnp.float32)).astype(jnp.bfloat16)
    return (attention_out, mixer_out)


def solution(mesh):
    placed = (
        P("ctx", "tp"),
        P("ctx", "tp"),
        P("ctx", "tp"),
        P("ctx", "tp"),
        P("ctx", "tp"),
        P("ctx", "tp"),
        P("ctx", "tp"),
        P("tp", "ctx"),
        P("tp", "ctx"),
        P("tp"),
        P("tp"),
    )
    return jax.shard_map(
        local,
        mesh=mesh,
        in_specs=placed,
        out_specs=(P("ctx", "tp"), P("ctx", "tp")),
        check_vma=False,
    )
```

time: 743 us -> 229 us (0.31)
  the two profiles are of different devices: /device:TPU:2 before, /device:TPU:230 now
where the time goes in v1:
time: 229 us; the launch traced here: 225 us
  Pallas kernels  110 us (48%)
  blocking collectives  63.1 us (28%)
  waiting for transfers between devices  19.5 us (9%)
  between operations  14.2 us (6%)
  other arithmetic  10.8 us (5%)
  matrix products  3.98 us (2%)
  local copies, waits for them, and re-layouts  3.12 us (1%)
    pallas_call x1, Pallas kernels, causal_attention(): pl.pallas_call(kernel, grid_spec=grid_spec, out_shape=jax.ShapeDtypeStruc...  110 us
    all_gather x1, blocking collectives, local(): log_decays = lax.all_gather(block_log_decay, 'ctx')  36.8 us
    all_gather x1, blocking collectives, local(): square_parts = lax.all_gather(jnp.sum(gated * gated, axis=-1), 'tp')  26.4 us
    all_gather x1, waiting for transfers between devices, local(): gathered_kv = lax.all_gather(jnp.stack((key_rows, value_head_rows)), 'ctx')  19.5 us
    reduce_sum x1, other arithmetic, local(): jnp.sum(state_weight[..., None, None] * states.astype(jnp.float32), axis=0)  5.1 us
  transfers between devices with their start and end apart: 2, of which 1 were waited for; matrix products, arithmetic and copies ran while one was open for 3% of the time, Pallas kernels for 49%

profile of v1, /device:TPU:230, one launch (start us, length us, event | category | flops | bytes accessed | tf_op | source)
XLA Modules:
  0.0 225.1 jit_solution(1141091040309518100)
XLA Ops:
  7.2 0.0 copy-start
  7.2 0.0 copy-start.2
  7.2 0.0 all-gather.8.cloned.1.call-start
  7.2 1.5 pad_maximum_fusion
  8.8 0.0 all-gather.8.cloned.1.call-update
  8.8 0.0 all-gather.10.cloned.1.call-start
  8.9 0.7 reshape.256
  9.6 0.6 reduce-window.6
  10.2 0.2 slice_reduce_fusion
  10.4 0.1 copy.50
  10.5 1.2 copy.51
  11.8 0.1 broadcast.140
  11.9 0.3 fusion.22
  12.2 0.8 multiply_bitcast_fusion
  13.0 0.1 fusion.17
  13.1 1.8 convolution_convert_fusion
  14.9 0.0 all-gather.10.cloned.1.call-update
  14.9 0.1 copy.53
  15.0 36.8 %all-gather.1 = f32[32,16,1]{1,2,0:T(1,128)S(1)} all-gather(f32[1,16,1]{1,2,0:T(1,128)S(1)} %copy.53), channel_id=3, replica_groups=mesh['ctx'=32,'tp'=8] {'ctx'}, dimensions={0}, use_global_device_ids=true | all-gather | bytes 2112 | tf_op jit(solution)/shard_map/all_gather | solution.py:151
  51.8 0.1 copy.54
  51.9 0.7 convert_element_type.61
  52.6 0.1 select_reduce_fusion
  52.7 0.1 exponential_select_fusion
  52.8 0.0 copy-done
  52.8 0.0 copy-done.2
  52.8 0.2 fusion.23
  53.0 19.5 %all-gather.8.cloned.1.call-done = bf16[64,256,128]{2,1,0:T(8,128)(2,1)} async-done(((bf16[2,256,128]{2,1,0:T(8,128)(2,1)}), bf16[64,256,128]{2,1,0:T(8,128)(2,1)}) %all-gather.8.cloned.1.call-update) | async-done | bytes 4194320 | tf_op jit(solution)/shard_map/all_gather | solution.py:126
  72.5 110.3 %shard_map.122 = bf16[256,1024]{1,0:T(8,128)(2,1)} custom-call(s32[1]{0:T(128)} %bitcast.pos_ref, bf16[256,1024]{1,0:T(8,128)(2,1)} %q_ref.1, bf16[32,2,256,128]{3,2,1,0:T(8,128)(2,1)} %bitcast.86), custom_call_target="tpu_custom_call" | custom-call | flops 8589934592 | bytes 5242880 | tf_op jit(solution)/shard_map/pallas_call | solution.py:96
  182.8 0.0 all-gather.10.cloned.1.call-done
  182.8 0.0 copy-start.3
  182.8 0.0 copy-start.4
  182.8 5.1 %fusion = f32[16,64,128]{2,1,0:T(8,128)S(1)} fusion(bf16[32,1,16,64,128]{4,3,2,0,1:T(8,128)(2,1)} %bitcast.71, f32[32,16]{1,0:T(8,128)S(1)} %exponential_select_fusion), kind=kLoop, calls=%fused_computation.1 | loop fusion | flops 12451840 | bytes 8914944 | tf_op jit(solution)/shard_map/reduce_sum | solution.py:160
  188.0 0.6 fusion.10
  188.5 0.0 copy-done.3
  188.6 0.0 copy-done.4
  188.6 0.0 copy-start.1
  188.6 1.4 fusion.12
  190.0 0.3 copy.56
  190.3 0.0 copy-done.1
  190.3 0.4 multiply_reduce_fusion
  190.7 26.4 %all-gather.4 = f32[8,1,256]{2,1,0:T(1,128)S(1)} all-gather(f32[1,1,256]{2,1,0:T(1,128)S(1)} %bitcast.85), channel_id=5, replica_groups=mesh['ctx'=32,'tp'=8] {'tp'}, dimensions={0}, use_global_device_ids=true | all-gather | bytes 9216 | tf_op jit(solution)/shard_map/all_gather | solution.py:175
  217.1 1.2 multiply_convert_fusion
  (12 shorter events, 0.2 us)
Async XLA Ops:
  7.2 45.7 %copy-start = (bf16[256,128]{1,0:T(8,128)(2,1)S(1)}, bf16[256,128]{1,0:T(8,128)(2,1)}, u32[]{:S(2)}) copy-start(bf16[256,128]{1,0:T(8,128)(2,1)} %param.17) | copy-start | bytes 196612
  7.2 45.6 %copy-start.2 = (bf16[256,128]{1,0:T(8,128)(2,1)S(1)}, bf16[256,128]{1,0:T(8,128)(2,1)}, u32[]{:S(2)}) copy-start(bf16[256,128]{1,0:T(8,128)(2,1)} %param.16) | copy-start | bytes 196612
  7.2 65.3 %all-gather.8.cloned.1.call-start = ((), (), s32[]{:S(2)}) async-start(), calls=%async_computation | async-start | bytes 4325376 | tf_op jit(solution)/shard_map/all_gather | solution.py:126
  8.8 174.0 %all-gather.10.cloned.1.call-start = ((), (), s32[]{:S(2)}) async-start(), calls=%async_computation.1 | async-start | bytes 8650752 | tf_op jit(solution)/shard_map/all_gather | solution.py:150
  182.8 5.7 %copy-start.3 = (f32[16,256]{1,0:T(8,128)S(1)}, f32[16,256]{1,0:T(8,128)}, u32[]{:S(2)}) copy-start(f32[16,256]{1,0:T(8,128)} %param.18) | copy-start | bytes 49156
  182.8 5.7 %copy-start.4 = (f32[16]{0:T(128)S(1)}, f32[16]{0:T(128)}, u32[]{:S(2)}) copy-start(f32[16]{0:T(128)} %param.20) | copy-start | bytes 196
  188.6 1.7 copy-start.1
Sparse Core Ops, SparseCore 0:
  10.5 62.0 all-gather.7
  74.9 67.7 all-gather.9

commit v2 on v1

--- a/solution.py
+++ b/solution.py
@@ -106,6 +106,39 @@
     )(position.reshape(1), queries, gathered_kv)
 
 
+def shifted(block, axis, distance):
+    devices = range(lax.axis_size(axis))
+    route = [(i - distance, i) for i in devices if i - distance in devices]
+    return lax.ppermute(block, axis, route)
+
+
+def summed_over(part, axis):
+    count = lax.axis_size(axis)
+    total = part
+    for distance in range(1, count):
+        route = [(i, (i + distance) % count) for i in range(count)]
+        total = total + lax.ppermute(part, axis, route)
+    return total
+
+
+def carried_scan(local_state, block_log_decay, position, ctx_count):
+    sent = local_state.astype(jnp.bfloat16)
+    one_back_state = shifted(sent, "ctx", 1).astype(jnp.float32)
+    one_back_decay = shifted(block_log_decay, "ctx", 1)
+    two_back_state = shifted(sent, "ctx", 2).astype(jnp.float32)
+    two_back_decay = shifted(block_log_decay, "ctx", 2)
+    state = jnp.exp(one_back_decay)[..., None, None] * two_back_state + one_back_state
+    log_span = one_back_decay + two_back_decay
+    distance = 2
+    while distance < ctx_count:
+        earlier_state = shifted(state.astype(jnp.bfloat16), "ctx", distance).astype(jnp.float32)
+        earlier_span = shifted(log_span, "ctx", distance)
+        state = jnp.exp(log_span)[..., None, None] * earlier_state + state
+        log_span = log_span + earlier_span
+        distance *= 2
+    return state
+
+
 def local(
     queries,
     key_rows,
@@ -147,19 +180,7 @@
     )
     block_log_decay = cumul[..., -1]
 
-    states = lax.all_gather(local_state.astype(jnp.bfloat16), "ctx")
-    log_decays = lax.all_gather(block_log_decay, "ctx")
-    source = jnp.arange(ctx_count, dtype=jnp.int32)
-    between = (source[None, :] > source[:, None]) & (source[None, :] < position)
-    span_decay = jnp.sum(
-        jnp.where(between[:, :, None, None], log_decays[None, :], 0.0), axis=1
-    )
-    state_weight = jnp.where(
-        (source < position)[:, None, None], jnp.exp(span_decay), 0.0
-    )
-    incoming = jnp.sum(
-        state_weight[..., None, None] * states.astype(jnp.float32), axis=0
-    )
+    incoming = carried_scan(local_state, block_log_decay, position, ctx_count)
 
     attention_out = causal_attention(position, queries, gathered_kv)
 
@@ -172,8 +193,7 @@
     )
     outputs = (inner + carried_out + direct).reshape(tok_rows, -1)
     gated = outputs * jax.nn.silu(gate_input.astype(jnp.float32))
-    square_parts = lax.all_gather(jnp.sum(gated * gated, axis=-1), "tp")
-    square_total = jnp.sum(square_parts, axis=0)
+    square_total = summed_over(jnp.sum(gated * gated, axis=-1), "tp")
     scaling = lax.rsqrt(square_total / (STATE_HEADS * P_SIZE) + 1e-05)
     mixer_out = (gated * scaling[:, None] * norm_gain.astype(jnp.float32)).astype(jnp.bfloat16)
     return (attention_out, mixer_out)

time: 229 us -> 236 us (1.031); the launches traced: 225 us -> 236 us
  blocking collectives: 63.1 us -> 0 us
  waiting for transfers between devices: 19.5 us -> 64.7 us
  starting transfers between devices: 0.08 us -> 34 us
  other arithmetic: 10.8 us -> 5.87 us
    ppermute x0 -> x18, waiting for transfers between devices: none -> 64.7 us  [the longest x11 55.1 us: shifted(): return lax.ppermute(block, axis, route)]
    all_gather x2 -> x0, blocking collectives: 63.1 us -> none  [the longest x1 36.8 us: local(): log_decays = lax.all_gather(block_log_decay, 'ctx')]
    ppermute x0 -> x18, starting transfers between devices: none -> 34 us  [the longest x7 18.4 us: summed_over(): total = total + lax.ppermute(part, axis, route)]
    all_gather x1, waiting for transfers between devices: 19.5 us -> 0.01 us  [local(): gathered_kv = lax.all_gather(jnp.stack((key_rows, value_head_rows)), 'ctx')]
    reduce_sum x4 -> x1, other arithmetic: 5.67 us -> 0.4 us  [local(): square_total = summed_over(jnp.sum(gated * gated, axis=-1), 'tp')]
  transfers between devices with their start and end apart: 2 -> 19, of which waited for: 1 -> 8; matrix products, arithmetic and copies ran while one was open for 3% -> 5% of each run, Pallas kernels for 49% -> 0%
where the time goes in v2:
time: 236 us
  Pallas kernels  110 us (47%)
  waiting for transfers between devices  64.7 us (27%)
  starting transfers between devices  34 us (14%)
  between operations  14.4 us (6%)
  other arithmetic  5.87 us (2%)
  matrix products  3.41 us (1%)
  local copies, waits for them, and re-layouts  2.98 us (1%)
    pallas_call x1, Pallas kernels, causal_attention(): pl.pallas_call(kernel, grid_spec=grid_spec, out_shape=jax.ShapeDtypeStruc...  110 us
    ppermute x11, waiting for transfers between devices, shifted(): return lax.ppermute(block, axis, route)  55.1 us
    ppermute x7, starting transfers between devices, summed_over(): total = total + lax.ppermute(part, axis, route)  18.4 us
    ppermute x11, starting transfers between devices, shifted(): return lax.ppermute(block, axis, route)  15.6 us
    ppermute x7, waiting for transfers between devices, summed_over(): total = total + lax.ppermute(part, axis, route)  9.55 us
  transfers between devices with their start and end apart: 19, of which 8 were waited for; matrix products, arithmetic and copies ran while one was open for 5% of the time, Pallas kernels for 0%

profile of v2, /device:TPU:230, one launch (start us, length us, event | category | flops | bytes accessed | tf_op | source)
XLA Modules:
  0.0 235.7 jit_solution(13111393487220177576)
XLA Ops:
  7.2 0.0 copy-start
  7.2 0.0 copy-start.2
  7.2 0.0 all-gather.3.cloned.1.call-start
  7.2 1.5 pad_maximum_fusion
  8.8 0.0 all-gather.3.cloned.1.call-update
  8.8 0.7 reshape.195
  9.5 0.6 reduce-window.6
  10.2 0.0 copy-start.3
  10.2 1.2 copy.39
  11.4 0.2 slice_reduce_fusion
  11.6 0.1 copy.38
  11.7 0.1 broadcast.73
  11.8 0.3 slice_reduce_fusion.1
  12.1 0.8 multiply_bitcast_fusion
  12.9 0.1 fusion.17
  13.0 1.1 fusion.12
  14.2 1.9 collective-permute-start.6
  16.1 1.3 collective-permute-start.5
  17.4 1.9 collective-permute-start
  19.3 1.3 collective-permute-start.1
  20.6 10.0 %collective-permute-done = f32[1,16]{1,0:T(1,128)S(1)} collective-permute-done((f32[1,16]{1,0:T(1,128)S(1)}, f32[1,16]{1,0:T(1,128)S(1)}, u32[]{:S(2)}, u32[]{:S(2)}) %collective-permute-start) | collective-permute-done | bytes 96 | tf_op jit(solution)/shard_map/ppermute | solution.py:112
  30.6 0.0 collective-permute-done.1
  30.6 0.0 collective-permute-done.6
  30.6 0.0 collective-permute-done.5
  30.6 0.2 fusion.22
  30.8 1.3 collective-permute-start.7
  32.1 1.3 collective-permute-start.2
  33.4 10.2 %collective-permute-done.7 = bf16[1,16,64,128]{3,2,1,0:T(8,128)(2,1)S(1)} collective-permute-done((bf16[1,16,64,128]{3,2,1,0:T(8,128)(2,1)S(1)}, bf16[1,16,64,128]{3,2,1,0:T(8,128)(2,1)S(1)}, u32[]{:S(2)}, u32[]{:S(2)}) %collective-permute-start.7) | collective-permute-done | bytes 262176 | tf_op jit(solution)/shard_map/ppermute | solution.py:112
  43.6 0.3 fusion.29
  43.9 1.3 collective-permute-start.8
  45.2 0.2 fusion.30
  45.4 0.0 collective-permute-done.2
  45.4 1.3 collective-permute-start.3
  46.7 12.4 %collective-permute-done.8 = bf16[1,16,64,128]{3,2,1,0:T(8,128)(2,1)S(1)} collective-permute-done((bf16[1,16,64,128]{3,2,1,0:T(8,128)(2,1)S(1)}, bf16[1,16,64,128]{3,2,1,0:T(8,128)(2,1)S(1)}, u32[]{:S(2)}, u32[]{:S(2)}) %collective-permute-start.8) | collective-permute-done | bytes 262176 | tf_op jit(solution)/shard_map/ppermute | solution.py:112
  59.1 0.3 fusion.23
  59.4 1.3 collective-permute-start.9
  60.8 0.0 collective-permute-done.3
  60.8 9.3 %collective-permute-done.9 = bf16[1,16,64,128]{3,2,1,0:T(8,128)(2,1)S(1)} collective-permute-done((bf16[1,16,64,128]{3,2,1,0:T(8,128)(2,1)S(1)}, bf16[1,16,64,128]{3,2,1,0:T(8,128)(2,1)S(1)}, u32[]{:S(2)}, u32[]{:S(2)}) %collective-permute-start.9) | collective-permute-done | bytes 262176 | tf_op jit(solution)/shard_map/ppermute | solution.py:112
  70.1 0.4 fusion.28
  70.5 1.3 collective-permute-start.10
  71.8 0.0 copy-start.5
  71.8 1.3 fusion.7
  73.1 0.0 copy-start.4
  73.1 1.4 collective-permute-start.4
  74.6 6.2 %collective-permute-done.4 = f32[1,16]{1,0:T(1,128)S(1)} collective-permute-done((f32[1,16]{1,0:T(1,128)S(1)}, f32[1,16]{1,0:T(1,128)S(1)}, u32[]{:S(2)}, u32[]{:S(2)}) %collective-permute-start.4) | collective-permute-done | bytes 96 | tf_op jit(solution)/shard_map/ppermute | solution.py:112
  80.8 7.0 %collective-permute-done.10 = bf16[1,16,64,128]{3,2,1,0:T(8,128)(2,1)S(1)} collective-permute-done((bf16[1,16,64,128]{3,2,1,0:T(8,128)(2,1)S(1)}, bf16[1,16,64,128]{3,2,1,0:T(8,128)(2,1)S(1)}, u32[]{:S(2)}, u32[]{:S(2)}) %collective-permute-start.10) | collective-permute-done | bytes 262176 | tf_op jit(solution)/shard_map/ppermute | solution.py:112
  87.8 0.8 fusion.11
  88.6 0.3 copy.42
  89.0 0.4 multiply_reduce_fusion
  89.4 2.1 collective-permute-start.17
  91.5 0.4 collective-permute-start.16
  91.9 6.8 %collective-permute-start.15 = (f32[256]{0:T(256)S(1)}, f32[256]{0:T(256)S(1)}, u32[]{:S(2)}, u32[]{:S(2)}) collective-permute-start(f32[256]{0:T(256)S(1)} %multiply_reduce_fusion), channel_id=1, source_target_pairs={{0,5},{1,6},{2,7},{3,0},{4,1},{5,2},{6,3},{7,4},{8,13},{9,14},{10,... | collective-permute-start | bytes 3080 | tf_op jit(solution)/shard_map/ppermute | solution.py:120
  98.6 0.0 collective-permute-start.14
  98.6 3.0 %collective-permute-start.13 = (f32[256]{0:T(256)S(1)}, f32[256]{0:T(256)S(1)}, u32[]{:S(2)}, u32[]{:S(2)}) collective-permute-start(f32[256]{0:T(256)S(1)} %multiply_reduce_fusion), channel_id=1, source_target_pairs={{0,3},{1,4},{2,5},{3,6},{4,7},{5,0},{6,1},{7,2},{8,11},{9,12},{10,... | collective-permute-start | bytes 3080 | tf_op jit(solution)/shard_map/ppermute | solution.py:120
  101.7 0.0 collective-permute-done.17
  101.7 6.1 %collective-permute-start.12 = (f32[256]{0:T(256)S(1)}, f32[256]{0:T(256)S(1)}, u32[]{:S(2)}, u32[]{:S(2)}) collective-permute-start(f32[256]{0:T(256)S(1)} %multiply_reduce_fusion), channel_id=1, source_target_pairs={{0,2},{1,3},{2,4},{3,5},{4,6},{5,7},{6,0},{7,1},{8,10},{9,11},{10,... | collective-permute-start | bytes 3080 | tf_op jit(solution)/shard_map/ppermute | solution.py:120
  107.7 0.0 collective-permute-done.16
  107.7 0.0 collective-permute-start.11
  107.8 0.0 collective-permute-done.15
  107.8 0.0 collective-permute-done.13
  107.8 3.8 %collective-permute-done.12 = f32[256]{0:T(256)S(1)} collective-permute-done((f32[256]{0:T(256)S(1)}, f32[256]{0:T(256)S(1)}, u32[]{:S(2)}, u32[]{:S(2)}) %collective-permute-start.12) | collective-permute-done | bytes 1056 | tf_op jit(solution)/shard_map/ppermute | solution.py:120
  111.6 5.8 %collective-permute-done.11 = f32[256]{0:T(256)S(1)} collective-permute-done((f32[256]{0:T(256)S(1)}, f32[256]{0:T(256)S(1)}, u32[]{:S(2)}, u32[]{:S(2)}) %collective-permute-start.11) | collective-permute-done | bytes 1056 | tf_op jit(solution)/shard_map/ppermute | solution.py:120
  117.3 1.2 multiply_convert_fusion
  118.5 110.3 %shard_map.122 = bf16[256,1024]{1,0:T(8,128)(2,1)} custom-call(s32[1]{0:T(128)} %bitcast.pos_ref, bf16[256,1024]{1,0:T(8,128)(2,1)} %q_ref.1, bf16[32,2,256,128]{3,2,1,0:T(8,128)(2,1)} %bitcast.100), custom_call_target="tpu_custom_call" | custom-call | flops 8589934592 | bytes 5242880 | tf_op jit(solution)/shard_map/pallas_call | solution.py:96
  (23 shorter events, 0.2 us)
Async XLA Ops:
  7.2 38.0 %copy-start = (bf16[256,128]{1,0:T(8,128)(2,1)S(1)}, bf16[256,128]{1,0:T(8,128)(2,1)}, u32[]{:S(2)}) copy-start(bf16[256,128]{1,0:T(8,128)(2,1)} %param.17) | copy-start | bytes 196612
  7.2 38.0 %copy-start.2 = (bf16[256,128]{1,0:T(8,128)(2,1)S(1)}, bf16[256,128]{1,0:T(8,128)(2,1)}, u32[]{:S(2)}) copy-start(bf16[256,128]{1,0:T(8,128)(2,1)} %param.16) | copy-start | bytes 196612
  7.2 111.3 %all-gather.3.cloned.1.call-start = ((), (), s32[]{:S(2)}) async-start(), calls=%async_computation | async-start | bytes 4325376 | tf_op jit(solution)/shard_map/all_gather | solution.py:159
  10.2 61.6 %copy-start.3 = (f32[16,256]{1,0:T(8,128)S(1)}, f32[16,256]{1,0:T(8,128)}, u32[]{:S(2)}) copy-start(f32[16,256]{1,0:T(8,128)} %param.18) | copy-start | bytes 49156
  14.2 16.4 %collective-permute-start.6 = (bf16[1,16,64,128]{3,2,1,0:T(8,128)(2,1)S(1)}, bf16[1,16,64,128]{3,2,1,0:T(8,128)(2,1)S(1)}, u32[]{:S(2)}, u32[]{:S(2)}) collective-permute-start(bf16[1,16,64,128]{3,2,1,0:T(8,128)(2,1)S(1)} %fusion.12), channel_id=1, source_target_pairs={{0,8},{8,16},{16,24},{24,32},{32,40},{40,48},{48,56},{56,64},{64,7... | collective-permute-start | bytes 786440 | tf_op jit(solution)/shard_map/ppermute | solution.py:112
  16.1 14.5 %collective-permute-start.5 = (bf16[1,16,64,128]{3,2,1,0:T(8,128)(2,1)S(1)}, bf16[1,16,64,128]{3,2,1,0:T(8,128)(2,1)S(1)}, u32[]{:S(2)}, u32[]{:S(2)}) collective-permute-start(bf16[1,16,64,128]{3,2,1,0:T(8,128)(2,1)S(1)} %fusion.12), channel_id=1, source_target_pairs={{0,16},{8,24},{16,32},{24,40},{32,48},{40,56},{48,64},{56,72},{64,... | collective-permute-start | bytes 786440 | tf_op jit(solution)/shard_map/ppermute | solution.py:112
  17.4 13.2 %collective-permute-start = (f32[1,16]{1,0:T(1,128)S(1)}, f32[1,16]{1,0:T(1,128)S(1)}, u32[]{:S(2)}, u32[]{:S(2)}) collective-permute-start(f32[1,16]{1,0:T(1,128)S(1)} %bitcast.98), channel_id=1, source_target_pairs={{0,8},{8,16},{16,24},{24,32},{32,40},{40,48},{48,56},{56,64},{64,7... | collective-permute-start | bytes 200 | tf_op jit(solution)/shard_map/ppermute | solution.py:112
  19.3 11.3 %collective-permute-start.1 = (f32[1,16]{1,0:T(1,128)S(1)}, f32[1,16]{1,0:T(1,128)S(1)}, u32[]{:S(2)}, u32[]{:S(2)}) collective-permute-start(f32[1,16]{1,0:T(1,128)S(1)} %bitcast.99), channel_id=1, source_target_pairs={{0,16},{8,24},{16,32},{24,40},{32,48},{40,56},{48,64},{56,72},{64,... | collective-permute-start | bytes 200 | tf_op jit(solution)/shard_map/ppermute | solution.py:112
  30.8 12.8 %collective-permute-start.7 = (bf16[1,16,64,128]{3,2,1,0:T(8,128)(2,1)S(1)}, bf16[1,16,64,128]{3,2,1,0:T(8,128)(2,1)S(1)}, u32[]{:S(2)}, u32[]{:S(2)}) collective-permute-start(bf16[1,16,64,128]{3,2,1,0:T(8,128)(2,1)S(1)} %fusion.22), channel_id=1, source_target_pairs={{0,16},{8,24},{16,32},{24,40},{32,48},{40,56},{48,64},{56,72},{64,... | collective-permute-start | bytes 786440 | tf_op jit(solution)/shard_map/ppermute | solution.py:112
  32.1 13.3 %collective-permute-start.2 = (f32[1,16]{1,0:T(1,128)S(1)}, f32[1,16]{1,0:T(1,128)S(1)}, u32[]{:S(2)}, u32[]{:S(2)}) collective-permute-start(f32[1,16]{1,0:T(1,128)S(1)} %get-tuple-element.7), channel_id=1, source_target_pairs={{0,16},{8,24},{16,32},{24,40},{32,48},{40,56},{48,64},{56,72},{64,... | collective-permute-start | bytes 200 | tf_op jit(solution)/shard_map/ppermute | solution.py:112
  43.9 15.2 %collective-permute-start.8 = (bf16[1,16,64,128]{3,2,1,0:T(8,128)(2,1)S(1)}, bf16[1,16,64,128]{3,2,1,0:T(8,128)(2,1)S(1)}, u32[]{:S(2)}, u32[]{:S(2)}) collective-permute-start(bf16[1,16,64,128]{3,2,1,0:T(8,128)(2,1)S(1)} %fusion.29), channel_id=1, source_target_pairs={{0,32},{8,40},{16,48},{24,56},{32,64},{40,72},{48,80},{56,88},{64,... | collective-permute-start | bytes 786440 | tf_op jit(solution)/shard_map/ppermute | solution.py:112
  45.4 15.4 %collective-permute-start.3 = (f32[1,16]{1,0:T(1,128)S(1)}, f32[1,16]{1,0:T(1,128)S(1)}, u32[]{:S(2)}, u32[]{:S(2)}) collective-permute-start(f32[1,16]{1,0:T(1,128)S(1)} %get-tuple-element.5), channel_id=1, source_target_pairs={{0,32},{8,40},{16,48},{24,56},{32,64},{40,72},{48,80},{56,88},{64,... | collective-permute-start | bytes 200 | tf_op jit(solution)/shard_map/ppermute | solution.py:112
  59.4 10.7 %collective-permute-start.9 = (bf16[1,16,64,128]{3,2,1,0:T(8,128)(2,1)S(1)}, bf16[1,16,64,128]{3,2,1,0:T(8,128)(2,1)S(1)}, u32[]{:S(2)}, u32[]{:S(2)}) collective-permute-start(bf16[1,16,64,128]{3,2,1,0:T(8,128)(2,1)S(1)} %fusion.23), channel_id=1, source_target_pairs={{0,64},{8,72},{16,80},{24,88},{32,96},{40,104},{48,112},{56,120},{... | collective-permute-start | bytes 786440 | tf_op jit(solution)/shard_map/ppermute | solution.py:112
  70.5 17.3 %collective-permute-start.10 = (bf16[1,16,64,128]{3,2,1,0:T(8,128)(2,1)S(1)}, bf16[1,16,64,128]{3,2,1,0:T(8,128)(2,1)S(1)}, u32[]{:S(2)}, u32[]{:S(2)}) collective-permute-start(bf16[1,16,64,128]{3,2,1,0:T(8,128)(2,1)S(1)} %fusion.28), channel_id=1, source_target_pairs={{0,128},{8,136},{16,144},{24,152},{32,160},{40,168},{48,176},{56,1... | collective-permute-start | bytes 786440 | tf_op jit(solution)/shard_map/ppermute | solution.py:112
  71.8 16.0 %copy-start.5 = (f32[16]{0:T(128)S(1)}, f32[16]{0:T(128)}, u32[]{:S(2)}) copy-start(f32[16]{0:T(128)} %param.20) | copy-start | bytes 196
  73.1 15.8 %copy-start.1 = (bf16[256,1024]{1,0:T(8,128)(2,1)S(1)}, bf16[256,1024]{1,0:T(8,128)(2,1)}, u32[]{:S(2)}) copy-start(bf16[256,1024]{1,0:T(8,128)(2,1)} %param.15) | copy-start | bytes 1572868
  73.1 34.6 %copy-start.4 = (bf16[1024]{0:T(1024)(128)(2,1)S(1)}, bf16[1024]{0:T(1024)(128)(2,1)}, u32[]{:S(2)}) copy-start(bf16[1024]{0:T(1024)(128)(2,1)} %param.21) | copy-start | bytes 6148
  73.1 7.7 %collective-permute-start.4 = (f32[1,16]{1,0:T(1,128)S(1)}, f32[1,16]{1,0:T(1,128)S(1)}, u32[]{:S(2)}, u32[]{:S(2)}) collective-permute-start(f32[1,16]{1,0:T(1,128)S(1)} %get-tuple-element.3), channel_id=1, source_target_pairs={{0,64},{8,72},{16,80},{24,88},{32,96},{40,104},{48,112},{56,120},{... | collective-permute-start | bytes 200 | tf_op jit(solution)/shard_map/ppermute | solution.py:112
  89.4 12.3 %collective-permute-start.17 = (f32[256]{0:T(256)S(1)}, f32[256]{0:T(256)S(1)}, u32[]{:S(2)}, u32[]{:S(2)}) collective-permute-start(f32[256]{0:T(256)S(1)} %multiply_reduce_fusion), channel_id=1, source_target_pairs={{0,7},{1,0},{2,1},{3,2},{4,3},{5,4},{6,5},{7,6},{8,15},{9,8},{10,9... | collective-permute-start | bytes 3080 | tf_op jit(solution)/shard_map/ppermute | solution.py:120
  91.5 16.3 %collective-permute-start.16 = (f32[256]{0:T(256)S(1)}, f32[256]{0:T(256)S(1)}, u32[]{:S(2)}, u32[]{:S(2)}) collective-permute-start(f32[256]{0:T(256)S(1)} %multiply_reduce_fusion), channel_id=1, source_target_pairs={{0,6},{1,7},{2,0},{3,1},{4,2},{5,3},{6,4},{7,5},{8,14},{9,15},{10,... | collective-permute-start | bytes 3080 | tf_op jit(solution)/shard_map/ppermute | solution.py:120
  91.9 15.9 %collective-permute-start.15 = (f32[256]{0:T(256)S(1)}, f32[256]{0:T(256)S(1)}, u32[]{:S(2)}, u32[]{:S(2)}) collective-permute-start(f32[256]{0:T(256)S(1)} %multiply_reduce_fusion), channel_id=1, source_target_pairs={{0,5},{1,6},{2,7},{3,0},{4,1},{5,2},{6,3},{7,4},{8,13},{9,14},{10,... | collective-permute-start | bytes 3080 | tf_op jit(solution)/shard_map/ppermute | solution.py:120
  98.6 9.1 %collective-permute-start.14 = (f32[256]{0:T(256)S(1)}, f32[256]{0:T(256)S(1)}, u32[]{:S(2)}, u32[]{:S(2)}) collective-permute-start(f32[256]{0:T(256)S(1)} %multiply_reduce_fusion), channel_id=1, source_target_pairs={{0,4},{1,5},{2,6},{3,7},{4,0},{5,1},{6,2},{7,3},{8,12},{9,13},{10,... | collective-permute-start | bytes 3080 | tf_op jit(solution)/shard_map/ppermute | solution.py:120
  98.6 9.1 %collective-permute-start.13 = (f32[256]{0:T(256)S(1)}, f32[256]{0:T(256)S(1)}, u32[]{:S(2)}, u32[]{:S(2)}) collective-permute-start(f32[256]{0:T(256)S(1)} %multiply_reduce_fusion), channel_id=1, source_target_pairs={{0,3},{1,4},{2,5},{3,6},{4,7},{5,0},{6,1},{7,2},{8,11},{9,12},{10,... | collective-permute-start | bytes 3080 | tf_op jit(solution)/shard_map/ppermute | solution.py:120
  101.7 9.9 %collective-permute-start.12 = (f32[256]{0:T(256)S(1)}, f32[256]{0:T(256)S(1)}, u32[]{:S(2)}, u32[]{:S(2)}) collective-permute-start(f32[256]{0:T(256)S(1)} %multiply_reduce_fusion), channel_id=1, source_target_pairs={{0,2},{1,3},{2,4},{3,5},{4,6},{5,7},{6,0},{7,1},{8,10},{9,11},{10,... | collective-permute-start | bytes 3080 | tf_op jit(solution)/shard_map/ppermute | solution.py:120
  107.7 9.6 %collective-permute-start.11 = (f32[256]{0:T(256)S(1)}, f32[256]{0:T(256)S(1)}, u32[]{:S(2)}, u32[]{:S(2)}) collective-permute-start(f32[256]{0:T(256)S(1)} %multiply_reduce_fusion), channel_id=1, source_target_pairs={{0,1},{1,2},{2,3},{3,4},{4,5},{5,6},{6,7},{7,0},{8,9},{9,10},{10,1... | collective-permute-start | bytes 3080 | tf_op jit(solution)/shard_map/ppermute | solution.py:120
Sparse Core Ops, SparseCore 0:
  10.5 79.0 all-gather.2

commit v3 on v2

--- a/solution.py
+++ b/solution.py
@@ -16,94 +16,66 @@
 causal_score = -1e30
 
 
-def attend_kernel(pos_ref, q_ref, kv_ref, o_ref, m_sc, l_sc, acc_sc, *, heads, width):
-    key_block = pl.program_id(0)
+def attend_kernel(pos_ref, qt_ref, kv_ref, o_ref, p_sc, m_sc, l_sc, c_sc, acc_sc, *, tok, width, chunk):
     position = pos_ref[0]
     score_factor = width ** (-0.5)
+    rows = qt_ref.shape[1]
+    block_rows = kv_ref.shape[2]
+    m_sc[...] = jnp.full(m_sc.shape, causal_score, jnp.float32)
+    l_sc[...] = jnp.zeros(l_sc.shape, jnp.float32)
+    acc_sc[...] = jnp.zeros(acc_sc.shape, jnp.float32)
 
-    @pl.when(key_block == 0)
-    def _init():
-        m_sc[...] = jnp.full(m_sc.shape, causal_score, jnp.float32)
-        l_sc[...] = jnp.zeros(l_sc.shape, jnp.float32)
-        acc_sc[...] = jnp.zeros(acc_sc.shape, jnp.float32)
-
-    def run_block(masked):
-        key_portion = kv_ref[0]
-        value_portion = kv_ref[1]
-        rows = q_ref.shape[0]
-        if masked:
-            query_idx = lax.broadcasted_iota(jnp.int32, (rows, key_portion.shape[0]), 0)
-            key_idx = lax.broadcasted_iota(jnp.int32, (rows, key_portion.shape[0]), 1)
-            is_valid = key_idx <= query_idx
-        for h in range(heads):
-            query_rows = q_ref[:, h * width:(h + 1) * width]
-            score_matrix = (
-                lax.dot_general(
-                    query_rows,
-                    key_portion,
-                    (((1,), (1,)), ((), ())),
-                    preferred_element_type=jnp.float32,
-                )
-                * score_factor
-            )
+    def run_block(kb, masked):
+        key_portion = kv_ref[kb, 0]
+        for c in range(rows // chunk):
+            r0 = c * chunk
+            score_t = jnp.dot(key_portion, qt_ref[:, r0:r0 + chunk],
+                              preferred_element_type=jnp.float32) * score_factor
             if masked:
-                score_matrix = jnp.where(is_valid, score_matrix, causal_score)
-            run_max = m_sc[h]
-            new_max = jnp.maximum(run_max, jnp.max(score_matrix, axis=-1, keepdims=True))
-            weights = jnp.exp(score_matrix - new_max)
+                key_idx = lax.broadcasted_iota(jnp.int32, (block_rows, chunk), 0)
+                query_idx = (r0 % tok) + lax.broadcasted_iota(jnp.int32, (block_rows, chunk), 1)
+                is_valid = key_idx <= query_idx
+                score_t = jnp.where(is_valid, score_t, causal_score)
+            run_max = m_sc[:, r0:r0 + chunk]
+            new_max = jnp.maximum(run_max, jnp.max(score_t, axis=0, keepdims=True))
+            weights = jnp.exp(score_t - new_max)
             if masked:
                 weights = jnp.where(is_valid, weights, 0.0)
             correction_factor = jnp.exp(run_max - new_max)
-            l_sc[h] = l_sc[h] * correction_factor + jnp.sum(weights, axis=-1, keepdims=True)
-            acc_sc[h] = acc_sc[h] * correction_factor + jnp.dot(
-                weights.astype(jnp.bfloat16), value_portion, preferred_element_type=jnp.float32
-            )
-            m_sc[h] = new_max
+            l_sc[:, r0:r0 + chunk] = l_sc[:, r0:r0 + chunk] * correction_factor + jnp.sum(weights, axis=0, keepdims=True)
+            m_sc[:, r0:r0 + chunk] = new_max
+            c_sc[:, r0:r0 + chunk] = correction_factor
+            p_sc[:, r0:r0 + chunk] = weights.astype(jnp.bfloat16)
+        acc_sc[...] = acc_sc[...] * c_sc[...] + lax.dot_general(kv_ref[kb, 1], p_sc[...], (((0,), (0,)), ((), ())), preferred_element_type=jnp.float32)
 
-    @pl.when(key_block < position)
-    def _full():
-        run_block(False)
-
-    @pl.when(key_block == position)
-    def _diagonal():
-        run_block(True)
-        for h in range(heads):
-            o_ref[:, h * width:(h + 1) * width] = (acc_sc[h] / l_sc[h]).astype(o_ref.dtype)
+    def body(kb, carry):
+        run_block(kb, False)
+        return carry
+    lax.fori_loop(0, position, body, 0)
+    run_block(position, True)
+    o_ref[...] = (acc_sc[...] / l_sc[...]).astype(o_ref.dtype)
 
 
-def causal_attention(position, queries, gathered_kv):
+def causal_attention(position, queries, gathered_kv, chunk=256):
     blocks, _, tok_rows, width = gathered_kv.shape
     heads = queries.shape[1] // width
-    kernel = functools.partial(attend_kernel, heads=heads, width=width)
-    grid_spec = pltpu.PrefetchScalarGridSpec(
-        num_scalar_prefetch=1,
-        grid=(blocks,),
-        in_specs=[
-            pl.BlockSpec(queries.shape, lambda kb, pos: (0, 0)),
-            pl.BlockSpec(
-                (None, 2, tok_rows, width),
-                lambda kb, pos: (jnp.minimum(kb, pos[0]), 0, 0, 0),
-            ),
+    rows = heads * tok_rows
+    queries_t = queries.reshape(tok_rows, heads, width).transpose(2, 1, 0).reshape(width, rows)
+    kernel = functools.partial(attend_kernel, tok=tok_rows, width=width, chunk=chunk)
+    out_t = pl.pallas_call(
+        kernel,
+        in_specs=[pl.BlockSpec(memory_space=pltpu.SMEM)] + [pl.BlockSpec(memory_space=pltpu.VMEM)] * 2,
+        out_specs=pl.BlockSpec(memory_space=pltpu.VMEM),
+        out_shape=jax.ShapeDtypeStruct((width, rows), queries.dtype),
+        scratch_shapes=[
+            pltpu.VMEM((tok_rows, rows), jnp.bfloat16),
+            pltpu.VMEM((1, rows), jnp.float32),
+            pltpu.VMEM((1, rows), jnp.float32),
+            pltpu.VMEM((1, rows), jnp.float32),
+            pltpu.VMEM((width, rows), jnp.float32),
         ],
-        out_specs=pl.BlockSpec(queries.shape, lambda kb, pos: (0, 0)),
-        scratch_shapes=[
-            pltpu.VMEM((heads, tok_rows, 1), jnp.float32),
-            pltpu.VMEM((heads, tok_rows, 1), jnp.float32),
-            pltpu.VMEM((heads, tok_rows, width), jnp.float32),
-        ],
-    )
-    flops = 4 * queries.shape[0] * queries.shape[1] * tok_rows * blocks
-    return pl.pallas_call(
-        kernel,
-        grid_spec=grid_spec,
-        out_shape=jax.ShapeDtypeStruct(queries.shape, queries.dtype),
-        compiler_params=pltpu.CompilerParams(dimension_semantics=("arbitrary",)),
-        cost_estimate=pl.CostEstimate(
-            flops=flops,
-            transcendentals=heads * queries.shape[0] * tok_rows * blocks,
-            bytes_accessed=2 * queries.size * 2 + gathered_kv.size * 2,
-        ),
-    )(position.reshape(1), queries, gathered_kv)
+    )(position.reshape(1), queries_t, gathered_kv)
+    return out_t.reshape(width, heads, tok_rows).transpose(2, 1, 0).reshape(tok_rows, heads * width)
 
 
 def shifted(block, axis, distance):

time: 236 us -> 168 us (0.71)
  Pallas kernels: 110 us -> 39.5 us
  local copies, waits for them, and re-layouts: 2.98 us -> 7.17 us
    pallas_call x1, Pallas kernels: 110 us -> 39.5 us  [causal_attention(): pl.pallas_call(kernel, in_specs=[pl.BlockSpec(memory_space=pltpu.SMEM)] +...]
    unnamed x14 -> x20, local copies, waits for them, and re-layouts: 1.29 us -> 4.34 us
  transfers between devices with their start and end apart: 19 -> 19, of which waited for: 8 -> 8; matrix products, arithmetic and copies ran while one was open for 5% -> 7% of each run, Pallas kernels for 0% -> 0%
where the time goes in v3:
time: 168 us; the launch traced here: 167 us
  waiting for transfers between devices  62.8 us (37%)
  Pallas kernels  39.5 us (24%)
  starting transfers between devices  34.3 us (20%)
  between operations  14.4 us (9%)
  local copies, waits for them, and re-layouts  7.17 us (4%)
  other arithmetic  5.87 us (3%)
  matrix products  3.4 us (2%)
    ppermute x11, waiting for transfers between devices, shifted(): return lax.ppermute(block, axis, route)  54.8 us
    pallas_call x1, Pallas kernels, causal_attention(): pl.pallas_call(kernel, in_specs=[pl.BlockSpec(memory_space=pltpu.SMEM)] +...  39.5 us
    ppermute x7, starting transfers between devices, summed_over(): total = total + lax.ppermute(part, axis, route)  18.6 us
    ppermute x11, starting transfers between devices, shifted(): return lax.ppermute(block, axis, route)  15.6 us
    ppermute x7, waiting for transfers between devices, summed_over(): total = total + lax.ppermute(part, axis, route)  7.97 us
    unnamed x20, local copies, waits for them, and re-layouts  4.34 us
  transfers between devices with their start and end apart: 19, of which 8 were waited for; matrix products, arithmetic and copies ran while one was open for 7% of the time, Pallas kernels for 0%

profile of v3, /device:TPU:230, one launch (start us, length us, event | category | flops | bytes accessed | tf_op | source)
XLA Modules:
  0.0 167.4 jit_solution(153710224011147206)
XLA Ops:
  7.2 0.0 copy-start
  7.2 0.0 copy-start.3
  7.2 0.0 all-gather.3.cloned.1.call-start
  7.2 1.5 pad_maximum_fusion
  8.8 0.0 all-gather.3.cloned.1.call-update
  8.8 0.7 reshape.211
  9.6 0.6 reduce-window.6
  10.2 0.0 copy-start.4
  10.2 1.2 copy.47
  11.4 0.2 slice_reduce_fusion
  11.6 0.1 copy.46
  11.7 0.1 broadcast.73
  11.9 0.3 slice_reduce_fusion.1
  12.1 0.8 multiply_bitcast_fusion
  12.9 0.1 fusion.17
  13.0 1.1 fusion.12
  14.2 1.9 %collective-permute-start.6 = (bf16[1,16,64,128]{3,2,1,0:T(8,128)(2,1)S(1)}, bf16[1,16,64,128]{3,2,1,0:T(8,128)(2,1)S(1)}, u32[]{:S(2)}, u32[]{:S(2)}) collective-permute-start(bf16[1,16,64,128]{3,2,1,0:T(8,128)(2,1)S(1)} %fusion.12), channel_id=1, source_target_pairs={{0,8},{8,16},{16,24},{24,32},{32,40},{40,48},{48,56},{56,64},{64,7... | collective-permute-start | bytes 786440 | tf_op jit(solution)/shard_map/ppermute | solution.py:84
  16.1 1.3 collective-permute-start.5
  17.4 1.9 %collective-permute-start = (f32[1,16]{1,0:T(1,128)S(1)}, f32[1,16]{1,0:T(1,128)S(1)}, u32[]{:S(2)}, u32[]{:S(2)}) collective-permute-start(f32[1,16]{1,0:T(1,128)S(1)} %bitcast.120), channel_id=1, source_target_pairs={{0,8},{8,16},{16,24},{24,32},{32,40},{40,48},{48,56},{56,64},{64,7... | collective-permute-start | bytes 200 | tf_op jit(solution)/shard_map/ppermute | solution.py:84
  19.3 1.3 collective-permute-start.1
  20.6 10.5 %collective-permute-done = f32[1,16]{1,0:T(1,128)S(1)} collective-permute-done((f32[1,16]{1,0:T(1,128)S(1)}, f32[1,16]{1,0:T(1,128)S(1)}, u32[]{:S(2)}, u32[]{:S(2)}) %collective-permute-start) | collective-permute-done | bytes 96 | tf_op jit(solution)/shard_map/ppermute | solution.py:84
  31.2 0.0 collective-permute-done.1
  31.2 0.0 collective-permute-done.5
  31.2 0.2 fusion.22
  31.4 1.3 collective-permute-start.7
  32.7 1.3 collective-permute-start.2
  34.0 10.0 %collective-permute-done.7 = bf16[1,16,64,128]{3,2,1,0:T(8,128)(2,1)S(1)} collective-permute-done((bf16[1,16,64,128]{3,2,1,0:T(8,128)(2,1)S(1)}, bf16[1,16,64,128]{3,2,1,0:T(8,128)(2,1)S(1)}, u32[]{:S(2)}, u32[]{:S(2)}) %collective-permute-start.7) | collective-permute-done | bytes 262176 | tf_op jit(solution)/shard_map/ppermute | solution.py:84
  44.0 0.3 fusion.29
  44.2 1.3 collective-permute-start.8
  45.6 0.2 fusion.30
  45.8 1.3 collective-permute-start.3
  47.1 12.0 %collective-permute-done.8 = bf16[1,16,64,128]{3,2,1,0:T(8,128)(2,1)S(1)} collective-permute-done((bf16[1,16,64,128]{3,2,1,0:T(8,128)(2,1)S(1)}, bf16[1,16,64,128]{3,2,1,0:T(8,128)(2,1)S(1)}, u32[]{:S(2)}, u32[]{:S(2)}) %collective-permute-start.8) | collective-permute-done | bytes 262176 | tf_op jit(solution)/shard_map/ppermute | solution.py:84
  59.0 0.3 fusion.23
  59.4 1.3 collective-permute-start.9
  60.7 8.2 %collective-permute-done.9 = bf16[1,16,64,128]{3,2,1,0:T(8,128)(2,1)S(1)} collective-permute-done((bf16[1,16,64,128]{3,2,1,0:T(8,128)(2,1)S(1)}, bf16[1,16,64,128]{3,2,1,0:T(8,128)(2,1)S(1)}, u32[]{:S(2)}, u32[]{:S(2)}) %collective-permute-start.9) | collective-permute-done | bytes 262176 | tf_op jit(solution)/shard_map/ppermute | solution.py:84
  68.9 0.4 fusion.28
  69.3 1.3 collective-permute-start.10
  70.6 0.0 copy-start.6
  70.6 1.3 fusion.7
  71.9 0.0 copy-start.2
  71.9 1.4 collective-permute-start.4
  73.3 6.7 %collective-permute-done.4 = f32[1,16]{1,0:T(1,128)S(1)} collective-permute-done((f32[1,16]{1,0:T(1,128)S(1)}, f32[1,16]{1,0:T(1,128)S(1)}, u32[]{:S(2)}, u32[]{:S(2)}) %collective-permute-start.4) | collective-permute-done | bytes 96 | tf_op jit(solution)/shard_map/ppermute | solution.py:84
  80.0 7.4 %collective-permute-done.10 = bf16[1,16,64,128]{3,2,1,0:T(8,128)(2,1)S(1)} collective-permute-done((bf16[1,16,64,128]{3,2,1,0:T(8,128)(2,1)S(1)}, bf16[1,16,64,128]{3,2,1,0:T(8,128)(2,1)S(1)}, u32[]{:S(2)}, u32[]{:S(2)}) %collective-permute-start.10) | collective-permute-done | bytes 262176 | tf_op jit(solution)/shard_map/ppermute | solution.py:84
  87.4 0.8 fusion.11
  88.3 0.0 copy-start.5
  88.3 0.3 copy.50
  88.6 0.4 multiply_reduce_fusion
  89.0 2.4 %collective-permute-start.17 = (f32[256]{0:T(256)S(1)}, f32[256]{0:T(256)S(1)}, u32[]{:S(2)}, u32[]{:S(2)}) collective-permute-start(f32[256]{0:T(256)S(1)} %multiply_reduce_fusion), channel_id=1, source_target_pairs={{0,7},{1,0},{2,1},{3,2},{4,3},{5,4},{6,5},{7,6},{8,15},{9,8},{10,9... | collective-permute-start | bytes 3080 | tf_op jit(solution)/shard_map/ppermute | solution.py:92
  91.5 0.6 collective-permute-start.16
  92.1 6.6 %collective-permute-start.15 = (f32[256]{0:T(256)S(1)}, f32[256]{0:T(256)S(1)}, u32[]{:S(2)}, u32[]{:S(2)}) collective-permute-start(f32[256]{0:T(256)S(1)} %multiply_reduce_fusion), channel_id=1, source_target_pairs={{0,5},{1,6},{2,7},{3,0},{4,1},{5,2},{6,3},{7,4},{8,13},{9,14},{10,... | collective-permute-start | bytes 3080 | tf_op jit(solution)/shard_map/ppermute | solution.py:92
  98.7 0.1 collective-permute-start.14
  98.8 2.6 %collective-permute-start.13 = (f32[256]{0:T(256)S(1)}, f32[256]{0:T(256)S(1)}, u32[]{:S(2)}, u32[]{:S(2)}) collective-permute-start(f32[256]{0:T(256)S(1)} %multiply_reduce_fusion), channel_id=1, source_target_pairs={{0,3},{1,4},{2,5},{3,6},{4,7},{5,0},{6,1},{7,2},{8,11},{9,12},{10,... | collective-permute-start | bytes 3080 | tf_op jit(solution)/shard_map/ppermute | solution.py:92
  101.5 6.2 %collective-permute-start.12 = (f32[256]{0:T(256)S(1)}, f32[256]{0:T(256)S(1)}, u32[]{:S(2)}, u32[]{:S(2)}) collective-permute-start(f32[256]{0:T(256)S(1)} %multiply_reduce_fusion), channel_id=1, source_target_pairs={{0,2},{1,3},{2,4},{3,5},{4,6},{5,7},{6,0},{7,1},{8,10},{9,11},{10,... | collective-permute-start | bytes 3080 | tf_op jit(solution)/shard_map/ppermute | solution.py:92
  107.7 0.0 collective-permute-start.11
  107.7 0.1 copy.52
  107.8 0.6 copy.42
  108.4 0.9 copy.53
  109.3 2.0 %collective-permute-done.12 = f32[256]{0:T(256)S(1)} collective-permute-done((f32[256]{0:T(256)S(1)}, f32[256]{0:T(256)S(1)}, u32[]{:S(2)}, u32[]{:S(2)}) %collective-permute-start.12) | collective-permute-done | bytes 1056 | tf_op jit(solution)/shard_map/ppermute | solution.py:92
  111.3 5.9 %collective-permute-done.11 = f32[256]{0:T(256)S(1)} collective-permute-done((f32[256]{0:T(256)S(1)}, f32[256]{0:T(256)S(1)}, u32[]{:S(2)}, u32[]{:S(2)}) %collective-permute-start.11) | collective-permute-done | bytes 1056 | tf_op jit(solution)/shard_map/ppermute | solution.py:92
  117.3 1.2 multiply_convert_fusion
  118.5 39.5 %shard_map.122 = bf16[128,2048]{1,0:T(8,128)(2,1)} custom-call(s32[1]{0:T(128)} %bitcast.pos_ref, bf16[128,2048]{1,0:T(8,128)(2,1)} %bitcast.108, bf16[32,2,256,128]{3,2,1,0:T(8,128)(2,1)} %bitcast.102), custom_call_target="tpu_custom_call" | custom-call | tf_op jit(solution)/shard_map/pallas_call | solution.py:65
  158.0 1.1 copy.54
  159.1 0.6 copy.43
  159.7 0.9 copy.64
  (31 shorter events, 0.2 us)
Async XLA Ops:
  7.2 38.4 %copy-start = (bf16[256,128]{1,0:T(8,128)(2,1)S(1)}, bf16[256,128]{1,0:T(8,128)(2,1)}, u32[]{:S(2)}) copy-start(bf16[256,128]{1,0:T(8,128)(2,1)} %param.17) | copy-start | bytes 196612
  7.2 38.4 %copy-start.3 = (bf16[256,128]{1,0:T(8,128)(2,1)S(1)}, bf16[256,128]{1,0:T(8,128)(2,1)}, u32[]{:S(2)}) copy-start(bf16[256,128]{1,0:T(8,128)(2,1)} %param.16) | copy-start | bytes 196612
  7.2 111.3 %all-gather.3.cloned.1.call-start = ((), (), s32[]{:S(2)}) async-start(), calls=%async_computation | async-start | bytes 4325376 | tf_op jit(solution)/shard_map/all_gather | solution.py:131
  10.2 60.4 %copy-start.4 = (f32[16,256]{1,0:T(8,128)S(1)}, f32[16,256]{1,0:T(8,128)}, u32[]{:S(2)}) copy-start(f32[16,256]{1,0:T(8,128)} %param.18) | copy-start | bytes 49156
  14.2 17.0 %collective-permute-start.6 = (bf16[1,16,64,128]{3,2,1,0:T(8,128)(2,1)S(1)}, bf16[1,16,64,128]{3,2,1,0:T(8,128)(2,1)S(1)}, u32[]{:S(2)}, u32[]{:S(2)}) collective-permute-start(bf16[1,16,64,128]{3,2,1,0:T(8,128)(2,1)S(1)} %fusion.12), channel_id=1, source_target_pairs={{0,8},{8,16},{16,24},{24,32},{32,40},{40,48},{48,56},{56,64},{64,7... | collective-permute-start | bytes 786440 | tf_op jit(solution)/shard_map/ppermute | solution.py:84
  16.1 15.1 %collective-permute-start.5 = (bf16[1,16,64,128]{3,2,1,0:T(8,128)(2,1)S(1)}, bf16[1,16,64,128]{3,2,1,0:T(8,128)(2,1)S(1)}, u32[]{:S(2)}, u32[]{:S(2)}) collective-permute-start(bf16[1,16,64,128]{3,2,1,0:T(8,128)(2,1)S(1)} %fusion.12), channel_id=1, source_target_pairs={{0,16},{8,24},{16,32},{24,40},{32,48},{40,56},{48,64},{56,72},{64,... | collective-permute-start | bytes 786440 | tf_op jit(solution)/shard_map/ppermute | solution.py:84
  17.4 13.7 %collective-permute-start = (f32[1,16]{1,0:T(1,128)S(1)}, f32[1,16]{1,0:T(1,128)S(1)}, u32[]{:S(2)}, u32[]{:S(2)}) collective-permute-start(f32[1,16]{1,0:T(1,128)S(1)} %bitcast.120), channel_id=1, source_target_pairs={{0,8},{8,16},{16,24},{24,32},{32,40},{40,48},{48,56},{56,64},{64,7... | collective-permute-start | bytes 200 | tf_op jit(solution)/shard_map/ppermute | solution.py:84
  19.3 11.8 %collective-permute-start.1 = (f32[1,16]{1,0:T(1,128)S(1)}, f32[1,16]{1,0:T(1,128)S(1)}, u32[]{:S(2)}, u32[]{:S(2)}) collective-permute-start(f32[1,16]{1,0:T(1,128)S(1)} %bitcast.121), channel_id=1, source_target_pairs={{0,16},{8,24},{16,32},{24,40},{32,48},{40,56},{48,64},{56,72},{64,... | collective-permute-start | bytes 200 | tf_op jit(solution)/shard_map/ppermute | solution.py:84
  31.4 12.6 %collective-permute-start.7 = (bf16[1,16,64,128]{3,2,1,0:T(8,128)(2,1)S(1)}, bf16[1,16,64,128]{3,2,1,0:T(8,128)(2,1)S(1)}, u32[]{:S(2)}, u32[]{:S(2)}) collective-permute-start(bf16[1,16,64,128]{3,2,1,0:T(8,128)(2,1)S(1)} %fusion.22), channel_id=1, source_target_pairs={{0,16},{8,24},{16,32},{24,40},{32,48},{40,56},{48,64},{56,72},{64,... | collective-permute-start | bytes 786440 | tf_op jit(solution)/shard_map/ppermute | solution.py:84
  32.7 13.1 %collective-permute-start.2 = (f32[1,16]{1,0:T(1,128)S(1)}, f32[1,16]{1,0:T(1,128)S(1)}, u32[]{:S(2)}, u32[]{:S(2)}) collective-permute-start(f32[1,16]{1,0:T(1,128)S(1)} %get-tuple-element.7), channel_id=1, source_target_pairs={{0,16},{8,24},{16,32},{24,40},{32,48},{40,56},{48,64},{56,72},{64,... | collective-permute-start | bytes 200 | tf_op jit(solution)/shard_map/ppermute | solution.py:84
  44.2 14.8 %collective-permute-start.8 = (bf16[1,16,64,128]{3,2,1,0:T(8,128)(2,1)S(1)}, bf16[1,16,64,128]{3,2,1,0:T(8,128)(2,1)S(1)}, u32[]{:S(2)}, u32[]{:S(2)}) collective-permute-start(bf16[1,16,64,128]{3,2,1,0:T(8,128)(2,1)S(1)} %fusion.29), channel_id=1, source_target_pairs={{0,32},{8,40},{16,48},{24,56},{32,64},{40,72},{48,80},{56,88},{64,... | collective-permute-start | bytes 786440 | tf_op jit(solution)/shard_map/ppermute | solution.py:84
  45.8 14.9 %collective-permute-start.3 = (f32[1,16]{1,0:T(1,128)S(1)}, f32[1,16]{1,0:T(1,128)S(1)}, u32[]{:S(2)}, u32[]{:S(2)}) collective-permute-start(f32[1,16]{1,0:T(1,128)S(1)} %get-tuple-element.5), channel_id=1, source_target_pairs={{0,32},{8,40},{16,48},{24,56},{32,64},{40,72},{48,80},{56,88},{64,... | collective-permute-start | bytes 200 | tf_op jit(solution)/shard_map/ppermute | solution.py:84
  59.4 9.5 %collective-permute-start.9 = (bf16[1,16,64,128]{3,2,1,0:T(8,128)(2,1)S(1)}, bf16[1,16,64,128]{3,2,1,0:T(8,128)(2,1)S(1)}, u32[]{:S(2)}, u32[]{:S(2)}) collective-permute-start(bf16[1,16,64,128]{3,2,1,0:T(8,128)(2,1)S(1)} %fusion.23), channel_id=1, source_target_pairs={{0,64},{8,72},{16,80},{24,88},{32,96},{40,104},{48,112},{56,120},{... | collective-permute-start | bytes 786440 | tf_op jit(solution)/shard_map/ppermute | solution.py:84
  69.3 18.2 %collective-permute-start.10 = (bf16[1,16,64,128]{3,2,1,0:T(8,128)(2,1)S(1)}, bf16[1,16,64,128]{3,2,1,0:T(8,128)(2,1)S(1)}, u32[]{:S(2)}, u32[]{:S(2)}) collective-permute-start(bf16[1,16,64,128]{3,2,1,0:T(8,128)(2,1)S(1)} %fusion.28), channel_id=1, source_target_pairs={{0,128},{8,136},{16,144},{24,152},{32,160},{40,168},{48,176},{56,1... | collective-permute-start | bytes 786440 | tf_op jit(solution)/shard_map/ppermute | solution.py:84
  70.6 16.9 %copy-start.6 = (f32[16]{0:T(128)S(1)}, f32[16]{0:T(128)}, u32[]{:S(2)}) copy-start(f32[16]{0:T(128)} %param.20) | copy-start | bytes 196
  71.9 16.8 %copy-start.1 = (bf16[256,1024]{1,0:T(8,128)(2,1)S(1)}, bf16[256,1024]{1,0:T(8,128)(2,1)}, u32[]{:S(2)}) copy-start(bf16[256,1024]{1,0:T(8,128)(2,1)} %param.15) | copy-start | bytes 1572868
  71.9 35.8 %copy-start.2 = (bf16[256,1024]{1,0:T(8,128)(2,1)S(1)}, bf16[256,1024]{1,0:T(8,128)(2,1)}, u32[]{:S(2)}) copy-start(bf16[256,1024]{1,0:T(8,128)(2,1)} %param.11) | copy-start | bytes 1572868
  71.9 8.1 %collective-permute-start.4 = (f32[1,16]{1,0:T(1,128)S(1)}, f32[1,16]{1,0:T(1,128)S(1)}, u32[]{:S(2)}, u32[]{:S(2)}) collective-permute-start(f32[1,16]{1,0:T(1,128)S(1)} %get-tuple-element.3), channel_id=1, source_target_pairs={{0,64},{8,72},{16,80},{24,88},{32,96},{40,104},{48,112},{56,120},{... | collective-permute-start | bytes 200 | tf_op jit(solution)/shard_map/ppermute | solution.py:84
  88.3 21.0 %copy-start.5 = (bf16[1024]{0:T(1024)(128)(2,1)S(1)}, bf16[1024]{0:T(1024)(128)(2,1)}, u32[]{:S(2)}) copy-start(bf16[1024]{0:T(1024)(128)(2,1)} %param.21) | copy-start | bytes 6148
  89.0 12.4 %collective-permute-start.17 = (f32[256]{0:T(256)S(1)}, f32[256]{0:T(256)S(1)}, u32[]{:S(2)}, u32[]{:S(2)}) collective-permute-start(f32[256]{0:T(256)S(1)} %multiply_reduce_fusion), channel_id=1, source_target_pairs={{0,7},{1,0},{2,1},{3,2},{4,3},{5,4},{6,5},{7,6},{8,15},{9,8},{10,9... | collective-permute-start | bytes 3080 | tf_op jit(solution)/shard_map/ppermute | solution.py:92
  91.5 16.2 %collective-permute-start.16 = (f32[256]{0:T(256)S(1)}, f32[256]{0:T(256)S(1)}, u32[]{:S(2)}, u32[]{:S(2)}) collective-permute-start(f32[256]{0:T(256)S(1)} %multiply_reduce_fusion), channel_id=1, source_target_pairs={{0,6},{1,7},{2,0},{3,1},{4,2},{5,3},{6,4},{7,5},{8,14},{9,15},{10,... | collective-permute-start | bytes 3080 | tf_op jit(solution)/shard_map/ppermute | solution.py:92
  92.1 17.2 %collective-permute-start.15 = (f32[256]{0:T(256)S(1)}, f32[256]{0:T(256)S(1)}, u32[]{:S(2)}, u32[]{:S(2)}) collective-permute-start(f32[256]{0:T(256)S(1)} %multiply_reduce_fusion), channel_id=1, source_target_pairs={{0,5},{1,6},{2,7},{3,0},{4,1},{5,2},{6,3},{7,4},{8,13},{9,14},{10,... | collective-permute-start | bytes 3080 | tf_op jit(solution)/shard_map/ppermute | solution.py:92
  98.7 10.6 %collective-permute-start.14 = (f32[256]{0:T(256)S(1)}, f32[256]{0:T(256)S(1)}, u32[]{:S(2)}, u32[]{:S(2)}) collective-permute-start(f32[256]{0:T(256)S(1)} %multiply_reduce_fusion), channel_id=1, source_target_pairs={{0,4},{1,5},{2,6},{3,7},{4,0},{5,1},{6,2},{7,3},{8,12},{9,13},{10,... | collective-permute-start | bytes 3080 | tf_op jit(solution)/shard_map/ppermute | solution.py:92
  98.8 10.5 %collective-permute-start.13 = (f32[256]{0:T(256)S(1)}, f32[256]{0:T(256)S(1)}, u32[]{:S(2)}, u32[]{:S(2)}) collective-permute-start(f32[256]{0:T(256)S(1)} %multiply_reduce_fusion), channel_id=1, source_target_pairs={{0,3},{1,4},{2,5},{3,6},{4,7},{5,0},{6,1},{7,2},{8,11},{9,12},{10,... | collective-permute-start | bytes 3080 | tf_op jit(solution)/shard_map/ppermute | solution.py:92
  101.5 9.9 %collective-permute-start.12 = (f32[256]{0:T(256)S(1)}, f32[256]{0:T(256)S(1)}, u32[]{:S(2)}, u32[]{:S(2)}) collective-permute-start(f32[256]{0:T(256)S(1)} %multiply_reduce_fusion), channel_id=1, source_target_pairs={{0,2},{1,3},{2,4},{3,5},{4,6},{5,7},{6,0},{7,1},{8,10},{9,11},{10,... | collective-permute-start | bytes 3080 | tf_op jit(solution)/shard_map/ppermute | solution.py:92
  107.7 9.6 %collective-permute-start.11 = (f32[256]{0:T(256)S(1)}, f32[256]{0:T(256)S(1)}, u32[]{:S(2)}, u32[]{:S(2)}) collective-permute-start(f32[256]{0:T(256)S(1)} %multiply_reduce_fusion), channel_id=1, source_target_pairs={{0,1},{1,2},{2,3},{3,4},{4,5},{5,6},{6,7},{7,0},{8,9},{9,10},{10,1... | collective-permute-start | bytes 3080 | tf_op jit(solution)/shard_map/ppermute | solution.py:92
Sparse Core Ops, SparseCore 0:
  9.9 82.3 all-gather.2

commit v4 on v3

--- a/solution.py
+++ b/solution.py
@@ -87,24 +87,46 @@
 def summed_over(part, axis):
     count = lax.axis_size(axis)
     total = part
-    for distance in range(1, count):
-        route = [(i, (i + distance) % count) for i in range(count)]
-        total = total + lax.ppermute(part, axis, route)
+    distance = 1
+    while distance < count:
+        route = [(i, i ^ distance) for i in range(count)]
+        total = total + lax.ppermute(total, axis, route)
+        distance *= 2
     return total
 
 
+def packed(state, log_span):
+    heads = log_span.shape[-1]
+    lanes = state.shape[-1]
+    rows = state.astype(jnp.bfloat16).reshape(state.shape[0], -1, lanes)
+    high = lax.reduce_precision(log_span, exponent_bits=8, mantissa_bits=7)
+    rest = log_span - high
+    middle = lax.reduce_precision(rest, exponent_bits=8, mantissa_bits=7)
+    low = rest - middle
+    parts = jnp.stack((high, middle, low), axis=1).astype(jnp.bfloat16)
+    tail = jnp.pad(parts, ((0, 0), (0, 16 - parts.shape[1]), (0, lanes - heads)))
+    return jnp.concatenate((rows, tail), axis=1)
+
+
+def unpacked(block, state_shape):
+    heads = state_shape[1]
+    body_rows = block.shape[1] - 16
+    state = block[:, :body_rows].reshape(state_shape).astype(jnp.float32)
+    parts = block[:, body_rows:body_rows + 3, :heads].astype(jnp.float32)
+    return state, (parts[:, 0] + parts[:, 1]) + parts[:, 2]
+
+
 def carried_scan(local_state, block_log_decay, position, ctx_count):
-    sent = local_state.astype(jnp.bfloat16)
-    one_back_state = shifted(sent, "ctx", 1).astype(jnp.float32)
-    one_back_decay = shifted(block_log_decay, "ctx", 1)
-    two_back_state = shifted(sent, "ctx", 2).astype(jnp.float32)
-    two_back_decay = shifted(block_log_decay, "ctx", 2)
+    sent = packed(local_state, block_log_decay)
+    one_back_state, one_back_decay = unpacked(shifted(sent, "ctx", 1), local_state.shape)
+    two_back_state, two_back_decay = unpacked(shifted(sent, "ctx", 2), local_state.shape)
     state = jnp.exp(one_back_decay)[..., None, None] * two_back_state + one_back_state
     log_span = one_back_decay + two_back_decay
     distance = 2
     while distance < ctx_count:
-        earlier_state = shifted(state.astype(jnp.bfloat16), "ctx", distance).astype(jnp.float32)
-        earlier_span = shifted(log_span, "ctx", distance)
+        earlier_state, earlier_span = unpacked(
+            shifted(packed(state, log_span), "ctx", distance), local_state.shape
+        )
         state = jnp.exp(log_span)[..., None, None] * earlier_state + state
         log_span = log_span + earlier_span
         distance *= 2

time: 168 us -> 156 us (0.929)
  starting transfers between devices: 34.3 us -> 12.7 us
  waiting for transfers between devices: 62.8 us -> 69.1 us
  other arithmetic: 5.87 us -> 7.84 us
  local copies, waits for them, and re-layouts: 7.17 us -> 8.92 us
    ppermute x7 -> x3, starting transfers between devices: 18.6 us -> 4.28 us  [summed_over(): total = total + lax.ppermute(total, axis, route)]
    ppermute x11 -> x6, starting transfers between devices: 15.6 us -> 8.38 us  [shifted(): return lax.ppermute(block, axis, route)]
    ppermute x11 -> x6, waiting for transfers between devices: 54.8 us -> 59.8 us  [shifted(): return lax.ppermute(block, axis, route)]
    ppermute x7 -> x3, waiting for transfers between devices: 7.97 us -> 9.29 us  [summed_over(): total = total + lax.ppermute(total, axis, route)]
    unnamed x20 -> x18, local copies, waits for them, and re-layouts: 4.34 us -> 5.38 us
  transfers between devices with their start and end apart: 19 -> 10, of which waited for: 8 -> 9; matrix products, arithmetic and copies ran while one was open for 7% -> 8% of each run, Pallas kernels for 0% -> 0%
where the time goes in v4:
time: 156 us
  waiting for transfers between devices  69.1 us (44%)
  Pallas kernels  39.5 us (25%)
  between operations  14.4 us (9%)
  starting transfers between devices  12.7 us (8%)
  local copies, waits for them, and re-layouts  8.92 us (6%)
  other arithmetic  7.84 us (5%)
  matrix products  3.3 us (2%)
    ppermute x6, waiting for transfers between devices, shifted(): return lax.ppermute(block, axis, route)  59.8 us
    pallas_call x1, Pallas kernels, causal_attention(): pl.pallas_call(kernel, in_specs=[pl.BlockSpec(memory_space=pltpu.SMEM)] +...  39.5 us
    ppermute x3, waiting for transfers between devices, summed_over(): total = total + lax.ppermute(total, axis, route)  9.29 us
    ppermute x6, starting transfers between devices, shifted(): return lax.ppermute(block, axis, route)  8.38 us
    unnamed x18, local copies, waits for them, and re-layouts  5.38 us
    ppermute x3, starting transfers between devices, summed_over(): total = total + lax.ppermute(total, axis, route)  4.28 us
  transfers between devices with their start and end apart: 10, of which 9 were waited for; matrix products, arithmetic and copies ran while one was open for 8% of the time, Pallas kernels for 0%

profile of v4, /device:TPU:230, one launch (start us, length us, event | category | flops | bytes accessed | tf_op | source)
XLA Modules:
  0.0 155.8 jit_solution(14404843071244819161)
XLA Ops:
  7.2 0.0 copy-start
  7.2 0.0 all-gather.3.cloned.1.call-start
  7.2 0.7 reshape.965
  8.0 0.6 reduce-window.6
  8.6 0.2 slice_reduce_fusion
  8.8 0.1 copy.46
  8.9 0.1 broadcast.138
  9.0 0.3 slice_reduce_fusion.1
  9.3 1.3 copy.47
  10.5 0.8 multiply_bitcast_fusion
  11.3 0.1 fusion.16
  11.5 1.1 convolution_convert_fusion
  12.6 0.0 copy-start.2
  12.6 1.3 collective-permute-start.1
  13.9 1.9 %collective-permute-start = (bf16[1,1040,128]{2,1,0:T(8,128)(2,1)S(1)}, bf16[1,1040,128]{2,1,0:T(8,128)(2,1)S(1)}, u32[]{:S(2)}, u32[]{:S(2)}) collective-permute-start(bf16[1,1040,128]{2,1,0:T(8,128)(2,1)S(1)} %pad_maximum_fusion), channel_id=1, source_target_pairs={{0,8},{8,16},{16,24},{24,32},{32,40},{40,48},{48,56},{56,64},{64,7... | collective-permute-start | bytes 798728 | tf_op jit(solution)/shard_map/ppermute | solution.py:84
  15.9 1.5 pad_maximum_fusion.5
  17.4 0.0 all-gather.3.cloned.1.call-update
  17.4 6.4 %collective-permute-done.1 = bf16[1,1040,128]{2,1,0:T(8,128)(2,1)S(1)} collective-permute-done((bf16[1,1040,128]{2,1,0:T(8,128)(2,1)S(1)}, bf16[1,1040,128]{2,1,0:T(8,128)(2,1)S(1)}, u32[]{:S(2)}, u32[]{:S(2)}) %collective-permute-start.1) | collective-permute-done | bytes 266272 | tf_op jit(solution)/shard_map/ppermute | solution.py:84
  23.8 1.7 %collective-permute-done = bf16[1,1040,128]{2,1,0:T(8,128)(2,1)S(1)} collective-permute-done((bf16[1,1040,128]{2,1,0:T(8,128)(2,1)S(1)}, bf16[1,1040,128]{2,1,0:T(8,128)(2,1)S(1)}, u32[]{:S(2)}, u32[]{:S(2)}) %collective-permute-start) | collective-permute-done | bytes 266272 | tf_op jit(solution)/shard_map/ppermute | solution.py:84
  25.6 0.1 mul.209
  25.6 0.1 mul.210
  25.7 0.2 fusion.17
  26.0 1.3 collective-permute-start.2
  27.3 0.1 mul.213
  27.3 0.1 mul.214
  27.4 6.9 %collective-permute-done.2 = bf16[1,1040,128]{2,1,0:T(8,128)(2,1)S(1)} collective-permute-done((bf16[1,1040,128]{2,1,0:T(8,128)(2,1)S(1)}, bf16[1,1040,128]{2,1,0:T(8,128)(2,1)S(1)}, u32[]{:S(2)}, u32[]{:S(2)}) %collective-permute-start.2) | collective-permute-done | bytes 266272 | tf_op jit(solution)/shard_map/ppermute | solution.py:84
  34.3 0.3 fusion.72
  34.7 0.0 copy-start.3
  34.7 0.0 copy-start.5
  34.7 1.3 collective-permute-start.3
  36.0 0.1 mul.217
  36.1 0.1 mul.218
  36.2 10.3 %collective-permute-done.3 = bf16[1,1040,128]{2,1,0:T(8,128)(2,1)S(1)} collective-permute-done((bf16[1,1040,128]{2,1,0:T(8,128)(2,1)S(1)}, bf16[1,1040,128]{2,1,0:T(8,128)(2,1)S(1)}, u32[]{:S(2)}, u32[]{:S(2)}) %collective-permute-start.3) | collective-permute-done | bytes 266272 | tf_op jit(solution)/shard_map/ppermute | solution.py:84
  46.5 0.5 fusion.18
  47.0 1.3 collective-permute-start.4
  48.3 0.1 mul.224
  48.3 0.1 mul.225
  48.4 14.8 %collective-permute-done.4 = bf16[1,1040,128]{2,1,0:T(8,128)(2,1)S(1)} collective-permute-done((bf16[1,1040,128]{2,1,0:T(8,128)(2,1)S(1)}, bf16[1,1040,128]{2,1,0:T(8,128)(2,1)S(1)}, u32[]{:S(2)}, u32[]{:S(2)}) %collective-permute-start.4) | collective-permute-done | bytes 266272 | tf_op jit(solution)/shard_map/ppermute | solution.py:84
  63.2 0.9 fusion.71
  64.1 1.3 collective-permute-start.5
  65.5 0.2 fusion.73
  65.7 0.1 mul.221
  65.8 0.1 mul.222
  65.8 19.9 %collective-permute-done.5 = bf16[1,1040,128]{2,1,0:T(8,128)(2,1)S(1)} collective-permute-done((bf16[1,1040,128]{2,1,0:T(8,128)(2,1)S(1)}, bf16[1,1040,128]{2,1,0:T(8,128)(2,1)S(1)}, u32[]{:S(2)}, u32[]{:S(2)}) %collective-permute-start.5) | collective-permute-done | bytes 266272 | tf_op jit(solution)/shard_map/ppermute | solution.py:84
  85.7 0.9 multiply_add_fusion
  86.6 0.6 fusion.9
  87.3 0.0 copy-start.1
  87.3 1.4 fusion.11
  88.7 0.3 copy.50
  89.0 0.4 multiply_reduce_fusion
  89.4 1.6 %collective-permute-start.6 = (f32[256]{0:T(256)S(1)}, f32[256]{0:T(256)S(1)}, u32[]{:S(2)}, u32[]{:S(2)}) collective-permute-start(f32[256]{0:T(256)S(1)} %multiply_reduce_fusion), channel_id=1, source_target_pairs={{0,1},{1,0},{2,3},{3,2},{4,5},{5,4},{6,7},{7,6},{8,9},{9,8},{10,11... | collective-permute-start | bytes 3080 | tf_op jit(solution)/shard_map/ppermute | solution.py:93
  91.0 2.1 %collective-permute-done.6 = f32[256]{0:T(256)S(1)} collective-permute-done((f32[256]{0:T(256)S(1)}, f32[256]{0:T(256)S(1)}, u32[]{:S(2)}, u32[]{:S(2)}) %collective-permute-start.6) | collective-permute-done | bytes 1056 | tf_op jit(solution)/shard_map/ppermute | solution.py:93
  93.1 2.7 %collective-permute-start.7 = (f32[256]{0:T(256)S(1)}, f32[256]{0:T(256)S(1)}, u32[]{:S(2)}, u32[]{:S(2)}) collective-permute-start(f32[256]{0:T(256)S(1)} %add.600), channel_id=1, source_target_pairs={{0,2},{1,3},{2,0},{3,1},{4,6},{5,7},{6,4},{7,5},{8,10},{9,11},{10,... | collective-permute-start | bytes 3080 | tf_op jit(solution)/shard_map/ppermute | solution.py:93
  95.8 2.4 %collective-permute-done.7 = f32[256]{0:T(256)S(1)} collective-permute-done((f32[256]{0:T(256)S(1)}, f32[256]{0:T(256)S(1)}, u32[]{:S(2)}, u32[]{:S(2)}) %collective-permute-start.7) | collective-permute-done | bytes 1056 | tf_op jit(solution)/shard_map/ppermute | solution.py:93
  98.2 0.0 collective-permute-start.8
  98.2 1.1 copy.52
  99.3 0.6 copy.42
  99.9 0.9 copy.53
  100.8 4.8 %collective-permute-done.8 = f32[256]{0:T(256)S(1)} collective-permute-done((f32[256]{0:T(256)S(1)}, f32[256]{0:T(256)S(1)}, u32[]{:S(2)}, u32[]{:S(2)}) %collective-permute-start.8) | collective-permute-done | bytes 1056 | tf_op jit(solution)/shard_map/ppermute | solution.py:93
  105.6 1.2 multiply_convert_fusion
  106.8 39.5 %shard_map.122 = bf16[128,2048]{1,0:T(8,128)(2,1)} custom-call(s32[1]{0:T(128)} %bitcast.pos_ref, bf16[128,2048]{1,0:T(8,128)(2,1)} %bitcast.114, bf16[32,2,256,128]{3,2,1,0:T(8,128)(2,1)} %bitcast.105), custom_call_target="tpu_custom_call" | custom-call | tf_op jit(solution)/shard_map/pallas_call | solution.py:65
  146.3 1.1 copy.54
  147.5 0.6 copy.43
  148.0 0.9 copy.64
  (45 shorter events, 0.4 us)
Async XLA Ops:
  7.2 58.3 %copy-start = (bf16[256,128]{1,0:T(8,128)(2,1)S(1)}, bf16[256,128]{1,0:T(8,128)(2,1)}, u32[]{:S(2)}) copy-start(bf16[256,128]{1,0:T(8,128)(2,1)} %param.17) | copy-start | bytes 196612
  7.2 99.6 %all-gather.3.cloned.1.call-start = ((), (), s32[]{:S(2)}) async-start(), calls=%async_computation | async-start | bytes 4325376 | tf_op jit(solution)/shard_map/all_gather | solution.py:153
  12.6 52.9 %copy-start.2 = (bf16[256,128]{1,0:T(8,128)(2,1)S(1)}, bf16[256,128]{1,0:T(8,128)(2,1)}, u32[]{:S(2)}) copy-start(bf16[256,128]{1,0:T(8,128)(2,1)} %param.16) | copy-start | bytes 196612
  12.6 11.2 %collective-permute-start.1 = (bf16[1,1040,128]{2,1,0:T(8,128)(2,1)S(1)}, bf16[1,1040,128]{2,1,0:T(8,128)(2,1)S(1)}, u32[]{:S(2)}, u32[]{:S(2)}) collective-permute-start(bf16[1,1040,128]{2,1,0:T(8,128)(2,1)S(1)} %pad_maximum_fusion), channel_id=1, source_target_pairs={{0,16},{8,24},{16,32},{24,40},{32,48},{40,56},{48,64},{56,72},{64,... | collective-permute-start | bytes 798728 | tf_op jit(solution)/shard_map/ppermute | solution.py:84
  13.9 11.6 %collective-permute-start = (bf16[1,1040,128]{2,1,0:T(8,128)(2,1)S(1)}, bf16[1,1040,128]{2,1,0:T(8,128)(2,1)S(1)}, u32[]{:S(2)}, u32[]{:S(2)}) collective-permute-start(bf16[1,1040,128]{2,1,0:T(8,128)(2,1)S(1)} %pad_maximum_fusion), channel_id=1, source_target_pairs={{0,8},{8,16},{16,24},{24,32},{32,40},{40,48},{48,56},{56,64},{64,7... | collective-permute-start | bytes 798728 | tf_op jit(solution)/shard_map/ppermute | solution.py:84
  26.0 8.3 %collective-permute-start.2 = (bf16[1,1040,128]{2,1,0:T(8,128)(2,1)S(1)}, bf16[1,1040,128]{2,1,0:T(8,128)(2,1)S(1)}, u32[]{:S(2)}, u32[]{:S(2)}) collective-permute-start(bf16[1,1040,128]{2,1,0:T(8,128)(2,1)S(1)} %pad_maximum_fusion.1), channel_id=1, source_target_pairs={{0,16},{8,24},{16,32},{24,40},{32,48},{40,56},{48,64},{56,72},{64,... | collective-permute-start | bytes 798728 | tf_op jit(solution)/shard_map/ppermute | solution.py:84
  34.7 52.6 %copy-start.3 = (f32[16,256]{1,0:T(8,128)S(1)}, f32[16,256]{1,0:T(8,128)}, u32[]{:S(2)}) copy-start(f32[16,256]{1,0:T(8,128)} %param.18) | copy-start | bytes 49156
  34.7 52.5 %copy-start.5 = (f32[16]{0:T(128)S(1)}, f32[16]{0:T(128)}, u32[]{:S(2)}) copy-start(f32[16]{0:T(128)} %param.20) | copy-start | bytes 196
  34.7 11.7 %collective-permute-start.3 = (bf16[1,1040,128]{2,1,0:T(8,128)(2,1)S(1)}, bf16[1,1040,128]{2,1,0:T(8,128)(2,1)S(1)}, u32[]{:S(2)}, u32[]{:S(2)}) collective-permute-start(bf16[1,1040,128]{2,1,0:T(8,128)(2,1)S(1)} %pad_maximum_fusion.2), channel_id=1, source_target_pairs={{0,32},{8,40},{16,48},{24,56},{32,64},{40,72},{48,80},{56,88},{64,... | collective-permute-start | bytes 798728 | tf_op jit(solution)/shard_map/ppermute | solution.py:84
  47.0 16.2 %collective-permute-start.4 = (bf16[1,1040,128]{2,1,0:T(8,128)(2,1)S(1)}, bf16[1,1040,128]{2,1,0:T(8,128)(2,1)S(1)}, u32[]{:S(2)}, u32[]{:S(2)}) collective-permute-start(bf16[1,1040,128]{2,1,0:T(8,128)(2,1)S(1)} %pad_maximum_fusion.3), channel_id=1, source_target_pairs={{0,64},{8,72},{16,80},{24,88},{32,96},{40,104},{48,112},{56,120},{... | collective-permute-start | bytes 798728 | tf_op jit(solution)/shard_map/ppermute | solution.py:84
  64.1 21.6 %collective-permute-start.5 = (bf16[1,1040,128]{2,1,0:T(8,128)(2,1)S(1)}, bf16[1,1040,128]{2,1,0:T(8,128)(2,1)S(1)}, u32[]{:S(2)}, u32[]{:S(2)}) collective-permute-start(bf16[1,1040,128]{2,1,0:T(8,128)(2,1)S(1)} %pad_maximum_fusion.4), channel_id=1, source_target_pairs={{0,128},{8,136},{16,144},{24,152},{32,160},{40,168},{48,176},{56,1... | collective-permute-start | bytes 798728 | tf_op jit(solution)/shard_map/ppermute | solution.py:84
  87.3 1.8 %copy-start.1 = (bf16[256,1024]{1,0:T(8,128)(2,1)S(1)}, bf16[256,1024]{1,0:T(8,128)(2,1)}, u32[]{:S(2)}) copy-start(bf16[256,1024]{1,0:T(8,128)(2,1)} %param.15) | copy-start | bytes 1572868
  88.7 12.1 %copy-start.4 = (bf16[1024]{0:T(1024)(128)(2,1)S(1)}, bf16[1024]{0:T(1024)(128)(2,1)}, u32[]{:S(2)}) copy-start(bf16[1024]{0:T(1024)(128)(2,1)} %param.21) | copy-start | bytes 6148
  89.4 3.6 %collective-permute-start.6 = (f32[256]{0:T(256)S(1)}, f32[256]{0:T(256)S(1)}, u32[]{:S(2)}, u32[]{:S(2)}) collective-permute-start(f32[256]{0:T(256)S(1)} %multiply_reduce_fusion), channel_id=1, source_target_pairs={{0,1},{1,0},{2,3},{3,2},{4,5},{5,4},{6,7},{7,6},{8,9},{9,8},{10,11... | collective-permute-start | bytes 3080 | tf_op jit(solution)/shard_map/ppermute | solution.py:93
  93.1 5.1 %collective-permute-start.7 = (f32[256]{0:T(256)S(1)}, f32[256]{0:T(256)S(1)}, u32[]{:S(2)}, u32[]{:S(2)}) collective-permute-start(f32[256]{0:T(256)S(1)} %add.600), channel_id=1, source_target_pairs={{0,2},{1,3},{2,0},{3,1},{4,6},{5,7},{6,4},{7,5},{8,10},{9,11},{10,... | collective-permute-start | bytes 3080 | tf_op jit(solution)/shard_map/ppermute | solution.py:93
  98.2 7.5 %collective-permute-start.8 = (f32[256]{0:T(256)S(1)}, f32[256]{0:T(256)S(1)}, u32[]{:S(2)}, u32[]{:S(2)}) collective-permute-start(f32[256]{0:T(256)S(1)} %add.601), channel_id=1, source_target_pairs={{0,4},{1,5},{2,6},{3,7},{4,0},{5,1},{6,2},{7,3},{8,12},{9,13},{10,... | collective-permute-start | bytes 3080 | tf_op jit(solution)/shard_map/ppermute | solution.py:93
Sparse Core Ops, SparseCore 0:
  17.6 73.7 all-gather.2

commit v5 on v4

--- a/solution.py
+++ b/solution.py
@@ -14,19 +14,24 @@
 
 
 causal_score = -1e30
-
-
-def attend_kernel(pos_ref, qt_ref, kv_ref, o_ref, p_sc, m_sc, l_sc, c_sc, acc_sc, *, tok, width, chunk):
+CTX = ("chip", "core")
+
+
+def attend_kernel(pos_ref, qt_ref, same_ref, other_ref, o_ref, p_sc, m_sc, l_sc, c_sc, acc_sc, *, tok, width, chunk):
     position = pos_ref[0]
+    core = lax.rem(position, 2)
     score_factor = width ** (-0.5)
     rows = qt_ref.shape[1]
-    block_rows = kv_ref.shape[2]
+    block_rows = same_ref.shape[2]
     m_sc[...] = jnp.full(m_sc.shape, causal_score, jnp.float32)
     l_sc[...] = jnp.zeros(l_sc.shape, jnp.float32)
     acc_sc[...] = jnp.zeros(acc_sc.shape, jnp.float32)
 
     def run_block(kb, masked):
-        key_portion = kv_ref[kb, 0]
+        chip = kb // 2
+        from_same = lax.rem(kb, 2) == core
+        key_portion = jnp.where(from_same, same_ref[chip, 0], other_ref[chip, 0])
+        value_portion = jnp.where(from_same, same_ref[chip, 1], other_ref[chip, 1])
         for c in range(rows // chunk):
             r0 = c * chunk
             score_t = jnp.dot(key_portion, qt_ref[:, r0:r0 + chunk],
@@ -46,7 +51,7 @@
             m_sc[:, r0:r0 + chunk] = new_max
             c_sc[:, r0:r0 + chunk] = correction_factor
             p_sc[:, r0:r0 + chunk] = weights.astype(jnp.bfloat16)
-        acc_sc[...] = acc_sc[...] * c_sc[...] + lax.dot_general(kv_ref[kb, 1], p_sc[...], (((0,), (0,)), ((), ())), preferred_element_type=jnp.float32)
+        acc_sc[...] = acc_sc[...] * c_sc[...] + lax.dot_general(value_portion, p_sc[...], (((0,), (0,)), ((), ())), preferred_element_type=jnp.float32)
 
     def body(kb, carry):
         run_block(kb, False)
@@ -56,15 +61,15 @@
     o_ref[...] = (acc_sc[...] / l_sc[...]).astype(o_ref.dtype)
 
 
-def causal_attention(position, queries, gathered_kv, chunk=256):
-    blocks, _, tok_rows, width = gathered_kv.shape
+def causal_attention(position, queries, same_core_kv, other_core_kv, chunk=256):
+    _, _, tok_rows, width = same_core_kv.shape
     heads = queries.shape[1] // width
     rows = heads * tok_rows
     queries_t = queries.reshape(tok_rows, heads, width).transpose(2, 1, 0).reshape(width, rows)
     kernel = functools.partial(attend_kernel, tok=tok_rows, width=width, chunk=chunk)
     out_t = pl.pallas_call(
         kernel,
-        in_specs=[pl.BlockSpec(memory_space=pltpu.SMEM)] + [pl.BlockSpec(memory_space=pltpu.VMEM)] * 2,
+        in_specs=[pl.BlockSpec(memory_space=pltpu.SMEM)] + [pl.BlockSpec(memory_space=pltpu.VMEM)] * 3,
         out_specs=pl.BlockSpec(memory_space=pltpu.VMEM),
         out_shape=jax.ShapeDtypeStruct((width, rows), queries.dtype),
         scratch_shapes=[
@@ -74,7 +79,7 @@
             pltpu.VMEM((1, rows), jnp.float32),
             pltpu.VMEM((width, rows), jnp.float32),
         ],
-    )(position.reshape(1), queries_t, gathered_kv)
+    )(position.reshape(1), queries_t, same_core_kv, other_core_kv)
     return out_t.reshape(width, heads, tok_rows).transpose(2, 1, 0).reshape(tok_rows, heads * width)
 
 
@@ -118,14 +123,14 @@
 
 def carried_scan(local_state, block_log_decay, position, ctx_count):
     sent = packed(local_state, block_log_decay)
-    one_back_state, one_back_decay = unpacked(shifted(sent, "ctx", 1), local_state.shape)
-    two_back_state, two_back_decay = unpacked(shifted(sent, "ctx", 2), local_state.shape)
+    one_back_state, one_back_decay = unpacked(shifted(sent, CTX, 1), local_state.shape)
+    two_back_state, two_back_decay = unpacked(shifted(sent, CTX, 2), local_state.shape)
     state = jnp.exp(one_back_decay)[..., None, None] * two_back_state + one_back_state
     log_span = one_back_decay + two_back_decay
     distance = 2
     while distance < ctx_count:
         earlier_state, earlier_span = unpacked(
-            shifted(packed(state, log_span), "ctx", distance), local_state.shape
+            shifted(packed(state, log_span), CTX, distance), local_state.shape
         )
         state = jnp.exp(log_span)[..., None, None] * earlier_state + state
         log_span = log_span + earlier_span
@@ -147,10 +152,11 @@
     norm_gain,
 ):
     tok_rows = queries.shape[0]
-    ctx_count = lax.axis_size("ctx")
-    position = lax.axis_index("ctx")
-
-    gathered_kv = lax.all_gather(jnp.stack((key_rows, value_head_rows)), "ctx")
+    ctx_count = lax.axis_size(("chip", "core"))
+    position = lax.axis_index(("chip", "core"))
+
+    same_core_kv = lax.all_gather(jnp.stack((key_rows, value_head_rows)), "chip")
+    other_core_kv = lax.ppermute(same_core_kv, "core", [(0, 1), (1, 0)])
 
     heads_local = step_size.shape[0]
     groups_local = b_matrix.shape[1] // N
@@ -176,7 +182,7 @@
 
     incoming = carried_scan(local_state, block_log_decay, position, ctx_count)
 
-    attention_out = causal_attention(position, queries, gathered_kv)
+    attention_out = causal_attention(position, queries, same_core_kv, other_core_kv)
 
     carried_out = jnp.einsum(
         "ghpn,tgn->tghp", incoming, out_maps.astype(jnp.float32), precision=lax.Precision.HIGHEST
@@ -207,10 +213,20 @@
         P("tp"),
         P("tp"),
     )
+    ctx_count = mesh.shape["ctx"]
+    fine_mesh = jax.sharding.Mesh(
+        mesh.devices.reshape(ctx_count // 2, 2, mesh.shape["tp"]), ("chip", "core", "tp")
+    )
+    ctx = ("chip", "core")
+    placed = tuple(P(*[ctx if axis == "ctx" else axis for axis in spec]) for spec in placed)
+
+    def fine_local(*args):
+        return local(*args)
+
     return jax.shard_map(
-        local,
-        mesh=mesh,
+        fine_local,
+        mesh=fine_mesh,
         in_specs=placed,
-        out_specs=(P("ctx", "tp"), P("ctx", "tp")),
+        out_specs=(P(ctx, "tp"), P(ctx, "tp")),
         check_vma=False,
     )

time: 156 us -> 216 us (1.38); the launches traced: 156 us -> 213 us
  waiting for transfers between devices: 69.1 us -> 108 us
  local copies, waits for them, and re-layouts: 8.92 us -> 17.1 us
  other arithmetic: 7.84 us -> 14.7 us
  starting transfers between devices: 12.7 us -> 15.3 us
    all_gather x1, waiting for transfers between devices: 0.01 us -> 51 us  [local(): lax.all_gather(jnp.stack((key_rows, value_head_rows)), 'chip')]
    ppermute x6, waiting for transfers between devices: 59.8 us -> 53.4 us  [shifted(): return lax.ppermute(block, axis, route)]
    ppermute x3, waiting for transfers between devices: 9.29 us -> 3.98 us  [summed_over(): total = total + lax.ppermute(total, axis, route)]
    unnamed x18 -> x42, local copies, waits for them, and re-layouts: 5.38 us -> 9.88 us
    ppermute x3, starting transfers between devices: 4.28 us -> 6.93 us  [summed_over(): total = total + lax.ppermute(total, axis, route)]
  transfers between devices with their start and end apart: 10 -> 11, of which waited for: 9 -> 9; matrix products, arithmetic and copies ran while one was open for 8% -> 12% of each run, Pallas kernels for 0% -> 0%
where the time goes in v5:
time: 216 us; the launch traced here: 213 us
  waiting for transfers between devices  108 us (50%)
  Pallas kernels  39.8 us (18%)
  local copies, waits for them, and re-layouts  17.1 us (8%)
  starting transfers between devices  15.3 us (7%)
  other arithmetic  14.7 us (7%)
  between operations  14.5 us (7%)
  matrix products  3.44 us (2%)
    ppermute x6, waiting for transfers between devices, shifted(): return lax.ppermute(block, axis, route)  53.4 us
    all_gather x1, waiting for transfers between devices, local(): lax.all_gather(jnp.stack((key_rows, value_head_rows)), 'chip')  51 us
    pallas_call x1, Pallas kernels, causal_attention(): pl.pallas_call(kernel, in_specs=[pl.BlockSpec(memory_space=pltpu.SMEM)] +...  39.8 us
    unnamed x42, local copies, waits for them, and re-layouts  9.88 us
    ppermute x6, starting transfers between devices, shifted(): return lax.ppermute(block, axis, route)  8.37 us
    ppermute x3, starting transfers between devices, summed_over(): total = total + lax.ppermute(total, axis, route)  6.93 us
  transfers between devices with their start and end apart: 11, of which 9 were waited for; matrix products, arithmetic and copies ran while one was open for 12% of the time, Pallas kernels for 0%

profile of v5, /device:TPU:230, one launch (start us, length us, event | category | flops | bytes accessed | tf_op | source)
XLA Modules:
  0.0 213.3 jit_solution(5193488502921078111)
XLA Ops:
  7.2 0.8 reshape.965
  8.0 0.6 reduce-window.6
  8.6 0.2 slice_reduce_fusion
  8.8 0.1 copy.46
  8.9 0.1 broadcast.138
  9.0 0.6 exponential_bitcast_fusion
  9.6 0.3 slice_reduce_fusion.1
  9.9 1.3 copy.47
  11.2 1.5 multiply_bitcast_fusion
  12.7 0.1 fusion.16
  12.9 0.3 convolution_convert_fusion
  13.2 1.3 collective-permute-start.2
  14.5 1.9 collective-permute-start.1
  16.4 8.0 %collective-permute-done.2 = bf16[1,1040,128]{2,1,0:T(8,128)(2,1)S(1)} collective-permute-done((bf16[1,1040,128]{2,1,0:T(8,128)(2,1)S(1)}, bf16[1,1040,128]{2,1,0:T(8,128)(2,1)S(1)}, u32[]{:S(2)}, u32[]{:S(2)}) %collective-permute-start.2) | collective-permute-done | bytes 266272 | tf_op jit(solution)/shard_map/ppermute | solution.py:89
  24.4 1.7 collective-permute-done.1
  26.1 0.1 mul.213
  26.2 0.1 mul.214
  26.3 0.2 fusion.17
  26.5 1.3 collective-permute-start.3
  27.8 0.7 pad_maximum_fusion.5
  28.5 0.1 mul.217
  28.6 0.1 mul.218
  28.7 6.1 %collective-permute-done.3 = bf16[1,1040,128]{2,1,0:T(8,128)(2,1)S(1)} collective-permute-done((bf16[1,1040,128]{2,1,0:T(8,128)(2,1)S(1)}, bf16[1,1040,128]{2,1,0:T(8,128)(2,1)S(1)}, u32[]{:S(2)}, u32[]{:S(2)}) %collective-permute-start.3) | collective-permute-done | bytes 266272 | tf_op jit(solution)/shard_map/ppermute | solution.py:89
  34.9 0.3 fusion.72
  35.3 1.3 collective-permute-start.4
  36.6 0.1 mul.221
  36.6 0.1 mul.222
  36.7 9.3 %collective-permute-done.4 = bf16[1,1040,128]{2,1,0:T(8,128)(2,1)S(1)} collective-permute-done((bf16[1,1040,128]{2,1,0:T(8,128)(2,1)S(1)}, bf16[1,1040,128]{2,1,0:T(8,128)(2,1)S(1)}, u32[]{:S(2)}, u32[]{:S(2)}) %collective-permute-start.4) | collective-permute-done | bytes 266272 | tf_op jit(solution)/shard_map/ppermute | solution.py:89
  46.0 0.5 fusion.18
  46.5 1.3 collective-permute-start.5
  47.8 0.1 mul.228
  47.9 0.1 mul.229
  48.0 20.1 %collective-permute-done.5 = bf16[1,1040,128]{2,1,0:T(8,128)(2,1)S(1)} collective-permute-done((bf16[1,1040,128]{2,1,0:T(8,128)(2,1)S(1)}, bf16[1,1040,128]{2,1,0:T(8,128)(2,1)S(1)}, u32[]{:S(2)}, u32[]{:S(2)}) %collective-permute-start.5) | collective-permute-done | bytes 266272 | tf_op jit(solution)/shard_map/ppermute | solution.py:89
  68.0 0.6 exponential_bitcast_fusion.1
  68.6 0.6 fusion.59
  69.2 0.9 fusion.71
  70.1 51.0 %all-gather.3.cloned.1.call-done = bf16[32,256,128]{2,1,0:T(8,128)(2,1)} async-done(((bf16[2,256,128]{2,1,0:T(8,128)(2,1)}), bf16[32,256,128]{2,1,0:T(8,128)(2,1)}) %all-gather.3.cloned.1.call-update) | async-done | bytes 2097168 | tf_op jit(solution)/shard_map/all_gather | solution.py:158
  121.2 1.4 pad_maximum_fusion.4
  122.6 1.3 collective-permute-start.6
  123.9 0.6 iota_compare_fusion
  124.5 1.3 copy.65
  125.8 0.2 fusion.73
  126.0 0.7 mul.225
  126.8 0.1 mul.226
  126.8 8.2 %collective-permute-done.6 = bf16[1,1040,128]{2,1,0:T(8,128)(2,1)} collective-permute-done((bf16[1,1040,128]{2,1,0:T(8,128)(2,1)}, bf16[1,1040,128]{2,1,0:T(8,128)(2,1)}, u32[]{:S(2)}, u32[]{:S(2)}) %collective-permute-start.6) | collective-permute-done | bytes 266272 | tf_op jit(solution)/shard_map/ppermute | solution.py:89
  135.1 2.1 %multiply_add_fusion = f32[1,1024,128]{2,1,0:T(8,128)S(1)} fusion(bf16[1,1040,128]{2,1,0:T(8,128)(2,1)} %collective-permute-done.6, f32[1024]{0:T(1024)S(1)} %mul.226, bf16[1,1040,128]{2,1,0:T(8,128)(2,1)S(1)} %collective-permute-done.4, f32[1024]{0:T(1024)} %copy-done.8, bf16[1,1040,128]{2,1,0:T(8,128)(2,1)} %copy-done.4, f32[1024]{0:T(1024)} %copy-done.13, ...), kind=kLoop, calls=%fused_computation.26 | loop fusion | flops 2097152 | bytes 2117632 | tf_op jit(solution)/shard_map/add | solution.py:135
  137.2 0.6 fusion.9
  137.9 2.4 %fusion.11 = f32[256,1,16,64]{0,3,2,1:T(8,128)} fusion(f32[256,1,16,64]{0,3,2,1:T(8,128)S(1)} %fusion.9, bf16[256,16,64]{0,2,1:T(8,128)(2,1)S(1)} %bitcast.107, f32[16,256]{1,0:T(8,128)S(1)} %copy-done.14, f32[16,256]{1,0:T(8,128)S(1)} %copy-done.15, f32[256,256]{1,0:T(8,128)S(1)} %fusion.73, pred[256,256]{1,0:T(8,128)(4,1)S(1)} %copy-done.10, ...), kind=kOutput, calls=%fused_computation.13 | convolution fusion | flops 141557760 | bytes 3506240 | tf_op jit(solution)/shard_map/ghts,sghp->tghp/dot_general | solution.py:175
  140.3 1.6 copy.50
  141.8 1.4 multiply_reduce_fusion
  143.3 1.7 collective-permute-start.7
  145.0 1.9 collective-permute-done.7
  146.9 3.0 %collective-permute-start.8 = (f32[256]{0:T(256)S(1)}, f32[256]{0:T(256)S(1)}, u32[]{:S(2)}, u32[]{:S(2)}) collective-permute-start(f32[256]{0:T(256)S(1)} %add.604), channel_id=1, source_target_pairs={{0,2},{1,3},{2,0},{3,1},{4,6},{5,7},{6,4},{7,5},{8,10},{9,11},{10,... | collective-permute-start | bytes 3080 | tf_op jit(solution)/shard_map/ppermute | solution.py:98
  150.0 2.1 collective-permute-done.8
  152.0 2.2 %collective-permute-start.9 = (f32[256]{0:T(256)S(1)}, f32[256]{0:T(256)S(1)}, u32[]{:S(2)}, u32[]{:S(2)}) collective-permute-start(f32[256]{0:T(256)S(1)} %add.605), channel_id=1, source_target_pairs={{0,4},{1,5},{2,6},{3,7},{4,0},{5,1},{6,2},{7,3},{8,12},{9,13},{10,... | collective-permute-start | bytes 3080 | tf_op jit(solution)/shard_map/ppermute | solution.py:98
  154.2 1.9 copy.52
  156.1 2.4 %copy.42 = bf16[256,8,128]{0,1,2:T(8,128)(2,1)} copy(bf16[256,8,128]{2,1,0:T(8,128)(2,1)} %bitcast.114) | data formatting | bytes 1048576 | tf_op jit(solution)/shard_map/reshape | solution.py:68
  158.5 2.0 copy.53
  160.5 2.2 %multiply_convert_fusion = bf16[256,1024]{1,0:T(8,128)(2,1)} fusion(f32[1024]{0:T(1024)S(1)} %convert_element_type.232, f32[256]{0:T(256)S(1)} %add_rsqrt_fusion, f32[256,1024]{1,0:T(8,128)S(1)} %copy.50, bf16[256,1024]{1,0:T(8,128)(2,1)} %param.15), kind=kLoop, calls=%fused_computation.23 | loop fusion | flops 2359296 | bytes 2102272 | tf_op jit(solution)/shard_map/convert_element_type | solution.py:198
  162.7 1.3 copy-done.1
  164.0 39.8 %shard_map.122 = bf16[128,2048]{1,0:T(8,128)(2,1)} custom-call(s32[1]{0:T(128)} %bitcast.pos_ref, bf16[128,2048]{1,0:T(8,128)(2,1)} %bitcast.115, bf16[16,2,256,128]{3,2,1,0:T(8,128)(2,1)} %bitcast.106, bf16[16,2,256,128]{3,2,1,0:T(8,128)(2,1)} %copy-done.1), custom_call_target="tpu_custom_call" | custom-call | tf_op jit(solution)/shard_map/pallas_call | solution.py:70
  203.8 1.1 copy.54
  204.9 0.6 copy.43
  205.5 0.9 copy.64
  (71 shorter events, 0.5 us)
Async XLA Ops:
  7.2 118.6 %copy-start = (bf16[256,128]{1,0:T(8,128)(2,1)S(1)}, bf16[256,128]{1,0:T(8,128)(2,1)}, u32[]{:S(2)}) copy-start(bf16[256,128]{1,0:T(8,128)(2,1)} %param.17) | copy-start | bytes 196612
  7.2 5.7 %copy-start.5 = (bf16[256,128]{1,0:T(8,128)(2,1)S(1)}, bf16[256,128]{1,0:T(8,128)(2,1)}, u32[]{:S(2)}) copy-start(bf16[256,128]{1,0:T(8,128)(2,1)} %param.16) | copy-start | bytes 196612
  7.2 114.0 %all-gather.3.cloned.1.call-start = ((), (), s32[]{:S(2)}) async-start(), calls=%async_computation | async-start | bytes 2228224 | tf_op jit(solution)/shard_map/all_gather | solution.py:158
  11.2 2.0 copy-start.2
  11.2 16.6 %copy-start.11 = (bf16[256,128]{1,0:T(8,128)(2,1)S(1)}, bf16[256,128]{1,0:T(8,128)(2,1)}, u32[]{:S(2)}) copy-start(bf16[256,128]{1,0:T(8,128)(2,1)} %param.13) | copy-start | bytes 196612
  11.2 16.6 %copy-start.12 = (bf16[256,128]{1,0:T(8,128)(2,1)S(1)}, bf16[256,128]{1,0:T(8,128)(2,1)}, u32[]{:S(2)}) copy-start(bf16[256,128]{1,0:T(8,128)(2,1)} %param.12) | copy-start | bytes 196612
  13.2 11.2 %collective-permute-start.2 = (bf16[1,1040,128]{2,1,0:T(8,128)(2,1)S(1)}, bf16[1,1040,128]{2,1,0:T(8,128)(2,1)S(1)}, u32[]{:S(2)}, u32[]{:S(2)}) collective-permute-start(bf16[1,1040,128]{2,1,0:T(8,128)(2,1)S(1)} %pad_maximum_fusion), channel_id=1, source_target_pairs={{0,16},{8,24},{16,32},{24,40},{32,48},{40,56},{48,64},{56,72},{64,... | collective-permute-start | bytes 798728 | tf_op jit(solution)/shard_map/ppermute | solution.py:89
  14.5 11.6 %collective-permute-start.1 = (bf16[1,1040,128]{2,1,0:T(8,128)(2,1)S(1)}, bf16[1,1040,128]{2,1,0:T(8,128)(2,1)S(1)}, u32[]{:S(2)}, u32[]{:S(2)}) collective-permute-start(bf16[1,1040,128]{2,1,0:T(8,128)(2,1)S(1)} %pad_maximum_fusion), channel_id=1, source_target_pairs={{0,8},{8,16},{16,24},{24,32},{32,40},{40,48},{48,56},{56,64},{64,7... | collective-permute-start | bytes 798728 | tf_op jit(solution)/shard_map/ppermute | solution.py:89
  26.3 43.0 %copy-start.6 = (f32[1024]{0:T(1024)}, f32[1024]{0:T(1024)S(1)}, u32[]{:S(2)}) copy-start(f32[1024]{0:T(1024)S(1)} %mul.214) | copy-start | bytes 12292
  26.5 8.3 %collective-permute-start.3 = (bf16[1,1040,128]{2,1,0:T(8,128)(2,1)S(1)}, bf16[1,1040,128]{2,1,0:T(8,128)(2,1)S(1)}, u32[]{:S(2)}, u32[]{:S(2)}) collective-permute-start(bf16[1,1040,128]{2,1,0:T(8,128)(2,1)S(1)} %pad_maximum_fusion.1), channel_id=1, source_target_pairs={{0,16},{8,24},{16,32},{24,40},{32,48},{40,56},{48,64},{56,72},{64,... | collective-permute-start | bytes 798728 | tf_op jit(solution)/shard_map/ppermute | solution.py:89
  28.7 41.4 %copy-start.7 = (f32[1024]{0:T(1024)}, f32[1024]{0:T(1024)S(1)}, u32[]{:S(2)}) copy-start(f32[1024]{0:T(1024)S(1)} %mul.218) | copy-start | bytes 12292
  35.3 10.7 %collective-permute-start.4 = (bf16[1,1040,128]{2,1,0:T(8,128)(2,1)S(1)}, bf16[1,1040,128]{2,1,0:T(8,128)(2,1)S(1)}, u32[]{:S(2)}, u32[]{:S(2)}) collective-permute-start(bf16[1,1040,128]{2,1,0:T(8,128)(2,1)S(1)} %pad_maximum_fusion.2), channel_id=1, source_target_pairs={{0,32},{8,40},{16,48},{24,56},{32,64},{40,72},{48,80},{56,88},{64,... | collective-permute-start | bytes 798728 | tf_op jit(solution)/shard_map/ppermute | solution.py:89
  36.7 84.4 %copy-start.8 = (f32[1024]{0:T(1024)}, f32[1024]{0:T(1024)S(1)}, u32[]{:S(2)}) copy-start(f32[1024]{0:T(1024)S(1)} %mul.222) | copy-start | bytes 12292
  46.5 21.5 %collective-permute-start.5 = (bf16[1,1040,128]{2,1,0:T(8,128)(2,1)S(1)}, bf16[1,1040,128]{2,1,0:T(8,128)(2,1)S(1)}, u32[]{:S(2)}, u32[]{:S(2)}) collective-permute-start(bf16[1,1040,128]{2,1,0:T(8,128)(2,1)S(1)} %pad_maximum_fusion.3), channel_id=1, source_target_pairs={{0,64},{8,72},{16,80},{24,88},{32,96},{40,104},{48,112},{56,120},{... | collective-permute-start | bytes 798728 | tf_op jit(solution)/shard_map/ppermute | solution.py:89
  48.0 73.2 %copy-start.13 = (f32[1024]{0:T(1024)}, f32[1024]{0:T(1024)S(1)}, u32[]{:S(2)}) copy-start(f32[1024]{0:T(1024)S(1)} %mul.229) | copy-start | bytes 12292
  68.0 53.1 %copy-start.4 = (bf16[1,1040,128]{2,1,0:T(8,128)(2,1)}, bf16[1,1040,128]{2,1,0:T(8,128)(2,1)S(1)}, u32[]{:S(2)}) copy-start(bf16[1,1040,128]{2,1,0:T(8,128)(2,1)S(1)} %collective-permute-done.5) | copy-start | bytes 798724
  121.2 41.6 %collective-permute-start = (bf16[16,2,256,128]{3,2,1,0:T(8,128)(2,1)}, bf16[16,2,256,128]{3,2,1,0:T(8,128)(2,1)S(1)}, u32[]{:S(2)}, u32[]{:S(2)}) collective-permute-start(bf16[16,2,256,128]{3,2,1,0:T(8,128)(2,1)} %bitcast.105), channel_id=1, source_target_pairs={{0,8},{8,0},{1,9},{9,1},{2,10},{10,2},{3,11},{11,3},{4,12},{12,4},... | collective-permute-start | bytes 6291464 | tf_op jit(solution)/shard_map/ppermute | solution.py:159
  122.6 12.5 %collective-permute-start.6 = (bf16[1,1040,128]{2,1,0:T(8,128)(2,1)}, bf16[1,1040,128]{2,1,0:T(8,128)(2,1)}, u32[]{:S(2)}, u32[]{:S(2)}) collective-permute-start(bf16[1,1040,128]{2,1,0:T(8,128)(2,1)} %pad_maximum_fusion.4), channel_id=1, source_target_pairs={{0,128},{8,136},{16,144},{24,152},{32,160},{40,168},{48,176},{56,1... | collective-permute-start | bytes 798728 | tf_op jit(solution)/shard_map/ppermute | solution.py:89
  126.0 11.2 %copy-start.9 = (f32[256,1,16]{0,2,1:T(8,128)S(1)}, f32[256,1,16]{0,2,1:T(8,128)}, u32[]{:S(2)}) copy-start(f32[256,1,16]{0,2,1:T(8,128)} %copy.65) | copy-start | bytes 49156
  126.0 11.8 %copy-start.14 = (f32[16,256]{1,0:T(8,128)S(1)}, f32[16,256]{1,0:T(8,128)}, u32[]{:S(2)}) copy-start(f32[16,256]{1,0:T(8,128)} %param.18) | copy-start | bytes 49156
  126.0 11.8 %copy-start.15 = (f32[16,256]{1,0:T(8,128)S(1)}, f32[16,256]{1,0:T(8,128)}, u32[]{:S(2)}) copy-start(f32[16,256]{1,0:T(8,128)} %get-tuple-element.14) | copy-start | bytes 49156
  126.0 11.8 %copy-start.17 = (f32[16]{0:T(128)S(1)}, f32[16]{0:T(128)}, u32[]{:S(2)}) copy-start(f32[16]{0:T(128)} %param.20) | copy-start | bytes 196
  126.8 11.0 %copy-start.3 = (bf16[256,1024]{0,1:T(8,128)(2,1)S(1)}, bf16[256,1024]{0,1:T(8,128)(2,1)}, u32[]{:S(2)}) copy-start(bf16[256,1024]{0,1:T(8,128)(2,1)} %copy-done.2) | copy-start | bytes 1572868
  126.8 11.0 %copy-start.10 = (pred[256,256]{1,0:T(8,128)(4,1)S(1)}, pred[256,256]{1,0:T(8,128)(4,1)}, u32[]{:S(2)}) copy-start(pred[256,256]{1,0:T(8,128)(4,1)} %iota_compare_fusion) | copy-start | bytes 196612
  141.8 18.7 %copy-start.16 = (bf16[1024]{0:T(1024)(128)(2,1)S(1)}, bf16[1024]{0:T(1024)(128)(2,1)}, u32[]{:S(2)}) copy-start(bf16[1024]{0:T(1024)(128)(2,1)} %param.21) | copy-start | bytes 6148
  143.3 3.6 %collective-permute-start.7 = (f32[256]{0:T(256)S(1)}, f32[256]{0:T(256)S(1)}, u32[]{:S(2)}, u32[]{:S(2)}) collective-permute-start(f32[256]{0:T(256)S(1)} %multiply_reduce_fusion), channel_id=1, source_target_pairs={{0,1},{1,0},{2,3},{3,2},{4,5},{5,4},{6,7},{7,6},{8,9},{9,8},{10,11... | collective-permute-start | bytes 3080 | tf_op jit(solution)/shard_map/ppermute | solution.py:98
  146.9 5.1 %collective-permute-start.8 = (f32[256]{0:T(256)S(1)}, f32[256]{0:T(256)S(1)}, u32[]{:S(2)}, u32[]{:S(2)}) collective-permute-start(f32[256]{0:T(256)S(1)} %add.604), channel_id=1, source_target_pairs={{0,2},{1,3},{2,0},{3,1},{4,6},{5,7},{6,4},{7,5},{8,10},{9,11},{10,... | collective-permute-start | bytes 3080 | tf_op jit(solution)/shard_map/ppermute | solution.py:98
  152.0 8.5 %collective-permute-start.9 = (f32[256]{0:T(256)S(1)}, f32[256]{0:T(256)S(1)}, u32[]{:S(2)}, u32[]{:S(2)}) collective-permute-start(f32[256]{0:T(256)S(1)} %add.605), channel_id=1, source_target_pairs={{0,4},{1,5},{2,6},{3,7},{4,0},{5,1},{6,2},{7,3},{8,12},{9,13},{10,... | collective-permute-start | bytes 3080 | tf_op jit(solution)/shard_map/ppermute | solution.py:98
  162.7 1.3 copy-start.1
Sparse Core Ops, SparseCore 0:
  28.7 92.4 all-gather.2

commit v6 on v4

--- a/solution.py
+++ b/solution.py
@@ -176,6 +176,7 @@
 
     incoming = carried_scan(local_state, block_log_decay, position, ctx_count)
 
+    incoming, gathered_kv = lax.optimization_barrier((incoming, gathered_kv))
     attention_out = causal_attention(position, queries, gathered_kv)
 
     carried_out = jnp.einsum(
@@ -187,7 +188,8 @@
     )
     outputs = (inner + carried_out + direct).reshape(tok_rows, -1)
     gated = outputs * jax.nn.silu(gate_input.astype(jnp.float32))
-    square_total = summed_over(jnp.sum(gated * gated, axis=-1), "tp")
+    square_part, attention_out = lax.optimization_barrier((jnp.sum(gated * gated, axis=-1), attention_out))
+    square_total = summed_over(square_part, "tp")
     scaling = lax.rsqrt(square_total / (STATE_HEADS * P_SIZE) + 1e-05)
     mixer_out = (gated * scaling[:, None] * norm_gain.astype(jnp.float32)).astype(jnp.bfloat16)
     return (attention_out, mixer_out)

time: 156 us -> 160 us (1.026)
  other arithmetic: 7.84 us -> 9.95 us
  matrix products: 3.3 us -> 4.96 us
    ppermute x3, waiting for transfers between devices: 9.29 us -> 11.2 us  [summed_over(): total = total + lax.ppermute(total, axis, route)]
    ppermute x6, waiting for transfers between devices: 59.8 us -> 58.1 us  [shifted(): return lax.ppermute(block, axis, route)]
    unnamed x18 -> x22, local copies, waits for them, and re-layouts: 5.38 us -> 4.35 us
  transfers between devices with their start and end apart: 10 -> 10, of which waited for: 9 -> 9; matrix products, arithmetic and copies ran while one was open for 8% -> 9% of each run, Pallas kernels for 0% -> 0%
where the time goes in v6:
time: 160 us; the launch traced here: 159 us
  waiting for transfers between devices  69.3 us (43%)
  Pallas kernels  39.5 us (25%)
  between operations  14.4 us (9%)
  starting transfers between devices  13.4 us (8%)
  other arithmetic  9.95 us (6%)
  local copies, waits for them, and re-layouts  7.77 us (5%)
  matrix products  4.96 us (3%)
    ppermute x6, waiting for transfers between devices, shifted(): return lax.ppermute(block, axis, route)  58.1 us
    pallas_call x1, Pallas kernels, causal_attention(): pl.pallas_call(kernel, in_specs=[pl.BlockSpec(memory_space=pltpu.SMEM)] +...  39.5 us
    ppermute x3, waiting for transfers between devices, summed_over(): total = total + lax.ppermute(total, axis, route)  11.2 us
    ppermute x6, starting transfers between devices, shifted(): return lax.ppermute(block, axis, route)  8.37 us
    ppermute x3, starting transfers between devices, summed_over(): total = total + lax.ppermute(total, axis, route)  5.03 us
    unnamed x22, local copies, waits for them, and re-layouts  4.35 us
  transfers between devices with their start and end apart: 10, of which 9 were waited for; matrix products, arithmetic and copies ran while one was open for 9% of the time, Pallas kernels for 0%

profile of v6, /device:TPU:230, one launch (start us, length us, event | category | flops | bytes accessed | tf_op | source)
XLA Modules:
  0.0 159.3 jit_solution(5676602984893409835)
XLA Ops:
  7.2 0.0 copy-start
  7.2 0.0 copy-start.3
  7.2 0.0 all-gather.3.cloned.1.call-start
  7.2 1.6 %pad_maximum_fusion.5 = bf16[2,256,128]{2,1,0:T(8,128)(2,1)} fusion(bf16[1,256,128]{2,1,0:T(8,128)(2,1)} %bitcast.138, bf16[1,256,128]{2,1,0:T(8,128)(2,1)} %bitcast.139), kind=kLoop, calls=%fused_computation.44 | loop fusion | flops 65536 | bytes 262144 | tf_op jit(solution)/shard_map/stack | solution.py:153
  8.9 0.0 all-gather.3.cloned.1.call-update
  8.9 0.7 reshape.1046
  9.6 0.6 reduce-window.6
  10.2 0.2 slice_reduce_fusion
  10.5 0.1 copy.44
  10.5 0.1 broadcast.153
  10.7 0.3 slice_reduce_fusion.1
  10.9 1.3 copy.45
  12.2 1.3 multiply_bitcast_fusion
  13.5 0.1 fusion.16
  13.6 1.1 convolution_convert_fusion
  14.8 1.3 collective-permute-start.1
  16.1 1.9 %collective-permute-start = (bf16[1,1040,128]{2,1,0:T(8,128)(2,1)S(1)}, bf16[1,1040,128]{2,1,0:T(8,128)(2,1)S(1)}, u32[]{:S(2)}, u32[]{:S(2)}) collective-permute-start(bf16[1,1040,128]{2,1,0:T(8,128)(2,1)S(1)} %pad_maximum_fusion), channel_id=1, source_target_pairs={{0,8},{8,16},{16,24},{24,32},{32,40},{40,48},{48,56},{56,64},{64,7... | collective-permute-start | bytes 798728 | tf_op jit(solution)/shard_map/ppermute | solution.py:84
  18.0 9.9 %collective-permute-done.1 = bf16[1,1040,128]{2,1,0:T(8,128)(2,1)S(1)} collective-permute-done((bf16[1,1040,128]{2,1,0:T(8,128)(2,1)S(1)}, bf16[1,1040,128]{2,1,0:T(8,128)(2,1)S(1)}, u32[]{:S(2)}, u32[]{:S(2)}) %collective-permute-start.1) | collective-permute-done | bytes 266272 | tf_op jit(solution)/shard_map/ppermute | solution.py:84
  28.0 3.9 %collective-permute-done = bf16[1,1040,128]{2,1,0:T(8,128)(2,1)S(1)} collective-permute-done((bf16[1,1040,128]{2,1,0:T(8,128)(2,1)S(1)}, bf16[1,1040,128]{2,1,0:T(8,128)(2,1)S(1)}, u32[]{:S(2)}, u32[]{:S(2)}) %collective-permute-start) | collective-permute-done | bytes 266272 | tf_op jit(solution)/shard_map/ppermute | solution.py:84
  32.0 0.1 mul.241
  32.0 0.1 mul.242
  32.1 0.2 fusion.19
  32.4 1.3 collective-permute-start.2
  33.7 0.9 fusion.74
  34.6 0.1 mul.245
  34.6 0.1 mul.246
  34.7 6.6 %collective-permute-done.2 = bf16[1,1040,128]{2,1,0:T(8,128)(2,1)S(1)} collective-permute-done((bf16[1,1040,128]{2,1,0:T(8,128)(2,1)S(1)}, bf16[1,1040,128]{2,1,0:T(8,128)(2,1)S(1)}, u32[]{:S(2)}, u32[]{:S(2)}) %collective-permute-start.2) | collective-permute-done | bytes 266272 | tf_op jit(solution)/shard_map/ppermute | solution.py:84
  41.4 0.3 fusion.73
  41.8 1.3 collective-permute-start.3
  43.1 0.6 iota_compare_fusion
  43.7 0.1 copy.54
  43.8 0.6 copy.49
  44.4 0.9 copy.55
  45.4 0.1 mul.249
  45.4 0.1 mul.250
  45.5 8.6 %collective-permute-done.3 = bf16[1,1040,128]{2,1,0:T(8,128)(2,1)S(1)} collective-permute-done((bf16[1,1040,128]{2,1,0:T(8,128)(2,1)S(1)}, bf16[1,1040,128]{2,1,0:T(8,128)(2,1)S(1)}, u32[]{:S(2)}, u32[]{:S(2)}) %collective-permute-start.3) | collective-permute-done | bytes 266272 | tf_op jit(solution)/shard_map/ppermute | solution.py:84
  54.1 0.5 fusion.20
  54.6 0.7 pad_maximum_fusion.3
  55.3 1.3 collective-permute-start.4
  56.7 0.1 mul.254
  56.8 0.1 mul.255
  56.8 8.6 %collective-permute-done.4 = bf16[1,1040,128]{2,1,0:T(8,128)(2,1)S(1)} collective-permute-done((bf16[1,1040,128]{2,1,0:T(8,128)(2,1)}, bf16[1,1040,128]{2,1,0:T(8,128)(2,1)S(1)}, u32[]{:S(2)}, u32[]{:S(2)}) %collective-permute-start.4) | collective-permute-done | bytes 266272 | tf_op jit(solution)/shard_map/ppermute | solution.py:84
  65.5 0.9 add_convert_fusion
  66.4 0.0 copy-start.4
  66.4 0.0 copy-start.7
  66.5 1.3 collective-permute-start.5
  67.9 20.4 %collective-permute-done.5 = bf16[1,1040,128]{2,1,0:T(8,128)(2,1)S(1)} collective-permute-done((bf16[1,1040,128]{2,1,0:T(8,128)(2,1)S(1)}, bf16[1,1040,128]{2,1,0:T(8,128)(2,1)S(1)}, u32[]{:S(2)}, u32[]{:S(2)}) %collective-permute-start.5) | collective-permute-done | bytes 266272 | tf_op jit(solution)/shard_map/ppermute | solution.py:84
  88.2 1.0 fusion.17
  89.2 0.0 all-gather.3.cloned.1.call-done
  89.2 0.6 fusion.9
  89.8 2.4 %fusion.11 = f32[256,1,16,64]{0,3,2,1:T(8,128)S(1)} fusion(f32[256,1,16,64]{0,3,2,1:T(8,128)S(1)} %fusion.9, bf16[256,16,64]{0,2,1:T(8,128)(2,1)S(1)} %bitcast.119, f32[16,256]{1,0:T(8,128)S(1)} %copy-done.4, f32[16,256]{1,0:T(8,128)} %get-tuple-element.22, f32[256,256]{1,0:T(8,128)} %fusion.74, pred[256,256]{1,0:T(8,128)(4,1)} %iota_compare_fusion, ...), kind=kOutput, calls=%fused_computation.13 | convolution fusion | flops 141557760 | bytes 3506240 | tf_op jit(solution)/shard_map/ghts,sghp->tghp/dot_general | solution.py:169
  92.2 0.3 copy.48
  92.5 0.0 copy-start.1
  92.6 39.5 %shard_map.122 = bf16[128,2048]{1,0:T(8,128)(2,1)} custom-call(s32[1]{0:T(128)} %bitcast.38.pos_ref, bf16[128,2048]{1,0:T(8,128)(2,1)} %bitcast.126, bf16[32,2,256,128]{3,2,1,0:T(8,128)(2,1)} %bitcast.113), custom_call_target="tpu_custom_call" | custom-call | tf_op jit(solution)/shard_map/pallas_call | solution.py:65
  132.1 1.1 copy.56
  133.2 0.6 copy.50
  133.8 0.9 copy.64
  134.7 0.4 multiply_reduce_fusion
  135.1 1.6 %collective-permute-start.6 = (f32[256]{0:T(256)S(1)}, f32[256]{0:T(256)S(1)}, u32[]{:S(2)}, u32[]{:S(2)}) collective-permute-start(f32[256]{0:T(256)S(1)} %multiply_reduce_fusion), channel_id=1, source_target_pairs={{0,1},{1,0},{2,3},{3,2},{4,5},{5,4},{6,7},{7,6},{8,9},{9,8},{10,11... | collective-permute-start | bytes 3080 | tf_op jit(solution)/shard_map/ppermute | solution.py:93
  136.7 2.0 %collective-permute-done.6 = f32[256]{0:T(256)S(1)} collective-permute-done((f32[256]{0:T(256)S(1)}, f32[256]{0:T(256)S(1)}, u32[]{:S(2)}, u32[]{:S(2)}) %collective-permute-start.6) | collective-permute-done | bytes 1056 | tf_op jit(solution)/shard_map/ppermute | solution.py:93
  138.8 3.4 %collective-permute-start.7 = (f32[256]{0:T(256)S(1)}, f32[256]{0:T(256)S(1)}, u32[]{:S(2)}, u32[]{:S(2)}) collective-permute-start(f32[256]{0:T(256)S(1)} %add.629), channel_id=1, source_target_pairs={{0,2},{1,3},{2,0},{3,1},{4,6},{5,7},{6,4},{7,5},{8,10},{9,11},{10,... | collective-permute-start | bytes 3080 | tf_op jit(solution)/shard_map/ppermute | solution.py:93
  142.2 1.7 %collective-permute-done.7 = f32[256]{0:T(256)S(1)} collective-permute-done((f32[256]{0:T(256)S(1)}, f32[256]{0:T(256)S(1)}, u32[]{:S(2)}, u32[]{:S(2)}) %collective-permute-start.7) | collective-permute-done | bytes 1056 | tf_op jit(solution)/shard_map/ppermute | solution.py:93
  143.9 7.5 %collective-permute-done.8 = f32[256]{0:T(256)S(1)} collective-permute-done((f32[256]{0:T(256)S(1)}, f32[256]{0:T(256)S(1)}, u32[]{:S(2)}, u32[]{:S(2)}) %collective-permute-start.8) | collective-permute-done | bytes 1056 | tf_op jit(solution)/shard_map/ppermute | solution.py:93
  151.3 1.2 multiply_convert_fusion
  (53 shorter events, 0.6 us)
Async XLA Ops:
  7.2 26.5 %copy-start = (bf16[256,128]{1,0:T(8,128)(2,1)S(1)}, bf16[256,128]{1,0:T(8,128)(2,1)}, u32[]{:S(2)}) copy-start(bf16[256,128]{1,0:T(8,128)(2,1)} %param.17) | copy-start | bytes 196612
  7.2 26.5 %copy-start.3 = (bf16[256,128]{1,0:T(8,128)(2,1)S(1)}, bf16[256,128]{1,0:T(8,128)(2,1)}, u32[]{:S(2)}) copy-start(bf16[256,128]{1,0:T(8,128)(2,1)} %param.16) | copy-start | bytes 196612
  7.2 36.5 %copy-start.2 = (bf16[256,1024]{1,0:T(8,128)(2,1)S(1)}, bf16[256,1024]{1,0:T(8,128)(2,1)}, u32[]{:S(2)}) copy-start(bf16[256,1024]{1,0:T(8,128)(2,1)} %param.11) | copy-start | bytes 1572868
  7.2 82.0 %all-gather.3.cloned.1.call-start = ((), (), s32[]{:S(2)}) async-start(), calls=%async_computation | async-start | bytes 4325376 | tf_op jit(solution)/shard_map/all_gather | solution.py:153
  14.8 13.2 %collective-permute-start.1 = (bf16[1,1040,128]{2,1,0:T(8,128)(2,1)S(1)}, bf16[1,1040,128]{2,1,0:T(8,128)(2,1)S(1)}, u32[]{:S(2)}, u32[]{:S(2)}) collective-permute-start(bf16[1,1040,128]{2,1,0:T(8,128)(2,1)S(1)} %pad_maximum_fusion), channel_id=1, source_target_pairs={{0,16},{8,24},{16,32},{24,40},{32,48},{40,56},{48,64},{56,72},{64,... | collective-permute-start | bytes 798728 | tf_op jit(solution)/shard_map/ppermute | solution.py:84
  16.1 15.8 %collective-permute-start = (bf16[1,1040,128]{2,1,0:T(8,128)(2,1)S(1)}, bf16[1,1040,128]{2,1,0:T(8,128)(2,1)S(1)}, u32[]{:S(2)}, u32[]{:S(2)}) collective-permute-start(bf16[1,1040,128]{2,1,0:T(8,128)(2,1)S(1)} %pad_maximum_fusion), channel_id=1, source_target_pairs={{0,8},{8,16},{16,24},{24,32},{32,40},{40,48},{48,56},{56,64},{64,7... | collective-permute-start | bytes 798728 | tf_op jit(solution)/shard_map/ppermute | solution.py:84
  31.9 11.8 %copy-start.5 = (f32[16]{0:T(128)}, f32[16]{0:T(128)S(1)}, u32[]{:S(2)}) copy-start(f32[16]{0:T(128)S(1)} %exponential_bitcast_fusion.5) | copy-start | bytes 196
  32.4 9.0 %collective-permute-start.2 = (bf16[1,1040,128]{2,1,0:T(8,128)(2,1)S(1)}, bf16[1,1040,128]{2,1,0:T(8,128)(2,1)S(1)}, u32[]{:S(2)}, u32[]{:S(2)}) collective-permute-start(bf16[1,1040,128]{2,1,0:T(8,128)(2,1)S(1)} %pad_maximum_fusion.1), channel_id=1, source_target_pairs={{0,16},{8,24},{16,32},{24,40},{32,48},{40,56},{48,64},{56,72},{64,... | collective-permute-start | bytes 798728 | tf_op jit(solution)/shard_map/ppermute | solution.py:84
  41.8 12.3 %collective-permute-start.3 = (bf16[1,1040,128]{2,1,0:T(8,128)(2,1)S(1)}, bf16[1,1040,128]{2,1,0:T(8,128)(2,1)S(1)}, u32[]{:S(2)}, u32[]{:S(2)}) collective-permute-start(bf16[1,1040,128]{2,1,0:T(8,128)(2,1)S(1)} %pad_maximum_fusion.2), channel_id=1, source_target_pairs={{0,32},{8,40},{16,48},{24,56},{32,64},{40,72},{48,80},{56,88},{64,... | collective-permute-start | bytes 798728 | tf_op jit(solution)/shard_map/ppermute | solution.py:84
  55.3 10.1 %collective-permute-start.4 = (bf16[1,1040,128]{2,1,0:T(8,128)(2,1)}, bf16[1,1040,128]{2,1,0:T(8,128)(2,1)S(1)}, u32[]{:S(2)}, u32[]{:S(2)}) collective-permute-start(bf16[1,1040,128]{2,1,0:T(8,128)(2,1)} %pad_maximum_fusion.3), channel_id=1, source_target_pairs={{0,64},{8,72},{16,80},{24,88},{32,96},{40,104},{48,112},{56,120},{... | collective-permute-start | bytes 798728 | tf_op jit(solution)/shard_map/ppermute | solution.py:84
  66.4 23.4 %copy-start.4 = (f32[16,256]{1,0:T(8,128)S(1)}, f32[16,256]{1,0:T(8,128)}, u32[]{:S(2)}) copy-start(f32[16,256]{1,0:T(8,128)} %param.18) | copy-start | bytes 49156
  66.4 23.4 %copy-start.7 = (f32[16]{0:T(128)S(1)}, f32[16]{0:T(128)}, u32[]{:S(2)}) copy-start(f32[16]{0:T(128)} %param.20) | copy-start | bytes 196
  66.5 21.7 %collective-permute-start.5 = (bf16[1,1040,128]{2,1,0:T(8,128)(2,1)S(1)}, bf16[1,1040,128]{2,1,0:T(8,128)(2,1)S(1)}, u32[]{:S(2)}, u32[]{:S(2)}) collective-permute-start(bf16[1,1040,128]{2,1,0:T(8,128)(2,1)S(1)} %pad_maximum_fusion.4), channel_id=1, source_target_pairs={{0,128},{8,136},{16,144},{24,152},{32,160},{40,168},{48,176},{56,1... | collective-permute-start | bytes 798728 | tf_op jit(solution)/shard_map/ppermute | solution.py:84
  92.5 42.2 %copy-start.1 = (bf16[256,1024]{1,0:T(8,128)(2,1)S(1)}, bf16[256,1024]{1,0:T(8,128)(2,1)}, u32[]{:S(2)}) copy-start(bf16[256,1024]{1,0:T(8,128)(2,1)} %param.15) | copy-start | bytes 1572868
  92.5 51.3 %copy-start.6 = (bf16[1024]{0:T(1024)(128)(2,1)S(1)}, bf16[1024]{0:T(1024)(128)(2,1)}, u32[]{:S(2)}) copy-start(bf16[1024]{0:T(1024)(128)(2,1)} %param.21) | copy-start | bytes 6148
  135.1 3.6 %collective-permute-start.6 = (f32[256]{0:T(256)S(1)}, f32[256]{0:T(256)S(1)}, u32[]{:S(2)}, u32[]{:S(2)}) collective-permute-start(f32[256]{0:T(256)S(1)} %multiply_reduce_fusion), channel_id=1, source_target_pairs={{0,1},{1,0},{2,3},{3,2},{4,5},{5,4},{6,7},{7,6},{8,9},{9,8},{10,11... | collective-permute-start | bytes 3080 | tf_op jit(solution)/shard_map/ppermute | solution.py:93
  138.8 5.1 %collective-permute-start.7 = (f32[256]{0:T(256)S(1)}, f32[256]{0:T(256)S(1)}, u32[]{:S(2)}, u32[]{:S(2)}) collective-permute-start(f32[256]{0:T(256)S(1)} %add.629), channel_id=1, source_target_pairs={{0,2},{1,3},{2,0},{3,1},{4,6},{5,7},{6,4},{7,5},{8,10},{9,11},{10,... | collective-permute-start | bytes 3080 | tf_op jit(solution)/shard_map/ppermute | solution.py:93
  143.8 7.5 %collective-permute-start.8 = (f32[256]{0:T(256)S(1)}, f32[256]{0:T(256)S(1)}, u32[]{:S(2)}, u32[]{:S(2)}) collective-permute-start(f32[256]{0:T(256)S(1)} %add.630), channel_id=1, source_target_pairs={{0,4},{1,5},{2,6},{3,7},{4,0},{5,1},{6,2},{7,3},{8,12},{9,13},{10,... | collective-permute-start | bytes 3080 | tf_op jit(solution)/shard_map/ppermute | solution.py:93
Sparse Core Ops, SparseCore 0:
  9.9 75.8 all-gather.2

commit v7 on v4

--- a/solution.py
+++ b/solution.py
@@ -74,6 +74,11 @@
             pltpu.VMEM((1, rows), jnp.float32),
             pltpu.VMEM((width, rows), jnp.float32),
         ],
+        cost_estimate=pl.CostEstimate(
+            flops=4 * rows * width * tok_rows * blocks,
+            transcendentals=rows * tok_rows * blocks,
+            bytes_accessed=2 * (queries.size * 2 + gathered_kv.size),
+        ),
     )(position.reshape(1), queries_t, gathered_kv)
     return out_t.reshape(width, heads, tok_rows).transpose(2, 1, 0).reshape(tok_rows, heads * width)
 
@@ -87,11 +92,9 @@
 def summed_over(part, axis):
     count = lax.axis_size(axis)
     total = part
-    distance = 1
-    while distance < count:
-        route = [(i, i ^ distance) for i in range(count)]
-        total = total + lax.ppermute(total, axis, route)
-        distance *= 2
+    for distance in range(1, count):
+        route = [(i, (i + distance) % count) for i in range(count)]
+        total = total + lax.ppermute(part, axis, route)
     return total
 
 
@@ -176,6 +179,7 @@
 
     incoming = carried_scan(local_state, block_log_decay, position, ctx_count)
 
+    incoming, gathered_kv = lax.optimization_barrier((incoming, gathered_kv))
     attention_out = causal_attention(position, queries, gathered_kv)
 
     carried_out = jnp.einsum(

time: 156 us -> 172 us (1.10)
  the two profiles are of different devices: /device:TPU:230 before, /device:TPU:118 now
where the time goes in v7:
time: 172 us
  waiting for transfers between devices  55 us (32%)
  Pallas kernels  39.6 us (23%)
  starting transfers between devices  36.6 us (21%)
  between operations  14.5 us (8%)
  local copies, waits for them, and re-layouts  10 us (6%)
  other arithmetic  9.88 us (6%)
  matrix products  6.04 us (4%)
    ppermute x6, waiting for transfers between devices, shifted(): return lax.ppermute(block, axis, route)  54.9 us
    pallas_call x1, Pallas kernels, causal_attention(): pl.pallas_call(kernel, in_specs=[pl.BlockSpec(memory_space=pltpu.SMEM)] +...  39.6 us
    ppermute x7, starting transfers between devices, summed_over(): total = total + lax.ppermute(part, axis, route)  28.2 us
    ppermute x6, starting transfers between devices, shifted(): return lax.ppermute(block, axis, route)  8.37 us
    unnamed x20, local copies, waits for them, and re-layouts  5.39 us
  transfers between devices with their start and end apart: 14, of which 6 were waited for; matrix products, arithmetic and copies ran while one was open for 10% of the time, Pallas kernels for 23%

profile of v7, /device:TPU:118, one launch (start us, length us, event | category | flops | bytes accessed | tf_op | source)
XLA Modules:
  0.0 171.7 jit_solution(5196153315578084303)
XLA Ops:
  7.2 0.0 copy-start
  7.2 0.0 copy-start.2
  7.2 0.0 all-gather.3.cloned.1.call-start
  7.2 1.5 pad_maximum_fusion.5
  8.8 0.0 all-gather.3.cloned.1.call-update
  8.8 0.7 reshape.1049
  9.5 0.6 reduce-window.6
  10.1 0.2 slice_reduce_fusion
  10.4 0.1 copy.46
  10.5 0.1 broadcast.153
  10.6 0.3 slice_reduce_fusion.1
  10.9 1.3 copy.43
  12.1 1.3 multiply_bitcast_fusion
  13.5 0.1 fusion.16
  13.6 1.1 convolution_convert_fusion
  14.8 1.3 collective-permute-start.1
  16.1 1.9 %collective-permute-start = (bf16[1,1040,128]{2,1,0:T(8,128)(2,1)S(1)}, bf16[1,1040,128]{2,1,0:T(8,128)(2,1)S(1)}, u32[]{:S(2)}, u32[]{:S(2)}) collective-permute-start(bf16[1,1040,128]{2,1,0:T(8,128)(2,1)S(1)} %pad_maximum_fusion), channel_id=1, source_target_pairs={{0,8},{8,16},{16,24},{24,32},{32,40},{40,48},{48,56},{56,64},{64,7... | collective-permute-start | bytes 798728 | tf_op jit(solution)/shard_map/ppermute | solution.py:89
  18.0 9.5 %collective-permute-done.1 = bf16[1,1040,128]{2,1,0:T(8,128)(2,1)S(1)} collective-permute-done((bf16[1,1040,128]{2,1,0:T(8,128)(2,1)S(1)}, bf16[1,1040,128]{2,1,0:T(8,128)(2,1)S(1)}, u32[]{:S(2)}, u32[]{:S(2)}) %collective-permute-start.1) | collective-permute-done | bytes 266272 | tf_op jit(solution)/shard_map/ppermute | solution.py:89
  27.5 3.6 %collective-permute-done = bf16[1,1040,128]{2,1,0:T(8,128)(2,1)S(1)} collective-permute-done((bf16[1,1040,128]{2,1,0:T(8,128)(2,1)S(1)}, bf16[1,1040,128]{2,1,0:T(8,128)(2,1)S(1)}, u32[]{:S(2)}, u32[]{:S(2)}) %collective-permute-start) | collective-permute-done | bytes 266272 | tf_op jit(solution)/shard_map/ppermute | solution.py:89
  31.2 0.1 mul.237
  31.3 0.1 mul.238
  31.4 0.2 fusion.19
  31.6 1.3 collective-permute-start.2
  32.9 0.9 fusion.74
  33.8 0.1 mul.241
  33.9 0.1 mul.242
  33.9 9.4 %collective-permute-done.2 = bf16[1,1040,128]{2,1,0:T(8,128)(2,1)S(1)} collective-permute-done((bf16[1,1040,128]{2,1,0:T(8,128)(2,1)S(1)}, bf16[1,1040,128]{2,1,0:T(8,128)(2,1)S(1)}, u32[]{:S(2)}, u32[]{:S(2)}) %collective-permute-start.2) | collective-permute-done | bytes 266272 | tf_op jit(solution)/shard_map/ppermute | solution.py:89
  43.4 0.3 fusion.73
  43.8 1.3 collective-permute-start.3
  45.1 0.6 iota_compare_fusion
  45.8 0.1 mul.245
  45.9 0.1 mul.246
  46.0 10.2 %collective-permute-done.3 = bf16[1,1040,128]{2,1,0:T(8,128)(2,1)S(1)} collective-permute-done((bf16[1,1040,128]{2,1,0:T(8,128)(2,1)S(1)}, bf16[1,1040,128]{2,1,0:T(8,128)(2,1)S(1)}, u32[]{:S(2)}, u32[]{:S(2)}) %collective-permute-start.3) | collective-permute-done | bytes 266272 | tf_op jit(solution)/shard_map/ppermute | solution.py:89
  56.2 0.5 fusion.20
  56.7 0.7 pad_maximum_fusion.3
  57.4 1.3 collective-permute-start.4
  58.8 0.1 mul.250
  58.9 0.1 mul.251
  59.0 8.2 %collective-permute-done.4 = bf16[1,1040,128]{2,1,0:T(8,128)(2,1)S(1)} collective-permute-done((bf16[1,1040,128]{2,1,0:T(8,128)(2,1)}, bf16[1,1040,128]{2,1,0:T(8,128)(2,1)S(1)}, u32[]{:S(2)}, u32[]{:S(2)}) %collective-permute-start.4) | collective-permute-done | bytes 266272 | tf_op jit(solution)/shard_map/ppermute | solution.py:89
  67.2 0.9 add_convert_fusion
  68.1 1.3 collective-permute-start.5
  69.5 13.9 %collective-permute-done.5 = bf16[1,1040,128]{2,1,0:T(8,128)(2,1)S(1)} collective-permute-done((bf16[1,1040,128]{2,1,0:T(8,128)(2,1)S(1)}, bf16[1,1040,128]{2,1,0:T(8,128)(2,1)S(1)}, u32[]{:S(2)}, u32[]{:S(2)}) %collective-permute-start.5) | collective-permute-done | bytes 266272 | tf_op jit(solution)/shard_map/ppermute | solution.py:89
  83.4 1.0 fusion.17
  84.4 0.0 all-gather.3.cloned.1.call-done
  84.4 0.6 fusion.9
  85.0 0.0 copy-start.1
  85.1 3.4 %fusion.11 = f32[256,1,16,64]{0,3,2,1:T(8,128)} fusion(f32[256,1,16,64]{0,3,2,1:T(8,128)S(1)} %fusion.9, bf16[256,16,64]{0,2,1:T(8,128)(2,1)S(1)} %bitcast.118, f32[16,256]{1,0:T(8,128)S(1)} %copy-done.3, f32[16,256]{1,0:T(8,128)} %get-tuple-element.18, f32[256,256]{1,0:T(8,128)} %fusion.74, pred[256,256]{1,0:T(8,128)(4,1)} %iota_compare_fusion, ...), kind=kOutput, calls=%fused_computation.13 | convolution fusion | flops 141557760 | bytes 3506240 | tf_op jit(solution)/shard_map/ghts,sghp->tghp/dot_general | solution.py:172
  88.5 1.6 copy.50
  90.1 0.4 multiply_reduce_fusion
  90.5 10.0 %collective-permute-start.10 = (f32[256]{0:T(256)S(1)}, f32[256]{0:T(256)S(1)}, u32[]{:S(2)}, u32[]{:S(2)}) collective-permute-start(f32[256]{0:T(256)S(1)} %multiply_reduce_fusion), channel_id=1, source_target_pairs={{0,5},{1,6},{2,7},{3,0},{4,1},{5,2},{6,3},{7,4},{8,13},{9,14},{10,... | collective-permute-start | bytes 3080 | tf_op jit(solution)/shard_map/ppermute | solution.py:97
  100.5 0.8 collective-permute-start.11
  101.3 1.1 copy.52
  102.5 0.6 copy.42
  103.1 0.9 copy.53
  104.0 0.8 collective-permute-start.12
  104.8 1.6 collective-permute-start.6
  106.4 7.0 %collective-permute-start.7 = (f32[256]{0:T(256)S(1)}, f32[256]{0:T(256)S(1)}, u32[]{:S(2)}, u32[]{:S(2)}) collective-permute-start(f32[256]{0:T(256)S(1)} %multiply_reduce_fusion), channel_id=1, source_target_pairs={{0,2},{1,3},{2,4},{3,5},{4,6},{5,7},{6,0},{7,1},{8,10},{9,11},{10,... | collective-permute-start | bytes 3080 | tf_op jit(solution)/shard_map/ppermute | solution.py:97
  113.5 0.7 collective-permute-start.8
  114.2 7.1 %collective-permute-start.9 = (f32[256]{0:T(256)S(1)}, f32[256]{0:T(256)S(1)}, u32[]{:S(2)}, u32[]{:S(2)}) collective-permute-start(f32[256]{0:T(256)S(1)} %multiply_reduce_fusion), channel_id=1, source_target_pairs={{0,4},{1,5},{2,6},{3,7},{4,0},{5,1},{6,2},{7,3},{8,12},{9,13},{10,... | collective-permute-start | bytes 3080 | tf_op jit(solution)/shard_map/ppermute | solution.py:97
  121.3 39.6 %shard_map.122 = bf16[128,2048]{1,0:T(8,128)(2,1)} custom-call(s32[1]{0:T(128)} %bitcast.pos_ref, bf16[128,2048]{1,0:T(8,128)(2,1)} %bitcast.130, bf16[32,2,256,128]{3,2,1,0:T(8,128)(2,1)} %bitcast.140), custom_call_target="tpu_custom_call" | custom-call | flops 8589934592 | bytes 5242880 | tf_op jit(solution)/shard_map/pallas_call | solution.py:65
  161.0 1.1 copy.56
  162.1 0.6 copy.48
  162.7 0.9 copy.64
  163.6 1.2 multiply_convert_fusion
  (57 shorter events, 0.6 us)
Async XLA Ops:
  7.2 25.7 %copy-start = (bf16[256,128]{1,0:T(8,128)(2,1)S(1)}, bf16[256,128]{1,0:T(8,128)(2,1)}, u32[]{:S(2)}) copy-start(bf16[256,128]{1,0:T(8,128)(2,1)} %param.17) | copy-start | bytes 196612
  7.2 25.7 %copy-start.2 = (bf16[256,128]{1,0:T(8,128)(2,1)S(1)}, bf16[256,128]{1,0:T(8,128)(2,1)}, u32[]{:S(2)}) copy-start(bf16[256,128]{1,0:T(8,128)(2,1)} %param.16) | copy-start | bytes 196612
  7.2 77.2 %all-gather.3.cloned.1.call-start = ((), (), s32[]{:S(2)}) async-start(), calls=%async_computation | async-start | bytes 4325376 | tf_op jit(solution)/shard_map/all_gather | solution.py:156
  14.8 12.7 %collective-permute-start.1 = (bf16[1,1040,128]{2,1,0:T(8,128)(2,1)S(1)}, bf16[1,1040,128]{2,1,0:T(8,128)(2,1)S(1)}, u32[]{:S(2)}, u32[]{:S(2)}) collective-permute-start(bf16[1,1040,128]{2,1,0:T(8,128)(2,1)S(1)} %pad_maximum_fusion), channel_id=1, source_target_pairs={{0,16},{8,24},{16,32},{24,40},{32,48},{40,56},{48,64},{56,72},{64,... | collective-permute-start | bytes 798728 | tf_op jit(solution)/shard_map/ppermute | solution.py:89
  16.1 15.1 %collective-permute-start = (bf16[1,1040,128]{2,1,0:T(8,128)(2,1)S(1)}, bf16[1,1040,128]{2,1,0:T(8,128)(2,1)S(1)}, u32[]{:S(2)}, u32[]{:S(2)}) collective-permute-start(bf16[1,1040,128]{2,1,0:T(8,128)(2,1)S(1)} %pad_maximum_fusion), channel_id=1, source_target_pairs={{0,8},{8,16},{16,24},{24,32},{32,40},{40,48},{48,56},{56,64},{64,7... | collective-permute-start | bytes 798728 | tf_op jit(solution)/shard_map/ppermute | solution.py:89
  31.2 14.6 %copy-start.4 = (f32[16]{0:T(128)}, f32[16]{0:T(128)S(1)}, u32[]{:S(2)}) copy-start(f32[16]{0:T(128)S(1)} %exponential_bitcast_fusion.5) | copy-start | bytes 196
  31.6 11.8 %collective-permute-start.2 = (bf16[1,1040,128]{2,1,0:T(8,128)(2,1)S(1)}, bf16[1,1040,128]{2,1,0:T(8,128)(2,1)S(1)}, u32[]{:S(2)}, u32[]{:S(2)}) collective-permute-start(bf16[1,1040,128]{2,1,0:T(8,128)(2,1)S(1)} %pad_maximum_fusion.1), channel_id=1, source_target_pairs={{0,16},{8,24},{16,32},{24,40},{32,48},{40,56},{48,64},{56,72},{64,... | collective-permute-start | bytes 798728 | tf_op jit(solution)/shard_map/ppermute | solution.py:89
  43.8 12.4 %collective-permute-start.3 = (bf16[1,1040,128]{2,1,0:T(8,128)(2,1)S(1)}, bf16[1,1040,128]{2,1,0:T(8,128)(2,1)S(1)}, u32[]{:S(2)}, u32[]{:S(2)}) collective-permute-start(bf16[1,1040,128]{2,1,0:T(8,128)(2,1)S(1)} %pad_maximum_fusion.2), channel_id=1, source_target_pairs={{0,32},{8,40},{16,48},{24,56},{32,64},{40,72},{48,80},{56,88},{64,... | collective-permute-start | bytes 798728 | tf_op jit(solution)/shard_map/ppermute | solution.py:89
  57.4 9.7 %collective-permute-start.4 = (bf16[1,1040,128]{2,1,0:T(8,128)(2,1)}, bf16[1,1040,128]{2,1,0:T(8,128)(2,1)S(1)}, u32[]{:S(2)}, u32[]{:S(2)}) collective-permute-start(bf16[1,1040,128]{2,1,0:T(8,128)(2,1)} %pad_maximum_fusion.3), channel_id=1, source_target_pairs={{0,64},{8,72},{16,80},{24,88},{32,96},{40,104},{48,112},{56,120},{... | collective-permute-start | bytes 798728 | tf_op jit(solution)/shard_map/ppermute | solution.py:89
  68.1 16.9 %copy-start.3 = (f32[16,256]{1,0:T(8,128)S(1)}, f32[16,256]{1,0:T(8,128)}, u32[]{:S(2)}) copy-start(f32[16,256]{1,0:T(8,128)} %param.18) | copy-start | bytes 49156
  68.1 16.9 %copy-start.6 = (f32[16]{0:T(128)S(1)}, f32[16]{0:T(128)}, u32[]{:S(2)}) copy-start(f32[16]{0:T(128)} %param.20) | copy-start | bytes 196
  68.1 15.3 %collective-permute-start.5 = (bf16[1,1040,128]{2,1,0:T(8,128)(2,1)S(1)}, bf16[1,1040,128]{2,1,0:T(8,128)(2,1)S(1)}, u32[]{:S(2)}, u32[]{:S(2)}) collective-permute-start(bf16[1,1040,128]{2,1,0:T(8,128)(2,1)S(1)} %pad_maximum_fusion.4), channel_id=1, source_target_pairs={{0,128},{8,136},{16,144},{24,152},{32,160},{40,168},{48,176},{56,1... | collective-permute-start | bytes 798728 | tf_op jit(solution)/shard_map/ppermute | solution.py:89
  85.0 5.0 %copy-start.1 = (bf16[256,1024]{1,0:T(8,128)(2,1)S(1)}, bf16[256,1024]{1,0:T(8,128)(2,1)}, u32[]{:S(2)}) copy-start(bf16[256,1024]{1,0:T(8,128)(2,1)} %param.15) | copy-start | bytes 1572868
  85.0 16.3 %copy-start.5 = (bf16[1024]{0:T(1024)(128)(2,1)S(1)}, bf16[1024]{0:T(1024)(128)(2,1)}, u32[]{:S(2)}) copy-start(bf16[1024]{0:T(1024)(128)(2,1)} %param.21) | copy-start | bytes 6148
  90.5 23.0 %collective-permute-start.10 = (f32[256]{0:T(256)S(1)}, f32[256]{0:T(256)S(1)}, u32[]{:S(2)}, u32[]{:S(2)}) collective-permute-start(f32[256]{0:T(256)S(1)} %multiply_reduce_fusion), channel_id=1, source_target_pairs={{0,5},{1,6},{2,7},{3,0},{4,1},{5,2},{6,3},{7,4},{8,13},{9,14},{10,... | collective-permute-start | bytes 3080 | tf_op jit(solution)/shard_map/ppermute | solution.py:97
  100.5 13.7 %collective-permute-start.11 = (f32[256]{0:T(256)S(1)}, f32[256]{0:T(256)S(1)}, u32[]{:S(2)}, u32[]{:S(2)}) collective-permute-start(f32[256]{0:T(256)S(1)} %multiply_reduce_fusion), channel_id=1, source_target_pairs={{0,6},{1,7},{2,0},{3,1},{4,2},{5,3},{6,4},{7,5},{8,14},{9,15},{10,... | collective-permute-start | bytes 3080 | tf_op jit(solution)/shard_map/ppermute | solution.py:97
  104.0 59.6 %collective-permute-start.12 = (f32[256]{0:T(256)S(1)}, f32[256]{0:T(256)S(1)}, u32[]{:S(2)}, u32[]{:S(2)}) collective-permute-start(f32[256]{0:T(256)S(1)} %multiply_reduce_fusion), channel_id=1, source_target_pairs={{0,7},{1,0},{2,1},{3,2},{4,3},{5,4},{6,5},{7,6},{8,15},{9,8},{10,9... | collective-permute-start | bytes 3080 | tf_op jit(solution)/shard_map/ppermute | solution.py:97
  104.8 58.8 %collective-permute-start.6 = (f32[256]{0:T(256)S(1)}, f32[256]{0:T(256)S(1)}, u32[]{:S(2)}, u32[]{:S(2)}) collective-permute-start(f32[256]{0:T(256)S(1)} %multiply_reduce_fusion), channel_id=1, source_target_pairs={{0,1},{1,2},{2,3},{3,4},{4,5},{5,6},{6,7},{7,0},{8,9},{9,10},{10,1... | collective-permute-start | bytes 3080 | tf_op jit(solution)/shard_map/ppermute | solution.py:97
  106.4 57.2 %collective-permute-start.7 = (f32[256]{0:T(256)S(1)}, f32[256]{0:T(256)S(1)}, u32[]{:S(2)}, u32[]{:S(2)}) collective-permute-start(f32[256]{0:T(256)S(1)} %multiply_reduce_fusion), channel_id=1, source_target_pairs={{0,2},{1,3},{2,4},{3,5},{4,6},{5,7},{6,0},{7,1},{8,10},{9,11},{10,... | collective-permute-start | bytes 3080 | tf_op jit(solution)/shard_map/ppermute | solution.py:97
  113.5 50.1 %collective-permute-start.8 = (f32[256]{0:T(256)S(1)}, f32[256]{0:T(256)S(1)}, u32[]{:S(2)}, u32[]{:S(2)}) collective-permute-start(f32[256]{0:T(256)S(1)} %multiply_reduce_fusion), channel_id=1, source_target_pairs={{0,3},{1,4},{2,5},{3,6},{4,7},{5,0},{6,1},{7,2},{8,11},{9,12},{10,... | collective-permute-start | bytes 3080 | tf_op jit(solution)/shard_map/ppermute | solution.py:97
  114.2 49.4 %collective-permute-start.9 = (f32[256]{0:T(256)S(1)}, f32[256]{0:T(256)S(1)}, u32[]{:S(2)}, u32[]{:S(2)}) collective-permute-start(f32[256]{0:T(256)S(1)} %multiply_reduce_fusion), channel_id=1, source_target_pairs={{0,4},{1,5},{2,6},{3,7},{4,0},{5,1},{6,2},{7,3},{8,12},{9,13},{10,... | collective-permute-start | bytes 3080 | tf_op jit(solution)/shard_map/ppermute | solution.py:97
Sparse Core Ops, SparseCore 0:
  9.9 72.4 all-gather.2

commit v8 on v7

--- a/solution.py
+++ b/solution.py
@@ -89,13 +89,8 @@
     return lax.ppermute(block, axis, route)
 
 
-def summed_over(part, axis):
-    count = lax.axis_size(axis)
-    total = part
-    for distance in range(1, count):
-        route = [(i, (i + distance) % count) for i in range(count)]
-        total = total + lax.ppermute(part, axis, route)
-    return total
+def padded(part, width=16384):
+    return jnp.zeros((width,), part.dtype).at[: part.shape[0]].set(part)
 
 
 def packed(state, log_span):
@@ -179,8 +174,6 @@
 
     incoming = carried_scan(local_state, block_log_decay, position, ctx_count)
 
-    incoming, gathered_kv = lax.optimization_barrier((incoming, gathered_kv))
-    attention_out = causal_attention(position, queries, gathered_kv)
 
     carried_out = jnp.einsum(
         "ghpn,tgn->tghp", incoming, out_maps.astype(jnp.float32), precision=lax.Precision.HIGHEST
@@ -191,7 +184,11 @@
     )
     outputs = (inner + carried_out + direct).reshape(tok_rows, -1)
     gated = outputs * jax.nn.silu(gate_input.astype(jnp.float32))
-    square_total = summed_over(jnp.sum(gated * gated, axis=-1), "tp")
+    square_parts, gathered_kv = lax.optimization_barrier(
+        (padded(jnp.sum(gated * gated, axis=-1)), gathered_kv)
+    )
+    square_total = lax.psum(square_parts, "tp")[:tok_rows]
+    attention_out = causal_attention(position, queries, gathered_kv)
     scaling = lax.rsqrt(square_total / (STATE_HEADS * P_SIZE) + 1e-05)
     mixer_out = (gated * scaling[:, None] * norm_gain.astype(jnp.float32)).astype(jnp.bfloat16)
     return (attention_out, mixer_out)

time: 172 us -> 211 us (1.23)
  the two profiles are of different devices: /device:TPU:118 before, /device:TPU:2 now
where the time goes in v8:
time: 211 us; the launch traced here: 210 us
  waiting for transfers between devices  147 us (70%)
  between operations  14.4 us (7%)
  Pallas kernels  13.7 us (6%)
  starting transfers between devices  13.6 us (6%)
  other arithmetic  9.43 us (4%)
  local copies, waits for them, and re-layouts  8.53 us (4%)
  matrix products  3.35 us (2%)
    psum x1, waiting for transfers between devices, local(): square_total = lax.psum(square_parts, 'tp')[:tok_rows]  94.5 us
    ppermute x6, waiting for transfers between devices, shifted(): return lax.ppermute(block, axis, route)  52.3 us
    pallas_call x1, Pallas kernels, causal_attention(): pl.pallas_call(kernel, in_specs=[pl.BlockSpec(memory_space=pltpu.SMEM)] +...  13.7 us
    ppermute x6, starting transfers between devices, shifted(): return lax.ppermute(block, axis, route)  13.5 us
    unnamed x20, local copies, waits for them, and re-layouts  4.35 us
  transfers between devices with their start and end apart: 8, of which 7 were waited for; matrix products, arithmetic and copies ran while one was open for 9% of the time, Pallas kernels for 7%

profile of v8, /device:TPU:2, one launch (start us, length us, event | category | flops | bytes accessed | tf_op | source)
XLA Modules:
  0.0 209.9 jit_solution(5933463591744921047)
XLA Ops:
  7.2 0.0 copy-start
  7.2 0.0 all-gather.3.cloned.1.call-start
  7.2 1.5 pad_maximum_fusion.5
  8.8 0.0 all-gather.3.cloned.1.call-update
  8.8 0.0 all-reduce.8.cloned.1.call-start
  8.8 0.7 reshape.985
  9.6 0.6 reduce-window.6
  10.2 0.2 slice_reduce_fusion
  10.4 0.1 copy.45
  10.5 0.1 broadcast.155
  10.6 0.3 slice_reduce_fusion.1
  10.9 1.3 copy.46
  12.2 0.8 multiply_bitcast_fusion
  13.0 0.1 fusion.16
  13.1 0.0 copy-start.5
  13.1 0.0 copy-start.2
  13.1 1.2 convolution_convert_fusion
  14.3 3.8 %collective-permute-start.1 = (bf16[1,1040,128]{2,1,0:T(8,128)(2,1)S(1)}, bf16[1,1040,128]{2,1,0:T(8,128)(2,1)S(1)}, u32[]{:S(2)}, u32[]{:S(2)}) collective-permute-start(bf16[1,1040,128]{2,1,0:T(8,128)(2,1)S(1)} %pad_maximum_fusion), channel_id=1, source_target_pairs={{0,16},{8,24},{16,32},{24,40},{32,48},{40,56},{48,64},{56,72},{64,... | collective-permute-start | bytes 798728 | tf_op jit(solution)/shard_map/ppermute | solution.py:89
  18.2 1.9 collective-permute-start
  20.1 8.2 %collective-permute-done.1 = bf16[1,1040,128]{2,1,0:T(8,128)(2,1)S(1)} collective-permute-done((bf16[1,1040,128]{2,1,0:T(8,128)(2,1)S(1)}, bf16[1,1040,128]{2,1,0:T(8,128)(2,1)S(1)}, u32[]{:S(2)}, u32[]{:S(2)}) %collective-permute-start.1) | collective-permute-done | bytes 266272 | tf_op jit(solution)/shard_map/ppermute | solution.py:89
  28.3 3.1 %collective-permute-done = bf16[1,1040,128]{2,1,0:T(8,128)(2,1)S(1)} collective-permute-done((bf16[1,1040,128]{2,1,0:T(8,128)(2,1)S(1)}, bf16[1,1040,128]{2,1,0:T(8,128)(2,1)S(1)}, u32[]{:S(2)}, u32[]{:S(2)}) %collective-permute-start) | collective-permute-done | bytes 266272 | tf_op jit(solution)/shard_map/ppermute | solution.py:89
  31.5 0.1 mul.209
  31.6 0.1 mul.210
  31.7 0.2 fusion.17
  31.9 1.9 collective-permute-start.2
  33.9 0.1 mul.213
  33.9 0.1 mul.214
  34.0 10.9 %collective-permute-done.2 = bf16[1,1040,128]{2,1,0:T(8,128)(2,1)S(1)} collective-permute-done((bf16[1,1040,128]{2,1,0:T(8,128)(2,1)S(1)}, bf16[1,1040,128]{2,1,0:T(8,128)(2,1)S(1)}, u32[]{:S(2)}, u32[]{:S(2)}) %collective-permute-start.2) | collective-permute-done | bytes 266272 | tf_op jit(solution)/shard_map/ppermute | solution.py:89
  45.0 0.3 fusion.74
  45.3 0.0 copy-start.3
  45.3 1.9 collective-permute-start.3
  47.3 0.1 mul.217
  47.3 0.1 mul.218
  47.4 14.8 %collective-permute-done.3 = bf16[1,1040,128]{2,1,0:T(8,128)(2,1)S(1)} collective-permute-done((bf16[1,1040,128]{2,1,0:T(8,128)(2,1)S(1)}, bf16[1,1040,128]{2,1,0:T(8,128)(2,1)S(1)}, u32[]{:S(2)}, u32[]{:S(2)}) %collective-permute-start.3) | collective-permute-done | bytes 266272 | tf_op jit(solution)/shard_map/ppermute | solution.py:89
  62.3 0.5 fusion.18
  62.8 1.9 collective-permute-start.4
  64.7 0.1 mul.224
  64.8 0.1 mul.225
  64.8 12.1 %collective-permute-done.4 = bf16[1,1040,128]{2,1,0:T(8,128)(2,1)S(1)} collective-permute-done((bf16[1,1040,128]{2,1,0:T(8,128)(2,1)S(1)}, bf16[1,1040,128]{2,1,0:T(8,128)(2,1)S(1)}, u32[]{:S(2)}, u32[]{:S(2)}) %collective-permute-start.4) | collective-permute-done | bytes 266272 | tf_op jit(solution)/shard_map/ppermute | solution.py:89
  77.0 0.9 fusion.73
  77.9 0.0 copy-start.4
  78.0 2.0 collective-permute-start.5
  80.0 0.1 copy.52
  80.1 0.6 copy.42
  80.7 0.9 copy.53
  81.6 0.2 fusion.75
  81.8 0.1 mul.221
  81.9 0.1 mul.222
  82.0 3.0 %collective-permute-done.5 = bf16[1,1040,128]{2,1,0:T(8,128)(2,1)} collective-permute-done((bf16[1,1040,128]{2,1,0:T(8,128)(2,1)S(1)}, bf16[1,1040,128]{2,1,0:T(8,128)(2,1)}, u32[]{:S(2)}, u32[]{:S(2)}) %collective-permute-start.5) | collective-permute-done | bytes 266272 | tf_op jit(solution)/shard_map/ppermute | solution.py:89
  85.0 1.9 multiply_add_fusion
  86.9 0.6 fusion.9
  87.5 0.0 copy-start.1
  87.5 1.4 fusion.11
  88.9 0.3 copy.49
  89.2 0.4 multiply_reduce_fusion
  89.6 0.6 scatter.4
  90.3 0.0 all-reduce.8.cloned.1.call-update
  90.3 13.7 %shard_map.122 = bf16[128,2048]{1,0:T(8,128)(2,1)} custom-call(s32[1]{0:T(128)} %bitcast.pos_ref, bf16[128,2048]{1,0:T(8,128)(2,1)} %bitcast.116, bf16[32,2,256,128]{3,2,1,0:T(8,128)(2,1)} %bitcast.127), custom_call_target="tpu_custom_call" | custom-call | flops 8589934592 | bytes 5242880 | tf_op jit(solution)/shard_map/pallas_call | solution.py:65
  104.0 1.1 copy.56
  105.2 0.6 copy.50
  105.8 0.9 copy.64
  106.7 94.5 %all-reduce.8.cloned.1.call-done = f32[16384]{0:T(1024)} async-done(((f32[16384]{0:T(1024)}), f32[16384]{0:T(1024)}) %all-reduce.8.cloned.1.call-update) | async-done | bytes 65552 | tf_op jit(solution)/shard_map/psum | solution.py:190
  201.2 0.7 fusion.63
  201.9 1.2 multiply_convert_fusion
  (43 shorter events, 0.4 us)
Async XLA Ops:
  7.2 74.5 %copy-start = (bf16[256,128]{1,0:T(8,128)(2,1)S(1)}, bf16[256,128]{1,0:T(8,128)(2,1)}, u32[]{:S(2)}) copy-start(bf16[256,128]{1,0:T(8,128)(2,1)} %param.19) | copy-start | bytes 196612
  7.2 83.1 %all-gather.3.cloned.1.call-start = ((), (), s32[]{:S(2)}) async-start(), calls=%async_computation.1 | async-start | bytes 4325376 | tf_op jit(solution)/shard_map/all_gather | solution.py:151
  8.8 192.4 %all-reduce.8.cloned.1.call-start = ((), (), s32[]{:S(2)}) async-start(), calls=%async_computation | async-start | bytes 131072 | tf_op jit(solution)/shard_map/psum | solution.py:190
  13.1 66.9 %copy-start.5 = (bf16[1024]{0:T(1024)(128)(2,1)S(1)}, bf16[1024]{0:T(1024)(128)(2,1)}, u32[]{:S(2)}) copy-start(bf16[1024]{0:T(1024)(128)(2,1)} %param.23) | copy-start | bytes 6148
  13.1 66.9 %copy-start.2 = (bf16[256,1024]{1,0:T(8,128)(2,1)S(1)}, bf16[256,1024]{1,0:T(8,128)(2,1)}, u32[]{:S(2)}) copy-start(bf16[256,1024]{1,0:T(8,128)(2,1)} %param.13) | copy-start | bytes 1572868
  14.3 14.0 %collective-permute-start.1 = (bf16[1,1040,128]{2,1,0:T(8,128)(2,1)S(1)}, bf16[1,1040,128]{2,1,0:T(8,128)(2,1)S(1)}, u32[]{:S(2)}, u32[]{:S(2)}) collective-permute-start(bf16[1,1040,128]{2,1,0:T(8,128)(2,1)S(1)} %pad_maximum_fusion), channel_id=1, source_target_pairs={{0,16},{8,24},{16,32},{24,40},{32,48},{40,56},{48,64},{56,72},{64,... | collective-permute-start | bytes 798728 | tf_op jit(solution)/shard_map/ppermute | solution.py:89
  18.2 13.3 %collective-permute-start = (bf16[1,1040,128]{2,1,0:T(8,128)(2,1)S(1)}, bf16[1,1040,128]{2,1,0:T(8,128)(2,1)S(1)}, u32[]{:S(2)}, u32[]{:S(2)}) collective-permute-start(bf16[1,1040,128]{2,1,0:T(8,128)(2,1)S(1)} %pad_maximum_fusion), channel_id=1, source_target_pairs={{0,8},{8,16},{16,24},{24,32},{32,40},{40,48},{48,56},{56,64},{64,7... | collective-permute-start | bytes 798728 | tf_op jit(solution)/shard_map/ppermute | solution.py:89
  31.9 13.0 %collective-permute-start.2 = (bf16[1,1040,128]{2,1,0:T(8,128)(2,1)S(1)}, bf16[1,1040,128]{2,1,0:T(8,128)(2,1)S(1)}, u32[]{:S(2)}, u32[]{:S(2)}) collective-permute-start(bf16[1,1040,128]{2,1,0:T(8,128)(2,1)S(1)} %pad_maximum_fusion.1), channel_id=1, source_target_pairs={{0,16},{8,24},{16,32},{24,40},{32,48},{40,56},{48,64},{56,72},{64,... | collective-permute-start | bytes 798728 | tf_op jit(solution)/shard_map/ppermute | solution.py:89
  45.3 36.3 %copy-start.3 = (bf16[256,128]{1,0:T(8,128)(2,1)S(1)}, bf16[256,128]{1,0:T(8,128)(2,1)}, u32[]{:S(2)}) copy-start(bf16[256,128]{1,0:T(8,128)(2,1)} %param.18) | copy-start | bytes 196612
  45.3 16.9 %collective-permute-start.3 = (bf16[1,1040,128]{2,1,0:T(8,128)(2,1)S(1)}, bf16[1,1040,128]{2,1,0:T(8,128)(2,1)S(1)}, u32[]{:S(2)}, u32[]{:S(2)}) collective-permute-start(bf16[1,1040,128]{2,1,0:T(8,128)(2,1)S(1)} %pad_maximum_fusion.2), channel_id=1, source_target_pairs={{0,32},{8,40},{16,48},{24,56},{32,64},{40,72},{48,80},{56,88},{64,... | collective-permute-start | bytes 798728 | tf_op jit(solution)/shard_map/ppermute | solution.py:89
  62.8 14.2 %collective-permute-start.4 = (bf16[1,1040,128]{2,1,0:T(8,128)(2,1)S(1)}, bf16[1,1040,128]{2,1,0:T(8,128)(2,1)S(1)}, u32[]{:S(2)}, u32[]{:S(2)}) collective-permute-start(bf16[1,1040,128]{2,1,0:T(8,128)(2,1)S(1)} %pad_maximum_fusion.3), channel_id=1, source_target_pairs={{0,64},{8,72},{16,80},{24,88},{32,96},{40,104},{48,112},{56,120},{... | collective-permute-start | bytes 798728 | tf_op jit(solution)/shard_map/ppermute | solution.py:89
  77.9 9.5 %copy-start.4 = (f32[16,256]{1,0:T(8,128)S(1)}, f32[16,256]{1,0:T(8,128)}, u32[]{:S(2)}) copy-start(f32[16,256]{1,0:T(8,128)} %param.20) | copy-start | bytes 49156
  77.9 9.5 %copy-start.6 = (f32[16]{0:T(128)S(1)}, f32[16]{0:T(128)}, u32[]{:S(2)}) copy-start(f32[16]{0:T(128)} %param.22) | copy-start | bytes 196
  78.0 7.0 %collective-permute-start.5 = (bf16[1,1040,128]{2,1,0:T(8,128)(2,1)S(1)}, bf16[1,1040,128]{2,1,0:T(8,128)(2,1)}, u32[]{:S(2)}, u32[]{:S(2)}) collective-permute-start(bf16[1,1040,128]{2,1,0:T(8,128)(2,1)S(1)} %pad_maximum_fusion.4), channel_id=1, source_target_pairs={{0,128},{8,136},{16,144},{24,152},{32,160},{40,168},{48,176},{56,1... | collective-permute-start | bytes 798728 | tf_op jit(solution)/shard_map/ppermute | solution.py:89
  87.5 1.8 copy-start.1
Sparse Core Ops, SparseCore 0:
  10.4 75.1 all-gather.2
  90.4 110.7 all-reduce.7

commit v9 on v4

--- a/solution.py
+++ b/solution.py
@@ -14,6 +14,7 @@
 
 
 causal_score = -1e30
+CTX = ("chip", "core")
 
 
 def attend_kernel(pos_ref, qt_ref, kv_ref, o_ref, p_sc, m_sc, l_sc, c_sc, acc_sc, *, tok, width, chunk):
@@ -116,21 +117,51 @@
     return state, (parts[:, 0] + parts[:, 1]) + parts[:, 2]
 
 
-def carried_scan(local_state, block_log_decay, position, ctx_count):
+def carried_scan(local_state, block_log_decay, axis, count):
     sent = packed(local_state, block_log_decay)
-    one_back_state, one_back_decay = unpacked(shifted(sent, "ctx", 1), local_state.shape)
-    two_back_state, two_back_decay = unpacked(shifted(sent, "ctx", 2), local_state.shape)
+    one_back_state, one_back_decay = unpacked(shifted(sent, axis, 1), local_state.shape)
+    two_back_state, two_back_decay = unpacked(shifted(sent, axis, 2), local_state.shape)
     state = jnp.exp(one_back_decay)[..., None, None] * two_back_state + one_back_state
     log_span = one_back_decay + two_back_decay
     distance = 2
-    while distance < ctx_count:
+    while distance < count:
         earlier_state, earlier_span = unpacked(
-            shifted(packed(state, log_span), "ctx", distance), local_state.shape
+            shifted(packed(state, log_span), axis, distance), local_state.shape
         )
         state = jnp.exp(log_span)[..., None, None] * earlier_state + state
         log_span = log_span + earlier_span
         distance *= 2
     return state
+
+
+def chip_carried_scan(local_state, block_log_decay):
+    core = lax.axis_index("core")
+    swap = [(0, 1), (1, 0)]
+    sent = packed(local_state, block_log_decay)
+    own_state, own_decay = unpacked(sent, local_state.shape)
+    mate_state, mate_decay = unpacked(lax.ppermute(sent, "core", swap), local_state.shape)
+    first_state = jnp.where(core == 0, own_state, mate_state)
+    first_decay = jnp.where(core == 0, own_decay, mate_decay)
+    second_state = jnp.where(core == 0, mate_state, own_state)
+    second_decay = jnp.where(core == 0, mate_decay, own_decay)
+    chip_state = jnp.exp(second_decay)[..., None, None] * first_state + second_state
+    chip_decay = first_decay + second_decay
+    half = local_state.shape[1] // 2
+    chip_prefix = carried_scan(
+        lax.dynamic_slice_in_dim(chip_state, core * half, half, axis=1),
+        lax.dynamic_slice_in_dim(chip_decay, core * half, half, axis=1),
+        "chip",
+        lax.axis_size("chip"),
+    )
+    other_prefix = lax.ppermute(chip_prefix.astype(jnp.bfloat16), "core", swap).astype(jnp.float32)
+    prefix = jnp.where(
+        core == 0,
+        jnp.concatenate((chip_prefix, other_prefix), axis=1),
+        jnp.concatenate((other_prefix, chip_prefix), axis=1),
+    )
+    return jnp.where(
+        core == 0, prefix, jnp.exp(first_decay)[..., None, None] * prefix + first_state
+    )
 
 
 def local(
@@ -147,10 +178,9 @@
     norm_gain,
 ):
     tok_rows = queries.shape[0]
-    ctx_count = lax.axis_size("ctx")
-    position = lax.axis_index("ctx")
-
-    gathered_kv = lax.all_gather(jnp.stack((key_rows, value_head_rows)), "ctx")
+    position = lax.axis_index(CTX)
+
+    gathered_kv = lax.all_gather(jnp.stack((key_rows, value_head_rows)), CTX)
 
     heads_local = step_size.shape[0]
     groups_local = b_matrix.shape[1] // N
@@ -174,7 +204,7 @@
     )
     block_log_decay = cumul[..., -1]
 
-    incoming = carried_scan(local_state, block_log_decay, position, ctx_count)
+    incoming = chip_carried_scan(local_state, block_log_decay)
 
     attention_out = causal_attention(position, queries, gathered_kv)
 
@@ -207,10 +237,14 @@
         P("tp"),
         P("tp"),
     )
+    fine_mesh = jax.sharding.Mesh(
+        mesh.devices.reshape(mesh.shape["ctx"] // 2, 2, mesh.shape["tp"]), CTX + ("tp",)
+    )
+    placed = tuple(P(*[CTX if axis == "ctx" else axis for axis in spec]) for spec in placed)
     return jax.shard_map(
         local,
-        mesh=mesh,
+        mesh=fine_mesh,
         in_specs=placed,
-        out_specs=(P("ctx", "tp"), P("ctx", "tp")),
+        out_specs=(P(CTX, "tp"), P(CTX, "tp")),
         check_vma=False,
     )

time: 156 us -> 134 us (0.86)
  waiting for transfers between devices: 69.1 us -> 49.7 us
  other arithmetic: 7.84 us -> 5.43 us
    ppermute x6 -> x5, waiting for transfers between devices: 59.8 us -> 38.9 us  [shifted(): return lax.ppermute(block, axis, route)]
    ppermute x0 -> x2, waiting for transfers between devices: none -> 1.97 us  [the longest x1 1.17 us: chip_carried_scan(): lax.ppermute(chip_prefix.astype(jnp.bfloat16), 'core', swap)]
    ppermute x6 -> x5, starting transfers between devices: 8.38 us -> 6.46 us  [shifted(): return lax.ppermute(block, axis, route)]
    unnamed x18 -> x22, local copies, waits for them, and re-layouts: 5.38 us -> 5.39 us
  transfers between devices with their start and end apart: 10 -> 11, of which waited for: 9 -> 10; matrix products, arithmetic and copies ran while one was open for 8% -> 8% of each run, Pallas kernels for 0% -> 0%
where the time goes in v9:
time: 134 us
  waiting for transfers between devices  49.7 us (37%)
  Pallas kernels  39.6 us (30%)
  between operations  14.5 us (11%)
  starting transfers between devices  11.4 us (9%)
  local copies, waits for them, and re-layouts  8.79 us (7%)
  other arithmetic  5.43 us (4%)
  matrix products  4.24 us (3%)
    pallas_call x1, Pallas kernels, causal_attention(): pl.pallas_call(kernel, in_specs=[pl.BlockSpec(memory_space=pltpu.SMEM)] +...  39.6 us
    ppermute x5, waiting for transfers between devices, shifted(): return lax.ppermute(block, axis, route)  38.9 us
    ppermute x3, waiting for transfers between devices, summed_over(): total = total + lax.ppermute(total, axis, route)  8.8 us
    ppermute x5, starting transfers between devices, shifted(): return lax.ppermute(block, axis, route)  6.46 us
    unnamed x22, local copies, waits for them, and re-layouts  5.39 us
    ppermute x3, starting transfers between devices, summed_over(): total = total + lax.ppermute(total, axis, route)  4.76 us
  transfers between devices with their start and end apart: 11, of which 10 were waited for; matrix products, arithmetic and copies ran while one was open for 8% of the time, Pallas kernels for 0%

profile of v9, /device:TPU:230, one launch (start us, length us, event | category | flops | bytes accessed | tf_op | source)
XLA Modules:
  0.0 133.7 jit_solution(9065430223511566631)
XLA Ops:
  7.2 0.0 copy-start
  7.2 0.0 all-gather.3.cloned.1.call-start
  7.2 0.8 reshape.1138
  8.0 0.0 copy-start.4
  8.0 0.6 reduce-window.6
  8.6 0.2 slice_reduce_fusion
  8.8 0.1 copy.46
  8.9 0.1 broadcast.184
  9.1 0.3 slice_reduce_fusion.1
  9.3 1.3 copy.47
  10.6 0.8 multiply_bitcast_fusion
  11.4 0.1 fusion.16
  11.5 0.3 fusion.79
  11.9 0.1 collective-permute-start
  12.0 0.7 pad_maximum_fusion.4
  12.7 0.0 all-gather.3.cloned.1.call-update
  12.7 0.8 collective-permute-done
  13.6 0.1 fusion.66
  13.7 0.1 dynamic-slice.5
  13.8 0.1 broadcast_select_fusion
  13.9 0.1 fusion.23
  14.0 1.3 collective-permute-start.2
  15.3 0.9 fusion.80
  16.2 1.3 collective-permute-start.1
  17.5 8.3 %collective-permute-done.2 = bf16[1,528,128]{2,1,0:T(8,128)(2,1)S(1)} collective-permute-done((bf16[1,528,128]{2,1,0:T(8,128)(2,1)S(1)}, bf16[1,528,128]{2,1,0:T(8,128)(2,1)S(1)}, u32[]{:S(2)}, u32[]{:S(2)}) %collective-permute-start.2) | collective-permute-done | bytes 135200 | tf_op jit(solution)/shard_map/ppermute | solution.py:85
  25.9 0.2 collective-permute-done.1
  26.1 0.1 mul.266
  26.2 0.1 mul.267
  26.3 0.1 fusion.28
  26.5 1.3 collective-permute-start.3
  27.8 0.1 mul.270
  27.8 0.1 mul.271
  28.0 6.7 %collective-permute-done.3 = bf16[1,528,128]{2,1,0:T(8,128)(2,1)S(1)} collective-permute-done((bf16[1,528,128]{2,1,0:T(8,128)(2,1)S(1)}, bf16[1,528,128]{2,1,0:T(8,128)(2,1)S(1)}, u32[]{:S(2)}, u32[]{:S(2)}) %collective-permute-start.3) | collective-permute-done | bytes 135200 | tf_op jit(solution)/shard_map/ppermute | solution.py:85
  34.7 0.2 fusion.77
  34.9 0.0 copy-start.5
  34.9 0.0 copy-start.7
  35.0 1.3 collective-permute-start.4
  36.3 0.1 mul.275
  36.4 0.1 mul.276
  36.5 10.6 %collective-permute-done.4 = bf16[1,528,128]{2,1,0:T(8,128)(2,1)S(1)} collective-permute-done((bf16[1,528,128]{2,1,0:T(8,128)(2,1)S(1)}, bf16[1,528,128]{2,1,0:T(8,128)(2,1)S(1)}, u32[]{:S(2)}, u32[]{:S(2)}) %collective-permute-start.4) | collective-permute-done | bytes 135200 | tf_op jit(solution)/shard_map/ppermute | solution.py:85
  47.1 0.3 add_convert_fusion.1
  47.4 1.3 collective-permute-start.5
  48.8 12.9 %collective-permute-done.5 = bf16[1,528,128]{2,1,0:T(8,128)(2,1)S(1)} collective-permute-done((bf16[1,528,128]{2,1,0:T(8,128)(2,1)S(1)}, bf16[1,528,128]{2,1,0:T(8,128)(2,1)S(1)}, u32[]{:S(2)}, u32[]{:S(2)}) %collective-permute-start.5) | collective-permute-done | bytes 135200 | tf_op jit(solution)/shard_map/ppermute | solution.py:85
  61.7 0.2 add_convert_fusion
  61.9 0.1 collective-permute-start.6
  62.0 0.2 add_add_fusion
  62.2 1.2 collective-permute-done.6
  63.4 0.7 fusion.9
  64.1 2.4 %fusion.11 = f32[256,1,16,64]{0,3,2,1:T(8,128)S(1)} fusion(f32[256,1,16,64]{0,3,2,1:T(8,128)S(1)} %fusion.9, bf16[256,16,64]{0,2,1:T(8,128)(2,1)S(1)} %bitcast.152, f32[16,256]{1,0:T(8,128)S(1)} %copy-done.5, f32[16,256]{1,0:T(8,128)S(1)} %get-tuple-element.15, f32[256,256]{1,0:T(8,128)} %fusion.80, pred[256,256]{1,0:T(8,128)(4,1)S(1)} %iota_compare_fusion.1, ...), kind=kOutput, calls=%fused_computation.13 | convolution fusion | flops 141557760 | bytes 3506240 | tf_op jit(solution)/shard_map/ghts,sghp->tghp/dot_general | solution.py:199
  66.5 0.3 copy.50
  66.8 0.4 multiply_reduce_fusion
  67.2 1.6 %collective-permute-start.7 = (f32[256]{0:T(256)S(1)}, f32[256]{0:T(256)S(1)}, u32[]{:S(2)}, u32[]{:S(2)}) collective-permute-start(f32[256]{0:T(256)S(1)} %multiply_reduce_fusion), channel_id=1, source_target_pairs={{0,1},{1,0},{2,3},{3,2},{4,5},{5,4},{6,7},{7,6},{8,9},{9,8},{10,11... | collective-permute-start | bytes 3080 | tf_op jit(solution)/shard_map/ppermute | solution.py:94
  68.8 2.1 %collective-permute-done.7 = f32[256]{0:T(256)S(1)} collective-permute-done((f32[256]{0:T(256)S(1)}, f32[256]{0:T(256)S(1)}, u32[]{:S(2)}, u32[]{:S(2)}) %collective-permute-start.7) | collective-permute-done | bytes 1056 | tf_op jit(solution)/shard_map/ppermute | solution.py:94
  70.9 3.2 %collective-permute-start.8 = (f32[256]{0:T(256)S(1)}, f32[256]{0:T(256)S(1)}, u32[]{:S(2)}, u32[]{:S(2)}) collective-permute-start(f32[256]{0:T(256)S(1)} %add.588), channel_id=1, source_target_pairs={{0,2},{1,3},{2,0},{3,1},{4,6},{5,7},{6,4},{7,5},{8,10},{9,11},{10,... | collective-permute-start | bytes 3080 | tf_op jit(solution)/shard_map/ppermute | solution.py:94
  74.0 1.9 %collective-permute-done.8 = f32[256]{0:T(256)S(1)} collective-permute-done((f32[256]{0:T(256)S(1)}, f32[256]{0:T(256)S(1)}, u32[]{:S(2)}, u32[]{:S(2)}) %collective-permute-start.8) | collective-permute-done | bytes 1056 | tf_op jit(solution)/shard_map/ppermute | solution.py:94
  76.0 1.1 copy.52
  77.1 0.6 copy.42
  77.7 0.9 copy.53
  78.6 4.8 %collective-permute-done.9 = f32[256]{0:T(256)S(1)} collective-permute-done((f32[256]{0:T(256)S(1)}, f32[256]{0:T(256)S(1)}, u32[]{:S(2)}, u32[]{:S(2)}) %collective-permute-start.9) | collective-permute-done | bytes 1056 | tf_op jit(solution)/shard_map/ppermute | solution.py:94
  83.4 1.2 multiply_convert_fusion
  84.6 39.6 %shard_map.122 = bf16[128,2048]{1,0:T(8,128)(2,1)} custom-call(s32[1]{0:T(128)} %bitcast.pos_ref, bf16[128,2048]{1,0:T(8,128)(2,1)} %bitcast.159, bf16[32,2,256,128]{3,2,1,0:T(8,128)(2,1)} %bitcast.137), custom_call_target="tpu_custom_call" | custom-call | tf_op jit(solution)/shard_map/pallas_call | solution.py:66
  124.2 1.1 copy.54
  125.4 0.6 copy.43
  126.0 0.9 copy.64
  (59 shorter events, 0.6 us)
Async XLA Ops:
  7.2 4.4 %copy-start = (bf16[256,128]{1,0:T(8,128)(2,1)S(1)}, bf16[256,128]{1,0:T(8,128)(2,1)}, u32[]{:S(2)}) copy-start(bf16[256,128]{1,0:T(8,128)(2,1)} %param.16) | copy-start | bytes 196612
  7.2 4.8 %copy-start.2 = (bf16[256,128]{1,0:T(8,128)(2,1)S(1)}, bf16[256,128]{1,0:T(8,128)(2,1)}, u32[]{:S(2)}) copy-start(bf16[256,128]{1,0:T(8,128)(2,1)} %param.13) | copy-start | bytes 196612
  7.2 4.8 %copy-start.3 = (bf16[256,128]{1,0:T(8,128)(2,1)S(1)}, bf16[256,128]{1,0:T(8,128)(2,1)}, u32[]{:S(2)}) copy-start(bf16[256,128]{1,0:T(8,128)(2,1)} %param.12) | copy-start | bytes 196612
  7.2 77.4 %all-gather.3.cloned.1.call-start = ((), (), s32[]{:S(2)}) async-start(), calls=%async_computation | async-start | bytes 4325376 | tf_op jit(solution)/shard_map/all_gather | solution.py:183
  8.0 7.3 %copy-start.4 = (bf16[256,128]{1,0:T(8,128)(2,1)S(1)}, bf16[256,128]{1,0:T(8,128)(2,1)}, u32[]{:S(2)}) copy-start(bf16[256,128]{1,0:T(8,128)(2,1)} %param.17) | copy-start | bytes 196612
  11.9 1.6 %collective-permute-start = (bf16[1,1040,128]{2,1,0:T(8,128)(2,1)S(1)}, bf16[1,1040,128]{2,1,0:T(8,128)(2,1)S(1)}, u32[]{:S(2)}, u32[]{:S(2)}) collective-permute-start(bf16[1,1040,128]{2,1,0:T(8,128)(2,1)S(1)} %fusion.21), channel_id=1, source_target_pairs={{0,8},{8,0},{1,9},{9,1},{2,10},{10,2},{3,11},{11,3},{4,12},{12,4},... | collective-permute-start | bytes 798728 | tf_op jit(solution)/shard_map/ppermute | solution.py:142
  14.0 11.9 %collective-permute-start.2 = (bf16[1,528,128]{2,1,0:T(8,128)(2,1)S(1)}, bf16[1,528,128]{2,1,0:T(8,128)(2,1)S(1)}, u32[]{:S(2)}, u32[]{:S(2)}) collective-permute-start(bf16[1,528,128]{2,1,0:T(8,128)(2,1)S(1)} %pad_maximum_fusion), channel_id=1, source_target_pairs={{0,32},{16,48},{32,64},{48,80},{64,96},{80,112},{96,128},{112,144}... | collective-permute-start | bytes 405512 | tf_op jit(solution)/shard_map/ppermute | solution.py:85
  16.2 9.9 %collective-permute-start.1 = (bf16[1,528,128]{2,1,0:T(8,128)(2,1)S(1)}, bf16[1,528,128]{2,1,0:T(8,128)(2,1)S(1)}, u32[]{:S(2)}, u32[]{:S(2)}) collective-permute-start(bf16[1,528,128]{2,1,0:T(8,128)(2,1)S(1)} %pad_maximum_fusion), channel_id=1, source_target_pairs={{0,16},{16,32},{32,48},{48,64},{64,80},{80,96},{96,112},{112,128},... | collective-permute-start | bytes 405512 | tf_op jit(solution)/shard_map/ppermute | solution.py:85
  26.5 8.2 %collective-permute-start.3 = (bf16[1,528,128]{2,1,0:T(8,128)(2,1)S(1)}, bf16[1,528,128]{2,1,0:T(8,128)(2,1)S(1)}, u32[]{:S(2)}, u32[]{:S(2)}) collective-permute-start(bf16[1,528,128]{2,1,0:T(8,128)(2,1)S(1)} %pad_maximum_fusion.1), channel_id=1, source_target_pairs={{0,32},{16,48},{32,64},{48,80},{64,96},{80,112},{96,128},{112,144}... | collective-permute-start | bytes 405512 | tf_op jit(solution)/shard_map/ppermute | solution.py:85
  34.9 29.1 %copy-start.5 = (f32[16,256]{1,0:T(8,128)S(1)}, f32[16,256]{1,0:T(8,128)}, u32[]{:S(2)}) copy-start(f32[16,256]{1,0:T(8,128)} %param.18) | copy-start | bytes 49156
  34.9 29.1 %copy-start.7 = (f32[16]{0:T(128)S(1)}, f32[16]{0:T(128)}, u32[]{:S(2)}) copy-start(f32[16]{0:T(128)} %param.20) | copy-start | bytes 196
  35.0 12.1 %collective-permute-start.4 = (bf16[1,528,128]{2,1,0:T(8,128)(2,1)S(1)}, bf16[1,528,128]{2,1,0:T(8,128)(2,1)S(1)}, u32[]{:S(2)}, u32[]{:S(2)}) collective-permute-start(bf16[1,528,128]{2,1,0:T(8,128)(2,1)S(1)} %pad_maximum_fusion.2), channel_id=1, source_target_pairs={{0,64},{16,80},{32,96},{48,112},{64,128},{80,144},{96,160},{112,17... | collective-permute-start | bytes 405512 | tf_op jit(solution)/shard_map/ppermute | solution.py:85
  47.4 14.3 %collective-permute-start.5 = (bf16[1,528,128]{2,1,0:T(8,128)(2,1)S(1)}, bf16[1,528,128]{2,1,0:T(8,128)(2,1)S(1)}, u32[]{:S(2)}, u32[]{:S(2)}) collective-permute-start(bf16[1,528,128]{2,1,0:T(8,128)(2,1)S(1)} %pad_maximum_fusion.3), channel_id=1, source_target_pairs={{0,128},{16,144},{32,160},{48,176},{64,192},{80,208},{96,224},{112... | collective-permute-start | bytes 405512 | tf_op jit(solution)/shard_map/ppermute | solution.py:85
  61.9 1.4 %collective-permute-start.6 = (bf16[1,8,64,128]{3,2,1,0:T(8,128)(2,1)S(1)}, bf16[1,8,64,128]{3,2,1,0:T(8,128)(2,1)S(1)}, u32[]{:S(2)}, u32[]{:S(2)}) collective-permute-start(bf16[1,8,64,128]{3,2,1,0:T(8,128)(2,1)S(1)} %add_convert_fusion), channel_id=1, source_target_pairs={{0,8},{8,0},{1,9},{9,1},{2,10},{10,2},{3,11},{11,3},{4,12},{12,4},... | collective-permute-start | bytes 393224 | tf_op jit(solution)/shard_map/ppermute | solution.py:156
  64.1 2.8 %copy-start.1 = (bf16[256,1024]{1,0:T(8,128)(2,1)S(1)}, bf16[256,1024]{1,0:T(8,128)(2,1)}, u32[]{:S(2)}) copy-start(bf16[256,1024]{1,0:T(8,128)(2,1)} %param.15) | copy-start | bytes 1572868
  66.5 12.1 %copy-start.6 = (bf16[1024]{0:T(1024)(128)(2,1)S(1)}, bf16[1024]{0:T(1024)(128)(2,1)}, u32[]{:S(2)}) copy-start(bf16[1024]{0:T(1024)(128)(2,1)} %param.21) | copy-start | bytes 6148
  67.2 3.6 %collective-permute-start.7 = (f32[256]{0:T(256)S(1)}, f32[256]{0:T(256)S(1)}, u32[]{:S(2)}, u32[]{:S(2)}) collective-permute-start(f32[256]{0:T(256)S(1)} %multiply_reduce_fusion), channel_id=1, source_target_pairs={{0,1},{1,0},{2,3},{3,2},{4,5},{5,4},{6,7},{7,6},{8,9},{9,8},{10,11... | collective-permute-start | bytes 3080 | tf_op jit(solution)/shard_map/ppermute | solution.py:94
  70.9 5.1 %collective-permute-start.8 = (f32[256]{0:T(256)S(1)}, f32[256]{0:T(256)S(1)}, u32[]{:S(2)}, u32[]{:S(2)}) collective-permute-start(f32[256]{0:T(256)S(1)} %add.588), channel_id=1, source_target_pairs={{0,2},{1,3},{2,0},{3,1},{4,6},{5,7},{6,4},{7,5},{8,10},{9,11},{10,... | collective-permute-start | bytes 3080 | tf_op jit(solution)/shard_map/ppermute | solution.py:94
  76.0 7.5 %collective-permute-start.9 = (f32[256]{0:T(256)S(1)}, f32[256]{0:T(256)S(1)}, u32[]{:S(2)}, u32[]{:S(2)}) collective-permute-start(f32[256]{0:T(256)S(1)} %add.589), channel_id=1, source_target_pairs={{0,4},{1,5},{2,6},{3,7},{4,0},{5,1},{6,2},{7,3},{8,12},{9,13},{10,... | collective-permute-start | bytes 3080 | tf_op jit(solution)/shard_map/ppermute | solution.py:94
Sparse Core Ops, SparseCore 0:
  12.8 65.2 all-gather.2

commit v10 on v9

--- a/solution.py
+++ b/solution.py
@@ -17,14 +17,24 @@
 CTX = ("chip", "core")
 
 
-def attend_kernel(pos_ref, qt_ref, kv_ref, o_ref, p_sc, m_sc, l_sc, c_sc, acc_sc, *, tok, width, chunk):
+def attend_kernel(*refs, tok, width, chunk, key_offset, first, last):
+    pos_ref, qt_ref, kv_ref = refs[:3]
+    rest = list(refs[3:])
+    state_in = () if first else (rest.pop(0), rest.pop(0), rest.pop(0))
+    outs = (rest.pop(0),) if last else (rest.pop(0), rest.pop(0), rest.pop(0))
+    p_sc, m_sc, l_sc, c_sc, acc_sc = rest
     position = pos_ref[0]
     score_factor = width ** (-0.5)
     rows = qt_ref.shape[1]
     block_rows = kv_ref.shape[2]
-    m_sc[...] = jnp.full(m_sc.shape, causal_score, jnp.float32)
-    l_sc[...] = jnp.zeros(l_sc.shape, jnp.float32)
-    acc_sc[...] = jnp.zeros(acc_sc.shape, jnp.float32)
+    if first:
+        m_sc[...] = jnp.full(m_sc.shape, causal_score, jnp.float32)
+        l_sc[...] = jnp.zeros(l_sc.shape, jnp.float32)
+        acc_sc[...] = jnp.zeros(acc_sc.shape, jnp.float32)
+    else:
+        m_sc[...] = state_in[0][...]
+        l_sc[...] = state_in[1][...]
+        acc_sc[...] = state_in[2][...]
 
     def run_block(kb, masked):
         key_portion = kv_ref[kb, 0]
@@ -33,7 +43,7 @@
             score_t = jnp.dot(key_portion, qt_ref[:, r0:r0 + chunk],
                               preferred_element_type=jnp.float32) * score_factor
             if masked:
-                key_idx = lax.broadcasted_iota(jnp.int32, (block_rows, chunk), 0)
+                key_idx = key_offset + lax.broadcasted_iota(jnp.int32, (block_rows, chunk), 0)
                 query_idx = (r0 % tok) + lax.broadcasted_iota(jnp.int32, (block_rows, chunk), 1)
                 is_valid = key_idx <= query_idx
                 score_t = jnp.where(is_valid, score_t, causal_score)
@@ -54,28 +64,58 @@
         return carry
     lax.fori_loop(0, position, body, 0)
     run_block(position, True)
-    o_ref[...] = (acc_sc[...] / l_sc[...]).astype(o_ref.dtype)
-
-
-def causal_attention(position, queries, gathered_kv, chunk=256):
-    blocks, _, tok_rows, width = gathered_kv.shape
-    heads = queries.shape[1] // width
-    rows = heads * tok_rows
-    queries_t = queries.reshape(tok_rows, heads, width).transpose(2, 1, 0).reshape(width, rows)
-    kernel = functools.partial(attend_kernel, tok=tok_rows, width=width, chunk=chunk)
-    out_t = pl.pallas_call(
+    if last:
+        outs[0][...] = (acc_sc[...] / l_sc[...]).astype(outs[0].dtype)
+    else:
+        outs[0][...] = m_sc[...]
+        outs[1][...] = l_sc[...]
+        outs[2][...] = acc_sc[...]
+
+
+def attend_part(position, queries_t, part_kv, state, key_offset, out_dtype, chunk=256):
+    blocks, _, part_rows, width = part_kv.shape
+    rows = queries_t.shape[1]
+    first, last = state is None, key_offset > 0
+    kernel = functools.partial(
+        attend_kernel, tok=2 * part_rows, width=width, chunk=chunk,
+        key_offset=key_offset, first=first, last=last,
+    )
+    stats = jax.ShapeDtypeStruct((1, rows), jnp.float32)
+    if last:
+        out_shape = jax.ShapeDtypeStruct((width, rows), out_dtype)
+        out_specs = pl.BlockSpec(memory_space=pltpu.VMEM)
+    else:
+        out_shape = (stats, stats, jax.ShapeDtypeStruct((width, rows), jnp.float32))
+        out_specs = (pl.BlockSpec(memory_space=pltpu.VMEM),) * 3
+    operands = (position.reshape(1), queries_t, part_kv) + (() if first else tuple(state))
+    return pl.pallas_call(
         kernel,
-        in_specs=[pl.BlockSpec(memory_space=pltpu.SMEM)] + [pl.BlockSpec(memory_space=pltpu.VMEM)] * 2,
-        out_specs=pl.BlockSpec(memory_space=pltpu.VMEM),
-        out_shape=jax.ShapeDtypeStruct((width, rows), queries.dtype),
+        in_specs=[pl.BlockSpec(memory_space=pltpu.SMEM)]
+        + [pl.BlockSpec(memory_space=pltpu.VMEM)] * (len(operands) - 1),
+        out_specs=out_specs,
+        out_shape=out_shape,
         scratch_shapes=[
-            pltpu.VMEM((tok_rows, rows), jnp.bfloat16),
+            pltpu.VMEM((part_rows, rows), jnp.bfloat16),
             pltpu.VMEM((1, rows), jnp.float32),
             pltpu.VMEM((1, rows), jnp.float32),
             pltpu.VMEM((1, rows), jnp.float32),
             pltpu.VMEM((width, rows), jnp.float32),
         ],
-    )(position.reshape(1), queries_t, gathered_kv)
+        cost_estimate=pl.CostEstimate(
+            flops=4 * rows * width * part_rows * blocks,
+            transcendentals=rows * part_rows * blocks,
+            bytes_accessed=2 * (queries_t.size + part_kv.size) + 4 * 4 * rows * width,
+        ),
+    )(*operands)
+
+
+def causal_attention(position, queries, first_kv, second_kv):
+    tok_rows = queries.shape[0]
+    width = first_kv.shape[-1]
+    heads = queries.shape[1] // width
+    queries_t = queries.reshape(tok_rows, heads, width).transpose(2, 1, 0).reshape(width, -1)
+    state = attend_part(position, queries_t, first_kv, None, 0, queries.dtype)
+    out_t = attend_part(position, queries_t, second_kv, state, first_kv.shape[2], queries.dtype)
     return out_t.reshape(width, heads, tok_rows).transpose(2, 1, 0).reshape(tok_rows, heads * width)
 
 
@@ -180,7 +220,10 @@
     tok_rows = queries.shape[0]
     position = lax.axis_index(CTX)
 
-    gathered_kv = lax.all_gather(jnp.stack((key_rows, value_head_rows)), CTX)
+    local_kv = jnp.stack((key_rows, value_head_rows))
+    half_rows = tok_rows // 2
+    first_kv = lax.all_gather(local_kv[:, :half_rows], CTX)
+    second_kv = lax.all_gather(local_kv[:, half_rows:], CTX)
 
     heads_local = step_size.shape[0]
     groups_local = b_matrix.shape[1] // N
@@ -206,7 +249,7 @@
 
     incoming = chip_carried_scan(local_state, block_log_decay)
 
-    attention_out = causal_attention(position, queries, gathered_kv)
+    attention_out = causal_attention(position, queries, first_kv, second_kv)
 
     carried_out = jnp.einsum(
         "ghpn,tgn->tghp", incoming, out_maps.astype(jnp.float32), precision=lax.Precision.HIGHEST

time: 134 us -> 172 us (1.28)
  waiting for transfers between devices: 49.7 us -> 76.5 us
  Pallas kernels: 39.6 us -> 50.3 us
  matrix products: 4.24 us -> 2.51 us
    all_gather x1 -> x2, waiting for transfers between devices: 0.01 us -> 31.3 us  [the longest x1 31.3 us: local(): second_kv = lax.all_gather(local_kv[:, half_rows:], CTX)]
    pallas_call x1 -> x2, Pallas kernels: 39.6 us -> 50.3 us  [attend_part(): pl.pallas_call(kernel, in_specs=[pl.BlockSpec(memory_space=pltpu.SMEM)] +...]
    ppermute x5, waiting for transfers between devices: 38.9 us -> 33.2 us  [shifted(): return lax.ppermute(block, axis, route)]
    unnamed x22 -> x20, local copies, waits for them, and re-layouts: 5.39 us -> 5.02 us
  transfers between devices with their start and end apart: 11 -> 12, of which waited for: 10 -> 11; matrix products, arithmetic and copies ran while one was open for 8% -> 7% of each run, Pallas kernels for 0% -> 15%
where the time goes in v10:
time: 172 us; the launch traced here: 170 us
  waiting for transfers between devices  76.5 us (44%)
  Pallas kernels  50.3 us (29%)
  between operations  14.5 us (8%)
  starting transfers between devices  12 us (7%)
  local copies, waits for them, and re-layouts  8.39 us (5%)
  other arithmetic  6.23 us (4%)
  matrix products  2.51 us (1%)
    pallas_call x2, Pallas kernels, attend_part(): pl.pallas_call(kernel, in_specs=[pl.BlockSpec(memory_space=pltpu.SMEM)] +...  50.3 us
    ppermute x5, waiting for transfers between devices, shifted(): return lax.ppermute(block, axis, route)  33.2 us
    all_gather x1, waiting for transfers between devices, local(): second_kv = lax.all_gather(local_kv[:, half_rows:], CTX)  31.3 us
    ppermute x3, waiting for transfers between devices, summed_over(): total = total + lax.ppermute(total, axis, route)  9.3 us
    ppermute x5, starting transfers between devices, shifted(): return lax.ppermute(block, axis, route)  6.46 us
    ppermute x3, starting transfers between devices, summed_over(): total = total + lax.ppermute(total, axis, route)  5.31 us
    unnamed x20, local copies, waits for them, and re-layouts  5.02 us
  transfers between devices with their start and end apart: 12, of which 11 were waited for; matrix products, arithmetic and copies ran while one was open for 7% of the time, Pallas kernels for 15%

profile of v10, /device:TPU:230, one launch (start us, length us, event | category | flops | bytes accessed | tf_op | source)
XLA Modules:
  0.0 170.5 jit_solution(1323338281072768935)
XLA Ops:
  7.2 0.0 all-gather.7.cloned.1.call-start
  7.2 1.5 pad_maximum_fusion.4
  8.7 0.0 all-gather.5.cloned.1.call-start
  8.8 0.7 reshape.1139
  9.5 0.6 reduce-window.6
  10.1 0.2 slice_reduce_fusion
  10.3 0.1 copy.46
  10.4 1.2 copy.47
  11.7 0.1 broadcast.184
  11.8 0.3 slice_reduce_fusion.1
  12.1 0.8 multiply_bitcast_fusion
  12.9 0.1 fusion.16
  13.0 0.3 fusion.80
  13.4 0.1 collective-permute-start
  13.5 1.5 collective-permute-done
  15.1 0.1 broadcast_select_fusion
  15.2 0.1 dynamic-slice.5
  15.3 0.1 fusion.67
  15.4 0.1 fusion.23
  15.5 1.3 collective-permute-start.2
  16.8 0.2 fusion.81
  17.0 1.3 collective-permute-start.1
  18.3 9.0 %collective-permute-done.2 = bf16[1,528,128]{2,1,0:T(8,128)(2,1)S(1)} collective-permute-done((bf16[1,528,128]{2,1,0:T(8,128)(2,1)S(1)}, bf16[1,528,128]{2,1,0:T(8,128)(2,1)S(1)}, u32[]{:S(2)}, u32[]{:S(2)}) %collective-permute-start.2) | collective-permute-done | bytes 135200 | tf_op jit(solution)/shard_map/ppermute | solution.py:125
  27.4 1.0 collective-permute-done.1
  28.4 0.1 mul.266
  28.5 0.1 mul.267
  28.6 0.1 fusion.29
  28.7 1.3 collective-permute-start.3
  30.0 0.1 mul.270
  30.1 0.1 mul.271
  30.2 9.2 %collective-permute-done.3 = bf16[1,528,128]{2,1,0:T(8,128)(2,1)S(1)} collective-permute-done((bf16[1,528,128]{2,1,0:T(8,128)(2,1)S(1)}, bf16[1,528,128]{2,1,0:T(8,128)(2,1)S(1)}, u32[]{:S(2)}, u32[]{:S(2)}) %collective-permute-start.3) | collective-permute-done | bytes 135200 | tf_op jit(solution)/shard_map/ppermute | solution.py:125
  39.5 0.2 fusion.78
  39.7 1.3 collective-permute-start.4
  41.0 0.1 mul.275
  41.1 0.1 mul.276
  41.2 5.7 %collective-permute-done.4 = bf16[1,528,128]{2,1,0:T(8,128)(2,1)S(1)} collective-permute-done((bf16[1,528,128]{2,1,0:T(8,128)(2,1)S(1)}, bf16[1,528,128]{2,1,0:T(8,128)(2,1)S(1)}, u32[]{:S(2)}, u32[]{:S(2)}) %collective-permute-start.4) | collective-permute-done | bytes 135200 | tf_op jit(solution)/shard_map/ppermute | solution.py:125
  47.0 0.3 add_convert_fusion.1
  47.3 1.3 collective-permute-start.5
  48.6 8.2 %collective-permute-done.5 = bf16[1,528,128]{2,1,0:T(8,128)(2,1)S(1)} collective-permute-done((bf16[1,528,128]{2,1,0:T(8,128)(2,1)S(1)}, bf16[1,528,128]{2,1,0:T(8,128)(2,1)S(1)}, u32[]{:S(2)}, u32[]{:S(2)}) %collective-permute-start.5) | collective-permute-done | bytes 135200 | tf_op jit(solution)/shard_map/ppermute | solution.py:125
  56.8 0.2 add_convert_fusion
  57.0 0.1 collective-permute-start.6
  57.1 0.2 add_add_fusion
  57.3 1.1 collective-permute-done.6
  58.5 0.7 fusion.9
  59.2 1.4 fusion.11
  60.6 0.3 copy.50
  60.9 0.7 copy-done.1
  61.6 0.4 multiply_reduce_fusion
  62.0 1.3 collective-permute-start.7
  63.3 2.4 %collective-permute-done.7 = f32[256]{0:T(256)S(1)} collective-permute-done((f32[256]{0:T(256)S(1)}, f32[256]{0:T(256)S(1)}, u32[]{:S(2)}, u32[]{:S(2)}) %collective-permute-start.7) | collective-permute-done | bytes 1056 | tf_op jit(solution)/shard_map/ppermute | solution.py:134
  65.7 2.8 %collective-permute-start.8 = (f32[256]{0:T(256)S(1)}, f32[256]{0:T(256)S(1)}, u32[]{:S(2)}, u32[]{:S(2)}) collective-permute-start(f32[256]{0:T(256)S(1)} %add.588), channel_id=1, source_target_pairs={{0,2},{1,3},{2,0},{3,1},{4,6},{5,7},{6,4},{7,5},{8,10},{9,11},{10,... | collective-permute-start | bytes 3080 | tf_op jit(solution)/shard_map/ppermute | solution.py:134
  68.5 2.2 %collective-permute-done.8 = f32[256]{0:T(256)S(1)} collective-permute-done((f32[256]{0:T(256)S(1)}, f32[256]{0:T(256)S(1)}, u32[]{:S(2)}, u32[]{:S(2)}) %collective-permute-start.8) | collective-permute-done | bytes 1056 | tf_op jit(solution)/shard_map/ppermute | solution.py:134
  70.7 1.2 collective-permute-start.9
  71.9 0.1 copy.52
  72.0 0.6 copy.42
  72.6 0.9 copy.53
  73.5 4.7 %collective-permute-done.9 = f32[256]{0:T(256)S(1)} collective-permute-done((f32[256]{0:T(256)S(1)}, f32[256]{0:T(256)S(1)}, u32[]{:S(2)}, u32[]{:S(2)}) %collective-permute-start.9) | collective-permute-done | bytes 1056 | tf_op jit(solution)/shard_map/ppermute | solution.py:134
  78.2 1.2 multiply_convert_fusion
  79.4 25.0 %shard_map.122 = (f32[1,2048]{1,0:T(1,128)}, f32[1,2048]{1,0:T(1,128)}, f32[128,2048]{1,0:T(8,128)}) custom-call(s32[1]{0:T(128)} %bitcast.refs_0_, bf16[128,2048]{1,0:T(8,128)(2,1)} %bitcast.161, bf16[32,2,128,128]{3,2,1,0:T(8,128)(2,1)} %bitcast.174), custom_call_target="tpu_custom_call" | custom-call | flops 4294967296 | bytes 6815744 | tf_op jit(solution)/shard_map/pallas_call | solution.py:91
  104.4 31.3 %all-gather.5.cloned.1.call-done = bf16[64,128,128]{2,1,0:T(8,128)(2,1)} async-done(((bf16[2,128,128]{2,1,0:T(8,128)(2,1)}), bf16[64,128,128]{2,1,0:T(8,128)(2,1)}) %all-gather.5.cloned.1.call-update) | async-done | bytes 2097168 | tf_op jit(solution)/shard_map/all_gather | solution.py:226
  135.8 25.3 %shard_map.123 = bf16[128,2048]{1,0:T(8,128)(2,1)} custom-call(s32[1]{0:T(128)} %bitcast.refs_0_, bf16[128,2048]{1,0:T(8,128)(2,1)} %bitcast.162, bf16[32,2,128,128]{3,2,1,0:T(8,128)(2,1)} %bitcast.175, f32[1,2048]{1,0:T(1,128)} %get-tuple-element.5.refs_3_, f32[1,2048]{1,0:T(1,128)} %get-tuple-element.6.refs_4_, f32[128,2048]{1,0:T(8,128)} %get-tuple-element.7.refs_5_), custom_call_target="tpu_custom_call" | custom-call | flops 4294967296 | bytes 6815744 | tf_op jit(solution)/shard_map/pallas_call | solution.py:91
  161.0 1.1 copy.54
  162.2 0.6 copy.43
  162.8 0.9 copy.64
  (61 shorter events, 0.6 us)
Async XLA Ops:
  7.2 5.9 %copy-start = (bf16[256,128]{1,0:T(8,128)(2,1)S(1)}, bf16[256,128]{1,0:T(8,128)(2,1)}, u32[]{:S(2)}) copy-start(bf16[256,128]{1,0:T(8,128)(2,1)} %param.16) | copy-start | bytes 196612
  7.2 72.2 %all-gather.7.cloned.1.call-start = ((), (), s32[]{:S(2)}) async-start(), calls=%async_computation.1 | async-start | bytes 2162688 | tf_op jit(solution)/shard_map/all_gather | solution.py:225
  8.7 127.0 %all-gather.5.cloned.1.call-start = ((), (), s32[]{:S(2)}) async-start(), calls=%async_computation | async-start | bytes 2162688 | tf_op jit(solution)/shard_map/all_gather | solution.py:226
  13.3 3.5 %copy-start.3 = (bf16[256,128]{1,0:T(8,128)(2,1)S(1)}, bf16[256,128]{1,0:T(8,128)(2,1)}, u32[]{:S(2)}) copy-start(bf16[256,128]{1,0:T(8,128)(2,1)} %param.17) | copy-start | bytes 196612
  13.4 1.6 collective-permute-start
  15.5 11.9 %collective-permute-start.2 = (bf16[1,528,128]{2,1,0:T(8,128)(2,1)S(1)}, bf16[1,528,128]{2,1,0:T(8,128)(2,1)S(1)}, u32[]{:S(2)}, u32[]{:S(2)}) collective-permute-start(bf16[1,528,128]{2,1,0:T(8,128)(2,1)S(1)} %pad_maximum_fusion), channel_id=1, source_target_pairs={{0,32},{16,48},{32,64},{48,80},{64,96},{80,112},{96,128},{112,144}... | collective-permute-start | bytes 405512 | tf_op jit(solution)/shard_map/ppermute | solution.py:125
  17.0 11.3 %collective-permute-start.1 = (bf16[1,528,128]{2,1,0:T(8,128)(2,1)S(1)}, bf16[1,528,128]{2,1,0:T(8,128)(2,1)S(1)}, u32[]{:S(2)}, u32[]{:S(2)}) collective-permute-start(bf16[1,528,128]{2,1,0:T(8,128)(2,1)S(1)} %pad_maximum_fusion), channel_id=1, source_target_pairs={{0,16},{16,32},{32,48},{48,64},{64,80},{80,96},{96,112},{112,128},... | collective-permute-start | bytes 405512 | tf_op jit(solution)/shard_map/ppermute | solution.py:125
  28.7 10.7 %collective-permute-start.3 = (bf16[1,528,128]{2,1,0:T(8,128)(2,1)S(1)}, bf16[1,528,128]{2,1,0:T(8,128)(2,1)S(1)}, u32[]{:S(2)}, u32[]{:S(2)}) collective-permute-start(bf16[1,528,128]{2,1,0:T(8,128)(2,1)S(1)} %pad_maximum_fusion.1), channel_id=1, source_target_pairs={{0,32},{16,48},{32,64},{48,80},{64,96},{80,112},{96,128},{112,144}... | collective-permute-start | bytes 405512 | tf_op jit(solution)/shard_map/ppermute | solution.py:125
  39.7 7.2 %collective-permute-start.4 = (bf16[1,528,128]{2,1,0:T(8,128)(2,1)S(1)}, bf16[1,528,128]{2,1,0:T(8,128)(2,1)S(1)}, u32[]{:S(2)}, u32[]{:S(2)}) collective-permute-start(bf16[1,528,128]{2,1,0:T(8,128)(2,1)S(1)} %pad_maximum_fusion.2), channel_id=1, source_target_pairs={{0,64},{16,80},{32,96},{48,112},{64,128},{80,144},{96,160},{112,17... | collective-permute-start | bytes 405512 | tf_op jit(solution)/shard_map/ppermute | solution.py:125
  47.3 9.6 %collective-permute-start.5 = (bf16[1,528,128]{2,1,0:T(8,128)(2,1)S(1)}, bf16[1,528,128]{2,1,0:T(8,128)(2,1)S(1)}, u32[]{:S(2)}, u32[]{:S(2)}) collective-permute-start(bf16[1,528,128]{2,1,0:T(8,128)(2,1)S(1)} %pad_maximum_fusion.3), channel_id=1, source_target_pairs={{0,128},{16,144},{32,160},{48,176},{64,192},{80,208},{96,224},{112... | collective-permute-start | bytes 405512 | tf_op jit(solution)/shard_map/ppermute | solution.py:125
  57.0 1.4 collective-permute-start.6
  57.1 2.0 %copy-start.4 = (f32[16,256]{1,0:T(8,128)S(1)}, f32[16,256]{1,0:T(8,128)}, u32[]{:S(2)}) copy-start(f32[16,256]{1,0:T(8,128)} %param.18) | copy-start | bytes 49156
  57.1 2.0 %copy-start.6 = (f32[16]{0:T(128)S(1)}, f32[16]{0:T(128)}, u32[]{:S(2)}) copy-start(f32[16]{0:T(128)} %param.20) | copy-start | bytes 196
  60.6 1.1 copy-start.1
  60.6 11.4 %copy-start.5 = (bf16[1024]{0:T(1024)(128)(2,1)S(1)}, bf16[1024]{0:T(1024)(128)(2,1)}, u32[]{:S(2)}) copy-start(bf16[1024]{0:T(1024)(128)(2,1)} %param.21) | copy-start | bytes 6148
  60.6 11.4 %copy-start.2 = (bf16[256,1024]{1,0:T(8,128)(2,1)S(1)}, bf16[256,1024]{1,0:T(8,128)(2,1)}, u32[]{:S(2)}) copy-start(bf16[256,1024]{1,0:T(8,128)(2,1)} %param.11) | copy-start | bytes 1572868
  62.0 3.6 %collective-permute-start.7 = (f32[256]{0:T(256)S(1)}, f32[256]{0:T(256)S(1)}, u32[]{:S(2)}, u32[]{:S(2)}) collective-permute-start(f32[256]{0:T(256)S(1)} %multiply_reduce_fusion), channel_id=1, source_target_pairs={{0,1},{1,0},{2,3},{3,2},{4,5},{5,4},{6,7},{7,6},{8,9},{9,8},{10,11... | collective-permute-start | bytes 3080 | tf_op jit(solution)/shard_map/ppermute | solution.py:134
  65.7 5.1 %collective-permute-start.8 = (f32[256]{0:T(256)S(1)}, f32[256]{0:T(256)S(1)}, u32[]{:S(2)}, u32[]{:S(2)}) collective-permute-start(f32[256]{0:T(256)S(1)} %add.588), channel_id=1, source_target_pairs={{0,2},{1,3},{2,0},{3,1},{4,6},{5,7},{6,4},{7,5},{8,10},{9,11},{10,... | collective-permute-start | bytes 3080 | tf_op jit(solution)/shard_map/ppermute | solution.py:134
  70.7 7.5 %collective-permute-start.9 = (f32[256]{0:T(256)S(1)}, f32[256]{0:T(256)S(1)}, u32[]{:S(2)}, u32[]{:S(2)}) collective-permute-start(f32[256]{0:T(256)S(1)} %add.589), channel_id=1, source_target_pairs={{0,4},{1,5},{2,6},{3,7},{4,0},{5,1},{6,2},{7,3},{8,12},{9,13},{10,... | collective-permute-start | bytes 3080 | tf_op jit(solution)/shard_map/ppermute | solution.py:134
Sparse Core Ops, SparseCore 0:
  9.9 63.7 all-gather.6
  75.6 60.1 all-gather.4

commit v11 on v9

--- a/solution.py
+++ b/solution.py
@@ -19,7 +19,7 @@
 
 def attend_kernel(pos_ref, qt_ref, kv_ref, o_ref, p_sc, m_sc, l_sc, c_sc, acc_sc, *, tok, width, chunk):
     position = pos_ref[0]
-    score_factor = width ** (-0.5)
+    score_factor = width ** (-0.5) * 1.4426950408889634
     rows = qt_ref.shape[1]
     block_rows = kv_ref.shape[2]
     m_sc[...] = jnp.full(m_sc.shape, causal_score, jnp.float32)
@@ -31,7 +31,7 @@
         for c in range(rows // chunk):
             r0 = c * chunk
             score_t = jnp.dot(key_portion, qt_ref[:, r0:r0 + chunk],
-                              preferred_element_type=jnp.float32) * score_factor
+                              preferred_element_type=jnp.float32)
             if masked:
                 key_idx = lax.broadcasted_iota(jnp.int32, (block_rows, chunk), 0)
                 query_idx = (r0 % tok) + lax.broadcasted_iota(jnp.int32, (block_rows, chunk), 1)
@@ -39,10 +39,10 @@
                 score_t = jnp.where(is_valid, score_t, causal_score)
             run_max = m_sc[:, r0:r0 + chunk]
             new_max = jnp.maximum(run_max, jnp.max(score_t, axis=0, keepdims=True))
-            weights = jnp.exp(score_t - new_max)
+            weights = jnp.exp2(score_t * score_factor - new_max * score_factor)
             if masked:
                 weights = jnp.where(is_valid, weights, 0.0)
-            correction_factor = jnp.exp(run_max - new_max)
+            correction_factor = jnp.exp2((run_max - new_max) * score_factor)
             l_sc[:, r0:r0 + chunk] = l_sc[:, r0:r0 + chunk] * correction_factor + jnp.sum(weights, axis=0, keepdims=True)
             m_sc[:, r0:r0 + chunk] = new_max
             c_sc[:, r0:r0 + chunk] = correction_factor

time: 134 us -> 132 us (0.985)
  Pallas kernels: 39.6 us -> 36.9 us
    pallas_call x1, Pallas kernels: 39.6 us -> 36.9 us  [causal_attention(): pl.pallas_call(kernel, in_specs=[pl.BlockSpec(memory_space=pltpu.SMEM)] +...]
  transfers between devices with their start and end apart: 11 -> 11, of which waited for: 10 -> 10; matrix products, arithmetic and copies ran while one was open for 8% -> 9% of each run, Pallas kernels for 0% -> 0%
where the time goes in v11:
time: 132 us; the launch traced here: 131 us
  waiting for transfers between devices  49.7 us (38%)
  Pallas kernels  36.9 us (28%)
  between operations  14.5 us (11%)
  starting transfers between devices  11.4 us (9%)
  local copies, waits for them, and re-layouts  8.79 us (7%)
  other arithmetic  5.43 us (4%)
  matrix products  4.24 us (3%)
    ppermute x5, waiting for transfers between devices, shifted(): return lax.ppermute(block, axis, route)  38.9 us
    pallas_call x1, Pallas kernels, causal_attention(): pl.pallas_call(kernel, in_specs=[pl.BlockSpec(memory_space=pltpu.SMEM)] +...  36.9 us
    ppermute x3, waiting for transfers between devices, summed_over(): total = total + lax.ppermute(total, axis, route)  8.8 us
    ppermute x5, starting transfers between devices, shifted(): return lax.ppermute(block, axis, route)  6.46 us
    unnamed x22, local copies, waits for them, and re-layouts  5.39 us
    ppermute x3, starting transfers between devices, summed_over(): total = total + lax.ppermute(total, axis, route)  4.76 us
  transfers between devices with their start and end apart: 11, of which 10 were waited for; matrix products, arithmetic and copies ran while one was open for 9% of the time, Pallas kernels for 0%

profile of v11, /device:TPU:230, one launch (start us, length us, event | category | flops | bytes accessed | tf_op | source)
XLA Modules:
  0.0 131.0 jit_solution(6400682666547421707)
XLA Ops:
  7.2 0.0 copy-start
  7.2 0.0 all-gather.3.cloned.1.call-start
  7.2 0.8 reshape.1138
  8.0 0.0 copy-start.4
  8.0 0.6 reduce-window.6
  8.6 0.2 slice_reduce_fusion
  8.8 0.1 copy.46
  8.9 0.1 broadcast.184
  9.1 0.3 slice_reduce_fusion.1
  9.3 1.3 copy.47
  10.6 0.8 multiply_bitcast_fusion
  11.4 0.1 fusion.16
  11.5 0.3 fusion.79
  11.9 0.1 collective-permute-start
  12.0 0.7 pad_maximum_fusion.4
  12.7 0.0 all-gather.3.cloned.1.call-update
  12.7 0.8 collective-permute-done
  13.6 0.1 fusion.66
  13.7 0.1 dynamic-slice.5
  13.8 0.1 broadcast_select_fusion
  13.9 0.1 fusion.23
  14.0 1.3 collective-permute-start.2
  15.3 0.9 fusion.80
  16.2 1.3 collective-permute-start.1
  17.5 8.3 %collective-permute-done.2 = bf16[1,528,128]{2,1,0:T(8,128)(2,1)S(1)} collective-permute-done((bf16[1,528,128]{2,1,0:T(8,128)(2,1)S(1)}, bf16[1,528,128]{2,1,0:T(8,128)(2,1)S(1)}, u32[]{:S(2)}, u32[]{:S(2)}) %collective-permute-start.2) | collective-permute-done | bytes 135200 | tf_op jit(solution)/shard_map/ppermute | solution.py:85
  25.9 0.2 collective-permute-done.1
  26.1 0.1 mul.266
  26.2 0.1 mul.267
  26.3 0.1 fusion.28
  26.5 1.3 collective-permute-start.3
  27.8 0.1 mul.270
  27.8 0.1 mul.271
  28.0 6.7 %collective-permute-done.3 = bf16[1,528,128]{2,1,0:T(8,128)(2,1)S(1)} collective-permute-done((bf16[1,528,128]{2,1,0:T(8,128)(2,1)S(1)}, bf16[1,528,128]{2,1,0:T(8,128)(2,1)S(1)}, u32[]{:S(2)}, u32[]{:S(2)}) %collective-permute-start.3) | collective-permute-done | bytes 135200 | tf_op jit(solution)/shard_map/ppermute | solution.py:85
  34.7 0.2 fusion.77
  34.9 0.0 copy-start.5
  34.9 0.0 copy-start.7
  35.0 1.3 collective-permute-start.4
  36.3 0.1 mul.275
  36.4 0.1 mul.276
  36.5 10.6 %collective-permute-done.4 = bf16[1,528,128]{2,1,0:T(8,128)(2,1)S(1)} collective-permute-done((bf16[1,528,128]{2,1,0:T(8,128)(2,1)S(1)}, bf16[1,528,128]{2,1,0:T(8,128)(2,1)S(1)}, u32[]{:S(2)}, u32[]{:S(2)}) %collective-permute-start.4) | collective-permute-done | bytes 135200 | tf_op jit(solution)/shard_map/ppermute | solution.py:85
  47.1 0.3 add_convert_fusion.1
  47.4 1.3 collective-permute-start.5
  48.8 12.9 %collective-permute-done.5 = bf16[1,528,128]{2,1,0:T(8,128)(2,1)S(1)} collective-permute-done((bf16[1,528,128]{2,1,0:T(8,128)(2,1)S(1)}, bf16[1,528,128]{2,1,0:T(8,128)(2,1)S(1)}, u32[]{:S(2)}, u32[]{:S(2)}) %collective-permute-start.5) | collective-permute-done | bytes 135200 | tf_op jit(solution)/shard_map/ppermute | solution.py:85
  61.7 0.2 add_convert_fusion
  61.9 0.1 collective-permute-start.6
  62.0 0.2 add_add_fusion
  62.2 1.2 collective-permute-done.6
  63.4 0.7 fusion.9
  64.1 2.4 %fusion.11 = f32[256,1,16,64]{0,3,2,1:T(8,128)S(1)} fusion(f32[256,1,16,64]{0,3,2,1:T(8,128)S(1)} %fusion.9, bf16[256,16,64]{0,2,1:T(8,128)(2,1)S(1)} %bitcast.152, f32[16,256]{1,0:T(8,128)S(1)} %copy-done.5, f32[16,256]{1,0:T(8,128)S(1)} %get-tuple-element.15, f32[256,256]{1,0:T(8,128)} %fusion.80, pred[256,256]{1,0:T(8,128)(4,1)S(1)} %iota_compare_fusion.1, ...), kind=kOutput, calls=%fused_computation.13 | convolution fusion | flops 141557760 | bytes 3506240 | tf_op jit(solution)/shard_map/ghts,sghp->tghp/dot_general | solution.py:199
  66.5 0.3 copy.50
  66.8 0.4 multiply_reduce_fusion
  67.2 1.6 %collective-permute-start.7 = (f32[256]{0:T(256)S(1)}, f32[256]{0:T(256)S(1)}, u32[]{:S(2)}, u32[]{:S(2)}) collective-permute-start(f32[256]{0:T(256)S(1)} %multiply_reduce_fusion), channel_id=1, source_target_pairs={{0,1},{1,0},{2,3},{3,2},{4,5},{5,4},{6,7},{7,6},{8,9},{9,8},{10,11... | collective-permute-start | bytes 3080 | tf_op jit(solution)/shard_map/ppermute | solution.py:94
  68.8 2.1 %collective-permute-done.7 = f32[256]{0:T(256)S(1)} collective-permute-done((f32[256]{0:T(256)S(1)}, f32[256]{0:T(256)S(1)}, u32[]{:S(2)}, u32[]{:S(2)}) %collective-permute-start.7) | collective-permute-done | bytes 1056 | tf_op jit(solution)/shard_map/ppermute | solution.py:94
  70.9 3.2 %collective-permute-start.8 = (f32[256]{0:T(256)S(1)}, f32[256]{0:T(256)S(1)}, u32[]{:S(2)}, u32[]{:S(2)}) collective-permute-start(f32[256]{0:T(256)S(1)} %add.588), channel_id=1, source_target_pairs={{0,2},{1,3},{2,0},{3,1},{4,6},{5,7},{6,4},{7,5},{8,10},{9,11},{10,... | collective-permute-start | bytes 3080 | tf_op jit(solution)/shard_map/ppermute | solution.py:94
  74.0 1.9 %collective-permute-done.8 = f32[256]{0:T(256)S(1)} collective-permute-done((f32[256]{0:T(256)S(1)}, f32[256]{0:T(256)S(1)}, u32[]{:S(2)}, u32[]{:S(2)}) %collective-permute-start.8) | collective-permute-done | bytes 1056 | tf_op jit(solution)/shard_map/ppermute | solution.py:94
  76.0 1.1 copy.52
  77.1 0.6 copy.42
  77.7 0.9 copy.53
  78.6 4.8 %collective-permute-done.9 = f32[256]{0:T(256)S(1)} collective-permute-done((f32[256]{0:T(256)S(1)}, f32[256]{0:T(256)S(1)}, u32[]{:S(2)}, u32[]{:S(2)}) %collective-permute-start.9) | collective-permute-done | bytes 1056 | tf_op jit(solution)/shard_map/ppermute | solution.py:94
  83.4 1.2 multiply_convert_fusion
  84.6 36.9 %shard_map.122 = bf16[128,2048]{1,0:T(8,128)(2,1)} custom-call(s32[1]{0:T(128)} %bitcast.pos_ref, bf16[128,2048]{1,0:T(8,128)(2,1)} %bitcast.159, bf16[32,2,256,128]{3,2,1,0:T(8,128)(2,1)} %bitcast.137), custom_call_target="tpu_custom_call" | custom-call | tf_op jit(solution)/shard_map/pallas_call | solution.py:66
  121.5 1.1 copy.54
  122.7 0.6 copy.43
  123.3 0.9 copy.64
  (59 shorter events, 0.6 us)
Async XLA Ops:
  7.2 4.4 %copy-start = (bf16[256,128]{1,0:T(8,128)(2,1)S(1)}, bf16[256,128]{1,0:T(8,128)(2,1)}, u32[]{:S(2)}) copy-start(bf16[256,128]{1,0:T(8,128)(2,1)} %param.16) | copy-start | bytes 196612
  7.2 4.8 %copy-start.2 = (bf16[256,128]{1,0:T(8,128)(2,1)S(1)}, bf16[256,128]{1,0:T(8,128)(2,1)}, u32[]{:S(2)}) copy-start(bf16[256,128]{1,0:T(8,128)(2,1)} %param.13) | copy-start | bytes 196612
  7.2 4.8 %copy-start.3 = (bf16[256,128]{1,0:T(8,128)(2,1)S(1)}, bf16[256,128]{1,0:T(8,128)(2,1)}, u32[]{:S(2)}) copy-start(bf16[256,128]{1,0:T(8,128)(2,1)} %param.12) | copy-start | bytes 196612
  7.2 77.4 %all-gather.3.cloned.1.call-start = ((), (), s32[]{:S(2)}) async-start(), calls=%async_computation | async-start | bytes 4325376 | tf_op jit(solution)/shard_map/all_gather | solution.py:183
  8.0 7.3 %copy-start.4 = (bf16[256,128]{1,0:T(8,128)(2,1)S(1)}, bf16[256,128]{1,0:T(8,128)(2,1)}, u32[]{:S(2)}) copy-start(bf16[256,128]{1,0:T(8,128)(2,1)} %param.17) | copy-start | bytes 196612
  11.9 1.6 %collective-permute-start = (bf16[1,1040,128]{2,1,0:T(8,128)(2,1)S(1)}, bf16[1,1040,128]{2,1,0:T(8,128)(2,1)S(1)}, u32[]{:S(2)}, u32[]{:S(2)}) collective-permute-start(bf16[1,1040,128]{2,1,0:T(8,128)(2,1)S(1)} %fusion.21), channel_id=1, source_target_pairs={{0,8},{8,0},{1,9},{9,1},{2,10},{10,2},{3,11},{11,3},{4,12},{12,4},... | collective-permute-start | bytes 798728 | tf_op jit(solution)/shard_map/ppermute | solution.py:142
  14.0 11.9 %collective-permute-start.2 = (bf16[1,528,128]{2,1,0:T(8,128)(2,1)S(1)}, bf16[1,528,128]{2,1,0:T(8,128)(2,1)S(1)}, u32[]{:S(2)}, u32[]{:S(2)}) collective-permute-start(bf16[1,528,128]{2,1,0:T(8,128)(2,1)S(1)} %pad_maximum_fusion), channel_id=1, source_target_pairs={{0,32},{16,48},{32,64},{48,80},{64,96},{80,112},{96,128},{112,144}... | collective-permute-start | bytes 405512 | tf_op jit(solution)/shard_map/ppermute | solution.py:85
  16.2 9.9 %collective-permute-start.1 = (bf16[1,528,128]{2,1,0:T(8,128)(2,1)S(1)}, bf16[1,528,128]{2,1,0:T(8,128)(2,1)S(1)}, u32[]{:S(2)}, u32[]{:S(2)}) collective-permute-start(bf16[1,528,128]{2,1,0:T(8,128)(2,1)S(1)} %pad_maximum_fusion), channel_id=1, source_target_pairs={{0,16},{16,32},{32,48},{48,64},{64,80},{80,96},{96,112},{112,128},... | collective-permute-start | bytes 405512 | tf_op jit(solution)/shard_map/ppermute | solution.py:85
  26.5 8.2 %collective-permute-start.3 = (bf16[1,528,128]{2,1,0:T(8,128)(2,1)S(1)}, bf16[1,528,128]{2,1,0:T(8,128)(2,1)S(1)}, u32[]{:S(2)}, u32[]{:S(2)}) collective-permute-start(bf16[1,528,128]{2,1,0:T(8,128)(2,1)S(1)} %pad_maximum_fusion.1), channel_id=1, source_target_pairs={{0,32},{16,48},{32,64},{48,80},{64,96},{80,112},{96,128},{112,144}... | collective-permute-start | bytes 405512 | tf_op jit(solution)/shard_map/ppermute | solution.py:85
  34.9 29.1 %copy-start.5 = (f32[16,256]{1,0:T(8,128)S(1)}, f32[16,256]{1,0:T(8,128)}, u32[]{:S(2)}) copy-start(f32[16,256]{1,0:T(8,128)} %param.18) | copy-start | bytes 49156
  34.9 29.1 %copy-start.7 = (f32[16]{0:T(128)S(1)}, f32[16]{0:T(128)}, u32[]{:S(2)}) copy-start(f32[16]{0:T(128)} %param.20) | copy-start | bytes 196
  35.0 12.1 %collective-permute-start.4 = (bf16[1,528,128]{2,1,0:T(8,128)(2,1)S(1)}, bf16[1,528,128]{2,1,0:T(8,128)(2,1)S(1)}, u32[]{:S(2)}, u32[]{:S(2)}) collective-permute-start(bf16[1,528,128]{2,1,0:T(8,128)(2,1)S(1)} %pad_maximum_fusion.2), channel_id=1, source_target_pairs={{0,64},{16,80},{32,96},{48,112},{64,128},{80,144},{96,160},{112,17... | collective-permute-start | bytes 405512 | tf_op jit(solution)/shard_map/ppermute | solution.py:85
  47.4 14.3 %collective-permute-start.5 = (bf16[1,528,128]{2,1,0:T(8,128)(2,1)S(1)}, bf16[1,528,128]{2,1,0:T(8,128)(2,1)S(1)}, u32[]{:S(2)}, u32[]{:S(2)}) collective-permute-start(bf16[1,528,128]{2,1,0:T(8,128)(2,1)S(1)} %pad_maximum_fusion.3), channel_id=1, source_target_pairs={{0,128},{16,144},{32,160},{48,176},{64,192},{80,208},{96,224},{112... | collective-permute-start | bytes 405512 | tf_op jit(solution)/shard_map/ppermute | solution.py:85
  61.9 1.4 %collective-permute-start.6 = (bf16[1,8,64,128]{3,2,1,0:T(8,128)(2,1)S(1)}, bf16[1,8,64,128]{3,2,1,0:T(8,128)(2,1)S(1)}, u32[]{:S(2)}, u32[]{:S(2)}) collective-permute-start(bf16[1,8,64,128]{3,2,1,0:T(8,128)(2,1)S(1)} %add_convert_fusion), channel_id=1, source_target_pairs={{0,8},{8,0},{1,9},{9,1},{2,10},{10,2},{3,11},{11,3},{4,12},{12,4},... | collective-permute-start | bytes 393224 | tf_op jit(solution)/shard_map/ppermute | solution.py:156
  64.1 2.8 %copy-start.1 = (bf16[256,1024]{1,0:T(8,128)(2,1)S(1)}, bf16[256,1024]{1,0:T(8,128)(2,1)}, u32[]{:S(2)}) copy-start(bf16[256,1024]{1,0:T(8,128)(2,1)} %param.15) | copy-start | bytes 1572868
  66.5 12.1 %copy-start.6 = (bf16[1024]{0:T(1024)(128)(2,1)S(1)}, bf16[1024]{0:T(1024)(128)(2,1)}, u32[]{:S(2)}) copy-start(bf16[1024]{0:T(1024)(128)(2,1)} %param.21) | copy-start | bytes 6148
  67.2 3.6 %collective-permute-start.7 = (f32[256]{0:T(256)S(1)}, f32[256]{0:T(256)S(1)}, u32[]{:S(2)}, u32[]{:S(2)}) collective-permute-start(f32[256]{0:T(256)S(1)} %multiply_reduce_fusion), channel_id=1, source_target_pairs={{0,1},{1,0},{2,3},{3,2},{4,5},{5,4},{6,7},{7,6},{8,9},{9,8},{10,11... | collective-permute-start | bytes 3080 | tf_op jit(solution)/shard_map/ppermute | solution.py:94
  70.9 5.1 %collective-permute-start.8 = (f32[256]{0:T(256)S(1)}, f32[256]{0:T(256)S(1)}, u32[]{:S(2)}, u32[]{:S(2)}) collective-permute-start(f32[256]{0:T(256)S(1)} %add.588), channel_id=1, source_target_pairs={{0,2},{1,3},{2,0},{3,1},{4,6},{5,7},{6,4},{7,5},{8,10},{9,11},{10,... | collective-permute-start | bytes 3080 | tf_op jit(solution)/shard_map/ppermute | solution.py:94
  76.0 7.5 %collective-permute-start.9 = (f32[256]{0:T(256)S(1)}, f32[256]{0:T(256)S(1)}, u32[]{:S(2)}, u32[]{:S(2)}) collective-permute-start(f32[256]{0:T(256)S(1)} %add.589), channel_id=1, source_target_pairs={{0,4},{1,5},{2,6},{3,7},{4,0},{5,1},{6,2},{7,3},{8,12},{9,13},{10,... | collective-permute-start | bytes 3080 | tf_op jit(solution)/shard_map/ppermute | solution.py:94
Sparse Core Ops, SparseCore 0:
  12.8 65.2 all-gather.2

commit v12 on v11

--- a/solution.py
+++ b/solution.py
@@ -17,7 +17,7 @@
 CTX = ("chip", "core")
 
 
-def attend_kernel(pos_ref, qt_ref, kv_ref, o_ref, p_sc, m_sc, l_sc, c_sc, acc_sc, *, tok, width, chunk):
+def attend_kernel(pos_ref, qt_ref, kv_ref, o_ref, p_sc, p2_sc, m_sc, l_sc, c_sc, acc_sc, *, tok, width, chunk):
     position = pos_ref[0]
     score_factor = width ** (-0.5) * 1.4426950408889634
     rows = qt_ref.shape[1]
@@ -49,10 +49,35 @@
             p_sc[:, r0:r0 + chunk] = weights.astype(jnp.bfloat16)
         acc_sc[...] = acc_sc[...] * c_sc[...] + lax.dot_general(kv_ref[kb, 1], p_sc[...], (((0,), (0,)), ((), ())), preferred_element_type=jnp.float32)
 
-    def body(kb, carry):
-        run_block(kb, False)
+    def run_pair(kb):
+        keys = (kv_ref[kb, 0], kv_ref[kb + 1, 0])
+        for c in range(rows // chunk):
+            r0 = c * chunk
+            scores = [jnp.dot(k, qt_ref[:, r0:r0 + chunk], preferred_element_type=jnp.float32) for k in keys]
+            run_max = m_sc[:, r0:r0 + chunk]
+            block_max = jnp.maximum(jnp.max(scores[0], axis=0, keepdims=True), jnp.max(scores[1], axis=0, keepdims=True))
+            new_max = jnp.maximum(run_max, block_max)
+            weights = [jnp.exp2(s * score_factor - new_max * score_factor) for s in scores]
+            correction_factor = jnp.exp2((run_max - new_max) * score_factor)
+            l_sc[:, r0:r0 + chunk] = l_sc[:, r0:r0 + chunk] * correction_factor + (
+                jnp.sum(weights[0], axis=0, keepdims=True) + jnp.sum(weights[1], axis=0, keepdims=True))
+            m_sc[:, r0:r0 + chunk] = new_max
+            c_sc[:, r0:r0 + chunk] = correction_factor
+            p_sc[:, r0:r0 + chunk] = weights[0].astype(jnp.bfloat16)
+            p2_sc[:, r0:r0 + chunk] = weights[1].astype(jnp.bfloat16)
+        acc_sc[...] = acc_sc[...] * c_sc[...] + (
+            lax.dot_general(kv_ref[kb, 1], p_sc[...], (((0,), (0,)), ((), ())), preferred_element_type=jnp.float32)
+            + lax.dot_general(kv_ref[kb + 1, 1], p2_sc[...], (((0,), (0,)), ((), ())), preferred_element_type=jnp.float32))
+
+    def pair_body(i, carry):
+        run_pair(2 * i)
         return carry
-    lax.fori_loop(0, position, body, 0)
+    lax.fori_loop(0, position // 2, pair_body, 0)
+
+    @pl.when(lax.rem(position, 2) == 1)
+    def _odd():
+        run_block(position - 1, False)
+
     run_block(position, True)
     o_ref[...] = (acc_sc[...] / l_sc[...]).astype(o_ref.dtype)
 
@@ -69,6 +94,7 @@
         out_specs=pl.BlockSpec(memory_space=pltpu.VMEM),
         out_shape=jax.ShapeDtypeStruct((width, rows), queries.dtype),
         scratch_shapes=[
+            pltpu.VMEM((tok_rows, rows), jnp.bfloat16),
             pltpu.VMEM((tok_rows, rows), jnp.bfloat16),
             pltpu.VMEM((1, rows), jnp.float32),
             pltpu.VMEM((1, rows), jnp.float32),

time: 132 us -> 127 us (0.962)
  Pallas kernels: 36.9 us -> 32.3 us
    pallas_call x1, Pallas kernels: 36.9 us -> 32.3 us  [causal_attention(): pl.pallas_call(kernel, in_specs=[pl.BlockSpec(memory_space=pltpu.SMEM)] +...]
where the time goes in v12:
time: 127 us; the launch traced here: 126 us
  waiting for transfers between devices  49.6 us (39%)
  Pallas kernels  32.3 us (25%)
  between operations  14.5 us (11%)
  starting transfers between devices  11.6 us (9%)
  local copies, waits for them, and re-layouts  8.79 us (7%)
  other arithmetic  5.43 us (4%)
  matrix products  4.24 us (3%)
    ppermute x5, waiting for transfers between devices, shifted(): return lax.ppermute(block, axis, route)  38.9 us
    pallas_call x1, Pallas kernels, causal_attention(): pl.pallas_call(kernel, in_specs=[pl.BlockSpec(memory_space=pltpu.SMEM)] +...  32.3 us
    ppermute x3, waiting for transfers between devices, summed_over(): total = total + lax.ppermute(total, axis, route)  8.64 us
    ppermute x5, starting transfers between devices, shifted(): return lax.ppermute(block, axis, route)  6.46 us
    unnamed x22, local copies, waits for them, and re-layouts  5.39 us
    ppermute x3, starting transfers between devices, summed_over(): total = total + lax.ppermute(total, axis, route)  4.92 us
  transfers between devices with their start and end apart: 11, of which 10 were waited for; matrix products, arithmetic and copies ran while one was open for 9% of the time, Pallas kernels for 0%

profile of v12, /device:TPU:230, one launch (start us, length us, event | category | flops | bytes accessed | tf_op | source)
XLA Modules:
  0.0 126.4 jit_solution(3100759176069144421)
XLA Ops:
  7.2 0.0 copy-start
  7.2 0.0 all-gather.3.cloned.1.call-start
  7.2 0.8 reshape.1138
  8.0 0.0 copy-start.4
  8.0 0.6 reduce-window.6
  8.6 0.2 slice_reduce_fusion
  8.8 0.1 copy.46
  8.9 0.1 broadcast.184
  9.1 0.3 slice_reduce_fusion.1
  9.3 1.3 copy.47
  10.6 0.8 multiply_bitcast_fusion
  11.4 0.1 fusion.16
  11.5 0.3 fusion.79
  11.9 0.1 collective-permute-start
  12.0 0.7 pad_maximum_fusion.4
  12.7 0.0 all-gather.3.cloned.1.call-update
  12.7 0.8 collective-permute-done
  13.6 0.1 fusion.66
  13.7 0.1 dynamic-slice.5
  13.8 0.1 broadcast_select_fusion
  13.9 0.1 fusion.23
  14.0 1.3 %collective-permute-start.2 = (bf16[1,528,128]{2,1,0:T(8,128)(2,1)S(1)}, bf16[1,528,128]{2,1,0:T(8,128)(2,1)S(1)}, u32[]{:S(2)}, u32[]{:S(2)}) collective-permute-start(bf16[1,528,128]{2,1,0:T(8,128)(2,1)S(1)} %pad_maximum_fusion), channel_id=1, source_target_pairs={{0,32},{16,48},{32,64},{48,80},{64,96},{80,112},{96,128},{112,144}... | collective-permute-start | bytes 405512 | tf_op jit(solution)/shard_map/ppermute | solution.py:111
  15.3 0.9 fusion.80
  16.2 1.3 %collective-permute-start.1 = (bf16[1,528,128]{2,1,0:T(8,128)(2,1)S(1)}, bf16[1,528,128]{2,1,0:T(8,128)(2,1)S(1)}, u32[]{:S(2)}, u32[]{:S(2)}) collective-permute-start(bf16[1,528,128]{2,1,0:T(8,128)(2,1)S(1)} %pad_maximum_fusion), channel_id=1, source_target_pairs={{0,16},{16,32},{32,48},{48,64},{64,80},{80,96},{96,112},{112,128},... | collective-permute-start | bytes 405512 | tf_op jit(solution)/shard_map/ppermute | solution.py:111
  17.5 8.3 %collective-permute-done.2 = bf16[1,528,128]{2,1,0:T(8,128)(2,1)S(1)} collective-permute-done((bf16[1,528,128]{2,1,0:T(8,128)(2,1)S(1)}, bf16[1,528,128]{2,1,0:T(8,128)(2,1)S(1)}, u32[]{:S(2)}, u32[]{:S(2)}) %collective-permute-start.2) | collective-permute-done | bytes 135200 | tf_op jit(solution)/shard_map/ppermute | solution.py:111
  25.9 0.2 collective-permute-done.1
  26.1 0.1 mul.266
  26.2 0.1 mul.267
  26.3 0.1 fusion.28
  26.5 1.3 %collective-permute-start.3 = (bf16[1,528,128]{2,1,0:T(8,128)(2,1)S(1)}, bf16[1,528,128]{2,1,0:T(8,128)(2,1)S(1)}, u32[]{:S(2)}, u32[]{:S(2)}) collective-permute-start(bf16[1,528,128]{2,1,0:T(8,128)(2,1)S(1)} %pad_maximum_fusion.1), channel_id=1, source_target_pairs={{0,32},{16,48},{32,64},{48,80},{64,96},{80,112},{96,128},{112,144}... | collective-permute-start | bytes 405512 | tf_op jit(solution)/shard_map/ppermute | solution.py:111
  27.8 0.1 mul.270
  27.8 0.1 mul.271
  28.0 6.7 %collective-permute-done.3 = bf16[1,528,128]{2,1,0:T(8,128)(2,1)S(1)} collective-permute-done((bf16[1,528,128]{2,1,0:T(8,128)(2,1)S(1)}, bf16[1,528,128]{2,1,0:T(8,128)(2,1)S(1)}, u32[]{:S(2)}, u32[]{:S(2)}) %collective-permute-start.3) | collective-permute-done | bytes 135200 | tf_op jit(solution)/shard_map/ppermute | solution.py:111
  34.7 0.2 fusion.77
  34.9 0.0 copy-start.5
  35.0 1.3 %collective-permute-start.4 = (bf16[1,528,128]{2,1,0:T(8,128)(2,1)S(1)}, bf16[1,528,128]{2,1,0:T(8,128)(2,1)S(1)}, u32[]{:S(2)}, u32[]{:S(2)}) collective-permute-start(bf16[1,528,128]{2,1,0:T(8,128)(2,1)S(1)} %pad_maximum_fusion.2), channel_id=1, source_target_pairs={{0,64},{16,80},{32,96},{48,112},{64,128},{80,144},{96,160},{112,17... | collective-permute-start | bytes 405512 | tf_op jit(solution)/shard_map/ppermute | solution.py:111
  36.3 0.1 mul.275
  36.4 0.1 mul.276
  36.5 10.7 %collective-permute-done.4 = bf16[1,528,128]{2,1,0:T(8,128)(2,1)S(1)} collective-permute-done((bf16[1,528,128]{2,1,0:T(8,128)(2,1)S(1)}, bf16[1,528,128]{2,1,0:T(8,128)(2,1)S(1)}, u32[]{:S(2)}, u32[]{:S(2)}) %collective-permute-start.4) | collective-permute-done | bytes 135200 | tf_op jit(solution)/shard_map/ppermute | solution.py:111
  47.2 0.3 add_convert_fusion.1
  47.5 1.3 %collective-permute-start.5 = (bf16[1,528,128]{2,1,0:T(8,128)(2,1)S(1)}, bf16[1,528,128]{2,1,0:T(8,128)(2,1)S(1)}, u32[]{:S(2)}, u32[]{:S(2)}) collective-permute-start(bf16[1,528,128]{2,1,0:T(8,128)(2,1)S(1)} %pad_maximum_fusion.3), channel_id=1, source_target_pairs={{0,128},{16,144},{32,160},{48,176},{64,192},{80,208},{96,224},{112... | collective-permute-start | bytes 405512 | tf_op jit(solution)/shard_map/ppermute | solution.py:111
  48.8 12.9 %collective-permute-done.5 = bf16[1,528,128]{2,1,0:T(8,128)(2,1)S(1)} collective-permute-done((bf16[1,528,128]{2,1,0:T(8,128)(2,1)S(1)}, bf16[1,528,128]{2,1,0:T(8,128)(2,1)S(1)}, u32[]{:S(2)}, u32[]{:S(2)}) %collective-permute-start.5) | collective-permute-done | bytes 135200 | tf_op jit(solution)/shard_map/ppermute | solution.py:111
  61.8 0.2 add_convert_fusion
  61.9 0.1 collective-permute-start.6
  62.0 0.2 add_add_fusion
  62.2 1.2 collective-permute-done.6
  63.4 0.7 fusion.9
  64.1 0.0 copy-start.1
  64.1 2.4 %fusion.11 = f32[256,1,16,64]{0,3,2,1:T(8,128)S(1)} fusion(f32[256,1,16,64]{0,3,2,1:T(8,128)S(1)} %fusion.9, bf16[256,16,64]{0,2,1:T(8,128)(2,1)S(1)} %bitcast.152, f32[16,256]{1,0:T(8,128)S(1)} %copy-done.5, f32[16,256]{1,0:T(8,128)S(1)} %get-tuple-element.15, f32[256,256]{1,0:T(8,128)} %fusion.80, pred[256,256]{1,0:T(8,128)(4,1)S(1)} %iota_compare_fusion.1, ...), kind=kOutput, calls=%fused_computation.13 | convolution fusion | flops 141557760 | bytes 3506240 | tf_op jit(solution)/shard_map/ghts,sghp->tghp/dot_general | solution.py:225
  66.5 0.3 copy.50
  66.9 0.4 multiply_reduce_fusion
  67.3 1.9 %collective-permute-start.7 = (f32[256]{0:T(256)S(1)}, f32[256]{0:T(256)S(1)}, u32[]{:S(2)}, u32[]{:S(2)}) collective-permute-start(f32[256]{0:T(256)S(1)} %multiply_reduce_fusion), channel_id=1, source_target_pairs={{0,1},{1,0},{2,3},{3,2},{4,5},{5,4},{6,7},{7,6},{8,9},{9,8},{10,11... | collective-permute-start | bytes 3080 | tf_op jit(solution)/shard_map/ppermute | solution.py:120
  69.1 1.8 %collective-permute-done.7 = f32[256]{0:T(256)S(1)} collective-permute-done((f32[256]{0:T(256)S(1)}, f32[256]{0:T(256)S(1)}, u32[]{:S(2)}, u32[]{:S(2)}) %collective-permute-start.7) | collective-permute-done | bytes 1056 | tf_op jit(solution)/shard_map/ppermute | solution.py:120
  70.9 3.1 %collective-permute-start.8 = (f32[256]{0:T(256)S(1)}, f32[256]{0:T(256)S(1)}, u32[]{:S(2)}, u32[]{:S(2)}) collective-permute-start(f32[256]{0:T(256)S(1)} %add.588), channel_id=1, source_target_pairs={{0,2},{1,3},{2,0},{3,1},{4,6},{5,7},{6,4},{7,5},{8,10},{9,11},{10,... | collective-permute-start | bytes 3080 | tf_op jit(solution)/shard_map/ppermute | solution.py:120
  74.0 2.0 %collective-permute-done.8 = f32[256]{0:T(256)S(1)} collective-permute-done((f32[256]{0:T(256)S(1)}, f32[256]{0:T(256)S(1)}, u32[]{:S(2)}, u32[]{:S(2)}) %collective-permute-start.8) | collective-permute-done | bytes 1056 | tf_op jit(solution)/shard_map/ppermute | solution.py:120
  76.0 1.1 copy.52
  77.1 0.6 copy.42
  77.7 0.9 copy.53
  78.6 4.8 %collective-permute-done.9 = f32[256]{0:T(256)S(1)} collective-permute-done((f32[256]{0:T(256)S(1)}, f32[256]{0:T(256)S(1)}, u32[]{:S(2)}, u32[]{:S(2)}) %collective-permute-start.9) | collective-permute-done | bytes 1056 | tf_op jit(solution)/shard_map/ppermute | solution.py:120
  83.5 1.2 multiply_convert_fusion
  84.7 32.3 %shard_map.122 = bf16[128,2048]{1,0:T(8,128)(2,1)} custom-call(s32[1]{0:T(128)} %bitcast.pos_ref, bf16[128,2048]{1,0:T(8,128)(2,1)} %bitcast.159, bf16[32,2,256,128]{3,2,1,0:T(8,128)(2,1)} %bitcast.137), custom_call_target="tpu_custom_call" | custom-call | tf_op jit(solution)/shard_map/pallas_call | solution.py:91
  117.0 1.1 copy.54
  118.1 0.6 copy.43
  118.7 0.9 copy.64
  (59 shorter events, 0.6 us)
Async XLA Ops:
  7.2 4.4 %copy-start = (bf16[256,128]{1,0:T(8,128)(2,1)S(1)}, bf16[256,128]{1,0:T(8,128)(2,1)}, u32[]{:S(2)}) copy-start(bf16[256,128]{1,0:T(8,128)(2,1)} %param.16) | copy-start | bytes 196612
  7.2 4.8 %copy-start.2 = (bf16[256,128]{1,0:T(8,128)(2,1)S(1)}, bf16[256,128]{1,0:T(8,128)(2,1)}, u32[]{:S(2)}) copy-start(bf16[256,128]{1,0:T(8,128)(2,1)} %param.13) | copy-start | bytes 196612
  7.2 4.8 %copy-start.3 = (bf16[256,128]{1,0:T(8,128)(2,1)S(1)}, bf16[256,128]{1,0:T(8,128)(2,1)}, u32[]{:S(2)}) copy-start(bf16[256,128]{1,0:T(8,128)(2,1)} %param.12) | copy-start | bytes 196612
  7.2 77.5 %all-gather.3.cloned.1.call-start = ((), (), s32[]{:S(2)}) async-start(), calls=%async_computation | async-start | bytes 4325376 | tf_op jit(solution)/shard_map/all_gather | solution.py:209
  8.0 7.3 %copy-start.4 = (bf16[256,128]{1,0:T(8,128)(2,1)S(1)}, bf16[256,128]{1,0:T(8,128)(2,1)}, u32[]{:S(2)}) copy-start(bf16[256,128]{1,0:T(8,128)(2,1)} %param.17) | copy-start | bytes 196612
  11.9 1.6 %collective-permute-start = (bf16[1,1040,128]{2,1,0:T(8,128)(2,1)S(1)}, bf16[1,1040,128]{2,1,0:T(8,128)(2,1)S(1)}, u32[]{:S(2)}, u32[]{:S(2)}) collective-permute-start(bf16[1,1040,128]{2,1,0:T(8,128)(2,1)S(1)} %fusion.21), channel_id=1, source_target_pairs={{0,8},{8,0},{1,9},{9,1},{2,10},{10,2},{3,11},{11,3},{4,12},{12,4},... | collective-permute-start | bytes 798728 | tf_op jit(solution)/shard_map/ppermute | solution.py:168
  14.0 11.9 %collective-permute-start.2 = (bf16[1,528,128]{2,1,0:T(8,128)(2,1)S(1)}, bf16[1,528,128]{2,1,0:T(8,128)(2,1)S(1)}, u32[]{:S(2)}, u32[]{:S(2)}) collective-permute-start(bf16[1,528,128]{2,1,0:T(8,128)(2,1)S(1)} %pad_maximum_fusion), channel_id=1, source_target_pairs={{0,32},{16,48},{32,64},{48,80},{64,96},{80,112},{96,128},{112,144}... | collective-permute-start | bytes 405512 | tf_op jit(solution)/shard_map/ppermute | solution.py:111
  16.2 9.9 %collective-permute-start.1 = (bf16[1,528,128]{2,1,0:T(8,128)(2,1)S(1)}, bf16[1,528,128]{2,1,0:T(8,128)(2,1)S(1)}, u32[]{:S(2)}, u32[]{:S(2)}) collective-permute-start(bf16[1,528,128]{2,1,0:T(8,128)(2,1)S(1)} %pad_maximum_fusion), channel_id=1, source_target_pairs={{0,16},{16,32},{32,48},{48,64},{64,80},{80,96},{96,112},{112,128},... | collective-permute-start | bytes 405512 | tf_op jit(solution)/shard_map/ppermute | solution.py:111
  26.5 8.2 %collective-permute-start.3 = (bf16[1,528,128]{2,1,0:T(8,128)(2,1)S(1)}, bf16[1,528,128]{2,1,0:T(8,128)(2,1)S(1)}, u32[]{:S(2)}, u32[]{:S(2)}) collective-permute-start(bf16[1,528,128]{2,1,0:T(8,128)(2,1)S(1)} %pad_maximum_fusion.1), channel_id=1, source_target_pairs={{0,32},{16,48},{32,64},{48,80},{64,96},{80,112},{96,128},{112,144}... | collective-permute-start | bytes 405512 | tf_op jit(solution)/shard_map/ppermute | solution.py:111
  34.9 29.1 %copy-start.5 = (f32[16,256]{1,0:T(8,128)S(1)}, f32[16,256]{1,0:T(8,128)}, u32[]{:S(2)}) copy-start(f32[16,256]{1,0:T(8,128)} %param.18) | copy-start | bytes 49156
  35.0 29.1 %copy-start.7 = (f32[16]{0:T(128)S(1)}, f32[16]{0:T(128)}, u32[]{:S(2)}) copy-start(f32[16]{0:T(128)} %param.20) | copy-start | bytes 196
  35.0 12.2 %collective-permute-start.4 = (bf16[1,528,128]{2,1,0:T(8,128)(2,1)S(1)}, bf16[1,528,128]{2,1,0:T(8,128)(2,1)S(1)}, u32[]{:S(2)}, u32[]{:S(2)}) collective-permute-start(bf16[1,528,128]{2,1,0:T(8,128)(2,1)S(1)} %pad_maximum_fusion.2), channel_id=1, source_target_pairs={{0,64},{16,80},{32,96},{48,112},{64,128},{80,144},{96,160},{112,17... | collective-permute-start | bytes 405512 | tf_op jit(solution)/shard_map/ppermute | solution.py:111
  47.5 14.3 %collective-permute-start.5 = (bf16[1,528,128]{2,1,0:T(8,128)(2,1)S(1)}, bf16[1,528,128]{2,1,0:T(8,128)(2,1)S(1)}, u32[]{:S(2)}, u32[]{:S(2)}) collective-permute-start(bf16[1,528,128]{2,1,0:T(8,128)(2,1)S(1)} %pad_maximum_fusion.3), channel_id=1, source_target_pairs={{0,128},{16,144},{32,160},{48,176},{64,192},{80,208},{96,224},{112... | collective-permute-start | bytes 405512 | tf_op jit(solution)/shard_map/ppermute | solution.py:111
  61.9 1.4 %collective-permute-start.6 = (bf16[1,8,64,128]{3,2,1,0:T(8,128)(2,1)S(1)}, bf16[1,8,64,128]{3,2,1,0:T(8,128)(2,1)S(1)}, u32[]{:S(2)}, u32[]{:S(2)}) collective-permute-start(bf16[1,8,64,128]{3,2,1,0:T(8,128)(2,1)S(1)} %add_convert_fusion), channel_id=1, source_target_pairs={{0,8},{8,0},{1,9},{9,1},{2,10},{10,2},{3,11},{11,3},{4,12},{12,4},... | collective-permute-start | bytes 393224 | tf_op jit(solution)/shard_map/ppermute | solution.py:182
  64.1 2.8 %copy-start.1 = (bf16[256,1024]{1,0:T(8,128)(2,1)S(1)}, bf16[256,1024]{1,0:T(8,128)(2,1)}, u32[]{:S(2)}) copy-start(bf16[256,1024]{1,0:T(8,128)(2,1)} %param.15) | copy-start | bytes 1572868
  66.5 12.1 %copy-start.6 = (bf16[1024]{0:T(1024)(128)(2,1)S(1)}, bf16[1024]{0:T(1024)(128)(2,1)}, u32[]{:S(2)}) copy-start(bf16[1024]{0:T(1024)(128)(2,1)} %param.21) | copy-start | bytes 6148
  67.3 3.6 %collective-permute-start.7 = (f32[256]{0:T(256)S(1)}, f32[256]{0:T(256)S(1)}, u32[]{:S(2)}, u32[]{:S(2)}) collective-permute-start(f32[256]{0:T(256)S(1)} %multiply_reduce_fusion), channel_id=1, source_target_pairs={{0,1},{1,0},{2,3},{3,2},{4,5},{5,4},{6,7},{7,6},{8,9},{9,8},{10,11... | collective-permute-start | bytes 3080 | tf_op jit(solution)/shard_map/ppermute | solution.py:120
  70.9 5.1 %collective-permute-start.8 = (f32[256]{0:T(256)S(1)}, f32[256]{0:T(256)S(1)}, u32[]{:S(2)}, u32[]{:S(2)}) collective-permute-start(f32[256]{0:T(256)S(1)} %add.588), channel_id=1, source_target_pairs={{0,2},{1,3},{2,0},{3,1},{4,6},{5,7},{6,4},{7,5},{8,10},{9,11},{10,... | collective-permute-start | bytes 3080 | tf_op jit(solution)/shard_map/ppermute | solution.py:120
  76.0 7.5 %collective-permute-start.9 = (f32[256]{0:T(256)S(1)}, f32[256]{0:T(256)S(1)}, u32[]{:S(2)}, u32[]{:S(2)}) collective-permute-start(f32[256]{0:T(256)S(1)} %add.589), channel_id=1, source_target_pairs={{0,4},{1,5},{2,6},{3,7},{4,0},{5,1},{6,2},{7,3},{8,12},{9,13},{10,... | collective-permute-start | bytes 3080 | tf_op jit(solution)/shard_map/ppermute | solution.py:120
Sparse Core Ops, SparseCore 0:
  12.8 65.4 all-gather.2

commit v13 on v12

--- a/solution.py
+++ b/solution.py
@@ -79,7 +79,9 @@
         run_block(position - 1, False)
 
     run_block(position, True)
-    o_ref[...] = (acc_sc[...] / l_sc[...]).astype(o_ref.dtype)
+    for h in range(rows // tok):
+        columns = slice(h * tok, (h + 1) * tok)
+        o_ref[:, h * width:(h + 1) * width] = (acc_sc[:, columns] / l_sc[:, columns]).T.astype(o_ref.dtype)
 
 
 def causal_attention(position, queries, gathered_kv, chunk=256):
@@ -88,11 +90,11 @@
     rows = heads * tok_rows
     queries_t = queries.reshape(tok_rows, heads, width).transpose(2, 1, 0).reshape(width, rows)
     kernel = functools.partial(attend_kernel, tok=tok_rows, width=width, chunk=chunk)
-    out_t = pl.pallas_call(
+    return pl.pallas_call(
         kernel,
         in_specs=[pl.BlockSpec(memory_space=pltpu.SMEM)] + [pl.BlockSpec(memory_space=pltpu.VMEM)] * 2,
         out_specs=pl.BlockSpec(memory_space=pltpu.VMEM),
-        out_shape=jax.ShapeDtypeStruct((width, rows), queries.dtype),
+        out_shape=jax.ShapeDtypeStruct(queries.shape, queries.dtype),
         scratch_shapes=[
             pltpu.VMEM((tok_rows, rows), jnp.bfloat16),
             pltpu.VMEM((tok_rows, rows), jnp.bfloat16),
@@ -102,7 +104,6 @@
             pltpu.VMEM((width, rows), jnp.float32),
         ],
     )(position.reshape(1), queries_t, gathered_kv)
-    return out_t.reshape(width, heads, tok_rows).transpose(2, 1, 0).reshape(tok_rows, heads * width)
 
 
 def shifted(block, axis, distance):

time: 127 us -> 124 us (0.976)
  local copies, waits for them, and re-layouts: 8.79 us -> 6.18 us
    unnamed x22 -> x20, local copies, waits for them, and re-layouts: 5.39 us -> 3.35 us
where the time goes in v13:
time: 124 us; the launch traced here: 123 us
  waiting for transfers between devices  48.7 us (39%)
  Pallas kernels  32.2 us (26%)
  between operations  14.5 us (12%)
  starting transfers between devices  12.1 us (10%)
  local copies, waits for them, and re-layouts  6.18 us (5%)
  other arithmetic  5.42 us (4%)
  matrix products  4.25 us (3%)
    ppermute x5, waiting for transfers between devices, shifted(): return lax.ppermute(block, axis, route)  38.5 us
    pallas_call x1, Pallas kernels, causal_attention(): pl.pallas_call(kernel, in_specs=[pl.BlockSpec(memory_space=pltpu.SMEM)] +...  32.2 us
    ppermute x3, waiting for transfers between devices, summed_over(): total = total + lax.ppermute(total, axis, route)  8.17 us
    ppermute x5, starting transfers between devices, shifted(): return lax.ppermute(block, axis, route)  6.46 us
    ppermute x3, starting transfers between devices, summed_over(): total = total + lax.ppermute(total, axis, route)  5.44 us
    unnamed x20, local copies, waits for them, and re-layouts  3.35 us
  transfers between devices with their start and end apart: 11, of which 10 were waited for; matrix products, arithmetic and copies ran while one was open for 9% of the time, Pallas kernels for 0%

profile of v13, /device:TPU:230, one launch (start us, length us, event | category | flops | bytes accessed | tf_op | source)
XLA Modules:
  0.0 123.3 jit_solution(4607628251840014540)
XLA Ops:
  7.2 0.0 copy-start
  7.2 0.0 copy-start.2
  7.2 0.0 all-gather.3.cloned.1.call-start
  7.2 0.8 reshape.1130
  8.0 0.0 copy-start.4
  8.0 0.6 reduce-window.6
  8.6 0.2 slice_reduce_fusion
  8.8 0.1 copy.42
  8.9 0.1 broadcast.184
  9.1 0.3 slice_reduce_fusion.1
  9.3 1.3 %copy.43 = bf16[256,1024]{0,1:T(8,128)(2,1)S(1)} copy(bf16[256,1024]{1,0:T(8,128)(2,1)} %param.14) | data formatting | bytes 1048576 | tf_op args[3]
  10.6 0.8 multiply_bitcast_fusion
  11.4 0.1 fusion.16
  11.5 0.3 fusion.79
  11.9 0.1 collective-permute-start
  12.0 0.7 pad_maximum_fusion.4
  12.7 0.0 all-gather.3.cloned.1.call-update
  12.7 0.8 collective-permute-done
  13.6 0.1 fusion.66
  13.7 0.1 dynamic-slice.5
  13.8 0.1 broadcast_select_fusion
  13.9 0.1 fusion.23
  14.0 1.3 %collective-permute-start.2 = (bf16[1,528,128]{2,1,0:T(8,128)(2,1)S(1)}, bf16[1,528,128]{2,1,0:T(8,128)(2,1)S(1)}, u32[]{:S(2)}, u32[]{:S(2)}) collective-permute-start(bf16[1,528,128]{2,1,0:T(8,128)(2,1)S(1)} %pad_maximum_fusion), channel_id=1, source_target_pairs={{0,32},{16,48},{32,64},{48,80},{64,96},{80,112},{96,128},{112,144}... | collective-permute-start | bytes 405512 | tf_op jit(solution)/shard_map/ppermute | solution.py:112
  15.3 0.9 fusion.80
  16.2 1.3 %collective-permute-start.1 = (bf16[1,528,128]{2,1,0:T(8,128)(2,1)S(1)}, bf16[1,528,128]{2,1,0:T(8,128)(2,1)S(1)}, u32[]{:S(2)}, u32[]{:S(2)}) collective-permute-start(bf16[1,528,128]{2,1,0:T(8,128)(2,1)S(1)} %pad_maximum_fusion), channel_id=1, source_target_pairs={{0,16},{16,32},{32,48},{48,64},{64,80},{80,96},{96,112},{112,128},... | collective-permute-start | bytes 405512 | tf_op jit(solution)/shard_map/ppermute | solution.py:112
  17.5 8.3 %collective-permute-done.2 = bf16[1,528,128]{2,1,0:T(8,128)(2,1)S(1)} collective-permute-done((bf16[1,528,128]{2,1,0:T(8,128)(2,1)S(1)}, bf16[1,528,128]{2,1,0:T(8,128)(2,1)S(1)}, u32[]{:S(2)}, u32[]{:S(2)}) %collective-permute-start.2) | collective-permute-done | bytes 135200 | tf_op jit(solution)/shard_map/ppermute | solution.py:112
  25.9 0.2 collective-permute-done.1
  26.1 0.1 mul.266
  26.2 0.1 mul.267
  26.3 0.1 fusion.28
  26.4 1.3 %collective-permute-start.3 = (bf16[1,528,128]{2,1,0:T(8,128)(2,1)S(1)}, bf16[1,528,128]{2,1,0:T(8,128)(2,1)S(1)}, u32[]{:S(2)}, u32[]{:S(2)}) collective-permute-start(bf16[1,528,128]{2,1,0:T(8,128)(2,1)S(1)} %pad_maximum_fusion.1), channel_id=1, source_target_pairs={{0,32},{16,48},{32,64},{48,80},{64,96},{80,112},{96,128},{112,144}... | collective-permute-start | bytes 405512 | tf_op jit(solution)/shard_map/ppermute | solution.py:112
  27.7 0.1 mul.270
  27.8 0.1 mul.271
  27.9 6.7 %collective-permute-done.3 = bf16[1,528,128]{2,1,0:T(8,128)(2,1)S(1)} collective-permute-done((bf16[1,528,128]{2,1,0:T(8,128)(2,1)S(1)}, bf16[1,528,128]{2,1,0:T(8,128)(2,1)S(1)}, u32[]{:S(2)}, u32[]{:S(2)}) %collective-permute-start.3) | collective-permute-done | bytes 135200 | tf_op jit(solution)/shard_map/ppermute | solution.py:112
  34.7 0.2 fusion.77
  34.9 0.0 copy-start.5
  34.9 0.0 copy-start.7
  35.0 1.3 %collective-permute-start.4 = (bf16[1,528,128]{2,1,0:T(8,128)(2,1)S(1)}, bf16[1,528,128]{2,1,0:T(8,128)(2,1)S(1)}, u32[]{:S(2)}, u32[]{:S(2)}) collective-permute-start(bf16[1,528,128]{2,1,0:T(8,128)(2,1)S(1)} %pad_maximum_fusion.2), channel_id=1, source_target_pairs={{0,64},{16,80},{32,96},{48,112},{64,128},{80,144},{96,160},{112,17... | collective-permute-start | bytes 405512 | tf_op jit(solution)/shard_map/ppermute | solution.py:112
  36.3 0.1 mul.275
  36.3 0.1 mul.276
  36.4 10.5 %collective-permute-done.4 = bf16[1,528,128]{2,1,0:T(8,128)(2,1)S(1)} collective-permute-done((bf16[1,528,128]{2,1,0:T(8,128)(2,1)S(1)}, bf16[1,528,128]{2,1,0:T(8,128)(2,1)S(1)}, u32[]{:S(2)}, u32[]{:S(2)}) %collective-permute-start.4) | collective-permute-done | bytes 135200 | tf_op jit(solution)/shard_map/ppermute | solution.py:112
  46.9 0.3 add_convert_fusion.1
  47.2 1.3 %collective-permute-start.5 = (bf16[1,528,128]{2,1,0:T(8,128)(2,1)S(1)}, bf16[1,528,128]{2,1,0:T(8,128)(2,1)S(1)}, u32[]{:S(2)}, u32[]{:S(2)}) collective-permute-start(bf16[1,528,128]{2,1,0:T(8,128)(2,1)S(1)} %pad_maximum_fusion.3), channel_id=1, source_target_pairs={{0,128},{16,144},{32,160},{48,176},{64,192},{80,208},{96,224},{112... | collective-permute-start | bytes 405512 | tf_op jit(solution)/shard_map/ppermute | solution.py:112
  48.6 12.8 %collective-permute-done.5 = bf16[1,528,128]{2,1,0:T(8,128)(2,1)S(1)} collective-permute-done((bf16[1,528,128]{2,1,0:T(8,128)(2,1)S(1)}, bf16[1,528,128]{2,1,0:T(8,128)(2,1)S(1)}, u32[]{:S(2)}, u32[]{:S(2)}) %collective-permute-start.5) | collective-permute-done | bytes 135200 | tf_op jit(solution)/shard_map/ppermute | solution.py:112
  61.4 0.2 add_convert_fusion
  61.5 0.1 collective-permute-start.6
  61.6 0.2 add_add_fusion
  61.8 1.2 collective-permute-done.6
  63.0 0.7 fusion.9
  63.7 0.0 copy-start.1
  63.7 2.4 %fusion.11 = f32[256,1,16,64]{0,3,2,1:T(8,128)S(1)} fusion(f32[256,1,16,64]{0,3,2,1:T(8,128)S(1)} %fusion.9, bf16[256,16,64]{0,2,1:T(8,128)(2,1)S(1)} %bitcast.144, f32[16,256]{1,0:T(8,128)S(1)} %copy-done.5, f32[16,256]{1,0:T(8,128)S(1)} %get-tuple-element.15, f32[256,256]{1,0:T(8,128)} %fusion.80, pred[256,256]{1,0:T(8,128)(4,1)S(1)} %iota_compare_fusion.1, ...), kind=kOutput, calls=%fused_computation.13 | convolution fusion | flops 141557760 | bytes 3506240 | tf_op jit(solution)/shard_map/ghts,sghp->tghp/dot_general | solution.py:226
  66.1 0.3 copy.46
  66.5 0.4 multiply_reduce_fusion
  66.9 1.9 %collective-permute-start.7 = (f32[256]{0:T(256)S(1)}, f32[256]{0:T(256)S(1)}, u32[]{:S(2)}, u32[]{:S(2)}) collective-permute-start(f32[256]{0:T(256)S(1)} %multiply_reduce_fusion), channel_id=1, source_target_pairs={{0,1},{1,0},{2,3},{3,2},{4,5},{5,4},{6,7},{7,6},{8,9},{9,8},{10,11... | collective-permute-start | bytes 3080 | tf_op jit(solution)/shard_map/ppermute | solution.py:121
  68.7 1.8 %collective-permute-done.7 = f32[256]{0:T(256)S(1)} collective-permute-done((f32[256]{0:T(256)S(1)}, f32[256]{0:T(256)S(1)}, u32[]{:S(2)}, u32[]{:S(2)}) %collective-permute-start.7) | collective-permute-done | bytes 1056 | tf_op jit(solution)/shard_map/ppermute | solution.py:121
  70.5 3.6 %collective-permute-start.8 = (f32[256]{0:T(256)S(1)}, f32[256]{0:T(256)S(1)}, u32[]{:S(2)}, u32[]{:S(2)}) collective-permute-start(f32[256]{0:T(256)S(1)} %add.588), channel_id=1, source_target_pairs={{0,2},{1,3},{2,0},{3,1},{4,6},{5,7},{6,4},{7,5},{8,10},{9,11},{10,... | collective-permute-start | bytes 3080 | tf_op jit(solution)/shard_map/ppermute | solution.py:121
  74.1 1.5 %collective-permute-done.8 = f32[256]{0:T(256)S(1)} collective-permute-done((f32[256]{0:T(256)S(1)}, f32[256]{0:T(256)S(1)}, u32[]{:S(2)}, u32[]{:S(2)}) %collective-permute-start.8) | collective-permute-done | bytes 1056 | tf_op jit(solution)/shard_map/ppermute | solution.py:121
  75.6 0.0 collective-permute-start.9
  75.6 1.1 copy.48
  76.8 0.6 copy.39
  77.3 0.9 copy.49
  78.3 4.8 %collective-permute-done.9 = f32[256]{0:T(256)S(1)} collective-permute-done((f32[256]{0:T(256)S(1)}, f32[256]{0:T(256)S(1)}, u32[]{:S(2)}, u32[]{:S(2)}) %collective-permute-start.9) | collective-permute-done | bytes 1056 | tf_op jit(solution)/shard_map/ppermute | solution.py:121
  83.1 1.2 multiply_convert_fusion
  84.3 32.2 %shard_map.122 = bf16[256,1024]{1,0:T(8,128)(2,1)} custom-call(s32[1]{0:T(128)} %bitcast.pos_ref, bf16[128,2048]{1,0:T(8,128)(2,1)} %bitcast.149, bf16[32,2,256,128]{3,2,1,0:T(8,128)(2,1)} %bitcast.129), custom_call_target="tpu_custom_call" | custom-call | tf_op jit(solution)/shard_map/pallas_call | solution.py:93
  (56 shorter events, 0.6 us)
Async XLA Ops:
  7.2 4.4 %copy-start = (bf16[256,128]{1,0:T(8,128)(2,1)S(1)}, bf16[256,128]{1,0:T(8,128)(2,1)}, u32[]{:S(2)}) copy-start(bf16[256,128]{1,0:T(8,128)(2,1)} %param.16) | copy-start | bytes 196612
  7.2 4.8 %copy-start.2 = (bf16[256,128]{1,0:T(8,128)(2,1)S(1)}, bf16[256,128]{1,0:T(8,128)(2,1)}, u32[]{:S(2)}) copy-start(bf16[256,128]{1,0:T(8,128)(2,1)} %param.13) | copy-start | bytes 196612
  7.2 4.8 %copy-start.3 = (bf16[256,128]{1,0:T(8,128)(2,1)S(1)}, bf16[256,128]{1,0:T(8,128)(2,1)}, u32[]{:S(2)}) copy-start(bf16[256,128]{1,0:T(8,128)(2,1)} %param.12) | copy-start | bytes 196612
  7.2 77.1 %all-gather.3.cloned.1.call-start = ((), (), s32[]{:S(2)}) async-start(), calls=%async_computation | async-start | bytes 4325376 | tf_op jit(solution)/shard_map/all_gather | solution.py:210
  8.0 7.3 %copy-start.4 = (bf16[256,128]{1,0:T(8,128)(2,1)S(1)}, bf16[256,128]{1,0:T(8,128)(2,1)}, u32[]{:S(2)}) copy-start(bf16[256,128]{1,0:T(8,128)(2,1)} %param.17) | copy-start | bytes 196612
  11.9 1.6 %collective-permute-start = (bf16[1,1040,128]{2,1,0:T(8,128)(2,1)S(1)}, bf16[1,1040,128]{2,1,0:T(8,128)(2,1)S(1)}, u32[]{:S(2)}, u32[]{:S(2)}) collective-permute-start(bf16[1,1040,128]{2,1,0:T(8,128)(2,1)S(1)} %fusion.21), channel_id=1, source_target_pairs={{0,8},{8,0},{1,9},{9,1},{2,10},{10,2},{3,11},{11,3},{4,12},{12,4},... | collective-permute-start | bytes 798728 | tf_op jit(solution)/shard_map/ppermute | solution.py:169
  14.0 11.9 %collective-permute-start.2 = (bf16[1,528,128]{2,1,0:T(8,128)(2,1)S(1)}, bf16[1,528,128]{2,1,0:T(8,128)(2,1)S(1)}, u32[]{:S(2)}, u32[]{:S(2)}) collective-permute-start(bf16[1,528,128]{2,1,0:T(8,128)(2,1)S(1)} %pad_maximum_fusion), channel_id=1, source_target_pairs={{0,32},{16,48},{32,64},{48,80},{64,96},{80,112},{96,128},{112,144}... | collective-permute-start | bytes 405512 | tf_op jit(solution)/shard_map/ppermute | solution.py:112
  16.2 9.9 %collective-permute-start.1 = (bf16[1,528,128]{2,1,0:T(8,128)(2,1)S(1)}, bf16[1,528,128]{2,1,0:T(8,128)(2,1)S(1)}, u32[]{:S(2)}, u32[]{:S(2)}) collective-permute-start(bf16[1,528,128]{2,1,0:T(8,128)(2,1)S(1)} %pad_maximum_fusion), channel_id=1, source_target_pairs={{0,16},{16,32},{32,48},{48,64},{64,80},{80,96},{96,112},{112,128},... | collective-permute-start | bytes 405512 | tf_op jit(solution)/shard_map/ppermute | solution.py:112
  26.4 8.2 %collective-permute-start.3 = (bf16[1,528,128]{2,1,0:T(8,128)(2,1)S(1)}, bf16[1,528,128]{2,1,0:T(8,128)(2,1)S(1)}, u32[]{:S(2)}, u32[]{:S(2)}) collective-permute-start(bf16[1,528,128]{2,1,0:T(8,128)(2,1)S(1)} %pad_maximum_fusion.1), channel_id=1, source_target_pairs={{0,32},{16,48},{32,64},{48,80},{64,96},{80,112},{96,128},{112,144}... | collective-permute-start | bytes 405512 | tf_op jit(solution)/shard_map/ppermute | solution.py:112
  34.9 28.7 %copy-start.5 = (f32[16,256]{1,0:T(8,128)S(1)}, f32[16,256]{1,0:T(8,128)}, u32[]{:S(2)}) copy-start(f32[16,256]{1,0:T(8,128)} %param.18) | copy-start | bytes 49156
  34.9 28.7 %copy-start.7 = (f32[16]{0:T(128)S(1)}, f32[16]{0:T(128)}, u32[]{:S(2)}) copy-start(f32[16]{0:T(128)} %param.20) | copy-start | bytes 196
  35.0 11.9 %collective-permute-start.4 = (bf16[1,528,128]{2,1,0:T(8,128)(2,1)S(1)}, bf16[1,528,128]{2,1,0:T(8,128)(2,1)S(1)}, u32[]{:S(2)}, u32[]{:S(2)}) collective-permute-start(bf16[1,528,128]{2,1,0:T(8,128)(2,1)S(1)} %pad_maximum_fusion.2), channel_id=1, source_target_pairs={{0,64},{16,80},{32,96},{48,112},{64,128},{80,144},{96,160},{112,17... | collective-permute-start | bytes 405512 | tf_op jit(solution)/shard_map/ppermute | solution.py:112
  47.2 14.1 %collective-permute-start.5 = (bf16[1,528,128]{2,1,0:T(8,128)(2,1)S(1)}, bf16[1,528,128]{2,1,0:T(8,128)(2,1)S(1)}, u32[]{:S(2)}, u32[]{:S(2)}) collective-permute-start(bf16[1,528,128]{2,1,0:T(8,128)(2,1)S(1)} %pad_maximum_fusion.3), channel_id=1, source_target_pairs={{0,128},{16,144},{32,160},{48,176},{64,192},{80,208},{96,224},{112... | collective-permute-start | bytes 405512 | tf_op jit(solution)/shard_map/ppermute | solution.py:112
  61.5 1.4 %collective-permute-start.6 = (bf16[1,8,64,128]{3,2,1,0:T(8,128)(2,1)S(1)}, bf16[1,8,64,128]{3,2,1,0:T(8,128)(2,1)S(1)}, u32[]{:S(2)}, u32[]{:S(2)}) collective-permute-start(bf16[1,8,64,128]{3,2,1,0:T(8,128)(2,1)S(1)} %add_convert_fusion), channel_id=1, source_target_pairs={{0,8},{8,0},{1,9},{9,1},{2,10},{10,2},{3,11},{11,3},{4,12},{12,4},... | collective-permute-start | bytes 393224 | tf_op jit(solution)/shard_map/ppermute | solution.py:183
  63.7 2.8 %copy-start.1 = (bf16[256,1024]{1,0:T(8,128)(2,1)S(1)}, bf16[256,1024]{1,0:T(8,128)(2,1)}, u32[]{:S(2)}) copy-start(bf16[256,1024]{1,0:T(8,128)(2,1)} %param.15) | copy-start | bytes 1572868
  66.1 12.2 %copy-start.6 = (bf16[1024]{0:T(1024)(128)(2,1)S(1)}, bf16[1024]{0:T(1024)(128)(2,1)}, u32[]{:S(2)}) copy-start(bf16[1024]{0:T(1024)(128)(2,1)} %param.21) | copy-start | bytes 6148
  66.9 3.6 %collective-permute-start.7 = (f32[256]{0:T(256)S(1)}, f32[256]{0:T(256)S(1)}, u32[]{:S(2)}, u32[]{:S(2)}) collective-permute-start(f32[256]{0:T(256)S(1)} %multiply_reduce_fusion), channel_id=1, source_target_pairs={{0,1},{1,0},{2,3},{3,2},{4,5},{5,4},{6,7},{7,6},{8,9},{9,8},{10,11... | collective-permute-start | bytes 3080 | tf_op jit(solution)/shard_map/ppermute | solution.py:121
  70.5 5.1 %collective-permute-start.8 = (f32[256]{0:T(256)S(1)}, f32[256]{0:T(256)S(1)}, u32[]{:S(2)}, u32[]{:S(2)}) collective-permute-start(f32[256]{0:T(256)S(1)} %add.588), channel_id=1, source_target_pairs={{0,2},{1,3},{2,0},{3,1},{4,6},{5,7},{6,4},{7,5},{8,10},{9,11},{10,... | collective-permute-start | bytes 3080 | tf_op jit(solution)/shard_map/ppermute | solution.py:121
  75.6 7.5 %collective-permute-start.9 = (f32[256]{0:T(256)S(1)}, f32[256]{0:T(256)S(1)}, u32[]{:S(2)}, u32[]{:S(2)}) collective-permute-start(f32[256]{0:T(256)S(1)} %add.589), channel_id=1, source_target_pairs={{0,4},{1,5},{2,6},{3,7},{4,0},{5,1},{6,2},{7,3},{8,12},{9,13},{10,... | collective-permute-start | bytes 3080 | tf_op jit(solution)/shard_map/ppermute | solution.py:121
Sparse Core Ops, SparseCore 0:
  12.8 65.2 all-gather.2

commit v14 on v13

--- a/solution.py
+++ b/solution.py
@@ -49,15 +49,22 @@
             p_sc[:, r0:r0 + chunk] = weights.astype(jnp.bfloat16)
         acc_sc[...] = acc_sc[...] * c_sc[...] + lax.dot_general(kv_ref[kb, 1], p_sc[...], (((0,), (0,)), ((), ())), preferred_element_type=jnp.float32)
 
-    def run_pair(kb):
+    def run_pair(kb, masked=False):
         keys = (kv_ref[kb, 0], kv_ref[kb + 1, 0])
         for c in range(rows // chunk):
             r0 = c * chunk
             scores = [jnp.dot(k, qt_ref[:, r0:r0 + chunk], preferred_element_type=jnp.float32) for k in keys]
+            if masked:
+                key_idx = lax.broadcasted_iota(jnp.int32, (block_rows, chunk), 0)
+                query_idx = (r0 % tok) + lax.broadcasted_iota(jnp.int32, (block_rows, chunk), 1)
+                is_valid = key_idx <= query_idx
+                scores[1] = jnp.where(is_valid, scores[1], causal_score)
             run_max = m_sc[:, r0:r0 + chunk]
             block_max = jnp.maximum(jnp.max(scores[0], axis=0, keepdims=True), jnp.max(scores[1], axis=0, keepdims=True))
             new_max = jnp.maximum(run_max, block_max)
             weights = [jnp.exp2(s * score_factor - new_max * score_factor) for s in scores]
+            if masked:
+                weights[1] = jnp.where(is_valid, weights[1], 0.0)
             correction_factor = jnp.exp2((run_max - new_max) * score_factor)
             l_sc[:, r0:r0 + chunk] = l_sc[:, r0:r0 + chunk] * correction_factor + (
                 jnp.sum(weights[0], axis=0, keepdims=True) + jnp.sum(weights[1], axis=0, keepdims=True))
@@ -76,9 +83,12 @@
 
     @pl.when(lax.rem(position, 2) == 1)
     def _odd():
-        run_block(position - 1, False)
-
-    run_block(position, True)
+        run_pair(position - 1, masked=True)
+
+    @pl.when(lax.rem(position, 2) == 0)
+    def _even():
+        run_block(position, True)
+
     for h in range(rows // tok):
         columns = slice(h * tok, (h + 1) * tok)
         o_ref[:, h * width:(h + 1) * width] = (acc_sc[:, columns] / l_sc[:, columns]).T.astype(o_ref.dtype)

time: 124 us -> 125 us (level)
  no operation moved by 1% of the time
where the time goes in v14:
time: 125 us; the launch traced here: 124 us
  waiting for transfers between devices  49.4 us (40%)
  Pallas kernels  32.9 us (26%)
  between operations  14.5 us (12%)
  starting transfers between devices  11.5 us (9%)
  local copies, waits for them, and re-layouts  6.18 us (5%)
  other arithmetic  5.42 us (4%)
  matrix products  4.25 us (3%)
    ppermute x5, waiting for transfers between devices, shifted(): return lax.ppermute(block, axis, route)  38.7 us
    pallas_call x1, Pallas kernels, causal_attention(): pl.pallas_call(kernel, in_specs=[pl.BlockSpec(memory_space=pltpu.SMEM)] +...  32.9 us
    ppermute x3, waiting for transfers between devices, summed_over(): total = total + lax.ppermute(total, axis, route)  8.72 us
    ppermute x5, starting transfers between devices, shifted(): return lax.ppermute(block, axis, route)  6.46 us
    ppermute x3, starting transfers between devices, summed_over(): total = total + lax.ppermute(total, axis, route)  4.85 us
    unnamed x20, local copies, waits for them, and re-layouts  3.35 us
  transfers between devices with their start and end apart: 11, of which 10 were waited for; matrix products, arithmetic and copies ran while one was open for 9% of the time, Pallas kernels for 0%

profile of v14, /device:TPU:230, one launch (start us, length us, event | category | flops | bytes accessed | tf_op | source)
XLA Modules:
  0.0 124.2 jit_solution(11018140032294137104)
XLA Ops:
  7.2 0.0 copy-start
  7.2 0.0 copy-start.2
  7.2 0.0 all-gather.3.cloned.1.call-start
  7.2 0.8 reshape.1130
  8.0 0.0 copy-start.4
  8.0 0.6 reduce-window.6
  8.6 0.2 slice_reduce_fusion
  8.8 0.1 copy.42
  8.9 0.1 broadcast.184
  9.1 0.3 slice_reduce_fusion.1
  9.3 1.3 %copy.43 = bf16[256,1024]{0,1:T(8,128)(2,1)S(1)} copy(bf16[256,1024]{1,0:T(8,128)(2,1)} %param.14) | data formatting | bytes 1048576 | tf_op args[3]
  10.6 0.8 multiply_bitcast_fusion
  11.4 0.1 fusion.16
  11.5 0.3 fusion.79
  11.9 0.1 collective-permute-start
  12.0 0.7 pad_maximum_fusion.4
  12.7 0.0 all-gather.3.cloned.1.call-update
  12.7 0.8 collective-permute-done
  13.6 0.1 fusion.66
  13.7 0.1 dynamic-slice.5
  13.8 0.1 broadcast_select_fusion
  13.9 0.1 fusion.23
  14.0 1.3 %collective-permute-start.2 = (bf16[1,528,128]{2,1,0:T(8,128)(2,1)S(1)}, bf16[1,528,128]{2,1,0:T(8,128)(2,1)S(1)}, u32[]{:S(2)}, u32[]{:S(2)}) collective-permute-start(bf16[1,528,128]{2,1,0:T(8,128)(2,1)S(1)} %pad_maximum_fusion), channel_id=1, source_target_pairs={{0,32},{16,48},{32,64},{48,80},{64,96},{80,112},{96,128},{112,144}... | collective-permute-start | bytes 405512 | tf_op jit(solution)/shard_map/ppermute | solution.py:122
  15.3 0.9 fusion.80
  16.2 1.3 %collective-permute-start.1 = (bf16[1,528,128]{2,1,0:T(8,128)(2,1)S(1)}, bf16[1,528,128]{2,1,0:T(8,128)(2,1)S(1)}, u32[]{:S(2)}, u32[]{:S(2)}) collective-permute-start(bf16[1,528,128]{2,1,0:T(8,128)(2,1)S(1)} %pad_maximum_fusion), channel_id=1, source_target_pairs={{0,16},{16,32},{32,48},{48,64},{64,80},{80,96},{96,112},{112,128},... | collective-permute-start | bytes 405512 | tf_op jit(solution)/shard_map/ppermute | solution.py:122
  17.5 8.3 %collective-permute-done.2 = bf16[1,528,128]{2,1,0:T(8,128)(2,1)S(1)} collective-permute-done((bf16[1,528,128]{2,1,0:T(8,128)(2,1)S(1)}, bf16[1,528,128]{2,1,0:T(8,128)(2,1)S(1)}, u32[]{:S(2)}, u32[]{:S(2)}) %collective-permute-start.2) | collective-permute-done | bytes 135200 | tf_op jit(solution)/shard_map/ppermute | solution.py:122
  25.9 0.2 collective-permute-done.1
  26.1 0.1 mul.266
  26.2 0.1 mul.267
  26.3 0.1 fusion.28
  26.5 1.3 %collective-permute-start.3 = (bf16[1,528,128]{2,1,0:T(8,128)(2,1)S(1)}, bf16[1,528,128]{2,1,0:T(8,128)(2,1)S(1)}, u32[]{:S(2)}, u32[]{:S(2)}) collective-permute-start(bf16[1,528,128]{2,1,0:T(8,128)(2,1)S(1)} %pad_maximum_fusion.1), channel_id=1, source_target_pairs={{0,32},{16,48},{32,64},{48,80},{64,96},{80,112},{96,128},{112,144}... | collective-permute-start | bytes 405512 | tf_op jit(solution)/shard_map/ppermute | solution.py:122
  27.8 0.1 mul.270
  27.8 0.1 mul.271
  28.0 6.7 %collective-permute-done.3 = bf16[1,528,128]{2,1,0:T(8,128)(2,1)S(1)} collective-permute-done((bf16[1,528,128]{2,1,0:T(8,128)(2,1)S(1)}, bf16[1,528,128]{2,1,0:T(8,128)(2,1)S(1)}, u32[]{:S(2)}, u32[]{:S(2)}) %collective-permute-start.3) | collective-permute-done | bytes 135200 | tf_op jit(solution)/shard_map/ppermute | solution.py:122
  34.7 0.2 fusion.77
  34.9 0.0 copy-start.5
  34.9 0.0 copy-start.7
  35.0 1.3 %collective-permute-start.4 = (bf16[1,528,128]{2,1,0:T(8,128)(2,1)S(1)}, bf16[1,528,128]{2,1,0:T(8,128)(2,1)S(1)}, u32[]{:S(2)}, u32[]{:S(2)}) collective-permute-start(bf16[1,528,128]{2,1,0:T(8,128)(2,1)S(1)} %pad_maximum_fusion.2), channel_id=1, source_target_pairs={{0,64},{16,80},{32,96},{48,112},{64,128},{80,144},{96,160},{112,17... | collective-permute-start | bytes 405512 | tf_op jit(solution)/shard_map/ppermute | solution.py:122
  36.3 0.1 mul.275
  36.3 0.1 mul.276
  36.4 10.5 %collective-permute-done.4 = bf16[1,528,128]{2,1,0:T(8,128)(2,1)S(1)} collective-permute-done((bf16[1,528,128]{2,1,0:T(8,128)(2,1)S(1)}, bf16[1,528,128]{2,1,0:T(8,128)(2,1)S(1)}, u32[]{:S(2)}, u32[]{:S(2)}) %collective-permute-start.4) | collective-permute-done | bytes 135200 | tf_op jit(solution)/shard_map/ppermute | solution.py:122
  47.0 0.3 add_convert_fusion.1
  47.3 1.3 %collective-permute-start.5 = (bf16[1,528,128]{2,1,0:T(8,128)(2,1)S(1)}, bf16[1,528,128]{2,1,0:T(8,128)(2,1)S(1)}, u32[]{:S(2)}, u32[]{:S(2)}) collective-permute-start(bf16[1,528,128]{2,1,0:T(8,128)(2,1)S(1)} %pad_maximum_fusion.3), channel_id=1, source_target_pairs={{0,128},{16,144},{32,160},{48,176},{64,192},{80,208},{96,224},{112... | collective-permute-start | bytes 405512 | tf_op jit(solution)/shard_map/ppermute | solution.py:122
  48.6 12.9 %collective-permute-done.5 = bf16[1,528,128]{2,1,0:T(8,128)(2,1)S(1)} collective-permute-done((bf16[1,528,128]{2,1,0:T(8,128)(2,1)S(1)}, bf16[1,528,128]{2,1,0:T(8,128)(2,1)S(1)}, u32[]{:S(2)}, u32[]{:S(2)}) %collective-permute-start.5) | collective-permute-done | bytes 135200 | tf_op jit(solution)/shard_map/ppermute | solution.py:122
  61.6 0.2 add_convert_fusion
  61.7 0.1 collective-permute-start.6
  61.8 0.2 add_add_fusion
  62.0 1.2 collective-permute-done.6
  63.2 0.7 fusion.9
  63.9 0.0 copy-start.1
  63.9 2.4 %fusion.11 = f32[256,1,16,64]{0,3,2,1:T(8,128)S(1)} fusion(f32[256,1,16,64]{0,3,2,1:T(8,128)S(1)} %fusion.9, bf16[256,16,64]{0,2,1:T(8,128)(2,1)S(1)} %bitcast.144, f32[16,256]{1,0:T(8,128)S(1)} %copy-done.5, f32[16,256]{1,0:T(8,128)S(1)} %get-tuple-element.15, f32[256,256]{1,0:T(8,128)} %fusion.80, pred[256,256]{1,0:T(8,128)(4,1)S(1)} %iota_compare_fusion.1, ...), kind=kOutput, calls=%fused_computation.13 | convolution fusion | flops 141557760 | bytes 3506240 | tf_op jit(solution)/shard_map/ghts,sghp->tghp/dot_general | solution.py:236
  66.3 0.3 copy.46
  66.7 0.4 multiply_reduce_fusion
  67.1 1.8 %collective-permute-start.7 = (f32[256]{0:T(256)S(1)}, f32[256]{0:T(256)S(1)}, u32[]{:S(2)}, u32[]{:S(2)}) collective-permute-start(f32[256]{0:T(256)S(1)} %multiply_reduce_fusion), channel_id=1, source_target_pairs={{0,1},{1,0},{2,3},{3,2},{4,5},{5,4},{6,7},{7,6},{8,9},{9,8},{10,11... | collective-permute-start | bytes 3080 | tf_op jit(solution)/shard_map/ppermute | solution.py:131
  68.8 1.9 %collective-permute-done.7 = f32[256]{0:T(256)S(1)} collective-permute-done((f32[256]{0:T(256)S(1)}, f32[256]{0:T(256)S(1)}, u32[]{:S(2)}, u32[]{:S(2)}) %collective-permute-start.7) | collective-permute-done | bytes 1056 | tf_op jit(solution)/shard_map/ppermute | solution.py:131
  70.7 3.1 %collective-permute-start.8 = (f32[256]{0:T(256)S(1)}, f32[256]{0:T(256)S(1)}, u32[]{:S(2)}, u32[]{:S(2)}) collective-permute-start(f32[256]{0:T(256)S(1)} %add.588), channel_id=1, source_target_pairs={{0,2},{1,3},{2,0},{3,1},{4,6},{5,7},{6,4},{7,5},{8,10},{9,11},{10,... | collective-permute-start | bytes 3080 | tf_op jit(solution)/shard_map/ppermute | solution.py:131
  73.8 2.0 %collective-permute-done.8 = f32[256]{0:T(256)S(1)} collective-permute-done((f32[256]{0:T(256)S(1)}, f32[256]{0:T(256)S(1)}, u32[]{:S(2)}, u32[]{:S(2)}) %collective-permute-start.8) | collective-permute-done | bytes 1056 | tf_op jit(solution)/shard_map/ppermute | solution.py:131
  75.8 0.0 collective-permute-start.9
  75.8 1.1 copy.48
  76.9 0.6 copy.39
  77.5 0.9 copy.49
  78.4 4.8 %collective-permute-done.9 = f32[256]{0:T(256)S(1)} collective-permute-done((f32[256]{0:T(256)S(1)}, f32[256]{0:T(256)S(1)}, u32[]{:S(2)}, u32[]{:S(2)}) %collective-permute-start.9) | collective-permute-done | bytes 1056 | tf_op jit(solution)/shard_map/ppermute | solution.py:131
  83.3 1.2 multiply_convert_fusion
  84.4 32.9 %shard_map.122 = bf16[256,1024]{1,0:T(8,128)(2,1)} custom-call(s32[1]{0:T(128)} %bitcast.pos_ref, bf16[128,2048]{1,0:T(8,128)(2,1)} %bitcast.149, bf16[32,2,256,128]{3,2,1,0:T(8,128)(2,1)} %bitcast.129), custom_call_target="tpu_custom_call" | custom-call | tf_op jit(solution)/shard_map/pallas_call | solution.py:103
  (56 shorter events, 0.6 us)
Async XLA Ops:
  7.2 4.4 %copy-start = (bf16[256,128]{1,0:T(8,128)(2,1)S(1)}, bf16[256,128]{1,0:T(8,128)(2,1)}, u32[]{:S(2)}) copy-start(bf16[256,128]{1,0:T(8,128)(2,1)} %param.16) | copy-start | bytes 196612
  7.2 4.8 %copy-start.2 = (bf16[256,128]{1,0:T(8,128)(2,1)S(1)}, bf16[256,128]{1,0:T(8,128)(2,1)}, u32[]{:S(2)}) copy-start(bf16[256,128]{1,0:T(8,128)(2,1)} %param.13) | copy-start | bytes 196612
  7.2 4.8 %copy-start.3 = (bf16[256,128]{1,0:T(8,128)(2,1)S(1)}, bf16[256,128]{1,0:T(8,128)(2,1)}, u32[]{:S(2)}) copy-start(bf16[256,128]{1,0:T(8,128)(2,1)} %param.12) | copy-start | bytes 196612
  7.2 77.2 %all-gather.3.cloned.1.call-start = ((), (), s32[]{:S(2)}) async-start(), calls=%async_computation | async-start | bytes 4325376 | tf_op jit(solution)/shard_map/all_gather | solution.py:220
  8.0 7.3 %copy-start.4 = (bf16[256,128]{1,0:T(8,128)(2,1)S(1)}, bf16[256,128]{1,0:T(8,128)(2,1)}, u32[]{:S(2)}) copy-start(bf16[256,128]{1,0:T(8,128)(2,1)} %param.17) | copy-start | bytes 196612
  11.9 1.6 %collective-permute-start = (bf16[1,1040,128]{2,1,0:T(8,128)(2,1)S(1)}, bf16[1,1040,128]{2,1,0:T(8,128)(2,1)S(1)}, u32[]{:S(2)}, u32[]{:S(2)}) collective-permute-start(bf16[1,1040,128]{2,1,0:T(8,128)(2,1)S(1)} %fusion.21), channel_id=1, source_target_pairs={{0,8},{8,0},{1,9},{9,1},{2,10},{10,2},{3,11},{11,3},{4,12},{12,4},... | collective-permute-start | bytes 798728 | tf_op jit(solution)/shard_map/ppermute | solution.py:179
  14.0 11.9 %collective-permute-start.2 = (bf16[1,528,128]{2,1,0:T(8,128)(2,1)S(1)}, bf16[1,528,128]{2,1,0:T(8,128)(2,1)S(1)}, u32[]{:S(2)}, u32[]{:S(2)}) collective-permute-start(bf16[1,528,128]{2,1,0:T(8,128)(2,1)S(1)} %pad_maximum_fusion), channel_id=1, source_target_pairs={{0,32},{16,48},{32,64},{48,80},{64,96},{80,112},{96,128},{112,144}... | collective-permute-start | bytes 405512 | tf_op jit(solution)/shard_map/ppermute | solution.py:122
  16.2 9.9 %collective-permute-start.1 = (bf16[1,528,128]{2,1,0:T(8,128)(2,1)S(1)}, bf16[1,528,128]{2,1,0:T(8,128)(2,1)S(1)}, u32[]{:S(2)}, u32[]{:S(2)}) collective-permute-start(bf16[1,528,128]{2,1,0:T(8,128)(2,1)S(1)} %pad_maximum_fusion), channel_id=1, source_target_pairs={{0,16},{16,32},{32,48},{48,64},{64,80},{80,96},{96,112},{112,128},... | collective-permute-start | bytes 405512 | tf_op jit(solution)/shard_map/ppermute | solution.py:122
  26.5 8.2 %collective-permute-start.3 = (bf16[1,528,128]{2,1,0:T(8,128)(2,1)S(1)}, bf16[1,528,128]{2,1,0:T(8,128)(2,1)S(1)}, u32[]{:S(2)}, u32[]{:S(2)}) collective-permute-start(bf16[1,528,128]{2,1,0:T(8,128)(2,1)S(1)} %pad_maximum_fusion.1), channel_id=1, source_target_pairs={{0,32},{16,48},{32,64},{48,80},{64,96},{80,112},{96,128},{112,144}... | collective-permute-start | bytes 405512 | tf_op jit(solution)/shard_map/ppermute | solution.py:122
  34.9 28.9 %copy-start.5 = (f32[16,256]{1,0:T(8,128)S(1)}, f32[16,256]{1,0:T(8,128)}, u32[]{:S(2)}) copy-start(f32[16,256]{1,0:T(8,128)} %param.18) | copy-start | bytes 49156
  34.9 28.9 %copy-start.7 = (f32[16]{0:T(128)S(1)}, f32[16]{0:T(128)}, u32[]{:S(2)}) copy-start(f32[16]{0:T(128)} %param.20) | copy-start | bytes 196
  35.0 12.0 %collective-permute-start.4 = (bf16[1,528,128]{2,1,0:T(8,128)(2,1)S(1)}, bf16[1,528,128]{2,1,0:T(8,128)(2,1)S(1)}, u32[]{:S(2)}, u32[]{:S(2)}) collective-permute-start(bf16[1,528,128]{2,1,0:T(8,128)(2,1)S(1)} %pad_maximum_fusion.2), channel_id=1, source_target_pairs={{0,64},{16,80},{32,96},{48,112},{64,128},{80,144},{96,160},{112,17... | collective-permute-start | bytes 405512 | tf_op jit(solution)/shard_map/ppermute | solution.py:122
  47.3 14.3 %collective-permute-start.5 = (bf16[1,528,128]{2,1,0:T(8,128)(2,1)S(1)}, bf16[1,528,128]{2,1,0:T(8,128)(2,1)S(1)}, u32[]{:S(2)}, u32[]{:S(2)}) collective-permute-start(bf16[1,528,128]{2,1,0:T(8,128)(2,1)S(1)} %pad_maximum_fusion.3), channel_id=1, source_target_pairs={{0,128},{16,144},{32,160},{48,176},{64,192},{80,208},{96,224},{112... | collective-permute-start | bytes 405512 | tf_op jit(solution)/shard_map/ppermute | solution.py:122
  61.7 1.4 %collective-permute-start.6 = (bf16[1,8,64,128]{3,2,1,0:T(8,128)(2,1)S(1)}, bf16[1,8,64,128]{3,2,1,0:T(8,128)(2,1)S(1)}, u32[]{:S(2)}, u32[]{:S(2)}) collective-permute-start(bf16[1,8,64,128]{3,2,1,0:T(8,128)(2,1)S(1)} %add_convert_fusion), channel_id=1, source_target_pairs={{0,8},{8,0},{1,9},{9,1},{2,10},{10,2},{3,11},{11,3},{4,12},{12,4},... | collective-permute-start | bytes 393224 | tf_op jit(solution)/shard_map/ppermute | solution.py:193
  63.9 2.8 %copy-start.1 = (bf16[256,1024]{1,0:T(8,128)(2,1)S(1)}, bf16[256,1024]{1,0:T(8,128)(2,1)}, u32[]{:S(2)}) copy-start(bf16[256,1024]{1,0:T(8,128)(2,1)} %param.15) | copy-start | bytes 1572868
  66.3 12.1 %copy-start.6 = (bf16[1024]{0:T(1024)(128)(2,1)S(1)}, bf16[1024]{0:T(1024)(128)(2,1)}, u32[]{:S(2)}) copy-start(bf16[1024]{0:T(1024)(128)(2,1)} %param.21) | copy-start | bytes 6148
  67.1 3.6 %collective-permute-start.7 = (f32[256]{0:T(256)S(1)}, f32[256]{0:T(256)S(1)}, u32[]{:S(2)}, u32[]{:S(2)}) collective-permute-start(f32[256]{0:T(256)S(1)} %multiply_reduce_fusion), channel_id=1, source_target_pairs={{0,1},{1,0},{2,3},{3,2},{4,5},{5,4},{6,7},{7,6},{8,9},{9,8},{10,11... | collective-permute-start | bytes 3080 | tf_op jit(solution)/shard_map/ppermute | solution.py:131
  70.7 5.1 %collective-permute-start.8 = (f32[256]{0:T(256)S(1)}, f32[256]{0:T(256)S(1)}, u32[]{:S(2)}, u32[]{:S(2)}) collective-permute-start(f32[256]{0:T(256)S(1)} %add.588), channel_id=1, source_target_pairs={{0,2},{1,3},{2,0},{3,1},{4,6},{5,7},{6,4},{7,5},{8,10},{9,11},{10,... | collective-permute-start | bytes 3080 | tf_op jit(solution)/shard_map/ppermute | solution.py:131
  75.8 7.5 %collective-permute-start.9 = (f32[256]{0:T(256)S(1)}, f32[256]{0:T(256)S(1)}, u32[]{:S(2)}, u32[]{:S(2)}) collective-permute-start(f32[256]{0:T(256)S(1)} %add.589), channel_id=1, source_target_pairs={{0,4},{1,5},{2,6},{3,7},{4,0},{5,1},{6,2},{7,3},{8,12},{9,13},{10,... | collective-permute-start | bytes 3080 | tf_op jit(solution)/shard_map/ppermute | solution.py:131
Sparse Core Ops, SparseCore 0:
  12.8 65.2 all-gather.2

commit v15 on v13

--- a/solution.py
+++ b/solution.py
@@ -17,7 +17,7 @@
 CTX = ("chip", "core")
 
 
-def attend_kernel(pos_ref, qt_ref, kv_ref, o_ref, p_sc, p2_sc, m_sc, l_sc, c_sc, acc_sc, *, tok, width, chunk):
+def attend_kernel(pos_ref, qt_ref, kv_ref, o_ref, p_sc, m_sc, l_sc, c_sc, acc_sc, *, tok, width, chunk):
     position = pos_ref[0]
     score_factor = width ** (-0.5) * 1.4426950408889634
     rows = qt_ref.shape[1]
@@ -46,8 +46,8 @@
             l_sc[:, r0:r0 + chunk] = l_sc[:, r0:r0 + chunk] * correction_factor + jnp.sum(weights, axis=0, keepdims=True)
             m_sc[:, r0:r0 + chunk] = new_max
             c_sc[:, r0:r0 + chunk] = correction_factor
-            p_sc[:, r0:r0 + chunk] = weights.astype(jnp.bfloat16)
-        acc_sc[...] = acc_sc[...] * c_sc[...] + lax.dot_general(kv_ref[kb, 1], p_sc[...], (((0,), (0,)), ((), ())), preferred_element_type=jnp.float32)
+            p_sc[:block_rows, r0:r0 + chunk] = weights.astype(jnp.bfloat16)
+        acc_sc[...] = acc_sc[...] * c_sc[...] + lax.dot_general(kv_ref[kb, 1], p_sc[:block_rows], (((0,), (0,)), ((), ())), preferred_element_type=jnp.float32)
 
     def run_pair(kb):
         keys = (kv_ref[kb, 0], kv_ref[kb + 1, 0])
@@ -63,11 +63,11 @@
                 jnp.sum(weights[0], axis=0, keepdims=True) + jnp.sum(weights[1], axis=0, keepdims=True))
             m_sc[:, r0:r0 + chunk] = new_max
             c_sc[:, r0:r0 + chunk] = correction_factor
-            p_sc[:, r0:r0 + chunk] = weights[0].astype(jnp.bfloat16)
-            p2_sc[:, r0:r0 + chunk] = weights[1].astype(jnp.bfloat16)
-        acc_sc[...] = acc_sc[...] * c_sc[...] + (
-            lax.dot_general(kv_ref[kb, 1], p_sc[...], (((0,), (0,)), ((), ())), preferred_element_type=jnp.float32)
-            + lax.dot_general(kv_ref[kb + 1, 1], p2_sc[...], (((0,), (0,)), ((), ())), preferred_element_type=jnp.float32))
+            p_sc[:block_rows, r0:r0 + chunk] = weights[0].astype(jnp.bfloat16)
+            p_sc[block_rows:, r0:r0 + chunk] = weights[1].astype(jnp.bfloat16)
+        pair_values = kv_ref[pl.ds(kb, 2), 1].reshape(2 * block_rows, width)
+        acc_sc[...] = acc_sc[...] * c_sc[...] + lax.dot_general(
+            pair_values, p_sc[...], (((0,), (0,)), ((), ())), preferred_element_type=jnp.float32)
 
     def pair_body(i, carry):
         run_pair(2 * i)
@@ -96,8 +96,7 @@
         out_specs=pl.BlockSpec(memory_space=pltpu.VMEM),
         out_shape=jax.ShapeDtypeStruct(queries.shape, queries.dtype),
         scratch_shapes=[
-            pltpu.VMEM((tok_rows, rows), jnp.bfloat16),
-            pltpu.VMEM((tok_rows, rows), jnp.bfloat16),
+            pltpu.VMEM((2 * tok_rows, rows), jnp.bfloat16),
             pltpu.VMEM((1, rows), jnp.float32),
             pltpu.VMEM((1, rows), jnp.float32),
             pltpu.VMEM((1, rows), jnp.float32),

time: 124 us -> 125 us (level)
  no operation moved by 1% of the time
where the time goes in v15:
time: 125 us; the launch traced here: 124 us
  waiting for transfers between devices  48.7 us (39%)
  Pallas kernels  32.7 us (26%)
  between operations  14.5 us (12%)
  starting transfers between devices  12.1 us (10%)
  local copies, waits for them, and re-layouts  6.18 us (5%)
  other arithmetic  5.42 us (4%)
  matrix products  4.25 us (3%)
    ppermute x5, waiting for transfers between devices, shifted(): return lax.ppermute(block, axis, route)  38.5 us
    pallas_call x1, Pallas kernels, causal_attention(): pl.pallas_call(kernel, in_specs=[pl.BlockSpec(memory_space=pltpu.SMEM)] +...  32.7 us
    ppermute x3, waiting for transfers between devices, summed_over(): total = total + lax.ppermute(total, axis, route)  8.17 us
    ppermute x5, starting transfers between devices, shifted(): return lax.ppermute(block, axis, route)  6.46 us
    ppermute x3, starting transfers between devices, summed_over(): total = total + lax.ppermute(total, axis, route)  5.44 us
    unnamed x20, local copies, waits for them, and re-layouts  3.35 us
  transfers between devices with their start and end apart: 11, of which 10 were waited for; matrix products, arithmetic and copies ran while one was open for 9% of the time, Pallas kernels for 0%

profile of v15, /device:TPU:230, one launch (start us, length us, event | category | flops | bytes accessed | tf_op | source)
XLA Modules:
  0.0 123.8 jit_solution(8725409573572434150)
XLA Ops:
  7.2 0.0 copy-start
  7.2 0.0 copy-start.2
  7.2 0.0 all-gather.3.cloned.1.call-start
  7.2 0.8 reshape.1130
  8.0 0.0 copy-start.4
  8.0 0.6 reduce-window.6
  8.6 0.2 slice_reduce_fusion
  8.8 0.1 copy.42
  8.9 0.1 broadcast.184
  9.1 0.3 slice_reduce_fusion.1
  9.3 1.3 %copy.43 = bf16[256,1024]{0,1:T(8,128)(2,1)S(1)} copy(bf16[256,1024]{1,0:T(8,128)(2,1)} %param.14) | data formatting | bytes 1048576 | tf_op args[3]
  10.6 0.8 multiply_bitcast_fusion
  11.4 0.1 fusion.16
  11.5 0.3 fusion.79
  11.9 0.1 collective-permute-start
  12.0 0.7 pad_maximum_fusion.4
  12.7 0.0 all-gather.3.cloned.1.call-update
  12.7 0.8 collective-permute-done
  13.6 0.1 fusion.66
  13.7 0.1 dynamic-slice.5
  13.8 0.1 broadcast_select_fusion
  13.9 0.1 fusion.23
  14.0 1.3 %collective-permute-start.2 = (bf16[1,528,128]{2,1,0:T(8,128)(2,1)S(1)}, bf16[1,528,128]{2,1,0:T(8,128)(2,1)S(1)}, u32[]{:S(2)}, u32[]{:S(2)}) collective-permute-start(bf16[1,528,128]{2,1,0:T(8,128)(2,1)S(1)} %pad_maximum_fusion), channel_id=1, source_target_pairs={{0,32},{16,48},{32,64},{48,80},{64,96},{80,112},{96,128},{112,144}... | collective-permute-start | bytes 405512 | tf_op jit(solution)/shard_map/ppermute | solution.py:111
  15.3 0.9 fusion.80
  16.2 1.3 %collective-permute-start.1 = (bf16[1,528,128]{2,1,0:T(8,128)(2,1)S(1)}, bf16[1,528,128]{2,1,0:T(8,128)(2,1)S(1)}, u32[]{:S(2)}, u32[]{:S(2)}) collective-permute-start(bf16[1,528,128]{2,1,0:T(8,128)(2,1)S(1)} %pad_maximum_fusion), channel_id=1, source_target_pairs={{0,16},{16,32},{32,48},{48,64},{64,80},{80,96},{96,112},{112,128},... | collective-permute-start | bytes 405512 | tf_op jit(solution)/shard_map/ppermute | solution.py:111
  17.5 8.3 %collective-permute-done.2 = bf16[1,528,128]{2,1,0:T(8,128)(2,1)S(1)} collective-permute-done((bf16[1,528,128]{2,1,0:T(8,128)(2,1)S(1)}, bf16[1,528,128]{2,1,0:T(8,128)(2,1)S(1)}, u32[]{:S(2)}, u32[]{:S(2)}) %collective-permute-start.2) | collective-permute-done | bytes 135200 | tf_op jit(solution)/shard_map/ppermute | solution.py:111
  25.9 0.2 collective-permute-done.1
  26.1 0.1 mul.266
  26.2 0.1 mul.267
  26.3 0.1 fusion.28
  26.4 1.3 %collective-permute-start.3 = (bf16[1,528,128]{2,1,0:T(8,128)(2,1)S(1)}, bf16[1,528,128]{2,1,0:T(8,128)(2,1)S(1)}, u32[]{:S(2)}, u32[]{:S(2)}) collective-permute-start(bf16[1,528,128]{2,1,0:T(8,128)(2,1)S(1)} %pad_maximum_fusion.1), channel_id=1, source_target_pairs={{0,32},{16,48},{32,64},{48,80},{64,96},{80,112},{96,128},{112,144}... | collective-permute-start | bytes 405512 | tf_op jit(solution)/shard_map/ppermute | solution.py:111
  27.7 0.1 mul.270
  27.8 0.1 mul.271
  27.9 6.7 %collective-permute-done.3 = bf16[1,528,128]{2,1,0:T(8,128)(2,1)S(1)} collective-permute-done((bf16[1,528,128]{2,1,0:T(8,128)(2,1)S(1)}, bf16[1,528,128]{2,1,0:T(8,128)(2,1)S(1)}, u32[]{:S(2)}, u32[]{:S(2)}) %collective-permute-start.3) | collective-permute-done | bytes 135200 | tf_op jit(solution)/shard_map/ppermute | solution.py:111
  34.7 0.2 fusion.77
  34.9 0.0 copy-start.5
  34.9 0.0 copy-start.7
  35.0 1.3 %collective-permute-start.4 = (bf16[1,528,128]{2,1,0:T(8,128)(2,1)S(1)}, bf16[1,528,128]{2,1,0:T(8,128)(2,1)S(1)}, u32[]{:S(2)}, u32[]{:S(2)}) collective-permute-start(bf16[1,528,128]{2,1,0:T(8,128)(2,1)S(1)} %pad_maximum_fusion.2), channel_id=1, source_target_pairs={{0,64},{16,80},{32,96},{48,112},{64,128},{80,144},{96,160},{112,17... | collective-permute-start | bytes 405512 | tf_op jit(solution)/shard_map/ppermute | solution.py:111
  36.3 0.1 mul.275
  36.3 0.1 mul.276
  36.4 10.5 %collective-permute-done.4 = bf16[1,528,128]{2,1,0:T(8,128)(2,1)S(1)} collective-permute-done((bf16[1,528,128]{2,1,0:T(8,128)(2,1)S(1)}, bf16[1,528,128]{2,1,0:T(8,128)(2,1)S(1)}, u32[]{:S(2)}, u32[]{:S(2)}) %collective-permute-start.4) | collective-permute-done | bytes 135200 | tf_op jit(solution)/shard_map/ppermute | solution.py:111
  46.9 0.3 add_convert_fusion.1
  47.2 1.3 %collective-permute-start.5 = (bf16[1,528,128]{2,1,0:T(8,128)(2,1)S(1)}, bf16[1,528,128]{2,1,0:T(8,128)(2,1)S(1)}, u32[]{:S(2)}, u32[]{:S(2)}) collective-permute-start(bf16[1,528,128]{2,1,0:T(8,128)(2,1)S(1)} %pad_maximum_fusion.3), channel_id=1, source_target_pairs={{0,128},{16,144},{32,160},{48,176},{64,192},{80,208},{96,224},{112... | collective-permute-start | bytes 405512 | tf_op jit(solution)/shard_map/ppermute | solution.py:111
  48.6 12.8 %collective-permute-done.5 = bf16[1,528,128]{2,1,0:T(8,128)(2,1)S(1)} collective-permute-done((bf16[1,528,128]{2,1,0:T(8,128)(2,1)S(1)}, bf16[1,528,128]{2,1,0:T(8,128)(2,1)S(1)}, u32[]{:S(2)}, u32[]{:S(2)}) %collective-permute-start.5) | collective-permute-done | bytes 135200 | tf_op jit(solution)/shard_map/ppermute | solution.py:111
  61.4 0.2 add_convert_fusion
  61.5 0.1 collective-permute-start.6
  61.6 0.2 add_add_fusion
  61.8 1.2 collective-permute-done.6
  63.0 0.7 fusion.9
  63.7 0.0 copy-start.1
  63.7 2.4 %fusion.11 = f32[256,1,16,64]{0,3,2,1:T(8,128)S(1)} fusion(f32[256,1,16,64]{0,3,2,1:T(8,128)S(1)} %fusion.9, bf16[256,16,64]{0,2,1:T(8,128)(2,1)S(1)} %bitcast.144, f32[16,256]{1,0:T(8,128)S(1)} %copy-done.5, f32[16,256]{1,0:T(8,128)S(1)} %get-tuple-element.15, f32[256,256]{1,0:T(8,128)} %fusion.80, pred[256,256]{1,0:T(8,128)(4,1)S(1)} %iota_compare_fusion.1, ...), kind=kOutput, calls=%fused_computation.13 | convolution fusion | flops 141557760 | bytes 3506240 | tf_op jit(solution)/shard_map/ghts,sghp->tghp/dot_general | solution.py:225
  66.1 0.3 copy.46
  66.5 0.4 multiply_reduce_fusion
  66.9 1.9 %collective-permute-start.7 = (f32[256]{0:T(256)S(1)}, f32[256]{0:T(256)S(1)}, u32[]{:S(2)}, u32[]{:S(2)}) collective-permute-start(f32[256]{0:T(256)S(1)} %multiply_reduce_fusion), channel_id=1, source_target_pairs={{0,1},{1,0},{2,3},{3,2},{4,5},{5,4},{6,7},{7,6},{8,9},{9,8},{10,11... | collective-permute-start | bytes 3080 | tf_op jit(solution)/shard_map/ppermute | solution.py:120
  68.7 1.8 %collective-permute-done.7 = f32[256]{0:T(256)S(1)} collective-permute-done((f32[256]{0:T(256)S(1)}, f32[256]{0:T(256)S(1)}, u32[]{:S(2)}, u32[]{:S(2)}) %collective-permute-start.7) | collective-permute-done | bytes 1056 | tf_op jit(solution)/shard_map/ppermute | solution.py:120
  70.5 3.6 %collective-permute-start.8 = (f32[256]{0:T(256)S(1)}, f32[256]{0:T(256)S(1)}, u32[]{:S(2)}, u32[]{:S(2)}) collective-permute-start(f32[256]{0:T(256)S(1)} %add.588), channel_id=1, source_target_pairs={{0,2},{1,3},{2,0},{3,1},{4,6},{5,7},{6,4},{7,5},{8,10},{9,11},{10,... | collective-permute-start | bytes 3080 | tf_op jit(solution)/shard_map/ppermute | solution.py:120
  74.1 1.5 %collective-permute-done.8 = f32[256]{0:T(256)S(1)} collective-permute-done((f32[256]{0:T(256)S(1)}, f32[256]{0:T(256)S(1)}, u32[]{:S(2)}, u32[]{:S(2)}) %collective-permute-start.8) | collective-permute-done | bytes 1056 | tf_op jit(solution)/shard_map/ppermute | solution.py:120
  75.6 0.0 collective-permute-start.9
  75.6 1.1 copy.48
  76.8 0.6 copy.39
  77.3 0.9 copy.49
  78.3 4.8 %collective-permute-done.9 = f32[256]{0:T(256)S(1)} collective-permute-done((f32[256]{0:T(256)S(1)}, f32[256]{0:T(256)S(1)}, u32[]{:S(2)}, u32[]{:S(2)}) %collective-permute-start.9) | collective-permute-done | bytes 1056 | tf_op jit(solution)/shard_map/ppermute | solution.py:120
  83.1 1.2 multiply_convert_fusion
  84.3 32.7 %shard_map.122 = bf16[256,1024]{1,0:T(8,128)(2,1)} custom-call(s32[1]{0:T(128)} %bitcast.pos_ref, bf16[128,2048]{1,0:T(8,128)(2,1)} %bitcast.149, bf16[32,2,256,128]{3,2,1,0:T(8,128)(2,1)} %bitcast.129), custom_call_target="tpu_custom_call" | custom-call | tf_op jit(solution)/shard_map/pallas_call | solution.py:93
  (56 shorter events, 0.6 us)
Async XLA Ops:
  7.2 4.4 %copy-start = (bf16[256,128]{1,0:T(8,128)(2,1)S(1)}, bf16[256,128]{1,0:T(8,128)(2,1)}, u32[]{:S(2)}) copy-start(bf16[256,128]{1,0:T(8,128)(2,1)} %param.16) | copy-start | bytes 196612
  7.2 4.8 %copy-start.2 = (bf16[256,128]{1,0:T(8,128)(2,1)S(1)}, bf16[256,128]{1,0:T(8,128)(2,1)}, u32[]{:S(2)}) copy-start(bf16[256,128]{1,0:T(8,128)(2,1)} %param.13) | copy-start | bytes 196612
  7.2 4.8 %copy-start.3 = (bf16[256,128]{1,0:T(8,128)(2,1)S(1)}, bf16[256,128]{1,0:T(8,128)(2,1)}, u32[]{:S(2)}) copy-start(bf16[256,128]{1,0:T(8,128)(2,1)} %param.12) | copy-start | bytes 196612
  7.2 77.1 %all-gather.3.cloned.1.call-start = ((), (), s32[]{:S(2)}) async-start(), calls=%async_computation | async-start | bytes 4325376 | tf_op jit(solution)/shard_map/all_gather | solution.py:209
  8.0 7.3 %copy-start.4 = (bf16[256,128]{1,0:T(8,128)(2,1)S(1)}, bf16[256,128]{1,0:T(8,128)(2,1)}, u32[]{:S(2)}) copy-start(bf16[256,128]{1,0:T(8,128)(2,1)} %param.17) | copy-start | bytes 196612
  11.9 1.6 %collective-permute-start = (bf16[1,1040,128]{2,1,0:T(8,128)(2,1)S(1)}, bf16[1,1040,128]{2,1,0:T(8,128)(2,1)S(1)}, u32[]{:S(2)}, u32[]{:S(2)}) collective-permute-start(bf16[1,1040,128]{2,1,0:T(8,128)(2,1)S(1)} %fusion.21), channel_id=1, source_target_pairs={{0,8},{8,0},{1,9},{9,1},{2,10},{10,2},{3,11},{11,3},{4,12},{12,4},... | collective-permute-start | bytes 798728 | tf_op jit(solution)/shard_map/ppermute | solution.py:168
  14.0 11.9 %collective-permute-start.2 = (bf16[1,528,128]{2,1,0:T(8,128)(2,1)S(1)}, bf16[1,528,128]{2,1,0:T(8,128)(2,1)S(1)}, u32[]{:S(2)}, u32[]{:S(2)}) collective-permute-start(bf16[1,528,128]{2,1,0:T(8,128)(2,1)S(1)} %pad_maximum_fusion), channel_id=1, source_target_pairs={{0,32},{16,48},{32,64},{48,80},{64,96},{80,112},{96,128},{112,144}... | collective-permute-start | bytes 405512 | tf_op jit(solution)/shard_map/ppermute | solution.py:111
  16.2 9.9 %collective-permute-start.1 = (bf16[1,528,128]{2,1,0:T(8,128)(2,1)S(1)}, bf16[1,528,128]{2,1,0:T(8,128)(2,1)S(1)}, u32[]{:S(2)}, u32[]{:S(2)}) collective-permute-start(bf16[1,528,128]{2,1,0:T(8,128)(2,1)S(1)} %pad_maximum_fusion), channel_id=1, source_target_pairs={{0,16},{16,32},{32,48},{48,64},{64,80},{80,96},{96,112},{112,128},... | collective-permute-start | bytes 405512 | tf_op jit(solution)/shard_map/ppermute | solution.py:111
  26.4 8.2 %collective-permute-start.3 = (bf16[1,528,128]{2,1,0:T(8,128)(2,1)S(1)}, bf16[1,528,128]{2,1,0:T(8,128)(2,1)S(1)}, u32[]{:S(2)}, u32[]{:S(2)}) collective-permute-start(bf16[1,528,128]{2,1,0:T(8,128)(2,1)S(1)} %pad_maximum_fusion.1), channel_id=1, source_target_pairs={{0,32},{16,48},{32,64},{48,80},{64,96},{80,112},{96,128},{112,144}... | collective-permute-start | bytes 405512 | tf_op jit(solution)/shard_map/ppermute | solution.py:111
  34.9 28.7 %copy-start.5 = (f32[16,256]{1,0:T(8,128)S(1)}, f32[16,256]{1,0:T(8,128)}, u32[]{:S(2)}) copy-start(f32[16,256]{1,0:T(8,128)} %param.18) | copy-start | bytes 49156
  34.9 28.7 %copy-start.7 = (f32[16]{0:T(128)S(1)}, f32[16]{0:T(128)}, u32[]{:S(2)}) copy-start(f32[16]{0:T(128)} %param.20) | copy-start | bytes 196
  35.0 11.9 %collective-permute-start.4 = (bf16[1,528,128]{2,1,0:T(8,128)(2,1)S(1)}, bf16[1,528,128]{2,1,0:T(8,128)(2,1)S(1)}, u32[]{:S(2)}, u32[]{:S(2)}) collective-permute-start(bf16[1,528,128]{2,1,0:T(8,128)(2,1)S(1)} %pad_maximum_fusion.2), channel_id=1, source_target_pairs={{0,64},{16,80},{32,96},{48,112},{64,128},{80,144},{96,160},{112,17... | collective-permute-start | bytes 405512 | tf_op jit(solution)/shard_map/ppermute | solution.py:111
  47.2 14.1 %collective-permute-start.5 = (bf16[1,528,128]{2,1,0:T(8,128)(2,1)S(1)}, bf16[1,528,128]{2,1,0:T(8,128)(2,1)S(1)}, u32[]{:S(2)}, u32[]{:S(2)}) collective-permute-start(bf16[1,528,128]{2,1,0:T(8,128)(2,1)S(1)} %pad_maximum_fusion.3), channel_id=1, source_target_pairs={{0,128},{16,144},{32,160},{48,176},{64,192},{80,208},{96,224},{112... | collective-permute-start | bytes 405512 | tf_op jit(solution)/shard_map/ppermute | solution.py:111
  61.5 1.4 %collective-permute-start.6 = (bf16[1,8,64,128]{3,2,1,0:T(8,128)(2,1)S(1)}, bf16[1,8,64,128]{3,2,1,0:T(8,128)(2,1)S(1)}, u32[]{:S(2)}, u32[]{:S(2)}) collective-permute-start(bf16[1,8,64,128]{3,2,1,0:T(8,128)(2,1)S(1)} %add_convert_fusion), channel_id=1, source_target_pairs={{0,8},{8,0},{1,9},{9,1},{2,10},{10,2},{3,11},{11,3},{4,12},{12,4},... | collective-permute-start | bytes 393224 | tf_op jit(solution)/shard_map/ppermute | solution.py:182
  63.7 2.8 %copy-start.1 = (bf16[256,1024]{1,0:T(8,128)(2,1)S(1)}, bf16[256,1024]{1,0:T(8,128)(2,1)}, u32[]{:S(2)}) copy-start(bf16[256,1024]{1,0:T(8,128)(2,1)} %param.15) | copy-start | bytes 1572868
  66.1 12.2 %copy-start.6 = (bf16[1024]{0:T(1024)(128)(2,1)S(1)}, bf16[1024]{0:T(1024)(128)(2,1)}, u32[]{:S(2)}) copy-start(bf16[1024]{0:T(1024)(128)(2,1)} %param.21) | copy-start | bytes 6148
  66.9 3.6 %collective-permute-start.7 = (f32[256]{0:T(256)S(1)}, f32[256]{0:T(256)S(1)}, u32[]{:S(2)}, u32[]{:S(2)}) collective-permute-start(f32[256]{0:T(256)S(1)} %multiply_reduce_fusion), channel_id=1, source_target_pairs={{0,1},{1,0},{2,3},{3,2},{4,5},{5,4},{6,7},{7,6},{8,9},{9,8},{10,11... | collective-permute-start | bytes 3080 | tf_op jit(solution)/shard_map/ppermute | solution.py:120
  70.5 5.1 %collective-permute-start.8 = (f32[256]{0:T(256)S(1)}, f32[256]{0:T(256)S(1)}, u32[]{:S(2)}, u32[]{:S(2)}) collective-permute-start(f32[256]{0:T(256)S(1)} %add.588), channel_id=1, source_target_pairs={{0,2},{1,3},{2,0},{3,1},{4,6},{5,7},{6,4},{7,5},{8,10},{9,11},{10,... | collective-permute-start | bytes 3080 | tf_op jit(solution)/shard_map/ppermute | solution.py:120
  75.6 7.5 %collective-permute-start.9 = (f32[256]{0:T(256)S(1)}, f32[256]{0:T(256)S(1)}, u32[]{:S(2)}, u32[]{:S(2)}) collective-permute-start(f32[256]{0:T(256)S(1)} %add.589), channel_id=1, source_target_pairs={{0,4},{1,5},{2,6},{3,7},{4,0},{5,1},{6,2},{7,3},{8,12},{9,13},{10,... | collective-permute-start | bytes 3080 | tf_op jit(solution)/shard_map/ppermute | solution.py:120
Sparse Core Ops, SparseCore 0:
  12.8 65.2 all-gather.2
